TPU v7x, 32 devices: a whole 2x2x4 slice. The times are simulated.
32 devices in a mesh: section: 4 (over y, x), expert: 8 (over z, core).
Axes of the slice: x: 2, y: 2, z: 4, core: 2. Of those that a mesh axis runs over, the one named last changes fastest.
Arguments:
- tokens: bfloat16 [4, 128, 2048], P(None, 'expert'), may hold values from -6 to 6
- norm_gain: float32 [4, 2048], P('section'), may hold values from 0.1 to 1.9
- gate_weight: bfloat16 [4, 16, 2048, 768], P('section', 'expert'), may hold values from -0.125 to 0.125
- up_weight: bfloat16 [4, 16, 2048, 768], P('section', 'expert'), may hold values from -0.125 to 0.125
- down_weight: bfloat16 [4, 16, 768, 2048], P('section', 'expert'), may hold values from -0.21875 to 0.21875
- routes: int32 [4, 4, 128, 8], P('section', None, 'expert'), may hold values from 0 to 15, all different within a row; in each aligned block of 16 rows (0 to 15, 16 to 31, ..., all dimensions but the last counted through in order) at most 12 rows name the same one
- gates: float32 [4, 4, 128, 8], P('section', None, 'expert'), may hold values from 0.1 to 1
Outputs:
- hidden_states: bfloat16 [4, 4, 128, 2048], P('section', None, 'expert')
Inputs may be any that keep to these rules, and one draw needn't show every extreme that they name: `routes`: within one section and micro-batch, the 16 tokens of one device name any one expert at most 12 times, a bound that some expert reaches in some of these blocks; the 8 experts of a token differ.
All inputs are finite; a program needn't handle non-finite values.
Results may differ from a plain program's by a relative error of at most 0.012.
Values may be sent and summed in bfloat16 or wider, within the bound.
No kernel may reach another device: no remote copies, remote signals or barrier semaphores. Data moves between devices by JAX's collectives and lax.ppermute only.
A program may use at most 128 MiB of HBM per device.

v0:
```python
import jax
import jax.numpy as jnp
from jax import lax
from jax.sharding import PartitionSpec as P

MB = 4


EPSILON = 1e-06


def shifted(array, axis, by):
    count = lax.axis_size(axis)
    pairs = [(i, i + by) for i in range(count) if 0 <= i + by < count]
    return lax.ppermute(array, axis, pairs)


def place_slots(expert_ids, experts):
    onehot = (expert_ids[:, None] == jnp.arange(experts, dtype=jnp.int32)[None, :]).astype(
        jnp.int32
    )
    before = jnp.cumsum(onehot, axis=0) - onehot
    return jnp.sum(before * onehot, axis=1)


def rms_normed(hidden, gain):
    values = hidden.astype(jnp.float32)
    scale = lax.rsqrt(jnp.mean(values * values, axis=-1, keepdims=True) + EPSILON)
    return (values, (values * scale * gain).astype(jnp.bfloat16))


def on_device(tokens, norm_gain, gate_weight, up_weight, down_weight, routes, gates):
    devices = lax.axis_size("expert")
    sections = lax.axis_size("section")
    section_index = lax.axis_index("section")
    local_experts = gate_weight.shape[1]
    experts = local_experts * devices
    tok_rows = tokens.shape[1]
    width = tokens.shape[2]
    topk = routes.shape[3]
    capacity = tok_rows * topk * 3 // (2 * experts)
    gain = norm_gain[0]
    w_gate = gate_weight[0]
    w_up = up_weight[0]
    w_down = down_weight[0]
    held = jnp.zeros((tok_rows, width), jnp.bfloat16)
    collected = jnp.zeros((MB, tok_rows, width), jnp.bfloat16)
    for moment in range(MB + sections - 1):
        if moment > 0:
            arrived = shifted(held, "section", 1)
        else:
            arrived = held
        batch_index = moment - section_index
        active = (batch_index >= 0) & (batch_index < MB)
        clipped = jnp.clip(batch_index, 0, MB - 1)
        first_rows = lax.dynamic_index_in_dim(tokens, clipped, 0, keepdims=False)
        incoming = jnp.where(section_index == 0, first_rows, arrived)
        expert_ids = lax.dynamic_index_in_dim(routes[0], clipped, 0, keepdims=False)
        gate_values = lax.dynamic_index_in_dim(gates[0], clipped, 0, keepdims=False)
        values, normed = rms_normed(incoming, gain)
        flat_ids = expert_ids.reshape(-1)
        slot_index = place_slots(flat_ids, experts)
        token_index = jnp.arange(tok_rows * topk, dtype=jnp.int32) // topk
        outgoing = jnp.zeros((experts, capacity, width), jnp.bfloat16)
        outgoing = outgoing.at[flat_ids, slot_index].set(normed[token_index])
        outgoing = outgoing.reshape(devices, local_experts, capacity, width)
        received = lax.all_to_all(outgoing, "expert", split_axis=0, concat_axis=0, tiled=True)
        gate_part = jnp.einsum(
            "nesd,edf->nesf", received, w_gate, preferred_element_type=jnp.float32
        )
        up_part = jnp.einsum("nesd,edf->nesf", received, w_up, preferred_element_type=jnp.float32)
        inner = (jax.nn.silu(gate_part) * up_part).astype(jnp.bfloat16)
        returned = lax.all_to_all(
            jnp.einsum("nesf,efd->nesd", inner, w_down, preferred_element_type=jnp.float32).astype(
                jnp.bfloat16
            ),
            "expert",
            split_axis=0,
            concat_axis=0,
            tiled=True,
        )
        returned = returned.reshape(experts, capacity, width)
        picked = returned[flat_ids, slot_index].reshape(tok_rows, topk, width)
        weights = gate_values / jnp.sum(gate_values, axis=-1, keepdims=True)
        mixed = jnp.sum(weights[:, :, None] * picked.astype(jnp.float32), axis=1)
        produced = (values + mixed).astype(jnp.bfloat16)
        held = jnp.where(active, produced, incoming)
        updated = lax.dynamic_update_index_in_dim(collected, held, clipped, 0)
        collected = jnp.where(active, updated, collected)
    return collected[None]


def solution(mesh):
    placed = (
        P(None, "expert", None),
        P("section", None),
        P("section", "expert", None, None),
        P("section", "expert", None, None),
        P("section", "expert", None, None),
        P("section", None, "expert", None),
        P("section", None, "expert", None),
    )
    return jax.shard_map(
        on_device,
        mesh=mesh,
        in_specs=placed,
        out_specs=P("section", None, "expert", None),
        check_vma=False,
    )
```

profile of v0, /device:TPU:0, one launch (start us, length us, event | category | flops | bytes accessed | tf_op | source)
XLA Modules:
  0.0 596.5 jit_solution(2576998763865678790)
XLA Ops:
  5.2 11.9 %scatter_fusion = bf16[16,12,2048]{2,0,1:T(8,128)(2,1)S(1)} fusion(bf16[16,12,2048]{2,0,1:T(8,128)(2,1)S(1)} %broadcast.475.clone, s32[128]{0:T(128)S(1)} %get-tuple-element.46, bf16[128,2048]{1,0:T(8,128)(2,1)S(1)} %gather_fusion), kind=kCustom, calls=%fused_computation.14 | custom fusion | bytes 1573888 | tf_op jit(solution)/shard_map/scatter | solution.py:65
  18.2 27.1 %all_to_all.70 = bf16[8,2,12,2048]{3,1,2,0:T(2,128)(2,1)S(1)} all-to-all(bf16[8,2,12,2048]{3,1,2,0:T(2,128)(2,1)S(1)} %copy.67), channel_id=1, replica_groups=mesh['section'=4,'expert'=8] {'expert'}, dimensions={0} | all-to-all | bytes 1572864 | tf_op jit(solution)/shard_map/all_to_all | solution.py:67
  49.2 6.8 %fusion.81 = bf16[8,2,12,2048]{3,2,0,1:T(8,128)(2,1)S(1)} fusion(bf16[1,2,768,2048]{3,2,1,0:T(8,128)(2,1)} %param.11, bf16[1,2,2048,768]{3,2,1,0:T(8,128)(2,1)} %param.10, bf16[8,2,12,2048]{3,1,2,0:T(2,128)(2,1)S(1)} %all_to_all.70, f32[8,2,12,768]{3,2,0,1:T(8,128)S(1)} %fusion.84), kind=kOutput, calls=%fused_computation.76 | convolution fusion | flops 1209237504 | bytes 14745600 | tf_op jit(solution)/shard_map/nesf,efd->nesd/dot_general | solution.py:74
  61.4 20.7 %all-to-all-done.1 = bf16[8,2,12,2048]{3,1,2,0:T(2,128)(2,1)S(1)} async-done(((bf16[8,2,12,2048]{3,1,2,0:T(2,128)(2,1)}), bf16[8,2,12,2048]{3,1,2,0:T(2,128)(2,1)S(1)}, u32[]{:S(2)}, u32[]{:S(2)}) %all-to-all-start.1) | async-done | bytes 786464 | tf_op jit(solution)/shard_map/all_to_all | solution.py:73
  92.7 11.9 %scatter_fusion.1 = bf16[16,12,2048]{2,0,1:T(8,128)(2,1)S(1)} fusion(bf16[16,12,2048]{2,0,1:T(8,128)(2,1)S(1)} %broadcast.475.clone.1, s32[128]{0:T(128)S(1)} %get-tuple-element.62, bf16[128,2048]{1,0:T(8,128)(2,1)S(1)} %gather_fusion.2), kind=kCustom, calls=%fused_computation.15 | custom fusion | bytes 1573888 | tf_op jit(solution)/shard_map/scatter | solution.py:65
  105.6 23.4 %all_to_all.71 = bf16[8,2,12,2048]{3,1,2,0:T(2,128)(2,1)S(1)} all-to-all(bf16[8,2,12,2048]{3,1,2,0:T(2,128)(2,1)S(1)} %copy.75), channel_id=1, replica_groups=mesh['section'=4,'expert'=8] {'expert'}, dimensions={0} | all-to-all | bytes 1572864 | tf_op jit(solution)/shard_map/all_to_all | solution.py:67
  132.9 6.8 %fusion.78 = bf16[8,2,12,2048]{3,2,0,1:T(8,128)(2,1)S(1)} fusion(bf16[1,2,768,2048]{3,2,1,0:T(8,128)(2,1)} %param.11, bf16[1,2,2048,768]{3,2,1,0:T(8,128)(2,1)} %param.10, bf16[8,2,12,2048]{3,1,2,0:T(2,128)(2,1)S(1)} %all_to_all.71, f32[8,2,12,768]{3,2,0,1:T(8,128)S(1)} %fusion.87), kind=kOutput, calls=%fused_computation.75 | convolution fusion | flops 1209237504 | bytes 14745600 | tf_op jit(solution)/shard_map/nesf,efd->nesd/dot_general | solution.py:74
  146.5 19.3 %all-to-all-done.3 = bf16[8,2,12,2048]{3,1,2,0:T(2,128)(2,1)S(1)} async-done(((bf16[8,2,12,2048]{3,1,2,0:T(2,128)(2,1)}), bf16[8,2,12,2048]{3,1,2,0:T(2,128)(2,1)S(1)}, u32[]{:S(2)}, u32[]{:S(2)}) %all-to-all-start.3) | async-done | bytes 786464 | tf_op jit(solution)/shard_map/all_to_all | solution.py:73
  177.2 11.9 %scatter_fusion.2 = bf16[16,12,2048]{2,0,1:T(8,128)(2,1)S(1)} fusion(bf16[16,12,2048]{2,0,1:T(8,128)(2,1)S(1)} %broadcast.475.clone.2, s32[128]{0:T(128)S(1)} %get-tuple-element.38, bf16[128,2048]{1,0:T(8,128)(2,1)S(1)} %gather_fusion.4), kind=kCustom, calls=%fused_computation.16 | custom fusion | bytes 1573888 | tf_op jit(solution)/shard_map/scatter | solution.py:65
  190.1 23.4 %all_to_all.72 = bf16[8,2,12,2048]{3,1,2,0:T(2,128)(2,1)S(1)} all-to-all(bf16[8,2,12,2048]{3,1,2,0:T(2,128)(2,1)S(1)} %copy.83), channel_id=1, replica_groups=mesh['section'=4,'expert'=8] {'expert'}, dimensions={0} | all-to-all | bytes 1572864 | tf_op jit(solution)/shard_map/all_to_all | solution.py:67
  217.5 6.8 %fusion.75 = bf16[8,2,12,2048]{3,2,0,1:T(8,128)(2,1)S(1)} fusion(bf16[1,2,768,2048]{3,2,1,0:T(8,128)(2,1)} %param.11, bf16[1,2,2048,768]{3,2,1,0:T(8,128)(2,1)} %param.10, bf16[8,2,12,2048]{3,1,2,0:T(2,128)(2,1)S(1)} %all_to_all.72, f32[8,2,12,768]{3,2,0,1:T(8,128)S(1)} %fusion.90), kind=kOutput, calls=%fused_computation.74 | convolution fusion | flops 1209237504 | bytes 14745600 | tf_op jit(solution)/shard_map/nesf,efd->nesd/dot_general | solution.py:74
  229.6 20.8 %all-to-all-done.5 = bf16[8,2,12,2048]{3,1,2,0:T(2,128)(2,1)S(1)} async-done(((bf16[8,2,12,2048]{3,1,2,0:T(2,128)(2,1)}), bf16[8,2,12,2048]{3,1,2,0:T(2,128)(2,1)S(1)}, u32[]{:S(2)}, u32[]{:S(2)}) %all-to-all-start.5) | async-done | bytes 786464 | tf_op jit(solution)/shard_map/all_to_all | solution.py:73
  254.3 4.7 collective-permute-start.2
  261.8 11.8 %scatter_fusion.3 = bf16[16,12,2048]{2,0,1:T(8,128)(2,1)S(1)} fusion(bf16[16,12,2048]{2,0,1:T(8,128)(2,1)S(1)} %broadcast.475.clone.3, s32[128]{0:T(128)S(1)} %get-tuple-element.64, bf16[128,2048]{1,0:T(8,128)(2,1)S(1)} %gather_fusion.6), kind=kCustom, calls=%fused_computation.17 | custom fusion | bytes 1573888 | tf_op jit(solution)/shard_map/scatter | solution.py:65
  274.8 23.4 %all_to_all.73 = bf16[8,2,12,2048]{3,1,2,0:T(2,128)(2,1)S(1)} all-to-all(bf16[8,2,12,2048]{3,1,2,0:T(2,128)(2,1)S(1)} %copy.91), channel_id=1, replica_groups=mesh['section'=4,'expert'=8] {'expert'}, dimensions={0} | all-to-all | bytes 1572864 | tf_op jit(solution)/shard_map/all_to_all | solution.py:67
  302.1 6.8 %fusion.72 = bf16[8,2,12,2048]{3,2,0,1:T(8,128)(2,1)S(1)} fusion(bf16[1,2,768,2048]{3,2,1,0:T(8,128)(2,1)} %param.11, bf16[1,2,2048,768]{3,2,1,0:T(8,128)(2,1)} %param.10, bf16[8,2,12,2048]{3,1,2,0:T(2,128)(2,1)S(1)} %all_to_all.73, f32[8,2,12,768]{3,2,0,1:T(8,128)S(1)} %fusion.93), kind=kOutput, calls=%fused_computation.73 | convolution fusion | flops 1209237504 | bytes 14745600 | tf_op jit(solution)/shard_map/nesf,efd->nesd/dot_general | solution.py:74
  315.6 19.4 %all-to-all-done.7 = bf16[8,2,12,2048]{3,1,2,0:T(2,128)(2,1)S(1)} async-done(((bf16[8,2,12,2048]{3,1,2,0:T(2,128)(2,1)}), bf16[8,2,12,2048]{3,1,2,0:T(2,128)(2,1)S(1)}, u32[]{:S(2)}, u32[]{:S(2)}) %all-to-all-start.7) | async-done | bytes 786464 | tf_op jit(solution)/shard_map/all_to_all | solution.py:73
  338.9 5.3 collective-permute-start.3
  347.2 11.8 %scatter_fusion.4 = bf16[16,12,2048]{2,0,1:T(8,128)(2,1)S(1)} fusion(bf16[16,12,2048]{2,0,1:T(8,128)(2,1)S(1)} %broadcast.475.clone.4, s32[128]{0:T(128)S(1)} %get-tuple-element.26, bf16[128,2048]{1,0:T(8,128)(2,1)S(1)} %gather_fusion.8), kind=kCustom, calls=%fused_computation.18 | custom fusion | bytes 1573888 | tf_op jit(solution)/shard_map/scatter | solution.py:65
  360.2 23.4 %all_to_all.74 = bf16[8,2,12,2048]{3,1,2,0:T(2,128)(2,1)S(1)} all-to-all(bf16[8,2,12,2048]{3,1,2,0:T(2,128)(2,1)S(1)} %copy.99), channel_id=1, replica_groups=mesh['section'=4,'expert'=8] {'expert'}, dimensions={0} | all-to-all | bytes 1572864 | tf_op jit(solution)/shard_map/all_to_all | solution.py:67
  387.5 6.8 %fusion.69 = bf16[8,2,12,2048]{3,2,0,1:T(8,128)(2,1)S(1)} fusion(bf16[1,2,768,2048]{3,2,1,0:T(8,128)(2,1)} %param.11, bf16[1,2,2048,768]{3,2,1,0:T(8,128)(2,1)} %param.10, bf16[8,2,12,2048]{3,1,2,0:T(2,128)(2,1)S(1)} %all_to_all.74, f32[8,2,12,768]{3,2,0,1:T(8,128)S(1)} %fusion.96), kind=kOutput, calls=%fused_computation.72 | convolution fusion | flops 1209237504 | bytes 14745600 | tf_op jit(solution)/shard_map/nesf,efd->nesd/dot_general | solution.py:74
  399.6 20.8 %all-to-all-done.9 = bf16[8,2,12,2048]{3,1,2,0:T(2,128)(2,1)S(1)} async-done(((bf16[8,2,12,2048]{3,1,2,0:T(2,128)(2,1)}), bf16[8,2,12,2048]{3,1,2,0:T(2,128)(2,1)S(1)}, u32[]{:S(2)}, u32[]{:S(2)}) %all-to-all-start.9) | async-done | bytes 786464 | tf_op jit(solution)/shard_map/all_to_all | solution.py:73
  424.3 5.4 collective-permute-start.4
  432.7 11.8 %scatter_fusion.5 = bf16[16,12,2048]{2,0,1:T(8,128)(2,1)S(1)} fusion(bf16[16,12,2048]{2,0,1:T(8,128)(2,1)S(1)} %broadcast.475.clone.5, s32[128]{0:T(128)S(1)} %get-tuple-element.66, bf16[128,2048]{1,0:T(8,128)(2,1)S(1)} %gather_fusion.10), kind=kCustom, calls=%fused_computation.19 | custom fusion | bytes 1573888 | tf_op jit(solution)/shard_map/scatter | solution.py:65
  445.7 23.4 %all_to_all.75 = bf16[8,2,12,2048]{3,1,2,0:T(2,128)(2,1)S(1)} all-to-all(bf16[8,2,12,2048]{3,1,2,0:T(2,128)(2,1)S(1)} %copy.107), channel_id=1, replica_groups=mesh['section'=4,'expert'=8] {'expert'}, dimensions={0} | all-to-all | bytes 1572864 | tf_op jit(solution)/shard_map/all_to_all | solution.py:67
  473.0 6.8 %fusion.66 = bf16[8,2,12,2048]{3,2,0,1:T(8,128)(2,1)S(1)} fusion(bf16[1,2,768,2048]{3,2,1,0:T(8,128)(2,1)} %param.11, bf16[1,2,2048,768]{3,2,1,0:T(8,128)(2,1)} %param.10, bf16[8,2,12,2048]{3,1,2,0:T(2,128)(2,1)S(1)} %all_to_all.75, f32[8,2,12,768]{3,2,0,1:T(8,128)S(1)} %fusion.99), kind=kOutput, calls=%fused_computation.71 | convolution fusion | flops 1209237504 | bytes 14745600 | tf_op jit(solution)/shard_map/nesf,efd->nesd/dot_general | solution.py:74
  485.9 20.1 %all-to-all-done.11 = bf16[8,2,12,2048]{3,1,2,0:T(2,128)(2,1)S(1)} async-done(((bf16[8,2,12,2048]{3,1,2,0:T(2,128)(2,1)}), bf16[8,2,12,2048]{3,1,2,0:T(2,128)(2,1)S(1)}, u32[]{:S(2)}, u32[]{:S(2)}) %all-to-all-start.11) | async-done | bytes 786464 | tf_op jit(solution)/shard_map/all_to_all | solution.py:73
  509.9 5.4 collective-permute-start.5
  518.2 11.8 %scatter_fusion.6 = bf16[16,12,2048]{2,0,1:T(8,128)(2,1)S(1)} fusion(bf16[16,12,2048]{2,0,1:T(8,128)(2,1)S(1)} %broadcast.475, s32[128]{0:T(128)S(1)} %get-tuple-element.14, bf16[128,2048]{1,0:T(8,128)(2,1)S(1)} %gather_fusion.12), kind=kCustom, calls=%fused_computation.20 | custom fusion | bytes 1573888 | tf_op jit(solution)/shard_map/scatter | solution.py:65
  531.2 23.4 %all_to_all.76 = bf16[8,2,12,2048]{3,1,2,0:T(2,128)(2,1)S(1)} all-to-all(bf16[8,2,12,2048]{3,1,2,0:T(2,128)(2,1)S(1)} %copy.115), channel_id=1, replica_groups=mesh['section'=4,'expert'=8] {'expert'}, dimensions={0} | all-to-all | bytes 1572864 | tf_op jit(solution)/shard_map/all_to_all | solution.py:67
  558.6 6.8 %fusion.63 = bf16[8,2,12,2048]{3,2,0,1:T(8,128)(2,1)S(1)} fusion(bf16[1,2,768,2048]{3,2,1,0:T(8,128)(2,1)} %param.11, bf16[1,2,2048,768]{3,2,1,0:T(8,128)(2,1)} %param.10, bf16[8,2,12,2048]{3,1,2,0:T(2,128)(2,1)S(1)} %all_to_all.76, f32[8,2,12,768]{3,2,0,1:T(8,128)S(1)} %fusion.102), kind=kOutput, calls=%fused_computation.70 | convolution fusion | flops 1209237504 | bytes 14745600 | tf_op jit(solution)/shard_map/nesf,efd->nesd/dot_general | solution.py:74
  571.4 20.1 %all-to-all-done.13 = bf16[8,2,12,2048]{3,1,2,0:T(2,128)(2,1)S(1)} async-done(((bf16[8,2,12,2048]{3,1,2,0:T(2,128)(2,1)}), bf16[8,2,12,2048]{3,1,2,0:T(2,128)(2,1)S(1)}, u32[]{:S(2)}, u32[]{:S(2)}) %all-to-all-start.13) | async-done | bytes 786464 | tf_op jit(solution)/shard_map/all_to_all | solution.py:73
  (180 shorter events, 135.0 us)
Async XLA Ops:
  49.2 12.0 %copy-start.2 = (f32[1,4,16,8]{2,3,1,0:T(8,128)S(1)}, f32[1,4,16,8]{2,3,1,0:T(8,128)}, u32[]{:S(2)}) copy-start(f32[1,4,16,8]{2,3,1,0:T(8,128)} %param.13) | copy-start | bytes 6148
  56.0 30.0 %copy-start = (bf16[4,16,2048]{2,1,0:T(8,128)(2,1)S(1)}, bf16[4,16,2048]{2,1,0:T(8,128)(2,1)}, u32[]{:S(2)}) copy-start(bf16[4,16,2048]{2,1,0:T(8,128)(2,1)} %param.7) | copy-start | bytes 786436
  56.0 35.5 %copy-start.1 = (f32[1,2048]{1,0:T(1,128)S(1)}, f32[1,2048]{1,0:T(1,128)}, u32[]{:S(2)}) copy-start(f32[1,2048]{1,0:T(1,128)} %param.8) | copy-start | bytes 24580
  57.7 24.4 %all-to-all-start.1 = ((bf16[8,2,12,2048]{3,1,2,0:T(2,128)(2,1)}), bf16[8,2,12,2048]{3,1,2,0:T(2,128)(2,1)S(1)}, u32[]{:S(2)}, u32[]{:S(2)}) async-start(bf16[8,2,12,2048]{3,1,2,0:T(2,128)(2,1)} %copy.70), calls=%async_computation.1 | async-start | bytes 1572864 | tf_op jit(solution)/shard_map/all_to_all | solution.py:73
  86.1 5.3 collective-permute-start
  141.4 24.4 %all-to-all-start.3 = ((bf16[8,2,12,2048]{3,1,2,0:T(2,128)(2,1)}), bf16[8,2,12,2048]{3,1,2,0:T(2,128)(2,1)S(1)}, u32[]{:S(2)}, u32[]{:S(2)}) async-start(bf16[8,2,12,2048]{3,1,2,0:T(2,128)(2,1)} %copy.78), calls=%async_computation.3 | async-start | bytes 1572864 | tf_op jit(solution)/shard_map/all_to_all | solution.py:73
  169.8 6.2 %collective-permute-start.1 = (bf16[16,2048]{1,0:T(8,128)(2,1)S(1)}, bf16[16,2048]{1,0:T(8,128)(2,1)S(1)}, u32[]{:S(2)}, u32[]{:S(2)}) collective-permute-start(bf16[16,2048]{1,0:T(8,128)(2,1)S(1)} %get-tuple-element.41), channel_id=1, source_target_pairs={{0,8},{8,16},{16,24},{1,9},{9,17},{17,25},{2,10},{10,18},{18,26},{... | collective-permute-start | bytes 196616 | tf_op jit(solution)/shard_map/ppermute | solution.py:15
  226.0 24.4 %all-to-all-start.5 = ((bf16[8,2,12,2048]{3,1,2,0:T(2,128)(2,1)}), bf16[8,2,12,2048]{3,1,2,0:T(2,128)(2,1)S(1)}, u32[]{:S(2)}, u32[]{:S(2)}) async-start(bf16[8,2,12,2048]{3,1,2,0:T(2,128)(2,1)} %copy.86), calls=%async_computation.5 | async-start | bytes 1572864 | tf_op jit(solution)/shard_map/all_to_all | solution.py:73
  254.3 6.2 %collective-permute-start.2 = (bf16[16,2048]{1,0:T(8,128)(2,1)S(1)}, bf16[16,2048]{1,0:T(8,128)(2,1)S(1)}, u32[]{:S(2)}, u32[]{:S(2)}) collective-permute-start(bf16[16,2048]{1,0:T(8,128)(2,1)S(1)} %get-tuple-element.35), channel_id=1, source_target_pairs={{0,8},{8,16},{16,24},{1,9},{9,17},{17,25},{2,10},{10,18},{18,26},{... | collective-permute-start | bytes 196616 | tf_op jit(solution)/shard_map/ppermute | solution.py:15
  310.5 24.4 %all-to-all-start.7 = ((bf16[8,2,12,2048]{3,1,2,0:T(2,128)(2,1)}), bf16[8,2,12,2048]{3,1,2,0:T(2,128)(2,1)S(1)}, u32[]{:S(2)}, u32[]{:S(2)}) async-start(bf16[8,2,12,2048]{3,1,2,0:T(2,128)(2,1)} %copy.94), calls=%async_computation.7 | async-start | bytes 1572864 | tf_op jit(solution)/shard_map/all_to_all | solution.py:73
  338.9 7.0 %collective-permute-start.3 = (bf16[16,2048]{1,0:T(8,128)(2,1)S(1)}, bf16[16,2048]{1,0:T(8,128)(2,1)S(1)}, u32[]{:S(2)}, u32[]{:S(2)}) collective-permute-start(bf16[16,2048]{1,0:T(8,128)(2,1)S(1)} %get-tuple-element.29), channel_id=1, source_target_pairs={{0,8},{8,16},{16,24},{1,9},{9,17},{17,25},{2,10},{10,18},{18,26},{... | collective-permute-start | bytes 196616 | tf_op jit(solution)/shard_map/ppermute | solution.py:15
  396.0 24.4 %all-to-all-start.9 = ((bf16[8,2,12,2048]{3,1,2,0:T(2,128)(2,1)}), bf16[8,2,12,2048]{3,1,2,0:T(2,128)(2,1)S(1)}, u32[]{:S(2)}, u32[]{:S(2)}) async-start(bf16[8,2,12,2048]{3,1,2,0:T(2,128)(2,1)} %copy.102), calls=%async_computation.9 | async-start | bytes 1572864 | tf_op jit(solution)/shard_map/all_to_all | solution.py:73
  424.3 7.1 %collective-permute-start.4 = (bf16[16,2048]{1,0:T(8,128)(2,1)S(1)}, bf16[16,2048]{1,0:T(8,128)(2,1)S(1)}, u32[]{:S(2)}, u32[]{:S(2)}) collective-permute-start(bf16[16,2048]{1,0:T(8,128)(2,1)S(1)} %get-tuple-element.23), channel_id=1, source_target_pairs={{0,8},{8,16},{16,24},{1,9},{9,17},{17,25},{2,10},{10,18},{18,26},{... | collective-permute-start | bytes 196616 | tf_op jit(solution)/shard_map/ppermute | solution.py:15
  481.5 24.4 %all-to-all-start.11 = ((bf16[8,2,12,2048]{3,1,2,0:T(2,128)(2,1)}), bf16[8,2,12,2048]{3,1,2,0:T(2,128)(2,1)S(1)}, u32[]{:S(2)}, u32[]{:S(2)}) async-start(bf16[8,2,12,2048]{3,1,2,0:T(2,128)(2,1)} %copy.110), calls=%async_computation.11 | async-start | bytes 1572864 | tf_op jit(solution)/shard_map/all_to_all | solution.py:73
  509.9 7.1 %collective-permute-start.5 = (bf16[16,2048]{1,0:T(8,128)(2,1)S(1)}, bf16[16,2048]{1,0:T(8,128)(2,1)S(1)}, u32[]{:S(2)}, u32[]{:S(2)}) collective-permute-start(bf16[16,2048]{1,0:T(8,128)(2,1)S(1)} %get-tuple-element.17), channel_id=1, source_target_pairs={{0,8},{8,16},{16,24},{1,9},{9,17},{17,25},{2,10},{10,18},{18,26},{... | collective-permute-start | bytes 196616 | tf_op jit(solution)/shard_map/ppermute | solution.py:15
  567.1 24.4 %all-to-all-start.13 = ((bf16[8,2,12,2048]{3,1,2,0:T(2,128)(2,1)}), bf16[8,2,12,2048]{3,1,2,0:T(2,128)(2,1)S(1)}, u32[]{:S(2)}, u32[]{:S(2)}) async-start(bf16[8,2,12,2048]{3,1,2,0:T(2,128)(2,1)} %copy.118), calls=%async_computation.13 | async-start | bytes 1572864 | tf_op jit(solution)/shard_map/all_to_all | solution.py:73
where the time goes:
time: 608 us; the launch traced here: 596 us
  blocking collectives  167 us (27%)
  waiting for transfers between devices  151 us (25%)
  local copies, waits for them, and re-layouts  137 us (23%)
  matrix products  75 us (12%)
  starting transfers between devices  53.7 us (9%)
  other arithmetic  10.5 us (2%)
    all_to_all x7, blocking collectives, on_device(): lax.all_to_all(outgoing, 'expert', split_axis=0, concat_axis=0, tiled=True)  167 us
    all_to_all x7, waiting for transfers between devices, on_device(): lax.all_to_all(jnp.einsum('nesf,efd->nesd', inner, w_down, preferred_elem...  141 us
    scatter x7, local copies, waits for them, and re-layouts, on_device(): outgoing = outgoing.at[flat_ids, slot_index].set(normed[token_index])  83 us
    dot_general x7, matrix products, on_device(): jnp.einsum('nesf,efd->nesd', inner, w_down, preferred_element_type=jnp.fl...  47.4 us
    ppermute x6, starting transfers between devices, shifted(): return lax.ppermute(array, axis, pairs)  28.9 us
    dot_general x7, matrix products, on_device(): jnp.einsum('nesd,edf->nesf', received, w_gate, preferred_element_type=jnp...  27.6 us
    all_to_all x7, starting transfers between devices, on_device(): lax.all_to_all(jnp.einsum('nesf,efd->nesd', inner, w_down, preferred_elem...  24.8 us
    gather x7, local copies, waits for them, and re-layouts, on_device(): picked = returned[flat_ids, slot_index].reshape(tok_rows, topk, width)  17 us
  transfers between devices with their start and end apart: 13, of which 13 were waited for; matrix products, arithmetic and copies ran while one was open for 1% of the time, Pallas kernels for 0%

commit v1 on v0

v1 whole, which is shorter than its diff:
```python
import jax
import jax.numpy as jnp
from jax import lax
from jax.sharding import PartitionSpec as P

MB = 4


EPSILON = 1e-06


def shifted(array, axis, by):
    count = lax.axis_size(axis)
    pairs = [(i, i + by) for i in range(count) if 0 <= i + by < count]
    return lax.ppermute(array, axis, pairs)


def rms_normed(hidden, gain):
    values = hidden.astype(jnp.float32)
    scale = lax.rsqrt(jnp.mean(values * values, axis=-1, keepdims=True) + EPSILON)
    return (values, (values * scale * gain).astype(jnp.bfloat16))


def route_weights(routes, gates, first_expert, local_experts):
    weights = gates / jnp.sum(gates, axis=-1, keepdims=True)
    mine = first_expert + jnp.arange(local_experts, dtype=jnp.int32)
    hit = routes[..., None] == mine
    return jnp.sum(jnp.where(hit, weights[..., None], 0.0), axis=-2)


def on_device(tokens, norm_gain, gate_weight, up_weight, down_weight, routes, gates):
    sections = lax.axis_size("section")
    section_index = lax.axis_index("section")
    expert_index = lax.axis_index("expert")
    local_experts = gate_weight.shape[1]
    gain = norm_gain[0]
    w_gate = gate_weight[0]
    w_up = up_weight[0]
    w_down = down_weight[0]
    all_routes = lax.all_gather(routes[0], "expert", axis=1, tiled=True)
    all_gates = lax.all_gather(gates[0], "expert", axis=1, tiled=True)
    mixing = route_weights(all_routes, all_gates, expert_index * local_experts, local_experts)
    tok_rows = tokens.shape[1]
    width = tokens.shape[2]
    held = jnp.zeros((tok_rows, width), jnp.bfloat16)
    collected = jnp.zeros((MB, tok_rows, width), jnp.bfloat16)
    for moment in range(MB + sections - 1):
        if moment > 0:
            arrived = shifted(held, "section", 1)
        else:
            arrived = held
        batch_index = moment - section_index
        active = (batch_index >= 0) & (batch_index < MB)
        clipped = jnp.clip(batch_index, 0, MB - 1)
        first_rows = lax.dynamic_index_in_dim(tokens, clipped, 0, keepdims=False)
        incoming = jnp.where(section_index == 0, first_rows, arrived)
        weight = lax.dynamic_index_in_dim(mixing, clipped, 0, keepdims=False)
        values, normed = rms_normed(incoming, gain)
        rows = lax.all_gather(normed, "expert", axis=0, tiled=True)
        gate_part = jnp.einsum("td,edf->etf", rows, w_gate, preferred_element_type=jnp.float32)
        up_part = jnp.einsum("td,edf->etf", rows, w_up, preferred_element_type=jnp.float32)
        inner = (jax.nn.silu(gate_part) * up_part).astype(jnp.bfloat16)
        expert_out = jnp.einsum(
            "etf,efd->etd", inner, w_down, preferred_element_type=jnp.float32
        ).astype(jnp.bfloat16)
        partial = jnp.sum(weight.T[:, :, None] * expert_out.astype(jnp.float32), axis=0)
        mixed = lax.psum_scatter(partial, "expert", scatter_dimension=0, tiled=True)
        produced = (values + mixed).astype(jnp.bfloat16)
        held = jnp.where(active, produced, incoming)
        updated = lax.dynamic_update_index_in_dim(collected, held, clipped, 0)
        collected = jnp.where(active, updated, collected)
    return collected[None]


def solution(mesh):
    placed = (
        P(None, "expert", None),
        P("section", None),
        P("section", "expert", None, None),
        P("section", "expert", None, None),
        P("section", "expert", None, None),
        P("section", None, "expert", None),
        P("section", None, "expert", None),
    )
    return jax.shard_map(
        on_device,
        mesh=mesh,
        in_specs=placed,
        out_specs=P("section", None, "expert", None),
        check_vma=False,
    )
```

time: 608 us -> 500 us (0.82); the launches traced: 596 us -> 499 us
  local copies, waits for them, and re-layouts: 137 us -> 2.54 us
  waiting for transfers between devices: 151 us -> 234 us
  starting transfers between devices: 53.7 us -> 21.1 us
  blocking collectives: 167 us -> 135 us
  between operations: 1.46 us -> 13.8 us
    reduce_scatter x0 -> x7, waiting for transfers between devices: none -> 223 us  [on_device(): mixed = lax.psum_scatter(partial, 'expert', scatter_dimension=0, tiled=True)]
    all_to_all x7 -> x0, blocking collectives: 167 us -> none  [on_device(): lax.all_to_all(outgoing, 'expert', split_axis=0, concat_axis=0, tiled=True)]
    all_to_all x7 -> x0, waiting for transfers between devices: 141 us -> none  [on_device(): lax.all_to_all(jnp.einsum('nesf,efd->nesd', inner, w_down, preferred_elem...]
    all_gather x0 -> x9, blocking collectives: none -> 135 us  [the longest x7 105 us: on_device(): rows = lax.all_gather(normed, 'expert', axis=0, tiled=True)]
    scatter x7 -> x0, local copies, waits for them, and re-layouts: 83 us -> none  [on_device(): outgoing = outgoing.at[flat_ids, slot_index].set(normed[token_index])]
    all_to_all x7 -> x0, starting transfers between devices: 24.8 us -> none  [on_device(): lax.all_to_all(jnp.einsum('nesf,efd->nesd', inner, w_down, preferred_elem...]
    gather x14 -> x0, local copies, waits for them, and re-layouts: 23.5 us -> none  [the longest x7 17 us: on_device(): picked = returned[flat_ids, slot_index].reshape(tok_rows, topk, width)]
    convert_element_type x7 -> x0, local copies, waits for them, and re-layouts: 11.8 us -> none  [on_device(): jnp.einsum('nesf,efd->nesd', inner, w_down, preferred_element_type=jnp.fl...]
  transfers between devices with their start and end apart: 13 -> 13, of which waited for: 13 -> 13; matrix products, arithmetic and copies ran while one was open for 1% -> 0% of each run, Pallas kernels for 0% -> 0%
where the time goes in v1:
time: 500 us; the launch traced here: 499 us
  waiting for transfers between devices  234 us (47%)
  blocking collectives  135 us (27%)
  matrix products  80.9 us (16%)
  starting transfers between devices  21.1 us (4%)
  between operations  13.8 us (3%)
  other arithmetic  11 us (2%)
    reduce_scatter x7, waiting for transfers between devices, on_device(): mixed = lax.psum_scatter(partial, 'expert', scatter_dimension=0, tiled=True)  223 us
    all_gather x7, blocking collectives, on_device(): rows = lax.all_gather(normed, 'expert', axis=0, tiled=True)  105 us
    dot_general x7, matrix products, on_device(): jnp.einsum('etf,efd->etd', inner, w_down, preferred_element_type=jnp.floa...  54.5 us
    dot_general x7, matrix products, on_device(): jnp.einsum('td,edf->etf', rows, w_gate, preferred_element_type=jnp.float32)  26.4 us
    ppermute x6, starting transfers between devices, shifted(): return lax.ppermute(array, axis, pairs)  20.8 us
    all_gather x1, blocking collectives, on_device(): all_gates = lax.all_gather(gates[0], 'expert', axis=1, tiled=True)  15.9 us
    all_gather x1, blocking collectives, on_device(): all_routes = lax.all_gather(routes[0], 'expert', axis=1, tiled=True)  14.2 us
    ppermute x6, waiting for transfers between devices, shifted(): return lax.ppermute(array, axis, pairs)  11.3 us
  transfers between devices with their start and end apart: 13, of which 13 were waited for; matrix products, arithmetic and copies ran while one was open for 0% of the time, Pallas kernels for 0%

profile of v1, /device:TPU:0, one launch (start us, length us, event | category | flops | bytes accessed | tf_op | source)
XLA Modules:
  0.0 498.8 jit_solution(13108458287692976375)
XLA Ops:
  7.3 15.9 %all-gather.1 = f32[1,4,128,8]{3,1,0,2:T(4,128)S(1)} all-gather(f32[1,4,16,8]{3,1,0,2:T(4,128)S(1)} %copy.16), channel_id=3, replica_groups=mesh['section'=4,'expert'=8] {'expert'}, dimensions={2}, use_global_device_ids=true | all-gather | bytes 18432 | tf_op jit(solution)/shard_map/all_gather | solution.py:41
  24.5 14.2 %all-gather = s32[1,4,128,8]{3,1,0,2:T(4,128)S(1)} all-gather(s32[1,4,16,8]{3,1,0,2:T(4,128)S(1)} %copy.14), channel_id=2, replica_groups=mesh['section'=4,'expert'=8] {'expert'}, dimensions={2}, use_global_device_ids=true | all-gather | bytes 18432 | tf_op jit(solution)/shard_map/all_gather | solution.py:40
  40.8 14.8 %all_gather.29 = bf16[128,2048]{1,0:T(8,128)(2,1)S(1)} all-gather(bf16[16,2048]{1,0:T(8,128)(2,1)S(1)} %fusion.289), channel_id=1, replica_groups=mesh['section'=4,'expert'=8] {'expert'}, dimensions={0}, use_global_device_ids=true | all-gather | bytes 589824 | tf_op jit(solution)/shard_map/all_gather | solution.py:59
  55.6 3.8 fusion.126
  59.5 7.8 %fusion.123 = f32[128,2048]{1,0:T(8,128)} fusion(bf16[1,2,768,2048]{3,2,1,0:T(8,128)(2,1)} %param.11, f32[2,128]{1,0:T(2,128)S(1)} %get-tuple-element.35, bf16[1,2,2048,768]{3,2,1,0:T(8,128)(2,1)} %param.10, f32[2,128,768]{2,1,0:T(8,128)S(1)} %fusion.126, bf16[128,2048]{1,0:T(8,128)(2,1)S(1)} %all_gather.29), kind=kOutput, calls=%fused_computation.69 | convolution fusion | flops 1613627392 | bytes 14943232 | tf_op jit(solution)/shard_map/etf,efd->etd/dot_general | solution.py:63
  67.4 33.9 %reduce-scatter.8.cloned.1.call-done = f32[16,2048]{1,0:T(8,128)} async-done(((f32[128,2048]{1,0:T(8,128)}), f32[16,2048]{1,0:T(8,128)}) %reduce-scatter.8.cloned.1.call-update) | async-done | bytes 131088 | tf_op jit(solution)/shard_map/reduce_scatter | solution.py:67
  107.8 15.0 %all_gather.30 = bf16[128,2048]{1,0:T(8,128)(2,1)S(1)} all-gather(bf16[16,2048]{1,0:T(8,128)(2,1)S(1)} %fusion.293), channel_id=1, replica_groups=mesh['section'=4,'expert'=8] {'expert'}, dimensions={0}, use_global_device_ids=true | all-gather | bytes 589824 | tf_op jit(solution)/shard_map/all_gather | solution.py:59
  122.8 3.8 fusion.129
  126.6 7.8 %fusion.120 = f32[128,2048]{1,0:T(8,128)} fusion(bf16[1,2,768,2048]{3,2,1,0:T(8,128)(2,1)} %param.11, f32[2,128]{1,0:T(2,128)S(1)} %get-tuple-element.34, bf16[1,2,2048,768]{3,2,1,0:T(8,128)(2,1)} %param.10, f32[2,128,768]{2,1,0:T(8,128)S(1)} %fusion.129, bf16[128,2048]{1,0:T(8,128)(2,1)S(1)} %all_gather.30), kind=kOutput, calls=%fused_computation.68 | convolution fusion | flops 1613627392 | bytes 14943232 | tf_op jit(solution)/shard_map/etf,efd->etd/dot_general | solution.py:63
  134.4 31.6 %reduce-scatter.10.cloned.1.call-done = f32[16,2048]{1,0:T(8,128)} async-done(((f32[128,2048]{1,0:T(8,128)}), f32[16,2048]{1,0:T(8,128)}) %reduce-scatter.10.cloned.1.call-update) | async-done | bytes 131088 | tf_op jit(solution)/shard_map/reduce_scatter | solution.py:67
  172.3 15.2 %all_gather.31 = bf16[128,2048]{1,0:T(8,128)(2,1)S(1)} all-gather(bf16[16,2048]{1,0:T(8,128)(2,1)S(1)} %fusion.297), channel_id=1, replica_groups=mesh['section'=4,'expert'=8] {'expert'}, dimensions={0}, use_global_device_ids=true | all-gather | bytes 589824 | tf_op jit(solution)/shard_map/all_gather | solution.py:59
  187.5 3.8 fusion.132
  191.3 7.8 %fusion.117 = f32[128,2048]{1,0:T(8,128)} fusion(bf16[1,2,768,2048]{3,2,1,0:T(8,128)(2,1)} %param.11, f32[2,128]{1,0:T(2,128)S(1)} %get-tuple-element.33, bf16[1,2,2048,768]{3,2,1,0:T(8,128)(2,1)} %param.10, f32[2,128,768]{2,1,0:T(8,128)S(1)} %fusion.132, bf16[128,2048]{1,0:T(8,128)(2,1)S(1)} %all_gather.31), kind=kOutput, calls=%fused_computation.67 | convolution fusion | flops 1613627392 | bytes 14943232 | tf_op jit(solution)/shard_map/etf,efd->etd/dot_general | solution.py:63
  199.2 31.7 %reduce-scatter.12.cloned.1.call-done = f32[16,2048]{1,0:T(8,128)} async-done(((f32[128,2048]{1,0:T(8,128)}), f32[16,2048]{1,0:T(8,128)}) %reduce-scatter.12.cloned.1.call-update) | async-done | bytes 131088 | tf_op jit(solution)/shard_map/reduce_scatter | solution.py:67
  237.6 15.0 %all_gather.32 = bf16[128,2048]{1,0:T(8,128)(2,1)S(1)} all-gather(bf16[16,2048]{1,0:T(8,128)(2,1)S(1)} %fusion.301), channel_id=1, replica_groups=mesh['section'=4,'expert'=8] {'expert'}, dimensions={0}, use_global_device_ids=true | all-gather | bytes 589824 | tf_op jit(solution)/shard_map/all_gather | solution.py:59
  252.6 3.8 fusion.135
  256.4 7.8 %fusion.114 = f32[128,2048]{1,0:T(8,128)} fusion(bf16[1,2,768,2048]{3,2,1,0:T(8,128)(2,1)} %param.11, f32[2,128]{1,0:T(2,128)S(1)} %get-tuple-element.32, bf16[1,2,2048,768]{3,2,1,0:T(8,128)(2,1)} %param.10, f32[2,128,768]{2,1,0:T(8,128)S(1)} %fusion.135, bf16[128,2048]{1,0:T(8,128)(2,1)S(1)} %all_gather.32), kind=kOutput, calls=%fused_computation.66 | convolution fusion | flops 1613627392 | bytes 14943232 | tf_op jit(solution)/shard_map/etf,efd->etd/dot_general | solution.py:63
  264.3 31.5 %reduce-scatter.14.cloned.1.call-done = f32[16,2048]{1,0:T(8,128)} async-done(((f32[128,2048]{1,0:T(8,128)}), f32[16,2048]{1,0:T(8,128)}) %reduce-scatter.14.cloned.1.call-update) | async-done | bytes 131088 | tf_op jit(solution)/shard_map/reduce_scatter | solution.py:67
  296.7 3.7 collective-permute-start.3
  302.5 15.0 %all_gather.33 = bf16[128,2048]{1,0:T(8,128)(2,1)S(1)} all-gather(bf16[16,2048]{1,0:T(8,128)(2,1)S(1)} %fusion.305), channel_id=1, replica_groups=mesh['section'=4,'expert'=8] {'expert'}, dimensions={0}, use_global_device_ids=true | all-gather | bytes 589824 | tf_op jit(solution)/shard_map/all_gather | solution.py:59
  317.6 3.8 fusion.138
  321.4 7.8 %fusion.111 = f32[128,2048]{1,0:T(8,128)} fusion(bf16[1,2,768,2048]{3,2,1,0:T(8,128)(2,1)} %param.11, f32[2,128]{1,0:T(2,128)S(1)} %get-tuple-element.31, bf16[1,2,2048,768]{3,2,1,0:T(8,128)(2,1)} %param.10, f32[2,128,768]{2,1,0:T(8,128)S(1)} %fusion.138, bf16[128,2048]{1,0:T(8,128)(2,1)S(1)} %all_gather.33), kind=kOutput, calls=%fused_computation.65 | convolution fusion | flops 1613627392 | bytes 14943232 | tf_op jit(solution)/shard_map/etf,efd->etd/dot_general | solution.py:63
  329.2 31.7 %reduce-scatter.16.cloned.1.call-done = f32[16,2048]{1,0:T(8,128)} async-done(((f32[128,2048]{1,0:T(8,128)}), f32[16,2048]{1,0:T(8,128)}) %reduce-scatter.16.cloned.1.call-update) | async-done | bytes 131088 | tf_op jit(solution)/shard_map/reduce_scatter | solution.py:67
  367.3 15.2 %all_gather.34 = bf16[128,2048]{1,0:T(8,128)(2,1)S(1)} all-gather(bf16[16,2048]{1,0:T(8,128)(2,1)S(1)} %fusion.309), channel_id=1, replica_groups=mesh['section'=4,'expert'=8] {'expert'}, dimensions={0}, use_global_device_ids=true | all-gather | bytes 589824 | tf_op jit(solution)/shard_map/all_gather | solution.py:59
  382.5 3.8 fusion.141
  386.3 7.8 %fusion.108 = f32[128,2048]{1,0:T(8,128)} fusion(bf16[1,2,768,2048]{3,2,1,0:T(8,128)(2,1)} %param.11, f32[2,128]{1,0:T(2,128)S(1)} %get-tuple-element.30, bf16[1,2,2048,768]{3,2,1,0:T(8,128)(2,1)} %param.10, f32[2,128,768]{2,1,0:T(8,128)S(1)} %fusion.141, bf16[128,2048]{1,0:T(8,128)(2,1)S(1)} %all_gather.34), kind=kOutput, calls=%fused_computation.64 | convolution fusion | flops 1613627392 | bytes 14943232 | tf_op jit(solution)/shard_map/etf,efd->etd/dot_general | solution.py:63
  394.1 31.5 %reduce-scatter.18.cloned.1.call-done = f32[16,2048]{1,0:T(8,128)} async-done(((f32[128,2048]{1,0:T(8,128)}), f32[16,2048]{1,0:T(8,128)}) %reduce-scatter.18.cloned.1.call-update) | async-done | bytes 131088 | tf_op jit(solution)/shard_map/reduce_scatter | solution.py:67
  426.5 3.7 collective-permute-start.5
  432.3 15.0 %all_gather.35 = bf16[128,2048]{1,0:T(8,128)(2,1)S(1)} all-gather(bf16[16,2048]{1,0:T(8,128)(2,1)S(1)} %fusion.313), channel_id=1, replica_groups=mesh['section'=4,'expert'=8] {'expert'}, dimensions={0}, use_global_device_ids=true | all-gather | bytes 589824 | tf_op jit(solution)/shard_map/all_gather | solution.py:59
  447.4 3.8 fusion.144
  451.1 7.8 %fusion.105 = f32[128,2048]{1,0:T(8,128)} fusion(bf16[1,2,768,2048]{3,2,1,0:T(8,128)(2,1)} %param.11, f32[2,128]{1,0:T(2,128)S(1)} %get-tuple-element.29, bf16[1,2,2048,768]{3,2,1,0:T(8,128)(2,1)} %param.10, f32[2,128,768]{2,1,0:T(8,128)S(1)} %fusion.144, bf16[128,2048]{1,0:T(8,128)(2,1)S(1)} %all_gather.35), kind=kOutput, calls=%fused_computation.63 | convolution fusion | flops 1613627392 | bytes 14943232 | tf_op jit(solution)/shard_map/etf,efd->etd/dot_general | solution.py:63
  459.6 30.7 %reduce-scatter.20.cloned.1.call-done = f32[16,2048]{1,0:T(8,128)} async-done(((f32[128,2048]{1,0:T(8,128)}), f32[16,2048]{1,0:T(8,128)}) %reduce-scatter.20.cloned.1.call-update) | async-done | bytes 131088 | tf_op jit(solution)/shard_map/reduce_scatter | solution.py:67
  (67 shorter events, 38.8 us)
Async XLA Ops:
  6.5 94.7 %reduce-scatter.8.cloned.1.call-start = ((), (), s32[]{:S(2)}) async-start(), calls=%async_computation.7 | async-start | bytes 1179648 | tf_op jit(solution)/shard_map/reduce_scatter | solution.py:67
  59.5 41.8 %copy-start = (bf16[4,16,2048]{2,1,0:T(8,128)(2,1)S(1)}, bf16[4,16,2048]{2,1,0:T(8,128)(2,1)}, u32[]{:S(2)}) copy-start(bf16[4,16,2048]{2,1,0:T(8,128)(2,1)} %param.7) | copy-start | bytes 786436
  59.5 48.2 %copy-start.1 = (f32[1,2048]{1,0:T(1,128)S(1)}, f32[1,2048]{1,0:T(1,128)}, u32[]{:S(2)}) copy-start(f32[1,2048]{1,0:T(1,128)} %param.8) | copy-start | bytes 24580
  67.3 98.7 %reduce-scatter.10.cloned.1.call-start = ((), (), s32[]{:S(2)}) async-start(), calls=%async_computation.8 | async-start | bytes 1179648 | tf_op jit(solution)/shard_map/reduce_scatter | solution.py:67
  102.2 5.3 %collective-permute-start = (bf16[16,2048]{1,0:T(8,128)(2,1)S(1)}, bf16[16,2048]{1,0:T(8,128)(2,1)S(1)}, u32[]{:S(2)}, u32[]{:S(2)}) collective-permute-start(bf16[16,2048]{1,0:T(8,128)(2,1)S(1)} %get-tuple-element.28), channel_id=1, source_target_pairs={{0,8},{8,16},{16,24},{1,9},{9,17},{17,25},{2,10},{10,18},{18,26},{... | collective-permute-start | bytes 196616 | tf_op jit(solution)/shard_map/ppermute | solution.py:15
  134.4 96.5 %reduce-scatter.12.cloned.1.call-start = ((), (), s32[]{:S(2)}) async-start(), calls=%async_computation.9 | async-start | bytes 1179648 | tf_op jit(solution)/shard_map/reduce_scatter | solution.py:67
  167.0 5.1 %collective-permute-start.1 = (bf16[16,2048]{1,0:T(8,128)(2,1)S(1)}, bf16[16,2048]{1,0:T(8,128)(2,1)S(1)}, u32[]{:S(2)}, u32[]{:S(2)}) collective-permute-start(bf16[16,2048]{1,0:T(8,128)(2,1)S(1)} %get-tuple-element.24), channel_id=1, source_target_pairs={{0,8},{8,16},{16,24},{1,9},{9,17},{17,25},{2,10},{10,18},{18,26},{... | collective-permute-start | bytes 196616 | tf_op jit(solution)/shard_map/ppermute | solution.py:15
  199.1 96.7 %reduce-scatter.14.cloned.1.call-start = ((), (), s32[]{:S(2)}) async-start(), calls=%async_computation.10 | async-start | bytes 1179648 | tf_op jit(solution)/shard_map/reduce_scatter | solution.py:67
  231.9 5.5 %collective-permute-start.2 = (bf16[16,2048]{1,0:T(8,128)(2,1)S(1)}, bf16[16,2048]{1,0:T(8,128)(2,1)S(1)}, u32[]{:S(2)}, u32[]{:S(2)}) collective-permute-start(bf16[16,2048]{1,0:T(8,128)(2,1)S(1)} %get-tuple-element.20), channel_id=1, source_target_pairs={{0,8},{8,16},{16,24},{1,9},{9,17},{17,25},{2,10},{10,18},{18,26},{... | collective-permute-start | bytes 196616 | tf_op jit(solution)/shard_map/ppermute | solution.py:15
  264.3 96.6 %reduce-scatter.16.cloned.1.call-start = ((), (), s32[]{:S(2)}) async-start(), calls=%async_computation.11 | async-start | bytes 1179648 | tf_op jit(solution)/shard_map/reduce_scatter | solution.py:67
  296.7 5.5 %collective-permute-start.3 = (bf16[16,2048]{1,0:T(8,128)(2,1)S(1)}, bf16[16,2048]{1,0:T(8,128)(2,1)S(1)}, u32[]{:S(2)}, u32[]{:S(2)}) collective-permute-start(bf16[16,2048]{1,0:T(8,128)(2,1)S(1)} %get-tuple-element.16), channel_id=1, source_target_pairs={{0,8},{8,16},{16,24},{1,9},{9,17},{17,25},{2,10},{10,18},{18,26},{... | collective-permute-start | bytes 196616 | tf_op jit(solution)/shard_map/ppermute | solution.py:15
  329.2 96.4 %reduce-scatter.18.cloned.1.call-start = ((), (), s32[]{:S(2)}) async-start(), calls=%async_computation.12 | async-start | bytes 1179648 | tf_op jit(solution)/shard_map/reduce_scatter | solution.py:67
  361.8 5.2 %collective-permute-start.4 = (bf16[16,2048]{1,0:T(8,128)(2,1)S(1)}, bf16[16,2048]{1,0:T(8,128)(2,1)S(1)}, u32[]{:S(2)}, u32[]{:S(2)}) collective-permute-start(bf16[16,2048]{1,0:T(8,128)(2,1)S(1)} %get-tuple-element.12), channel_id=1, source_target_pairs={{0,8},{8,16},{16,24},{1,9},{9,17},{17,25},{2,10},{10,18},{18,26},{... | collective-permute-start | bytes 196616 | tf_op jit(solution)/shard_map/ppermute | solution.py:15
  394.1 96.3 %reduce-scatter.20.cloned.1.call-start = ((), (), s32[]{:S(2)}) async-start(), calls=%async_computation.13 | async-start | bytes 1179648 | tf_op jit(solution)/shard_map/reduce_scatter | solution.py:67
  426.5 5.6 %collective-permute-start.5 = (bf16[16,2048]{1,0:T(8,128)(2,1)S(1)}, bf16[16,2048]{1,0:T(8,128)(2,1)S(1)}, u32[]{:S(2)}, u32[]{:S(2)}) collective-permute-start(bf16[16,2048]{1,0:T(8,128)(2,1)S(1)} %get-tuple-element.8), channel_id=1, source_target_pairs={{0,8},{8,16},{16,24},{1,9},{9,17},{17,25},{2,10},{10,18},{18,26},{... | collective-permute-start | bytes 196616 | tf_op jit(solution)/shard_map/ppermute | solution.py:15
Sparse Core Ops, SparseCore 0:
  67.4 33.7 reduce-scatter.7
  134.5 31.4 reduce-scatter.9
  199.2 31.6 reduce-scatter.11
  264.4 31.3 reduce-scatter.13
  329.3 31.5 reduce-scatter.15
  394.2 31.3 reduce-scatter.17
  459.0 31.2 reduce-scatter.19

commit v2 on v1

--- a/solution.py
+++ b/solution.py
@@ -13,6 +13,18 @@
     count = lax.axis_size(axis)
     pairs = [(i, i + by) for i in range(count) if 0 <= i + by < count]
     return lax.ppermute(array, axis, pairs)
+
+
+def scatter_sum(partial, axis):
+    count = lax.axis_size(axis)
+    index = lax.axis_index(axis)
+    blocks = partial.reshape((count, partial.shape[0] // count) + partial.shape[1:])
+    total = lax.dynamic_index_in_dim(blocks, index, 0, keepdims=False).astype(jnp.bfloat16).astype(jnp.float32)
+    for by in range(1, count):
+        piece = lax.dynamic_index_in_dim(blocks, (index + by) % count, 0, keepdims=False)
+        pairs = [(i, (i + by) % count) for i in range(count)]
+        total = total + lax.ppermute(piece.astype(jnp.bfloat16), axis, pairs).astype(jnp.float32)
+    return total
 
 
 def rms_normed(hidden, gain):
@@ -64,7 +76,7 @@
             "etf,efd->etd", inner, w_down, preferred_element_type=jnp.float32
         ).astype(jnp.bfloat16)
         partial = jnp.sum(weight.T[:, :, None] * expert_out.astype(jnp.float32), axis=0)
-        mixed = lax.psum_scatter(partial, "expert", scatter_dimension=0, tiled=True)
+        mixed = scatter_sum(partial, "expert")
         produced = (values + mixed).astype(jnp.bfloat16)
         held = jnp.where(active, produced, incoming)
         updated = lax.dynamic_update_index_in_dim(collected, held, clipped, 0)

time: 500 us -> 358 us (0.72)
  waiting for transfers between devices: 234 us -> 52.9 us
  starting transfers between devices: 21.1 us -> 83.6 us
  between operations: 13.8 us -> 0.44 us
  matrix products: 80.9 us -> 73.4 us
  other arithmetic: 11 us -> 5.2 us
    reduce_scatter x7 -> x0, waiting for transfers between devices: 223 us -> none  [on_device(): mixed = lax.psum_scatter(partial, 'expert', scatter_dimension=0, tiled=True)]
    ppermute x0 -> x49, starting transfers between devices: none -> 55.4 us  [scatter_sum(): lax.ppermute(piece.astype(jnp.bfloat16), axis, pairs).astype(jnp.float32)]
    ppermute x0 -> x49, waiting for transfers between devices: none -> 41.1 us  [scatter_sum(): lax.ppermute(piece.astype(jnp.bfloat16), axis, pairs).astype(jnp.float32)]
    dot_general x7, matrix products: 54.5 us -> 47 us  [on_device(): jnp.einsum('etf,efd->etd', inner, w_down, preferred_element_type=jnp.floa...]
    ppermute x6, starting transfers between devices: 20.8 us -> 28.2 us  [shifted(): return lax.ppermute(array, axis, pairs)]
    select_n x7, other arithmetic: 7.18 us -> 1.34 us  [on_device(): collected = jnp.where(active, updated, collected)]
  transfers between devices with their start and end apart: 13 -> 55, of which waited for: 13 -> 28; matrix products, arithmetic and copies ran while one was open for 0% -> 0% of each run, Pallas kernels for 0% -> 0%
where the time goes in v2:
time: 358 us; the launch traced here: 353 us
  blocking collectives  135 us (38%)
  starting transfers between devices  83.6 us (23%)
  matrix products  73.4 us (21%)
  waiting for transfers between devices  52.9 us (15%)
  other arithmetic  5.2 us (1%)
    all_gather x7, blocking collectives, on_device(): rows = lax.all_gather(normed, 'expert', axis=0, tiled=True)  105 us
    ppermute x49, starting transfers between devices, scatter_sum(): lax.ppermute(piece.astype(jnp.bfloat16), axis, pairs).astype(jnp.float32)  55.4 us
    dot_general x7, matrix products, on_device(): jnp.einsum('etf,efd->etd', inner, w_down, preferred_element_type=jnp.floa...  47 us
    ppermute x49, waiting for transfers between devices, scatter_sum(): lax.ppermute(piece.astype(jnp.bfloat16), axis, pairs).astype(jnp.float32)  41.1 us
    ppermute x6, starting transfers between devices, shifted(): return lax.ppermute(array, axis, pairs)  28.2 us
    dot_general x7, matrix products, on_device(): jnp.einsum('td,edf->etf', rows, w_gate, preferred_element_type=jnp.float32)  26.4 us
    all_gather x1, blocking collectives, on_device(): all_gates = lax.all_gather(gates[0], 'expert', axis=1, tiled=True)  15.9 us
    all_gather x1, blocking collectives, on_device(): all_routes = lax.all_gather(routes[0], 'expert', axis=1, tiled=True)  14.2 us
  transfers between devices with their start and end apart: 55, of which 28 were waited for; matrix products, arithmetic and copies ran while one was open for 0% of the time, Pallas kernels for 0%

profile of v2, /device:TPU:0, one launch (start us, length us, event | category | flops | bytes accessed | tf_op | source)
XLA Modules:
  0.0 353.4 jit_solution(8086892317033034656)
XLA Ops:
  0.8 15.9 %all-gather.1 = f32[1,4,128,8]{3,1,0,2:T(4,128)S(1)} all-gather(f32[1,4,16,8]{3,1,0,2:T(4,128)S(1)} %copy.16), channel_id=3, replica_groups=mesh['section'=4,'expert'=8] {'expert'}, dimensions={2}, use_global_device_ids=true | all-gather | bytes 18432 | tf_op jit(solution)/shard_map/all_gather | solution.py:53
  18.0 14.2 %all-gather = s32[1,4,128,8]{3,1,0,2:T(4,128)S(1)} all-gather(s32[1,4,16,8]{3,1,0,2:T(4,128)S(1)} %copy.14), channel_id=2, replica_groups=mesh['section'=4,'expert'=8] {'expert'}, dimensions={2}, use_global_device_ids=true | all-gather | bytes 18432 | tf_op jit(solution)/shard_map/all_gather | solution.py:52
  34.2 14.8 %all_gather.29 = bf16[128,2048]{1,0:T(8,128)(2,1)S(1)} all-gather(bf16[16,2048]{1,0:T(8,128)(2,1)S(1)} %fusion.289), channel_id=1, replica_groups=mesh['section'=4,'expert'=8] {'expert'}, dimensions={0}, use_global_device_ids=true | all-gather | bytes 589824 | tf_op jit(solution)/shard_map/all_gather | solution.py:71
  49.1 3.8 %fusion.126 = f32[2,128,768]{2,1,0:T(8,128)S(1)} fusion(bf16[1,2,2048,768]{3,2,1,0:T(8,128)(2,1)} %param.9, bf16[128,2048]{1,0:T(8,128)(2,1)S(1)} %all_gather.29), kind=kOutput, calls=%fused_computation.70 | convolution fusion | flops 805306368 | bytes 7602176 | tf_op jit(solution)/shard_map/td,edf->etf/dot_general | solution.py:72
  53.0 6.7 %fusion.123 = bf16[128,2048]{1,0:T(8,128)(2,1)S(1)} fusion(bf16[1,2,768,2048]{3,2,1,0:T(8,128)(2,1)} %param.11, f32[2,128]{1,0:T(2,128)S(1)} %get-tuple-element.84, bf16[1,2,2048,768]{3,2,1,0:T(8,128)(2,1)} %param.10, f32[2,128,768]{2,1,0:T(8,128)S(1)} %fusion.126, bf16[128,2048]{1,0:T(8,128)(2,1)S(1)} %all_gather.29), kind=kOutput, calls=%fused_computation.69 | convolution fusion | flops 1613627392 | bytes 14418944 | tf_op jit(solution)/shard_map/etf,efd->etd/dot_general | solution.py:75
  79.5 14.7 %all_gather.30 = bf16[128,2048]{1,0:T(8,128)(2,1)S(1)} all-gather(bf16[16,2048]{1,0:T(8,128)(2,1)S(1)} %fusion.293), channel_id=1, replica_groups=mesh['section'=4,'expert'=8] {'expert'}, dimensions={0}, use_global_device_ids=true | all-gather | bytes 589824 | tf_op jit(solution)/shard_map/all_gather | solution.py:71
  97.9 6.7 %fusion.120 = bf16[128,2048]{1,0:T(8,128)(2,1)S(1)} fusion(bf16[1,2,768,2048]{3,2,1,0:T(8,128)(2,1)} %param.11, f32[2,128]{1,0:T(2,128)S(1)} %get-tuple-element.83, bf16[1,2,2048,768]{3,2,1,0:T(8,128)(2,1)} %param.10, f32[2,128,768]{2,1,0:T(8,128)S(1)} %fusion.129, bf16[128,2048]{1,0:T(8,128)(2,1)S(1)} %all_gather.30), kind=kOutput, calls=%fused_computation.68 | convolution fusion | flops 1613627392 | bytes 14418944 | tf_op jit(solution)/shard_map/etf,efd->etd/dot_general | solution.py:75
  117.0 4.5 %collective-permute-done.9 = bf16[16,2048]{1,0:T(8,128)(2,1)S(1)} collective-permute-done((bf16[16,2048]{1,0:T(8,128)(2,1)S(1)}, bf16[16,2048]{1,0:T(8,128)(2,1)S(1)}, u32[]{:S(2)}, u32[]{:S(2)}) %collective-permute-start.9) | collective-permute-done | bytes 65568 | tf_op jit(solution)/shard_map/ppermute | solution.py:26
  121.7 4.5 %collective-permute-start.15 = (bf16[16,2048]{1,0:T(8,128)(2,1)S(1)}, bf16[16,2048]{1,0:T(8,128)(2,1)S(1)}, u32[]{:S(2)}, u32[]{:S(2)}) collective-permute-start(bf16[16,2048]{1,0:T(8,128)(2,1)S(1)} %get-tuple-element.24), channel_id=1, source_target_pairs={{0,8},{8,16},{16,24},{1,9},{9,17},{17,25},{2,10},{10,18},{18,26},{... | collective-permute-start | bytes 196616 | tf_op jit(solution)/shard_map/ppermute | solution.py:15
  128.3 15.0 %all_gather.31 = bf16[128,2048]{1,0:T(8,128)(2,1)S(1)} all-gather(bf16[16,2048]{1,0:T(8,128)(2,1)S(1)} %fusion.297), channel_id=1, replica_groups=mesh['section'=4,'expert'=8] {'expert'}, dimensions={0}, use_global_device_ids=true | all-gather | bytes 589824 | tf_op jit(solution)/shard_map/all_gather | solution.py:71
  143.4 3.8 %fusion.132 = f32[2,128,768]{2,1,0:T(8,128)S(1)} fusion(bf16[1,2,2048,768]{3,2,1,0:T(8,128)(2,1)} %param.9, bf16[128,2048]{1,0:T(8,128)(2,1)S(1)} %all_gather.31), kind=kOutput, calls=%fused_computation.72 | convolution fusion | flops 805306368 | bytes 7602176 | tf_op jit(solution)/shard_map/td,edf->etf/dot_general | solution.py:72
  147.1 6.7 %fusion.117 = bf16[128,2048]{1,0:T(8,128)(2,1)S(1)} fusion(bf16[1,2,768,2048]{3,2,1,0:T(8,128)(2,1)} %param.11, f32[2,128]{1,0:T(2,128)S(1)} %get-tuple-element.82, bf16[1,2,2048,768]{3,2,1,0:T(8,128)(2,1)} %param.10, f32[2,128,768]{2,1,0:T(8,128)S(1)} %fusion.132, bf16[128,2048]{1,0:T(8,128)(2,1)S(1)} %all_gather.31), kind=kOutput, calls=%fused_computation.67 | convolution fusion | flops 1613627392 | bytes 14418944 | tf_op jit(solution)/shard_map/etf,efd->etd/dot_general | solution.py:75
  161.4 4.4 %collective-permute-done.18 = bf16[16,2048]{1,0:T(8,128)(2,1)S(1)} collective-permute-done((bf16[16,2048]{1,0:T(8,128)(2,1)S(1)}, bf16[16,2048]{1,0:T(8,128)(2,1)S(1)}, u32[]{:S(2)}, u32[]{:S(2)}) %collective-permute-start.18) | collective-permute-done | bytes 65568 | tf_op jit(solution)/shard_map/ppermute | solution.py:26
  166.1 4.3 %collective-permute-start.23 = (bf16[16,2048]{1,0:T(8,128)(2,1)S(1)}, bf16[16,2048]{1,0:T(8,128)(2,1)S(1)}, u32[]{:S(2)}, u32[]{:S(2)}) collective-permute-start(bf16[16,2048]{1,0:T(8,128)(2,1)S(1)} %get-tuple-element.20), channel_id=1, source_target_pairs={{0,8},{8,16},{16,24},{1,9},{9,17},{17,25},{2,10},{10,18},{18,26},{... | collective-permute-start | bytes 196616 | tf_op jit(solution)/shard_map/ppermute | solution.py:15
  172.6 16.0 %all_gather.32 = bf16[128,2048]{1,0:T(8,128)(2,1)S(1)} all-gather(bf16[16,2048]{1,0:T(8,128)(2,1)S(1)} %fusion.301), channel_id=1, replica_groups=mesh['section'=4,'expert'=8] {'expert'}, dimensions={0}, use_global_device_ids=true | all-gather | bytes 589824 | tf_op jit(solution)/shard_map/all_gather | solution.py:71
  188.6 3.8 %fusion.135 = f32[2,128,768]{2,1,0:T(8,128)S(1)} fusion(bf16[1,2,2048,768]{3,2,1,0:T(8,128)(2,1)} %param.9, bf16[128,2048]{1,0:T(8,128)(2,1)S(1)} %all_gather.32), kind=kOutput, calls=%fused_computation.73 | convolution fusion | flops 805306368 | bytes 7602176 | tf_op jit(solution)/shard_map/td,edf->etf/dot_general | solution.py:72
  192.4 6.7 %fusion.114 = bf16[128,2048]{1,0:T(8,128)(2,1)S(1)} fusion(bf16[1,2,768,2048]{3,2,1,0:T(8,128)(2,1)} %param.11, f32[2,128]{1,0:T(2,128)S(1)} %get-tuple-element.81, bf16[1,2,2048,768]{3,2,1,0:T(8,128)(2,1)} %param.10, f32[2,128,768]{2,1,0:T(8,128)S(1)} %fusion.135, bf16[128,2048]{1,0:T(8,128)(2,1)S(1)} %all_gather.32), kind=kOutput, calls=%fused_computation.66 | convolution fusion | flops 1613627392 | bytes 14418944 | tf_op jit(solution)/shard_map/etf,efd->etd/dot_general | solution.py:75
  207.2 3.8 %collective-permute-done.26 = bf16[16,2048]{1,0:T(8,128)(2,1)S(1)} collective-permute-done((bf16[16,2048]{1,0:T(8,128)(2,1)S(1)}, bf16[16,2048]{1,0:T(8,128)(2,1)S(1)}, u32[]{:S(2)}, u32[]{:S(2)}) %collective-permute-start.26) | collective-permute-done | bytes 65568 | tf_op jit(solution)/shard_map/ppermute | solution.py:26
  212.6 5.4 %collective-permute-start.31 = (bf16[16,2048]{1,0:T(8,128)(2,1)S(1)}, bf16[16,2048]{1,0:T(8,128)(2,1)S(1)}, u32[]{:S(2)}, u32[]{:S(2)}) collective-permute-start(bf16[16,2048]{1,0:T(8,128)(2,1)S(1)} %get-tuple-element.16), channel_id=1, source_target_pairs={{0,8},{8,16},{16,24},{1,9},{9,17},{17,25},{2,10},{10,18},{18,26},{... | collective-permute-start | bytes 196616 | tf_op jit(solution)/shard_map/ppermute | solution.py:15
  220.4 14.9 %all_gather.33 = bf16[128,2048]{1,0:T(8,128)(2,1)S(1)} all-gather(bf16[16,2048]{1,0:T(8,128)(2,1)S(1)} %fusion.305), channel_id=1, replica_groups=mesh['section'=4,'expert'=8] {'expert'}, dimensions={0}, use_global_device_ids=true | all-gather | bytes 589824 | tf_op jit(solution)/shard_map/all_gather | solution.py:71
  235.3 3.8 %fusion.138 = f32[2,128,768]{2,1,0:T(8,128)S(1)} fusion(bf16[1,2,2048,768]{3,2,1,0:T(8,128)(2,1)} %param.9, bf16[128,2048]{1,0:T(8,128)(2,1)S(1)} %all_gather.33), kind=kOutput, calls=%fused_computation.74 | convolution fusion | flops 805306368 | bytes 7602176 | tf_op jit(solution)/shard_map/td,edf->etf/dot_general | solution.py:72
  239.1 6.7 %fusion.111 = bf16[128,2048]{1,0:T(8,128)(2,1)S(1)} fusion(bf16[1,2,768,2048]{3,2,1,0:T(8,128)(2,1)} %param.11, f32[2,128]{1,0:T(2,128)S(1)} %get-tuple-element.80, bf16[1,2,2048,768]{3,2,1,0:T(8,128)(2,1)} %param.10, f32[2,128,768]{2,1,0:T(8,128)S(1)} %fusion.138, bf16[128,2048]{1,0:T(8,128)(2,1)S(1)} %all_gather.33), kind=kOutput, calls=%fused_computation.65 | convolution fusion | flops 1613627392 | bytes 14418944 | tf_op jit(solution)/shard_map/etf,efd->etd/dot_general | solution.py:75
  254.0 3.9 %collective-permute-done.34 = bf16[16,2048]{1,0:T(8,128)(2,1)S(1)} collective-permute-done((bf16[16,2048]{1,0:T(8,128)(2,1)S(1)}, bf16[16,2048]{1,0:T(8,128)(2,1)S(1)}, u32[]{:S(2)}, u32[]{:S(2)}) %collective-permute-start.34) | collective-permute-done | bytes 65568 | tf_op jit(solution)/shard_map/ppermute | solution.py:26
  259.5 5.3 %collective-permute-start.39 = (bf16[16,2048]{1,0:T(8,128)(2,1)S(1)}, bf16[16,2048]{1,0:T(8,128)(2,1)S(1)}, u32[]{:S(2)}, u32[]{:S(2)}) collective-permute-start(bf16[16,2048]{1,0:T(8,128)(2,1)S(1)} %get-tuple-element.12), channel_id=1, source_target_pairs={{0,8},{8,16},{16,24},{1,9},{9,17},{17,25},{2,10},{10,18},{18,26},{... | collective-permute-start | bytes 196616 | tf_op jit(solution)/shard_map/ppermute | solution.py:15
  267.2 14.7 %all_gather.34 = bf16[128,2048]{1,0:T(8,128)(2,1)S(1)} all-gather(bf16[16,2048]{1,0:T(8,128)(2,1)S(1)} %fusion.309), channel_id=1, replica_groups=mesh['section'=4,'expert'=8] {'expert'}, dimensions={0}, use_global_device_ids=true | all-gather | bytes 589824 | tf_op jit(solution)/shard_map/all_gather | solution.py:71
  281.8 3.8 %fusion.141 = f32[2,128,768]{2,1,0:T(8,128)S(1)} fusion(bf16[1,2,2048,768]{3,2,1,0:T(8,128)(2,1)} %param.9, bf16[128,2048]{1,0:T(8,128)(2,1)S(1)} %all_gather.34), kind=kOutput, calls=%fused_computation.75 | convolution fusion | flops 805306368 | bytes 7602176 | tf_op jit(solution)/shard_map/td,edf->etf/dot_general | solution.py:72
  285.6 6.7 %fusion.108 = bf16[128,2048]{1,0:T(8,128)(2,1)S(1)} fusion(bf16[1,2,768,2048]{3,2,1,0:T(8,128)(2,1)} %param.11, f32[2,128]{1,0:T(2,128)S(1)} %get-tuple-element.79, bf16[1,2,2048,768]{3,2,1,0:T(8,128)(2,1)} %param.10, f32[2,128,768]{2,1,0:T(8,128)S(1)} %fusion.141, bf16[128,2048]{1,0:T(8,128)(2,1)S(1)} %all_gather.34), kind=kOutput, calls=%fused_computation.64 | convolution fusion | flops 1613627392 | bytes 14418944 | tf_op jit(solution)/shard_map/etf,efd->etd/dot_general | solution.py:75
  300.6 3.9 %collective-permute-done.42 = bf16[16,2048]{1,0:T(8,128)(2,1)S(1)} collective-permute-done((bf16[16,2048]{1,0:T(8,128)(2,1)S(1)}, bf16[16,2048]{1,0:T(8,128)(2,1)S(1)}, u32[]{:S(2)}, u32[]{:S(2)}) %collective-permute-start.42) | collective-permute-done | bytes 65568 | tf_op jit(solution)/shard_map/ppermute | solution.py:26
  306.2 5.1 %collective-permute-start.47 = (bf16[16,2048]{1,0:T(8,128)(2,1)S(1)}, bf16[16,2048]{1,0:T(8,128)(2,1)S(1)}, u32[]{:S(2)}, u32[]{:S(2)}) collective-permute-start(bf16[16,2048]{1,0:T(8,128)(2,1)S(1)} %get-tuple-element.8), channel_id=1, source_target_pairs={{0,8},{8,16},{16,24},{1,9},{9,17},{17,25},{2,10},{10,18},{18,26},{... | collective-permute-start | bytes 196616 | tf_op jit(solution)/shard_map/ppermute | solution.py:15
  313.5 14.9 %all_gather.35 = bf16[128,2048]{1,0:T(8,128)(2,1)S(1)} all-gather(bf16[16,2048]{1,0:T(8,128)(2,1)S(1)} %fusion.313), channel_id=1, replica_groups=mesh['section'=4,'expert'=8] {'expert'}, dimensions={0}, use_global_device_ids=true | all-gather | bytes 589824 | tf_op jit(solution)/shard_map/all_gather | solution.py:71
  328.5 3.8 %fusion.144 = f32[2,128,768]{2,1,0:T(8,128)S(1)} fusion(bf16[1,2,2048,768]{3,2,1,0:T(8,128)(2,1)} %param.9, bf16[128,2048]{1,0:T(8,128)(2,1)S(1)} %all_gather.35), kind=kOutput, calls=%fused_computation.76 | convolution fusion | flops 805306368 | bytes 7602176 | tf_op jit(solution)/shard_map/td,edf->etf/dot_general | solution.py:72
  332.2 6.7 %fusion.105 = bf16[128,2048]{1,0:T(8,128)(2,1)S(1)} fusion(bf16[1,2,768,2048]{3,2,1,0:T(8,128)(2,1)} %param.11, f32[2,128]{1,0:T(2,128)S(1)} %get-tuple-element.78, bf16[1,2,2048,768]{3,2,1,0:T(8,128)(2,1)} %param.10, f32[2,128,768]{2,1,0:T(8,128)S(1)} %fusion.144, bf16[128,2048]{1,0:T(8,128)(2,1)S(1)} %all_gather.35), kind=kOutput, calls=%fused_computation.63 | convolution fusion | flops 1613627392 | bytes 14418944 | tf_op jit(solution)/shard_map/etf,efd->etd/dot_general | solution.py:75
  (151 shorter events, 103.1 us)
Async XLA Ops:
  59.8 7.1 %collective-permute-start = (bf16[16,2048]{1,0:T(8,128)(2,1)S(1)}, bf16[16,2048]{1,0:T(8,128)(2,1)S(1)}, u32[]{:S(2)}, u32[]{:S(2)}) collective-permute-start(bf16[16,2048]{1,0:T(8,128)(2,1)S(1)} %get-tuple-element.71), channel_id=1, source_target_pairs={{0,1},{1,2},{2,3},{3,4},{4,5},{5,6},{6,7},{7,0},{8,9},{9,10},{10,1... | collective-permute-start | bytes 196616 | tf_op jit(solution)/shard_map/ppermute | solution.py:26
  60.1 7.5 %collective-permute-start.1 = (bf16[16,2048]{1,0:T(8,128)(2,1)S(1)}, bf16[16,2048]{1,0:T(8,128)(2,1)S(1)}, u32[]{:S(2)}, u32[]{:S(2)}) collective-permute-start(bf16[16,2048]{1,0:T(8,128)(2,1)S(1)} %get-tuple-element.77), channel_id=1, source_target_pairs={{0,2},{1,3},{2,4},{3,5},{4,6},{5,7},{6,0},{7,1},{8,10},{9,11},{10,... | collective-permute-start | bytes 196616 | tf_op jit(solution)/shard_map/ppermute | solution.py:26
  62.1 9.8 %collective-permute-start.2 = (bf16[16,2048]{1,0:T(8,128)(2,1)S(1)}, bf16[16,2048]{1,0:T(8,128)(2,1)S(1)}, u32[]{:S(2)}, u32[]{:S(2)}) collective-permute-start(bf16[16,2048]{1,0:T(8,128)(2,1)S(1)} %get-tuple-element.76), channel_id=1, source_target_pairs={{0,3},{1,4},{2,5},{3,6},{4,7},{5,0},{6,1},{7,2},{8,11},{9,12},{10,... | collective-permute-start | bytes 196616 | tf_op jit(solution)/shard_map/ppermute | solution.py:26
  64.2 7.8 %collective-permute-start.3 = (bf16[16,2048]{1,0:T(8,128)(2,1)S(1)}, bf16[16,2048]{1,0:T(8,128)(2,1)S(1)}, u32[]{:S(2)}, u32[]{:S(2)}) collective-permute-start(bf16[16,2048]{1,0:T(8,128)(2,1)S(1)} %get-tuple-element.75), channel_id=1, source_target_pairs={{0,4},{1,5},{2,6},{3,7},{4,0},{5,1},{6,2},{7,3},{8,12},{9,13},{10,... | collective-permute-start | bytes 196616 | tf_op jit(solution)/shard_map/ppermute | solution.py:26
  106.3 8.4 %collective-permute-start.11 = (bf16[16,2048]{1,0:T(8,128)(2,1)S(1)}, bf16[16,2048]{1,0:T(8,128)(2,1)S(1)}, u32[]{:S(2)}, u32[]{:S(2)}) collective-permute-start(bf16[16,2048]{1,0:T(8,128)(2,1)S(1)} %get-tuple-element.68), channel_id=1, source_target_pairs={{0,4},{1,5},{2,6},{3,7},{4,0},{5,1},{6,2},{7,3},{8,12},{9,13},{10,... | collective-permute-start | bytes 196616 | tf_op jit(solution)/shard_map/ppermute | solution.py:26
  114.7 6.8 %collective-permute-start.9 = (bf16[16,2048]{1,0:T(8,128)(2,1)S(1)}, bf16[16,2048]{1,0:T(8,128)(2,1)S(1)}, u32[]{:S(2)}, u32[]{:S(2)}) collective-permute-start(bf16[16,2048]{1,0:T(8,128)(2,1)S(1)} %get-tuple-element.70), channel_id=1, source_target_pairs={{0,2},{1,3},{2,4},{3,5},{4,6},{5,7},{6,0},{7,1},{8,10},{9,11},{10,... | collective-permute-start | bytes 196616 | tf_op jit(solution)/shard_map/ppermute | solution.py:26
  154.3 6.9 %collective-permute-start.17 = (bf16[16,2048]{1,0:T(8,128)(2,1)S(1)}, bf16[16,2048]{1,0:T(8,128)(2,1)S(1)}, u32[]{:S(2)}, u32[]{:S(2)}) collective-permute-start(bf16[16,2048]{1,0:T(8,128)(2,1)S(1)} %get-tuple-element.63), channel_id=1, source_target_pairs={{0,2},{1,3},{2,4},{3,5},{4,6},{5,7},{6,0},{7,1},{8,10},{9,11},{10,... | collective-permute-start | bytes 196616 | tf_op jit(solution)/shard_map/ppermute | solution.py:26
  154.3 11.5 %collective-permute-start.18 = (bf16[16,2048]{1,0:T(8,128)(2,1)S(1)}, bf16[16,2048]{1,0:T(8,128)(2,1)S(1)}, u32[]{:S(2)}, u32[]{:S(2)}) collective-permute-start(bf16[16,2048]{1,0:T(8,128)(2,1)S(1)} %get-tuple-element.62), channel_id=1, source_target_pairs={{0,3},{1,4},{2,5},{3,6},{4,7},{5,0},{6,1},{7,2},{8,11},{9,12},{10,... | collective-permute-start | bytes 196616 | tf_op jit(solution)/shard_map/ppermute | solution.py:26
  156.4 9.6 %collective-permute-start.19 = (bf16[16,2048]{1,0:T(8,128)(2,1)S(1)}, bf16[16,2048]{1,0:T(8,128)(2,1)S(1)}, u32[]{:S(2)}, u32[]{:S(2)}) collective-permute-start(bf16[16,2048]{1,0:T(8,128)(2,1)S(1)} %get-tuple-element.61), channel_id=1, source_target_pairs={{0,4},{1,5},{2,6},{3,7},{4,0},{5,1},{6,2},{7,3},{8,12},{9,13},{10,... | collective-permute-start | bytes 196616 | tf_op jit(solution)/shard_map/ppermute | solution.py:26
  158.1 7.8 %collective-permute-start.20 = (bf16[16,2048]{1,0:T(8,128)(2,1)S(1)}, bf16[16,2048]{1,0:T(8,128)(2,1)S(1)}, u32[]{:S(2)}, u32[]{:S(2)}) collective-permute-start(bf16[16,2048]{1,0:T(8,128)(2,1)S(1)} %get-tuple-element.60), channel_id=1, source_target_pairs={{0,5},{1,6},{2,7},{3,0},{4,1},{5,2},{6,3},{7,4},{8,13},{9,14},{10,... | collective-permute-start | bytes 196616 | tf_op jit(solution)/shard_map/ppermute | solution.py:26
  199.6 6.9 %collective-permute-start.25 = (bf16[16,2048]{1,0:T(8,128)(2,1)S(1)}, bf16[16,2048]{1,0:T(8,128)(2,1)S(1)}, u32[]{:S(2)}, u32[]{:S(2)}) collective-permute-start(bf16[16,2048]{1,0:T(8,128)(2,1)S(1)} %get-tuple-element.56), channel_id=1, source_target_pairs={{0,2},{1,3},{2,4},{3,5},{4,6},{5,7},{6,0},{7,1},{8,10},{9,11},{10,... | collective-permute-start | bytes 196616 | tf_op jit(solution)/shard_map/ppermute | solution.py:26
  200.9 10.1 %collective-permute-start.26 = (bf16[16,2048]{1,0:T(8,128)(2,1)S(1)}, bf16[16,2048]{1,0:T(8,128)(2,1)S(1)}, u32[]{:S(2)}, u32[]{:S(2)}) collective-permute-start(bf16[16,2048]{1,0:T(8,128)(2,1)S(1)} %get-tuple-element.55), channel_id=1, source_target_pairs={{0,3},{1,4},{2,5},{3,6},{4,7},{5,0},{6,1},{7,2},{8,11},{9,12},{10,... | collective-permute-start | bytes 196616 | tf_op jit(solution)/shard_map/ppermute | solution.py:26
  203.0 8.4 %collective-permute-start.27 = (bf16[16,2048]{1,0:T(8,128)(2,1)S(1)}, bf16[16,2048]{1,0:T(8,128)(2,1)S(1)}, u32[]{:S(2)}, u32[]{:S(2)}) collective-permute-start(bf16[16,2048]{1,0:T(8,128)(2,1)S(1)} %get-tuple-element.54), channel_id=1, source_target_pairs={{0,4},{1,5},{2,6},{3,7},{4,0},{5,1},{6,2},{7,3},{8,12},{9,13},{10,... | collective-permute-start | bytes 196616 | tf_op jit(solution)/shard_map/ppermute | solution.py:26
  204.4 7.1 %collective-permute-start.28 = (bf16[16,2048]{1,0:T(8,128)(2,1)S(1)}, bf16[16,2048]{1,0:T(8,128)(2,1)S(1)}, u32[]{:S(2)}, u32[]{:S(2)}) collective-permute-start(bf16[16,2048]{1,0:T(8,128)(2,1)S(1)} %get-tuple-element.53), channel_id=1, source_target_pairs={{0,5},{1,6},{2,7},{3,0},{4,1},{5,2},{6,3},{7,4},{8,13},{9,14},{10,... | collective-permute-start | bytes 196616 | tf_op jit(solution)/shard_map/ppermute | solution.py:26
  212.6 7.5 %collective-permute-start.31 = (bf16[16,2048]{1,0:T(8,128)(2,1)S(1)}, bf16[16,2048]{1,0:T(8,128)(2,1)S(1)}, u32[]{:S(2)}, u32[]{:S(2)}) collective-permute-start(bf16[16,2048]{1,0:T(8,128)(2,1)S(1)} %get-tuple-element.16), channel_id=1, source_target_pairs={{0,8},{8,16},{16,24},{1,9},{9,17},{17,25},{2,10},{10,18},{18,26},{... | collective-permute-start | bytes 196616 | tf_op jit(solution)/shard_map/ppermute | solution.py:15
  246.2 7.0 %collective-permute-start.33 = (bf16[16,2048]{1,0:T(8,128)(2,1)S(1)}, bf16[16,2048]{1,0:T(8,128)(2,1)S(1)}, u32[]{:S(2)}, u32[]{:S(2)}) collective-permute-start(bf16[16,2048]{1,0:T(8,128)(2,1)S(1)} %get-tuple-element.49), channel_id=1, source_target_pairs={{0,2},{1,3},{2,4},{3,5},{4,6},{5,7},{6,0},{7,1},{8,10},{9,11},{10,... | collective-permute-start | bytes 196616 | tf_op jit(solution)/shard_map/ppermute | solution.py:26
  247.7 10.2 %collective-permute-start.34 = (bf16[16,2048]{1,0:T(8,128)(2,1)S(1)}, bf16[16,2048]{1,0:T(8,128)(2,1)S(1)}, u32[]{:S(2)}, u32[]{:S(2)}) collective-permute-start(bf16[16,2048]{1,0:T(8,128)(2,1)S(1)} %get-tuple-element.48), channel_id=1, source_target_pairs={{0,3},{1,4},{2,5},{3,6},{4,7},{5,0},{6,1},{7,2},{8,11},{9,12},{10,... | collective-permute-start | bytes 196616 | tf_op jit(solution)/shard_map/ppermute | solution.py:26
  249.8 8.3 %collective-permute-start.35 = (bf16[16,2048]{1,0:T(8,128)(2,1)S(1)}, bf16[16,2048]{1,0:T(8,128)(2,1)S(1)}, u32[]{:S(2)}, u32[]{:S(2)}) collective-permute-start(bf16[16,2048]{1,0:T(8,128)(2,1)S(1)} %get-tuple-element.47), channel_id=1, source_target_pairs={{0,4},{1,5},{2,6},{3,7},{4,0},{5,1},{6,2},{7,3},{8,12},{9,13},{10,... | collective-permute-start | bytes 196616 | tf_op jit(solution)/shard_map/ppermute | solution.py:26
  251.2 6.9 %collective-permute-start.36 = (bf16[16,2048]{1,0:T(8,128)(2,1)S(1)}, bf16[16,2048]{1,0:T(8,128)(2,1)S(1)}, u32[]{:S(2)}, u32[]{:S(2)}) collective-permute-start(bf16[16,2048]{1,0:T(8,128)(2,1)S(1)} %get-tuple-element.46), channel_id=1, source_target_pairs={{0,5},{1,6},{2,7},{3,0},{4,1},{5,2},{6,3},{7,4},{8,13},{9,14},{10,... | collective-permute-start | bytes 196616 | tf_op jit(solution)/shard_map/ppermute | solution.py:26
  252.5 6.9 %collective-permute-start.37 = (bf16[16,2048]{1,0:T(8,128)(2,1)S(1)}, bf16[16,2048]{1,0:T(8,128)(2,1)S(1)}, u32[]{:S(2)}, u32[]{:S(2)}) collective-permute-start(bf16[16,2048]{1,0:T(8,128)(2,1)S(1)} %get-tuple-element.45), channel_id=1, source_target_pairs={{0,6},{1,7},{2,0},{3,1},{4,2},{5,3},{6,4},{7,5},{8,14},{9,15},{10,... | collective-permute-start | bytes 196616 | tf_op jit(solution)/shard_map/ppermute | solution.py:26
  259.5 7.4 %collective-permute-start.39 = (bf16[16,2048]{1,0:T(8,128)(2,1)S(1)}, bf16[16,2048]{1,0:T(8,128)(2,1)S(1)}, u32[]{:S(2)}, u32[]{:S(2)}) collective-permute-start(bf16[16,2048]{1,0:T(8,128)(2,1)S(1)} %get-tuple-element.12), channel_id=1, source_target_pairs={{0,8},{8,16},{16,24},{1,9},{9,17},{17,25},{2,10},{10,18},{18,26},{... | collective-permute-start | bytes 196616 | tf_op jit(solution)/shard_map/ppermute | solution.py:15
  292.7 7.1 %collective-permute-start.41 = (bf16[16,2048]{1,0:T(8,128)(2,1)S(1)}, bf16[16,2048]{1,0:T(8,128)(2,1)S(1)}, u32[]{:S(2)}, u32[]{:S(2)}) collective-permute-start(bf16[16,2048]{1,0:T(8,128)(2,1)S(1)} %get-tuple-element.42), channel_id=1, source_target_pairs={{0,2},{1,3},{2,4},{3,5},{4,6},{5,7},{6,0},{7,1},{8,10},{9,11},{10,... | collective-permute-start | bytes 196616 | tf_op jit(solution)/shard_map/ppermute | solution.py:26
  294.3 10.2 %collective-permute-start.42 = (bf16[16,2048]{1,0:T(8,128)(2,1)S(1)}, bf16[16,2048]{1,0:T(8,128)(2,1)S(1)}, u32[]{:S(2)}, u32[]{:S(2)}) collective-permute-start(bf16[16,2048]{1,0:T(8,128)(2,1)S(1)} %get-tuple-element.41), channel_id=1, source_target_pairs={{0,3},{1,4},{2,5},{3,6},{4,7},{5,0},{6,1},{7,2},{8,11},{9,12},{10,... | collective-permute-start | bytes 196616 | tf_op jit(solution)/shard_map/ppermute | solution.py:26
  296.4 8.2 %collective-permute-start.43 = (bf16[16,2048]{1,0:T(8,128)(2,1)S(1)}, bf16[16,2048]{1,0:T(8,128)(2,1)S(1)}, u32[]{:S(2)}, u32[]{:S(2)}) collective-permute-start(bf16[16,2048]{1,0:T(8,128)(2,1)S(1)} %get-tuple-element.40), channel_id=1, source_target_pairs={{0,4},{1,5},{2,6},{3,7},{4,0},{5,1},{6,2},{7,3},{8,12},{9,13},{10,... | collective-permute-start | bytes 196616 | tf_op jit(solution)/shard_map/ppermute | solution.py:26
  297.7 6.9 %collective-permute-start.44 = (bf16[16,2048]{1,0:T(8,128)(2,1)S(1)}, bf16[16,2048]{1,0:T(8,128)(2,1)S(1)}, u32[]{:S(2)}, u32[]{:S(2)}) collective-permute-start(bf16[16,2048]{1,0:T(8,128)(2,1)S(1)} %get-tuple-element.39), channel_id=1, source_target_pairs={{0,5},{1,6},{2,7},{3,0},{4,1},{5,2},{6,3},{7,4},{8,13},{9,14},{10,... | collective-permute-start | bytes 196616 | tf_op jit(solution)/shard_map/ppermute | solution.py:26
  299.1 7.0 %collective-permute-start.45 = (bf16[16,2048]{1,0:T(8,128)(2,1)S(1)}, bf16[16,2048]{1,0:T(8,128)(2,1)S(1)}, u32[]{:S(2)}, u32[]{:S(2)}) collective-permute-start(bf16[16,2048]{1,0:T(8,128)(2,1)S(1)} %get-tuple-element.38), channel_id=1, source_target_pairs={{0,6},{1,7},{2,0},{3,1},{4,2},{5,3},{6,4},{7,5},{8,14},{9,15},{10,... | collective-permute-start | bytes 196616 | tf_op jit(solution)/shard_map/ppermute | solution.py:26
  306.2 7.1 %collective-permute-start.47 = (bf16[16,2048]{1,0:T(8,128)(2,1)S(1)}, bf16[16,2048]{1,0:T(8,128)(2,1)S(1)}, u32[]{:S(2)}, u32[]{:S(2)}) collective-permute-start(bf16[16,2048]{1,0:T(8,128)(2,1)S(1)} %get-tuple-element.8), channel_id=1, source_target_pairs={{0,8},{8,16},{16,24},{1,9},{9,17},{17,25},{2,10},{10,18},{18,26},{... | collective-permute-start | bytes 196616 | tf_op jit(solution)/shard_map/ppermute | solution.py:15
  339.4 7.0 %collective-permute-start.49 = (bf16[16,2048]{1,0:T(8,128)(2,1)S(1)}, bf16[16,2048]{1,0:T(8,128)(2,1)S(1)}, u32[]{:S(2)}, u32[]{:S(2)}) collective-permute-start(bf16[16,2048]{1,0:T(8,128)(2,1)S(1)} %get-tuple-element.35), channel_id=1, source_target_pairs={{0,2},{1,3},{2,4},{3,5},{4,6},{5,7},{6,0},{7,1},{8,10},{9,11},{10,... | collective-permute-start | bytes 196616 | tf_op jit(solution)/shard_map/ppermute | solution.py:26
  340.9 10.2 %collective-permute-start.50 = (bf16[16,2048]{1,0:T(8,128)(2,1)S(1)}, bf16[16,2048]{1,0:T(8,128)(2,1)S(1)}, u32[]{:S(2)}, u32[]{:S(2)}) collective-permute-start(bf16[16,2048]{1,0:T(8,128)(2,1)S(1)} %get-tuple-element.34), channel_id=1, source_target_pairs={{0,3},{1,4},{2,5},{3,6},{4,7},{5,0},{6,1},{7,2},{8,11},{9,12},{10,... | collective-permute-start | bytes 196616 | tf_op jit(solution)/shard_map/ppermute | solution.py:26
  343.0 8.3 %collective-permute-start.51 = (bf16[16,2048]{1,0:T(8,128)(2,1)S(1)}, bf16[16,2048]{1,0:T(8,128)(2,1)S(1)}, u32[]{:S(2)}, u32[]{:S(2)}) collective-permute-start(bf16[16,2048]{1,0:T(8,128)(2,1)S(1)} %get-tuple-element.33), channel_id=1, source_target_pairs={{0,4},{1,5},{2,6},{3,7},{4,0},{5,1},{6,2},{7,3},{8,12},{9,13},{10,... | collective-permute-start | bytes 196616 | tf_op jit(solution)/shard_map/ppermute | solution.py:26
  344.4 6.9 %collective-permute-start.52 = (bf16[16,2048]{1,0:T(8,128)(2,1)S(1)}, bf16[16,2048]{1,0:T(8,128)(2,1)S(1)}, u32[]{:S(2)}, u32[]{:S(2)}) collective-permute-start(bf16[16,2048]{1,0:T(8,128)(2,1)S(1)} %get-tuple-element.32), channel_id=1, source_target_pairs={{0,5},{1,6},{2,7},{3,0},{4,1},{5,2},{6,3},{7,4},{8,13},{9,14},{10,... | collective-permute-start | bytes 196616 | tf_op jit(solution)/shard_map/ppermute | solution.py:26
  345.7 7.0 %collective-permute-start.53 = (bf16[16,2048]{1,0:T(8,128)(2,1)S(1)}, bf16[16,2048]{1,0:T(8,128)(2,1)S(1)}, u32[]{:S(2)}, u32[]{:S(2)}) collective-permute-start(bf16[16,2048]{1,0:T(8,128)(2,1)S(1)} %get-tuple-element.31), channel_id=1, source_target_pairs={{0,6},{1,7},{2,0},{3,1},{4,2},{5,3},{6,4},{7,5},{8,14},{9,15},{10,... | collective-permute-start | bytes 196616 | tf_op jit(solution)/shard_map/ppermute | solution.py:26
  (25 other events, 189.8 us)

commit v3 on v1

--- a/solution.py
+++ b/solution.py
@@ -15,33 +15,64 @@
     return lax.ppermute(array, axis, pairs)
 
 
+def chip_shift(array, axis, by):
+    count = lax.axis_size(axis)
+    chips = count // 2
+    pairs = [(i, ((i // 2 + by) % chips) * 2 + i % 2) for i in range(count)]
+    return lax.ppermute(array, axis, pairs)
+
+
+def core_swap(array, axis):
+    count = lax.axis_size(axis)
+    return lax.ppermute(array, axis, [(i, i ^ 1) for i in range(count)])
+
+
+def gather_blocks(array, axis):
+    chips = lax.axis_size(axis) // 2
+    own = jnp.stack([array] + [chip_shift(array, axis, k) for k in range(1, chips)])
+    return jnp.stack([own, core_swap(own, axis)])
+
+
+def scatter_blocks(partial, axis):
+    chips = lax.axis_size(axis) // 2
+    swapped = core_swap(partial[1].astype(jnp.bfloat16), axis)
+    chip_sum = partial[0] + swapped.astype(jnp.float32)
+    total = chip_sum[0]
+    for k in range(1, chips):
+        total = total + chip_shift(chip_sum[k].astype(jnp.bfloat16), axis, -k).astype(jnp.float32)
+    return total
+
+
 def rms_normed(hidden, gain):
     values = hidden.astype(jnp.float32)
     scale = lax.rsqrt(jnp.mean(values * values, axis=-1, keepdims=True) + EPSILON)
     return (values, (values * scale * gain).astype(jnp.bfloat16))
 
 
-def route_weights(routes, gates, first_expert, local_experts):
+def route_table(routes, gates, experts):
     weights = gates / jnp.sum(gates, axis=-1, keepdims=True)
-    mine = first_expert + jnp.arange(local_experts, dtype=jnp.int32)
-    hit = routes[..., None] == mine
+    hit = routes[..., None] == jnp.arange(experts, dtype=jnp.int32)
     return jnp.sum(jnp.where(hit, weights[..., None], 0.0), axis=-2)
 
 
 def on_device(tokens, norm_gain, gate_weight, up_weight, down_weight, routes, gates):
+    devices = lax.axis_size("expert")
     sections = lax.axis_size("section")
     section_index = lax.axis_index("section")
     expert_index = lax.axis_index("expert")
     local_experts = gate_weight.shape[1]
+    experts = local_experts * devices
+    chips = devices // 2
     gain = norm_gain[0]
     w_gate = gate_weight[0]
     w_up = up_weight[0]
     w_down = down_weight[0]
-    all_routes = lax.all_gather(routes[0], "expert", axis=1, tiled=True)
-    all_gates = lax.all_gather(gates[0], "expert", axis=1, tiled=True)
-    mixing = route_weights(all_routes, all_gates, expert_index * local_experts, local_experts)
     tok_rows = tokens.shape[1]
     width = tokens.shape[2]
+    table = route_table(routes[0], gates[0], experts)
+    table = gather_blocks(table, "expert")
+    mine = lax.dynamic_slice_in_dim(table, expert_index * local_experts, local_experts, axis=4)
+    mixing = jnp.transpose(mine, (2, 4, 0, 1, 3)).reshape(MB, local_experts, 2 * chips * tok_rows)
     held = jnp.zeros((tok_rows, width), jnp.bfloat16)
     collected = jnp.zeros((MB, tok_rows, width), jnp.bfloat16)
     for moment in range(MB + sections - 1):
@@ -56,15 +87,12 @@
         incoming = jnp.where(section_index == 0, first_rows, arrived)
         weight = lax.dynamic_index_in_dim(mixing, clipped, 0, keepdims=False)
         values, normed = rms_normed(incoming, gain)
-        rows = lax.all_gather(normed, "expert", axis=0, tiled=True)
+        rows = gather_blocks(normed, "expert").reshape(2 * chips * tok_rows, width)
         gate_part = jnp.einsum("td,edf->etf", rows, w_gate, preferred_element_type=jnp.float32)
         up_part = jnp.einsum("td,edf->etf", rows, w_up, preferred_element_type=jnp.float32)
-        inner = (jax.nn.silu(gate_part) * up_part).astype(jnp.bfloat16)
-        expert_out = jnp.einsum(
-            "etf,efd->etd", inner, w_down, preferred_element_type=jnp.float32
-        ).astype(jnp.bfloat16)
-        partial = jnp.sum(weight.T[:, :, None] * expert_out.astype(jnp.float32), axis=0)
-        mixed = lax.psum_scatter(partial, "expert", scatter_dimension=0, tiled=True)
+        inner = (jax.nn.silu(gate_part) * up_part * weight[:, :, None]).astype(jnp.bfloat16)
+        partial = jnp.einsum("etf,efd->td", inner, w_down, preferred_element_type=jnp.float32)
+        mixed = scatter_blocks(partial.reshape(2, chips, tok_rows, width), "expert")
         produced = (values + mixed).astype(jnp.bfloat16)
         held = jnp.where(active, produced, incoming)
         updated = lax.dynamic_update_index_in_dim(collected, held, clipped, 0)

time: 500 us -> 275 us (0.55)
  waiting for transfers between devices: 234 us -> 89.5 us
  blocking collectives: 135 us -> 0 us
  starting transfers between devices: 21.1 us -> 98 us
  between operations: 13.8 us -> 0.75 us
  matrix products: 80.9 us -> 72.8 us
    reduce_scatter x7 -> x0, waiting for transfers between devices: 223 us -> none  [on_device(): mixed = lax.psum_scatter(partial, 'expert', scatter_dimension=0, tiled=True)]
    all_gather x9 -> x0, blocking collectives: 135 us -> none  [the longest x7 105 us: on_device(): rows = lax.all_gather(normed, 'expert', axis=0, tiled=True)]
    ppermute x0 -> x60, waiting for transfers between devices: none -> 78.2 us  [the longest x45 58.2 us: chip_shift(): return lax.ppermute(array, axis, pairs)]
    ppermute x0 -> x60, starting transfers between devices: none -> 70.6 us  [the longest x45 68.6 us: chip_shift(): return lax.ppermute(array, axis, pairs)]
    dot_general x7, matrix products: 54.5 us -> 46.4 us  [on_device(): jnp.einsum('etf,efd->td', inner, w_down, preferred_element_type=jnp.float32)]
    ppermute x6, starting transfers between devices: 20.8 us -> 27.5 us  [shifted(): return lax.ppermute(array, axis, pairs)]
    select_n x7, other arithmetic: 7.18 us -> 1.04 us  [on_device(): collected = jnp.where(active, updated, collected)]
  transfers between devices with their start and end apart: 13 -> 66, of which waited for: 13 -> 49; matrix products, arithmetic and copies ran while one was open for 0% -> 2% of each run, Pallas kernels for 0% -> 0%
where the time goes in v3:
time: 275 us; the launch traced here: 272 us
  starting transfers between devices  98 us (36%)
  waiting for transfers between devices  89.5 us (33%)
  matrix products  72.8 us (26%)
  other arithmetic  8.72 us (3%)
    ppermute x45, starting transfers between devices, chip_shift(): return lax.ppermute(array, axis, pairs)  68.6 us
    ppermute x45, waiting for transfers between devices, chip_shift(): return lax.ppermute(array, axis, pairs)  58.2 us
    dot_general x7, matrix products, on_device(): jnp.einsum('etf,efd->td', inner, w_down, preferred_element_type=jnp.float32)  46.4 us
    ppermute x6, starting transfers between devices, shifted(): return lax.ppermute(array, axis, pairs)  27.5 us
    dot_general x7, matrix products, on_device(): jnp.einsum('td,edf->etf', rows, w_gate, preferred_element_type=jnp.float32)  26.4 us
    ppermute x15, waiting for transfers between devices, core_swap(): return lax.ppermute(array, axis, [(i, i ^ 1) for i in range(count)])  20 us
    ppermute x6, waiting for transfers between devices, shifted(): return lax.ppermute(array, axis, pairs)  11.3 us
  transfers between devices with their start and end apart: 66, of which 49 were waited for; matrix products, arithmetic and copies ran while one was open for 2% of the time, Pallas kernels for 0%

profile of v3, /device:TPU:0, one launch (start us, length us, event | category | flops | bytes accessed | tf_op | source)
XLA Modules:
  0.0 272.3 jit_solution(17110561018283469743)
XLA Ops:
  20.9 3.8 %fusion.63 = f32[2,128,768]{2,1,0:T(8,128)S(1)} fusion(bf16[128,2048,1]{1,0,2:T(8,128)(2,1)S(1)} %bitcast.571, bf16[1,2,2048,768]{3,2,1,0:T(8,128)(2,1)} %param.9), kind=kOutput, calls=%fused_computation.49 | convolution fusion | flops 805306368 | bytes 7602176 | tf_op jit(solution)/shard_map/td,edf->etf/dot_general | solution.py:91
  24.7 6.7 %fusion.42 = f32[128,2048]{1,0:T(8,128)S(1)} fusion(bf16[1,2,768,2048]{3,2,1,0:T(8,128)(2,1)} %param.11, bf16[128,2048,1]{1,0,2:T(8,128)(2,1)S(1)} %bitcast.572, bf16[1,2,2048,768]{3,2,1,0:T(8,128)(2,1)} %param.10, f32[2,128,768]{2,1,0:T(8,128)S(1)} %fusion.63, f32[2,128]{1,0:T(2,128)S(1)} %get-tuple-element.86), kind=kOutput, calls=%fused_computation.42 | convolution fusion | flops 1611988992 | bytes 14943232 | tf_op jit(solution)/shard_map/etf,efd->td/dot_general | solution.py:94
  38.3 3.6 %collective-permute-done.11 = bf16[16,2048]{1,0:T(8,128)(2,1)S(1)} collective-permute-done((bf16[16,2048]{1,0:T(8,128)(2,1)S(1)}, bf16[16,2048]{1,0:T(8,128)(2,1)S(1)}, u32[]{:S(2)}, u32[]{:S(2)}) %collective-permute-start.11) | collective-permute-done | bytes 65568 | tf_op jit(solution)/shard_map/ppermute | solution.py:22
  42.1 3.4 %collective-permute-start.12 = (bf16[16,2048]{1,0:T(8,128)(2,1)S(1)}, bf16[16,2048]{1,0:T(8,128)(2,1)S(1)}, u32[]{:S(2)}, u32[]{:S(2)}) collective-permute-start(bf16[16,2048]{1,0:T(8,128)(2,1)S(1)} %get-tuple-element.40), channel_id=1, source_target_pairs={{0,8},{8,16},{16,24},{1,9},{9,17},{17,25},{2,10},{10,18},{18,26},{... | collective-permute-start | bytes 196616 | tf_op jit(solution)/shard_map/ppermute | solution.py:15
  57.2 3.8 %fusion.66 = f32[2,128,768]{2,1,0:T(8,128)S(1)} fusion(bf16[128,2048,1]{1,0,2:T(8,128)(2,1)S(1)} %bitcast.573, bf16[1,2,2048,768]{3,2,1,0:T(8,128)(2,1)} %param.9), kind=kOutput, calls=%fused_computation.50 | convolution fusion | flops 805306368 | bytes 7602176 | tf_op jit(solution)/shard_map/td,edf->etf/dot_general | solution.py:91
  61.0 6.6 %fusion.45 = f32[128,2048]{1,0:T(8,128)S(1)} fusion(bf16[1,2,768,2048]{3,2,1,0:T(8,128)(2,1)} %param.11, bf16[128,2048,1]{1,0,2:T(8,128)(2,1)S(1)} %bitcast.574, bf16[1,2,2048,768]{3,2,1,0:T(8,128)(2,1)} %param.10, f32[2,128,768]{2,1,0:T(8,128)S(1)} %fusion.66, f32[2,128]{1,0:T(2,128)S(1)} %get-tuple-element.85), kind=kOutput, calls=%fused_computation.43 | convolution fusion | flops 1611988992 | bytes 14943232 | tf_op jit(solution)/shard_map/etf,efd->td/dot_general | solution.py:94
  69.3 3.1 %collective-permute-start.18 = (bf16[16,2048]{1,0:T(8,128)(2,1)S(1)}, bf16[16,2048]{1,0:T(8,128)(2,1)S(1)}, u32[]{:S(2)}, u32[]{:S(2)}) collective-permute-start(bf16[16,2048]{1,0:T(8,128)(2,1)S(1)} %get-tuple-element.68), channel_id=1, source_target_pairs={{0,6},{1,7},{2,0},{3,1},{4,2},{5,3},{6,4},{7,5},{8,14},{9,15},{10,... | collective-permute-start | bytes 196616 | tf_op jit(solution)/shard_map/ppermute | solution.py:22
  74.9 4.1 %collective-permute-done.19 = bf16[16,2048]{1,0:T(8,128)(2,1)S(1)} collective-permute-done((bf16[16,2048]{1,0:T(8,128)(2,1)S(1)}, bf16[16,2048]{1,0:T(8,128)(2,1)S(1)}, u32[]{:S(2)}, u32[]{:S(2)}) %collective-permute-start.19) | collective-permute-done | bytes 65568 | tf_op jit(solution)/shard_map/ppermute | solution.py:22
  79.1 4.3 %collective-permute-start.21 = (bf16[16,2048]{1,0:T(8,128)(2,1)S(1)}, bf16[16,2048]{1,0:T(8,128)(2,1)S(1)}, u32[]{:S(2)}, u32[]{:S(2)}) collective-permute-start(bf16[16,2048]{1,0:T(8,128)(2,1)S(1)} %get-tuple-element.34), channel_id=1, source_target_pairs={{0,8},{8,16},{16,24},{1,9},{9,17},{17,25},{2,10},{10,18},{18,26},{... | collective-permute-start | bytes 196616 | tf_op jit(solution)/shard_map/ppermute | solution.py:15
  94.7 3.8 %fusion.69 = f32[2,128,768]{2,1,0:T(8,128)S(1)} fusion(bf16[128,2048,1]{1,0,2:T(8,128)(2,1)S(1)} %bitcast.575, bf16[1,2,2048,768]{3,2,1,0:T(8,128)(2,1)} %param.9), kind=kOutput, calls=%fused_computation.51 | convolution fusion | flops 805306368 | bytes 7602176 | tf_op jit(solution)/shard_map/td,edf->etf/dot_general | solution.py:91
  98.5 6.6 %fusion.48 = f32[128,2048]{1,0:T(8,128)S(1)} fusion(bf16[1,2,768,2048]{3,2,1,0:T(8,128)(2,1)} %param.11, bf16[128,2048,1]{1,0,2:T(8,128)(2,1)S(1)} %bitcast.576, bf16[1,2,2048,768]{3,2,1,0:T(8,128)(2,1)} %param.10, f32[2,128,768]{2,1,0:T(8,128)S(1)} %fusion.69, f32[2,128]{1,0:T(2,128)S(1)} %get-tuple-element.84), kind=kOutput, calls=%fused_computation.44 | convolution fusion | flops 1611988992 | bytes 14943232 | tf_op jit(solution)/shard_map/etf,efd->td/dot_general | solution.py:94
  106.9 3.5 %collective-permute-start.27 = (bf16[16,2048]{1,0:T(8,128)(2,1)S(1)}, bf16[16,2048]{1,0:T(8,128)(2,1)S(1)}, u32[]{:S(2)}, u32[]{:S(2)}) collective-permute-start(bf16[16,2048]{1,0:T(8,128)(2,1)S(1)} %get-tuple-element.63), channel_id=1, source_target_pairs={{0,6},{1,7},{2,0},{3,1},{4,2},{5,3},{6,4},{7,5},{8,14},{9,15},{10,... | collective-permute-start | bytes 196616 | tf_op jit(solution)/shard_map/ppermute | solution.py:22
  112.9 4.1 %collective-permute-done.28 = bf16[16,2048]{1,0:T(8,128)(2,1)S(1)} collective-permute-done((bf16[16,2048]{1,0:T(8,128)(2,1)S(1)}, bf16[16,2048]{1,0:T(8,128)(2,1)S(1)}, u32[]{:S(2)}, u32[]{:S(2)}) %collective-permute-start.28) | collective-permute-done | bytes 65568 | tf_op jit(solution)/shard_map/ppermute | solution.py:22
  117.0 4.3 %collective-permute-start.30 = (bf16[16,2048]{1,0:T(8,128)(2,1)S(1)}, bf16[16,2048]{1,0:T(8,128)(2,1)S(1)}, u32[]{:S(2)}, u32[]{:S(2)}) collective-permute-start(bf16[16,2048]{1,0:T(8,128)(2,1)S(1)} %get-tuple-element.28), channel_id=1, source_target_pairs={{0,8},{8,16},{16,24},{1,9},{9,17},{17,25},{2,10},{10,18},{18,26},{... | collective-permute-start | bytes 196616 | tf_op jit(solution)/shard_map/ppermute | solution.py:15
  132.7 3.8 %fusion.72 = f32[2,128,768]{2,1,0:T(8,128)S(1)} fusion(bf16[128,2048,1]{1,0,2:T(8,128)(2,1)S(1)} %bitcast.577, bf16[1,2,2048,768]{3,2,1,0:T(8,128)(2,1)} %param.9), kind=kOutput, calls=%fused_computation.52 | convolution fusion | flops 805306368 | bytes 7602176 | tf_op jit(solution)/shard_map/td,edf->etf/dot_general | solution.py:91
  136.5 6.6 %fusion.51 = f32[128,2048]{1,0:T(8,128)S(1)} fusion(bf16[1,2,768,2048]{3,2,1,0:T(8,128)(2,1)} %param.11, bf16[128,2048,1]{1,0,2:T(8,128)(2,1)S(1)} %bitcast.578, bf16[1,2,2048,768]{3,2,1,0:T(8,128)(2,1)} %param.10, f32[2,128,768]{2,1,0:T(8,128)S(1)} %fusion.72, f32[2,128]{1,0:T(2,128)S(1)} %get-tuple-element.83), kind=kOutput, calls=%fused_computation.45 | convolution fusion | flops 1611988992 | bytes 14943232 | tf_op jit(solution)/shard_map/etf,efd->td/dot_general | solution.py:94
  144.9 3.5 %collective-permute-start.36 = (bf16[16,2048]{1,0:T(8,128)(2,1)S(1)}, bf16[16,2048]{1,0:T(8,128)(2,1)S(1)}, u32[]{:S(2)}, u32[]{:S(2)}) collective-permute-start(bf16[16,2048]{1,0:T(8,128)(2,1)S(1)} %get-tuple-element.58), channel_id=1, source_target_pairs={{0,6},{1,7},{2,0},{3,1},{4,2},{5,3},{6,4},{7,5},{8,14},{9,15},{10,... | collective-permute-start | bytes 196616 | tf_op jit(solution)/shard_map/ppermute | solution.py:22
  150.9 4.1 %collective-permute-done.37 = bf16[16,2048]{1,0:T(8,128)(2,1)S(1)} collective-permute-done((bf16[16,2048]{1,0:T(8,128)(2,1)S(1)}, bf16[16,2048]{1,0:T(8,128)(2,1)S(1)}, u32[]{:S(2)}, u32[]{:S(2)}) %collective-permute-start.37) | collective-permute-done | bytes 65568 | tf_op jit(solution)/shard_map/ppermute | solution.py:22
  155.1 5.2 %collective-permute-start.39 = (bf16[16,2048]{1,0:T(8,128)(2,1)S(1)}, bf16[16,2048]{1,0:T(8,128)(2,1)S(1)}, u32[]{:S(2)}, u32[]{:S(2)}) collective-permute-start(bf16[16,2048]{1,0:T(8,128)(2,1)S(1)} %get-tuple-element.22), channel_id=1, source_target_pairs={{0,8},{8,16},{16,24},{1,9},{9,17},{17,25},{2,10},{10,18},{18,26},{... | collective-permute-start | bytes 196616 | tf_op jit(solution)/shard_map/ppermute | solution.py:15
  172.2 3.8 %fusion.75 = f32[2,128,768]{2,1,0:T(8,128)S(1)} fusion(bf16[128,2048,1]{1,0,2:T(8,128)(2,1)S(1)} %bitcast.579, bf16[1,2,2048,768]{3,2,1,0:T(8,128)(2,1)} %param.9), kind=kOutput, calls=%fused_computation.53 | convolution fusion | flops 805306368 | bytes 7602176 | tf_op jit(solution)/shard_map/td,edf->etf/dot_general | solution.py:91
  176.0 6.6 %fusion.54 = f32[128,2048]{1,0:T(8,128)S(1)} fusion(bf16[1,2,768,2048]{3,2,1,0:T(8,128)(2,1)} %param.11, bf16[128,2048,1]{1,0,2:T(8,128)(2,1)S(1)} %bitcast.580, bf16[1,2,2048,768]{3,2,1,0:T(8,128)(2,1)} %param.10, f32[2,128,768]{2,1,0:T(8,128)S(1)} %fusion.75, f32[2,128]{1,0:T(2,128)S(1)} %get-tuple-element.82), kind=kOutput, calls=%fused_computation.46 | convolution fusion | flops 1611988992 | bytes 14943232 | tf_op jit(solution)/shard_map/etf,efd->td/dot_general | solution.py:94
  189.9 4.1 %collective-permute-done.46 = bf16[16,2048]{1,0:T(8,128)(2,1)S(1)} collective-permute-done((bf16[16,2048]{1,0:T(8,128)(2,1)S(1)}, bf16[16,2048]{1,0:T(8,128)(2,1)S(1)}, u32[]{:S(2)}, u32[]{:S(2)}) %collective-permute-start.46) | collective-permute-done | bytes 65568 | tf_op jit(solution)/shard_map/ppermute | solution.py:22
  194.1 5.2 %collective-permute-start.48 = (bf16[16,2048]{1,0:T(8,128)(2,1)S(1)}, bf16[16,2048]{1,0:T(8,128)(2,1)S(1)}, u32[]{:S(2)}, u32[]{:S(2)}) collective-permute-start(bf16[16,2048]{1,0:T(8,128)(2,1)S(1)} %get-tuple-element.16), channel_id=1, source_target_pairs={{0,8},{8,16},{16,24},{1,9},{9,17},{17,25},{2,10},{10,18},{18,26},{... | collective-permute-start | bytes 196616 | tf_op jit(solution)/shard_map/ppermute | solution.py:15
  210.6 3.8 %fusion.78 = f32[2,128,768]{2,1,0:T(8,128)S(1)} fusion(bf16[128,2048,1]{1,0,2:T(8,128)(2,1)S(1)} %bitcast.581, bf16[1,2,2048,768]{3,2,1,0:T(8,128)(2,1)} %param.9), kind=kOutput, calls=%fused_computation.54 | convolution fusion | flops 805306368 | bytes 7602176 | tf_op jit(solution)/shard_map/td,edf->etf/dot_general | solution.py:91
  214.4 6.6 %fusion.57 = f32[128,2048]{1,0:T(8,128)S(1)} fusion(bf16[1,2,768,2048]{3,2,1,0:T(8,128)(2,1)} %param.11, bf16[128,2048,1]{1,0,2:T(8,128)(2,1)S(1)} %bitcast.582, bf16[1,2,2048,768]{3,2,1,0:T(8,128)(2,1)} %param.10, f32[2,128,768]{2,1,0:T(8,128)S(1)} %fusion.78, f32[2,128]{1,0:T(2,128)S(1)} %get-tuple-element.81), kind=kOutput, calls=%fused_computation.47 | convolution fusion | flops 1611988992 | bytes 14943232 | tf_op jit(solution)/shard_map/etf,efd->td/dot_general | solution.py:94
  222.7 3.5 %collective-permute-start.54 = (bf16[16,2048]{1,0:T(8,128)(2,1)S(1)}, bf16[16,2048]{1,0:T(8,128)(2,1)S(1)}, u32[]{:S(2)}, u32[]{:S(2)}) collective-permute-start(bf16[16,2048]{1,0:T(8,128)(2,1)S(1)} %get-tuple-element.48), channel_id=1, source_target_pairs={{0,6},{1,7},{2,0},{3,1},{4,2},{5,3},{6,4},{7,5},{8,14},{9,15},{10,... | collective-permute-start | bytes 196616 | tf_op jit(solution)/shard_map/ppermute | solution.py:22
  228.7 4.1 %collective-permute-done.55 = bf16[16,2048]{1,0:T(8,128)(2,1)S(1)} collective-permute-done((bf16[16,2048]{1,0:T(8,128)(2,1)S(1)}, bf16[16,2048]{1,0:T(8,128)(2,1)S(1)}, u32[]{:S(2)}, u32[]{:S(2)}) %collective-permute-start.55) | collective-permute-done | bytes 65568 | tf_op jit(solution)/shard_map/ppermute | solution.py:22
  232.9 5.2 %collective-permute-start.57 = (bf16[16,2048]{1,0:T(8,128)(2,1)S(1)}, bf16[16,2048]{1,0:T(8,128)(2,1)S(1)}, u32[]{:S(2)}, u32[]{:S(2)}) collective-permute-start(bf16[16,2048]{1,0:T(8,128)(2,1)S(1)} %get-tuple-element.10), channel_id=1, source_target_pairs={{0,8},{8,16},{16,24},{1,9},{9,17},{17,25},{2,10},{10,18},{18,26},{... | collective-permute-start | bytes 196616 | tf_op jit(solution)/shard_map/ppermute | solution.py:15
  249.4 3.8 %fusion.81 = f32[2,128,768]{2,1,0:T(8,128)S(1)} fusion(bf16[128,2048,1]{1,0,2:T(8,128)(2,1)S(1)} %bitcast.569, bf16[1,2,2048,768]{3,2,1,0:T(8,128)(2,1)} %param.9), kind=kOutput, calls=%fused_computation.55 | convolution fusion | flops 805306368 | bytes 7602176 | tf_op jit(solution)/shard_map/td,edf->etf/dot_general | solution.py:91
  253.2 6.6 %fusion.60 = f32[128,2048]{1,0:T(8,128)S(1)} fusion(bf16[1,2,768,2048]{3,2,1,0:T(8,128)(2,1)} %param.11, bf16[128,2048,1]{1,0,2:T(8,128)(2,1)S(1)} %bitcast.570, bf16[1,2,2048,768]{3,2,1,0:T(8,128)(2,1)} %param.10, f32[2,128,768]{2,1,0:T(8,128)S(1)} %fusion.81, f32[2,128]{1,0:T(2,128)S(1)} %get-tuple-element.80), kind=kOutput, calls=%fused_computation.48 | convolution fusion | flops 1611988992 | bytes 14943232 | tf_op jit(solution)/shard_map/etf,efd->td/dot_general | solution.py:94
  261.5 3.5 %collective-permute-start.63 = (bf16[16,2048]{1,0:T(8,128)(2,1)S(1)}, bf16[16,2048]{1,0:T(8,128)(2,1)S(1)}, u32[]{:S(2)}, u32[]{:S(2)}) collective-permute-start(bf16[16,2048]{1,0:T(8,128)(2,1)S(1)} %get-tuple-element.43), channel_id=1, source_target_pairs={{0,6},{1,7},{2,0},{3,1},{4,2},{5,3},{6,4},{7,5},{8,14},{9,15},{10,... | collective-permute-start | bytes 196616 | tf_op jit(solution)/shard_map/ppermute | solution.py:22
  267.5 4.1 %collective-permute-done.64 = bf16[16,2048]{1,0:T(8,128)(2,1)S(1)} collective-permute-done((bf16[16,2048]{1,0:T(8,128)(2,1)S(1)}, bf16[16,2048]{1,0:T(8,128)(2,1)S(1)}, u32[]{:S(2)}, u32[]{:S(2)}) %collective-permute-start.64) | collective-permute-done | bytes 65568 | tf_op jit(solution)/shard_map/ppermute | solution.py:22
  (207 shorter events, 125.9 us)
Async XLA Ops:
  1.9 11.6 %collective-permute-start = (bf16[16,2048]{1,0:T(8,128)(2,1)S(1)}, bf16[16,2048]{1,0:T(8,128)(2,1)S(1)}, u32[]{:S(2)}, u32[]{:S(2)}) collective-permute-start(bf16[16,2048]{1,0:T(8,128)(2,1)S(1)} %fusion.220), channel_id=1, source_target_pairs={{0,2},{1,3},{2,4},{3,5},{4,6},{5,7},{6,0},{7,1},{8,10},{9,11},{10,... | collective-permute-start | bytes 196616 | tf_op jit(solution)/shard_map/ppermute | solution.py:22
  5.0 11.4 %collective-permute-start.1 = (bf16[16,2048]{1,0:T(8,128)(2,1)S(1)}, bf16[16,2048]{1,0:T(8,128)(2,1)S(1)}, u32[]{:S(2)}, u32[]{:S(2)}) collective-permute-start(bf16[16,2048]{1,0:T(8,128)(2,1)S(1)} %fusion.220), channel_id=1, source_target_pairs={{0,4},{1,5},{2,6},{3,7},{4,0},{5,1},{6,2},{7,3},{8,12},{9,13},{10,... | collective-permute-start | bytes 196616 | tf_op jit(solution)/shard_map/ppermute | solution.py:22
  7.6 8.8 %collective-permute-start.2 = (bf16[16,2048]{1,0:T(8,128)(2,1)S(1)}, bf16[16,2048]{1,0:T(8,128)(2,1)S(1)}, u32[]{:S(2)}, u32[]{:S(2)}) collective-permute-start(bf16[16,2048]{1,0:T(8,128)(2,1)S(1)} %fusion.220), channel_id=1, source_target_pairs={{0,6},{1,7},{2,0},{3,1},{4,2},{5,3},{6,4},{7,5},{8,14},{9,15},{10,... | collective-permute-start | bytes 196616 | tf_op jit(solution)/shard_map/ppermute | solution.py:22
  34.4 7.5 %collective-permute-start.11 = (bf16[16,2048]{1,0:T(8,128)(2,1)S(1)}, bf16[16,2048]{1,0:T(8,128)(2,1)S(1)}, u32[]{:S(2)}, u32[]{:S(2)}) collective-permute-start(bf16[16,2048]{1,0:T(8,128)(2,1)S(1)} %get-tuple-element.74), channel_id=1, source_target_pairs={{0,2},{1,3},{2,4},{3,5},{4,6},{5,7},{6,0},{7,1},{8,10},{9,11},{10,... | collective-permute-start | bytes 196616 | tf_op jit(solution)/shard_map/ppermute | solution.py:22
  47.6 6.3 %collective-permute-start.13 = (bf16[16,2048]{1,0:T(8,128)(2,1)S(1)}, bf16[16,2048]{1,0:T(8,128)(2,1)S(1)}, u32[]{:S(2)}, u32[]{:S(2)}) collective-permute-start(bf16[16,2048]{1,0:T(8,128)(2,1)S(1)} %fusion.224), channel_id=1, source_target_pairs={{0,2},{1,3},{2,4},{3,5},{4,6},{5,7},{6,0},{7,1},{8,10},{9,11},{10,... | collective-permute-start | bytes 196616 | tf_op jit(solution)/shard_map/ppermute | solution.py:22
  48.8 6.6 %collective-permute-start.14 = (bf16[16,2048]{1,0:T(8,128)(2,1)S(1)}, bf16[16,2048]{1,0:T(8,128)(2,1)S(1)}, u32[]{:S(2)}, u32[]{:S(2)}) collective-permute-start(bf16[16,2048]{1,0:T(8,128)(2,1)S(1)} %fusion.224), channel_id=1, source_target_pairs={{0,4},{1,5},{2,6},{3,7},{4,0},{5,1},{6,2},{7,3},{8,12},{9,13},{10,... | collective-permute-start | bytes 196616 | tf_op jit(solution)/shard_map/ppermute | solution.py:22
  72.4 6.6 %collective-permute-start.19 = (bf16[16,2048]{1,0:T(8,128)(2,1)S(1)}, bf16[16,2048]{1,0:T(8,128)(2,1)S(1)}, u32[]{:S(2)}, u32[]{:S(2)}) collective-permute-start(bf16[16,2048]{1,0:T(8,128)(2,1)S(1)} %get-tuple-element.70), channel_id=1, source_target_pairs={{0,4},{1,5},{2,6},{3,7},{4,0},{5,1},{6,2},{7,3},{8,12},{9,13},{10,... | collective-permute-start | bytes 196616 | tf_op jit(solution)/shard_map/ppermute | solution.py:22
  72.4 6.6 %collective-permute-start.20 = (bf16[16,2048]{1,0:T(8,128)(2,1)S(1)}, bf16[16,2048]{1,0:T(8,128)(2,1)S(1)}, u32[]{:S(2)}, u32[]{:S(2)}) collective-permute-start(bf16[16,2048]{1,0:T(8,128)(2,1)S(1)} %get-tuple-element.69), channel_id=1, source_target_pairs={{0,2},{1,3},{2,4},{3,5},{4,6},{5,7},{6,0},{7,1},{8,10},{9,11},{10,... | collective-permute-start | bytes 196616 | tf_op jit(solution)/shard_map/ppermute | solution.py:22
  79.1 6.2 %collective-permute-start.21 = (bf16[16,2048]{1,0:T(8,128)(2,1)S(1)}, bf16[16,2048]{1,0:T(8,128)(2,1)S(1)}, u32[]{:S(2)}, u32[]{:S(2)}) collective-permute-start(bf16[16,2048]{1,0:T(8,128)(2,1)S(1)} %get-tuple-element.34), channel_id=1, source_target_pairs={{0,8},{8,16},{16,24},{1,9},{9,17},{17,25},{2,10},{10,18},{18,26},{... | collective-permute-start | bytes 196616 | tf_op jit(solution)/shard_map/ppermute | solution.py:15
  85.5 6.2 %collective-permute-start.22 = (bf16[16,2048]{1,0:T(8,128)(2,1)S(1)}, bf16[16,2048]{1,0:T(8,128)(2,1)S(1)}, u32[]{:S(2)}, u32[]{:S(2)}) collective-permute-start(bf16[16,2048]{1,0:T(8,128)(2,1)S(1)} %fusion.228), channel_id=1, source_target_pairs={{0,2},{1,3},{2,4},{3,5},{4,6},{5,7},{6,0},{7,1},{8,10},{9,11},{10,... | collective-permute-start | bytes 196616 | tf_op jit(solution)/shard_map/ppermute | solution.py:22
  85.9 7.1 %collective-permute-start.23 = (bf16[16,2048]{1,0:T(8,128)(2,1)S(1)}, bf16[16,2048]{1,0:T(8,128)(2,1)S(1)}, u32[]{:S(2)}, u32[]{:S(2)}) collective-permute-start(bf16[16,2048]{1,0:T(8,128)(2,1)S(1)} %fusion.228), channel_id=1, source_target_pairs={{0,4},{1,5},{2,6},{3,7},{4,0},{5,1},{6,2},{7,3},{8,12},{9,13},{10,... | collective-permute-start | bytes 196616 | tf_op jit(solution)/shard_map/ppermute | solution.py:22
  110.4 6.6 %collective-permute-start.28 = (bf16[16,2048]{1,0:T(8,128)(2,1)S(1)}, bf16[16,2048]{1,0:T(8,128)(2,1)S(1)}, u32[]{:S(2)}, u32[]{:S(2)}) collective-permute-start(bf16[16,2048]{1,0:T(8,128)(2,1)S(1)} %get-tuple-element.65), channel_id=1, source_target_pairs={{0,4},{1,5},{2,6},{3,7},{4,0},{5,1},{6,2},{7,3},{8,12},{9,13},{10,... | collective-permute-start | bytes 196616 | tf_op jit(solution)/shard_map/ppermute | solution.py:22
  110.4 6.6 %collective-permute-start.29 = (bf16[16,2048]{1,0:T(8,128)(2,1)S(1)}, bf16[16,2048]{1,0:T(8,128)(2,1)S(1)}, u32[]{:S(2)}, u32[]{:S(2)}) collective-permute-start(bf16[16,2048]{1,0:T(8,128)(2,1)S(1)} %get-tuple-element.64), channel_id=1, source_target_pairs={{0,2},{1,3},{2,4},{3,5},{4,6},{5,7},{6,0},{7,1},{8,10},{9,11},{10,... | collective-permute-start | bytes 196616 | tf_op jit(solution)/shard_map/ppermute | solution.py:22
  117.0 6.2 %collective-permute-start.30 = (bf16[16,2048]{1,0:T(8,128)(2,1)S(1)}, bf16[16,2048]{1,0:T(8,128)(2,1)S(1)}, u32[]{:S(2)}, u32[]{:S(2)}) collective-permute-start(bf16[16,2048]{1,0:T(8,128)(2,1)S(1)} %get-tuple-element.28), channel_id=1, source_target_pairs={{0,8},{8,16},{16,24},{1,9},{9,17},{17,25},{2,10},{10,18},{18,26},{... | collective-permute-start | bytes 196616 | tf_op jit(solution)/shard_map/ppermute | solution.py:15
  123.5 6.2 %collective-permute-start.31 = (bf16[16,2048]{1,0:T(8,128)(2,1)S(1)}, bf16[16,2048]{1,0:T(8,128)(2,1)S(1)}, u32[]{:S(2)}, u32[]{:S(2)}) collective-permute-start(bf16[16,2048]{1,0:T(8,128)(2,1)S(1)} %fusion.232), channel_id=1, source_target_pairs={{0,2},{1,3},{2,4},{3,5},{4,6},{5,7},{6,0},{7,1},{8,10},{9,11},{10,... | collective-permute-start | bytes 196616 | tf_op jit(solution)/shard_map/ppermute | solution.py:22
  123.9 7.1 %collective-permute-start.32 = (bf16[16,2048]{1,0:T(8,128)(2,1)S(1)}, bf16[16,2048]{1,0:T(8,128)(2,1)S(1)}, u32[]{:S(2)}, u32[]{:S(2)}) collective-permute-start(bf16[16,2048]{1,0:T(8,128)(2,1)S(1)} %fusion.232), channel_id=1, source_target_pairs={{0,4},{1,5},{2,6},{3,7},{4,0},{5,1},{6,2},{7,3},{8,12},{9,13},{10,... | collective-permute-start | bytes 196616 | tf_op jit(solution)/shard_map/ppermute | solution.py:22
  148.4 6.6 %collective-permute-start.37 = (bf16[16,2048]{1,0:T(8,128)(2,1)S(1)}, bf16[16,2048]{1,0:T(8,128)(2,1)S(1)}, u32[]{:S(2)}, u32[]{:S(2)}) collective-permute-start(bf16[16,2048]{1,0:T(8,128)(2,1)S(1)} %get-tuple-element.60), channel_id=1, source_target_pairs={{0,4},{1,5},{2,6},{3,7},{4,0},{5,1},{6,2},{7,3},{8,12},{9,13},{10,... | collective-permute-start | bytes 196616 | tf_op jit(solution)/shard_map/ppermute | solution.py:22
  148.4 6.6 %collective-permute-start.38 = (bf16[16,2048]{1,0:T(8,128)(2,1)S(1)}, bf16[16,2048]{1,0:T(8,128)(2,1)S(1)}, u32[]{:S(2)}, u32[]{:S(2)}) collective-permute-start(bf16[16,2048]{1,0:T(8,128)(2,1)S(1)} %get-tuple-element.59), channel_id=1, source_target_pairs={{0,2},{1,3},{2,4},{3,5},{4,6},{5,7},{6,0},{7,1},{8,10},{9,11},{10,... | collective-permute-start | bytes 196616 | tf_op jit(solution)/shard_map/ppermute | solution.py:22
  155.1 7.1 %collective-permute-start.39 = (bf16[16,2048]{1,0:T(8,128)(2,1)S(1)}, bf16[16,2048]{1,0:T(8,128)(2,1)S(1)}, u32[]{:S(2)}, u32[]{:S(2)}) collective-permute-start(bf16[16,2048]{1,0:T(8,128)(2,1)S(1)} %get-tuple-element.22), channel_id=1, source_target_pairs={{0,8},{8,16},{16,24},{1,9},{9,17},{17,25},{2,10},{10,18},{18,26},{... | collective-permute-start | bytes 196616 | tf_op jit(solution)/shard_map/ppermute | solution.py:15
  164.5 6.1 %collective-permute-start.40 = (bf16[16,2048]{1,0:T(8,128)(2,1)S(1)}, bf16[16,2048]{1,0:T(8,128)(2,1)S(1)}, u32[]{:S(2)}, u32[]{:S(2)}) collective-permute-start(bf16[16,2048]{1,0:T(8,128)(2,1)S(1)} %fusion.236), channel_id=1, source_target_pairs={{0,2},{1,3},{2,4},{3,5},{4,6},{5,7},{6,0},{7,1},{8,10},{9,11},{10,... | collective-permute-start | bytes 196616 | tf_op jit(solution)/shard_map/ppermute | solution.py:22
  187.4 6.6 %collective-permute-start.46 = (bf16[16,2048]{1,0:T(8,128)(2,1)S(1)}, bf16[16,2048]{1,0:T(8,128)(2,1)S(1)}, u32[]{:S(2)}, u32[]{:S(2)}) collective-permute-start(bf16[16,2048]{1,0:T(8,128)(2,1)S(1)} %get-tuple-element.55), channel_id=1, source_target_pairs={{0,4},{1,5},{2,6},{3,7},{4,0},{5,1},{6,2},{7,3},{8,12},{9,13},{10,... | collective-permute-start | bytes 196616 | tf_op jit(solution)/shard_map/ppermute | solution.py:22
  187.4 6.6 %collective-permute-start.47 = (bf16[16,2048]{1,0:T(8,128)(2,1)S(1)}, bf16[16,2048]{1,0:T(8,128)(2,1)S(1)}, u32[]{:S(2)}, u32[]{:S(2)}) collective-permute-start(bf16[16,2048]{1,0:T(8,128)(2,1)S(1)} %get-tuple-element.54), channel_id=1, source_target_pairs={{0,2},{1,3},{2,4},{3,5},{4,6},{5,7},{6,0},{7,1},{8,10},{9,11},{10,... | collective-permute-start | bytes 196616 | tf_op jit(solution)/shard_map/ppermute | solution.py:22
  194.1 7.1 %collective-permute-start.48 = (bf16[16,2048]{1,0:T(8,128)(2,1)S(1)}, bf16[16,2048]{1,0:T(8,128)(2,1)S(1)}, u32[]{:S(2)}, u32[]{:S(2)}) collective-permute-start(bf16[16,2048]{1,0:T(8,128)(2,1)S(1)} %get-tuple-element.16), channel_id=1, source_target_pairs={{0,8},{8,16},{16,24},{1,9},{9,17},{17,25},{2,10},{10,18},{18,26},{... | collective-permute-start | bytes 196616 | tf_op jit(solution)/shard_map/ppermute | solution.py:15
  201.4 6.2 %collective-permute-start.49 = (bf16[16,2048]{1,0:T(8,128)(2,1)S(1)}, bf16[16,2048]{1,0:T(8,128)(2,1)S(1)}, u32[]{:S(2)}, u32[]{:S(2)}) collective-permute-start(bf16[16,2048]{1,0:T(8,128)(2,1)S(1)} %fusion.240), channel_id=1, source_target_pairs={{0,2},{1,3},{2,4},{3,5},{4,6},{5,7},{6,0},{7,1},{8,10},{9,11},{10,... | collective-permute-start | bytes 196616 | tf_op jit(solution)/shard_map/ppermute | solution.py:22
  201.8 7.1 %collective-permute-start.50 = (bf16[16,2048]{1,0:T(8,128)(2,1)S(1)}, bf16[16,2048]{1,0:T(8,128)(2,1)S(1)}, u32[]{:S(2)}, u32[]{:S(2)}) collective-permute-start(bf16[16,2048]{1,0:T(8,128)(2,1)S(1)} %fusion.240), channel_id=1, source_target_pairs={{0,4},{1,5},{2,6},{3,7},{4,0},{5,1},{6,2},{7,3},{8,12},{9,13},{10,... | collective-permute-start | bytes 196616 | tf_op jit(solution)/shard_map/ppermute | solution.py:22
  226.2 6.6 %collective-permute-start.55 = (bf16[16,2048]{1,0:T(8,128)(2,1)S(1)}, bf16[16,2048]{1,0:T(8,128)(2,1)S(1)}, u32[]{:S(2)}, u32[]{:S(2)}) collective-permute-start(bf16[16,2048]{1,0:T(8,128)(2,1)S(1)} %get-tuple-element.50), channel_id=1, source_target_pairs={{0,4},{1,5},{2,6},{3,7},{4,0},{5,1},{6,2},{7,3},{8,12},{9,13},{10,... | collective-permute-start | bytes 196616 | tf_op jit(solution)/shard_map/ppermute | solution.py:22
  226.2 6.6 %collective-permute-start.56 = (bf16[16,2048]{1,0:T(8,128)(2,1)S(1)}, bf16[16,2048]{1,0:T(8,128)(2,1)S(1)}, u32[]{:S(2)}, u32[]{:S(2)}) collective-permute-start(bf16[16,2048]{1,0:T(8,128)(2,1)S(1)} %get-tuple-element.49), channel_id=1, source_target_pairs={{0,2},{1,3},{2,4},{3,5},{4,6},{5,7},{6,0},{7,1},{8,10},{9,11},{10,... | collective-permute-start | bytes 196616 | tf_op jit(solution)/shard_map/ppermute | solution.py:22
  232.9 7.1 %collective-permute-start.57 = (bf16[16,2048]{1,0:T(8,128)(2,1)S(1)}, bf16[16,2048]{1,0:T(8,128)(2,1)S(1)}, u32[]{:S(2)}, u32[]{:S(2)}) collective-permute-start(bf16[16,2048]{1,0:T(8,128)(2,1)S(1)} %get-tuple-element.10), channel_id=1, source_target_pairs={{0,8},{8,16},{16,24},{1,9},{9,17},{17,25},{2,10},{10,18},{18,26},{... | collective-permute-start | bytes 196616 | tf_op jit(solution)/shard_map/ppermute | solution.py:15
  240.2 6.2 %collective-permute-start.58 = (bf16[16,2048]{1,0:T(8,128)(2,1)S(1)}, bf16[16,2048]{1,0:T(8,128)(2,1)S(1)}, u32[]{:S(2)}, u32[]{:S(2)}) collective-permute-start(bf16[16,2048]{1,0:T(8,128)(2,1)S(1)} %fusion.244), channel_id=1, source_target_pairs={{0,2},{1,3},{2,4},{3,5},{4,6},{5,7},{6,0},{7,1},{8,10},{9,11},{10,... | collective-permute-start | bytes 196616 | tf_op jit(solution)/shard_map/ppermute | solution.py:22
  240.6 7.1 %collective-permute-start.59 = (bf16[16,2048]{1,0:T(8,128)(2,1)S(1)}, bf16[16,2048]{1,0:T(8,128)(2,1)S(1)}, u32[]{:S(2)}, u32[]{:S(2)}) collective-permute-start(bf16[16,2048]{1,0:T(8,128)(2,1)S(1)} %fusion.244), channel_id=1, source_target_pairs={{0,4},{1,5},{2,6},{3,7},{4,0},{5,1},{6,2},{7,3},{8,12},{9,13},{10,... | collective-permute-start | bytes 196616 | tf_op jit(solution)/shard_map/ppermute | solution.py:22
  265.0 6.6 %collective-permute-start.64 = (bf16[16,2048]{1,0:T(8,128)(2,1)S(1)}, bf16[16,2048]{1,0:T(8,128)(2,1)S(1)}, u32[]{:S(2)}, u32[]{:S(2)}) collective-permute-start(bf16[16,2048]{1,0:T(8,128)(2,1)S(1)} %get-tuple-element.45), channel_id=1, source_target_pairs={{0,4},{1,5},{2,6},{3,7},{4,0},{5,1},{6,2},{7,3},{8,12},{9,13},{10,... | collective-permute-start | bytes 196616 | tf_op jit(solution)/shard_map/ppermute | solution.py:22
  265.0 6.6 %collective-permute-start.65 = (bf16[16,2048]{1,0:T(8,128)(2,1)S(1)}, bf16[16,2048]{1,0:T(8,128)(2,1)S(1)}, u32[]{:S(2)}, u32[]{:S(2)}) collective-permute-start(bf16[16,2048]{1,0:T(8,128)(2,1)S(1)} %get-tuple-element.44), channel_id=1, source_target_pairs={{0,2},{1,3},{2,4},{3,5},{4,6},{5,7},{6,0},{7,1},{8,10},{9,11},{10,... | collective-permute-start | bytes 196616 | tf_op jit(solution)/shard_map/ppermute | solution.py:22
  (36 other events, 169.2 us)

commit v4 on v3

--- a/solution.py
+++ b/solution.py
@@ -33,14 +33,21 @@
     return jnp.stack([own, core_swap(own, axis)])
 
 
-def scatter_blocks(partial, axis):
-    chips = lax.axis_size(axis) // 2
+def chip_sums(partial, axis):
     swapped = core_swap(partial[1].astype(jnp.bfloat16), axis)
-    chip_sum = partial[0] + swapped.astype(jnp.float32)
-    total = chip_sum[0]
-    for k in range(1, chips):
-        total = total + chip_shift(chip_sum[k].astype(jnp.bfloat16), axis, -k).astype(jnp.float32)
-    return total
+    return (partial[0] + swapped.astype(jnp.float32)).astype(jnp.bfloat16)
+
+
+def to_next_section(array, by):
+    sections = lax.axis_size("section")
+    count = lax.axis_size("expert")
+    chips = count // 2
+    pairs = [
+        (s * count + i, (s + 1) * count + ((i // 2 - by) % chips) * 2 + i % 2)
+        for s in range(sections - 1)
+        for i in range(count)
+    ]
+    return lax.ppermute(array, ("section", "expert"), pairs)
 
 
 def rms_normed(hidden, gain):
@@ -73,30 +80,36 @@
     table = gather_blocks(table, "expert")
     mine = lax.dynamic_slice_in_dim(table, expert_index * local_experts, local_experts, axis=4)
     mixing = jnp.transpose(mine, (2, 4, 0, 1, 3)).reshape(MB, local_experts, 2 * chips * tok_rows)
-    held = jnp.zeros((tok_rows, width), jnp.bfloat16)
+    incoming_next = jnp.zeros((tok_rows, width), jnp.bfloat16)
     collected = jnp.zeros((MB, tok_rows, width), jnp.bfloat16)
+    last = MB + sections - 2
     for moment in range(MB + sections - 1):
-        if moment > 0:
-            arrived = shifted(held, "section", 1)
-        else:
-            arrived = held
         batch_index = moment - section_index
         active = (batch_index >= 0) & (batch_index < MB)
         clipped = jnp.clip(batch_index, 0, MB - 1)
         first_rows = lax.dynamic_index_in_dim(tokens, clipped, 0, keepdims=False)
-        incoming = jnp.where(section_index == 0, first_rows, arrived)
+        incoming = jnp.where(section_index == 0, first_rows, incoming_next)
         weight = lax.dynamic_index_in_dim(mixing, clipped, 0, keepdims=False)
         values, normed = rms_normed(incoming, gain)
+        if moment < last:
+            residual_next = shifted(incoming, "section", 1)
         rows = gather_blocks(normed, "expert").reshape(2 * chips * tok_rows, width)
         gate_part = jnp.einsum("td,edf->etf", rows, w_gate, preferred_element_type=jnp.float32)
         up_part = jnp.einsum("td,edf->etf", rows, w_up, preferred_element_type=jnp.float32)
         inner = (jax.nn.silu(gate_part) * up_part * weight[:, :, None]).astype(jnp.bfloat16)
         partial = jnp.einsum("etf,efd->td", inner, w_down, preferred_element_type=jnp.float32)
-        mixed = scatter_blocks(partial.reshape(2, chips, tok_rows, width), "expert")
-        produced = (values + mixed).astype(jnp.bfloat16)
-        held = jnp.where(active, produced, incoming)
-        updated = lax.dynamic_update_index_in_dim(collected, held, clipped, 0)
+        sums = chip_sums(partial.reshape(2, chips, tok_rows, width), "expert")
+        total = values + sums[0].astype(jnp.float32)
+        for k in range(1, chips):
+            total = total + chip_shift(sums[k], "expert", -k).astype(jnp.float32)
+        produced = total.astype(jnp.bfloat16)
+        updated = lax.dynamic_update_index_in_dim(collected, produced, clipped, 0)
         collected = jnp.where(active, updated, collected)
+        if moment < last:
+            ahead = residual_next.astype(jnp.float32)
+            for k in range(chips):
+                ahead = ahead + to_next_section(sums[k], k).astype(jnp.float32)
+            incoming_next = ahead.astype(jnp.bfloat16)
     return collected[None]
 
 

time: 275 us -> 305 us (1.11)
  starting transfers between devices: 98 us -> 155 us
  waiting for transfers between devices: 89.5 us -> 63.9 us
    ppermute x0 -> x24, starting transfers between devices: none -> 67.7 us  [to_next_section(): return lax.ppermute(array, ('section', 'expert'), pairs)]
    ppermute x45, waiting for transfers between devices: 58.2 us -> 30.8 us  [chip_shift(): return lax.ppermute(array, axis, pairs)]
    ppermute x0 -> x24, waiting for transfers between devices: none -> 13.2 us  [to_next_section(): return lax.ppermute(array, ('section', 'expert'), pairs)]
    ppermute x6, waiting for transfers between devices: 11.3 us -> 0.02 us  [shifted(): return lax.ppermute(array, axis, pairs)]
    ppermute x45, starting transfers between devices: 68.6 us -> 59.9 us  [chip_shift(): return lax.ppermute(array, axis, pairs)]
  transfers between devices with their start and end apart: 66 -> 90, of which waited for: 49 -> 37; matrix products, arithmetic and copies ran while one was open for 2% -> 2% of each run, Pallas kernels for 0% -> 0%
where the time goes in v4:
time: 305 us; the launch traced here: 304 us
  starting transfers between devices  155 us (51%)
  matrix products  73.1 us (24%)
  waiting for transfers between devices  63.9 us (21%)
  other arithmetic  8.65 us (3%)
    ppermute x24, starting transfers between devices, to_next_section(): return lax.ppermute(array, ('section', 'expert'), pairs)  67.7 us
    ppermute x45, starting transfers between devices, chip_shift(): return lax.ppermute(array, axis, pairs)  59.9 us
    dot_general x7, matrix products, on_device(): jnp.einsum('etf,efd->td', inner, w_down, preferred_element_type=jnp.float32)  46.6 us
    ppermute x45, waiting for transfers between devices, chip_shift(): return lax.ppermute(array, axis, pairs)  30.8 us
    dot_general x7, matrix products, on_device(): jnp.einsum('td,edf->etf', rows, w_gate, preferred_element_type=jnp.float32)  26.4 us
    ppermute x6, starting transfers between devices, shifted(): return lax.ppermute(array, axis, pairs)  25 us
    ppermute x15, waiting for transfers between devices, core_swap(): return lax.ppermute(array, axis, [(i, i ^ 1) for i in range(count)])  19.9 us
    ppermute x24, waiting for transfers between devices, to_next_section(): return lax.ppermute(array, ('section', 'expert'), pairs)  13.2 us
  transfers between devices with their start and end apart: 90, of which 37 were waited for; matrix products, arithmetic and copies ran while one was open for 2% of the time, Pallas kernels for 0%

profile of v4, /device:TPU:0, one launch (start us, length us, event | category | flops | bytes accessed | tf_op | source)
XLA Modules:
  0.0 304.1 jit_solution(5982683507946924833)
XLA Ops:
  1.8 3.1 %collective-permute-start = (bf16[16,2048]{1,0:T(8,128)(2,1)S(1)}, bf16[16,2048]{1,0:T(8,128)(2,1)S(1)}, u32[]{:S(2)}, u32[]{:S(2)}) collective-permute-start(bf16[16,2048]{1,0:T(8,128)(2,1)S(1)} %fusion.220), channel_id=1, source_target_pairs={{0,2},{1,3},{2,4},{3,5},{4,6},{5,7},{6,0},{7,1},{8,10},{9,11},{10,... | collective-permute-start | bytes 196616 | tf_op jit(solution)/shard_map/ppermute | solution.py:22
  13.4 2.9 collective-permute-start.6
  20.7 3.8 %fusion.63 = f32[2,128,768]{2,1,0:T(8,128)S(1)} fusion(bf16[128,2048,1]{1,0,2:T(8,128)(2,1)S(1)} %bitcast.512, bf16[1,2,2048,768]{3,2,1,0:T(8,128)(2,1)} %param.9), kind=kOutput, calls=%fused_computation.49 | convolution fusion | flops 805306368 | bytes 7602176 | tf_op jit(solution)/shard_map/td,edf->etf/dot_general | solution.py:97
  24.5 6.7 %fusion.42 = f32[128,2048]{1,0:T(8,128)S(1)} fusion(bf16[1,2,768,2048]{3,2,1,0:T(8,128)(2,1)} %param.11, bf16[128,2048,1]{1,0,2:T(8,128)(2,1)S(1)} %bitcast.513, bf16[1,2,2048,768]{3,2,1,0:T(8,128)(2,1)} %param.10, f32[2,128,768]{2,1,0:T(8,128)S(1)} %fusion.63, f32[2,128]{1,0:T(2,128)S(1)} %get-tuple-element.74), kind=kOutput, calls=%fused_computation.42 | convolution fusion | flops 1611988992 | bytes 14943232 | tf_op jit(solution)/shard_map/etf,efd->td/dot_general | solution.py:100
  38.1 3.4 %collective-permute-start.12 = (bf16[16,2048]{1,0:T(8,128)(2,1)S(1)}, bf16[16,2048]{1,0:T(8,128)(2,1)S(1)}, u32[]{:S(2)}, u32[]{:S(2)}) collective-permute-start(bf16[16,2048]{1,0:T(8,128)(2,1)S(1)} %get-tuple-element.18), channel_id=1, source_target_pairs={{0,8},{8,16},{16,24},{1,9},{9,17},{17,25},{2,10},{10,18},{18,26},{... | collective-permute-start | bytes 196616 | tf_op jit(solution)/shard_map/ppermute | solution.py:15
  41.5 4.2 %collective-permute-start.14 = (bf16[16,2048]{1,0:T(8,128)(2,1)S(1)}, bf16[16,2048]{1,0:T(8,128)(2,1)S(1)}, u32[]{:S(2)}, u32[]{:S(2)}) collective-permute-start(bf16[16,2048]{1,0:T(8,128)(2,1)S(1)} %get-tuple-element.61), channel_id=1, source_target_pairs={{0,14},{1,15},{2,8},{3,9},{4,10},{5,11},{6,12},{7,13},{8,22},{9,23... | collective-permute-start | bytes 196616 | tf_op jit(solution)/shard_map/ppermute | solution.py:50
  45.7 3.7 %collective-permute-start.15 = (bf16[16,2048]{1,0:T(8,128)(2,1)S(1)}, bf16[16,2048]{1,0:T(8,128)(2,1)S(1)}, u32[]{:S(2)}, u32[]{:S(2)}) collective-permute-start(bf16[16,2048]{1,0:T(8,128)(2,1)S(1)} %get-tuple-element.63), channel_id=1, source_target_pairs={{0,12},{1,13},{2,14},{3,15},{4,8},{5,9},{6,10},{7,11},{8,20},{9,21... | collective-permute-start | bytes 196616 | tf_op jit(solution)/shard_map/ppermute | solution.py:50
  65.0 3.8 %fusion.66 = f32[2,128,768]{2,1,0:T(8,128)S(1)} fusion(bf16[128,2048,1]{1,0,2:T(8,128)(2,1)S(1)} %bitcast.514, bf16[1,2,2048,768]{3,2,1,0:T(8,128)(2,1)} %param.9), kind=kOutput, calls=%fused_computation.50 | convolution fusion | flops 805306368 | bytes 7602176 | tf_op jit(solution)/shard_map/td,edf->etf/dot_general | solution.py:97
  68.8 6.6 %fusion.45 = f32[128,2048]{1,0:T(8,128)S(1)} fusion(bf16[1,2,768,2048]{3,2,1,0:T(8,128)(2,1)} %param.11, bf16[128,2048,1]{1,0,2:T(8,128)(2,1)S(1)} %bitcast.515, bf16[1,2,2048,768]{3,2,1,0:T(8,128)(2,1)} %param.10, f32[2,128,768]{2,1,0:T(8,128)S(1)} %fusion.66, f32[2,128]{1,0:T(2,128)S(1)} %get-tuple-element.73), kind=kOutput, calls=%fused_computation.43 | convolution fusion | flops 1611988992 | bytes 14943232 | tf_op jit(solution)/shard_map/etf,efd->td/dot_general | solution.py:100
  80.5 4.3 %collective-permute-start.25 = (bf16[16,2048]{1,0:T(8,128)(2,1)S(1)}, bf16[16,2048]{1,0:T(8,128)(2,1)S(1)}, u32[]{:S(2)}, u32[]{:S(2)}) collective-permute-start(bf16[16,2048]{1,0:T(8,128)(2,1)S(1)} %get-tuple-element.16), channel_id=1, source_target_pairs={{0,8},{8,16},{16,24},{1,9},{9,17},{17,25},{2,10},{10,18},{18,26},{... | collective-permute-start | bytes 196616 | tf_op jit(solution)/shard_map/ppermute | solution.py:15
  84.8 5.6 %collective-permute-start.27 = (bf16[16,2048]{1,0:T(8,128)(2,1)S(1)}, bf16[16,2048]{1,0:T(8,128)(2,1)S(1)}, u32[]{:S(2)}, u32[]{:S(2)}) collective-permute-start(bf16[16,2048]{1,0:T(8,128)(2,1)S(1)} %get-tuple-element.54), channel_id=1, source_target_pairs={{0,14},{1,15},{2,8},{3,9},{4,10},{5,11},{6,12},{7,13},{8,22},{9,23... | collective-permute-start | bytes 196616 | tf_op jit(solution)/shard_map/ppermute | solution.py:50
  108.6 3.8 %fusion.69 = f32[2,128,768]{2,1,0:T(8,128)S(1)} fusion(bf16[128,2048,1]{1,0,2:T(8,128)(2,1)S(1)} %bitcast.516, bf16[1,2,2048,768]{3,2,1,0:T(8,128)(2,1)} %param.9), kind=kOutput, calls=%fused_computation.51 | convolution fusion | flops 805306368 | bytes 7602176 | tf_op jit(solution)/shard_map/td,edf->etf/dot_general | solution.py:97
  112.4 6.7 %fusion.48 = f32[128,2048]{1,0:T(8,128)S(1)} fusion(bf16[1,2,768,2048]{3,2,1,0:T(8,128)(2,1)} %param.11, bf16[128,2048,1]{1,0,2:T(8,128)(2,1)S(1)} %bitcast.517, bf16[1,2,2048,768]{3,2,1,0:T(8,128)(2,1)} %param.10, f32[2,128,768]{2,1,0:T(8,128)S(1)} %fusion.69, f32[2,128]{1,0:T(2,128)S(1)} %get-tuple-element.72), kind=kOutput, calls=%fused_computation.44 | convolution fusion | flops 1611988992 | bytes 14943232 | tf_op jit(solution)/shard_map/etf,efd->td/dot_general | solution.py:100
  123.9 4.3 %collective-permute-start.38 = (bf16[16,2048]{1,0:T(8,128)(2,1)S(1)}, bf16[16,2048]{1,0:T(8,128)(2,1)S(1)}, u32[]{:S(2)}, u32[]{:S(2)}) collective-permute-start(bf16[16,2048]{1,0:T(8,128)(2,1)S(1)} %get-tuple-element.14), channel_id=1, source_target_pairs={{0,8},{8,16},{16,24},{1,9},{9,17},{17,25},{2,10},{10,18},{18,26},{... | collective-permute-start | bytes 196616 | tf_op jit(solution)/shard_map/ppermute | solution.py:15
  128.2 5.9 %collective-permute-start.40 = (bf16[16,2048]{1,0:T(8,128)(2,1)S(1)}, bf16[16,2048]{1,0:T(8,128)(2,1)S(1)}, u32[]{:S(2)}, u32[]{:S(2)}) collective-permute-start(bf16[16,2048]{1,0:T(8,128)(2,1)S(1)} %get-tuple-element.47), channel_id=1, source_target_pairs={{0,14},{1,15},{2,8},{3,9},{4,10},{5,11},{6,12},{7,13},{8,22},{9,23... | collective-permute-start | bytes 196616 | tf_op jit(solution)/shard_map/ppermute | solution.py:50
  151.8 3.8 %fusion.72 = f32[2,128,768]{2,1,0:T(8,128)S(1)} fusion(bf16[128,2048,1]{1,0,2:T(8,128)(2,1)S(1)} %bitcast.518, bf16[1,2,2048,768]{3,2,1,0:T(8,128)(2,1)} %param.9), kind=kOutput, calls=%fused_computation.52 | convolution fusion | flops 805306368 | bytes 7602176 | tf_op jit(solution)/shard_map/td,edf->etf/dot_general | solution.py:97
  155.6 6.7 %fusion.51 = f32[128,2048]{1,0:T(8,128)S(1)} fusion(bf16[1,2,768,2048]{3,2,1,0:T(8,128)(2,1)} %param.11, bf16[128,2048,1]{1,0,2:T(8,128)(2,1)S(1)} %bitcast.519, bf16[1,2,2048,768]{3,2,1,0:T(8,128)(2,1)} %param.10, f32[2,128,768]{2,1,0:T(8,128)S(1)} %fusion.72, f32[2,128]{1,0:T(2,128)S(1)} %get-tuple-element.71), kind=kOutput, calls=%fused_computation.45 | convolution fusion | flops 1611988992 | bytes 14943232 | tf_op jit(solution)/shard_map/etf,efd->td/dot_general | solution.py:100
  167.3 4.4 %collective-permute-start.51 = (bf16[16,2048]{1,0:T(8,128)(2,1)S(1)}, bf16[16,2048]{1,0:T(8,128)(2,1)S(1)}, u32[]{:S(2)}, u32[]{:S(2)}) collective-permute-start(bf16[16,2048]{1,0:T(8,128)(2,1)S(1)} %get-tuple-element.12), channel_id=1, source_target_pairs={{0,8},{8,16},{16,24},{1,9},{9,17},{17,25},{2,10},{10,18},{18,26},{... | collective-permute-start | bytes 196616 | tf_op jit(solution)/shard_map/ppermute | solution.py:15
  171.8 5.2 %collective-permute-start.53 = (bf16[16,2048]{1,0:T(8,128)(2,1)S(1)}, bf16[16,2048]{1,0:T(8,128)(2,1)S(1)}, u32[]{:S(2)}, u32[]{:S(2)}) collective-permute-start(bf16[16,2048]{1,0:T(8,128)(2,1)S(1)} %get-tuple-element.40), channel_id=1, source_target_pairs={{0,14},{1,15},{2,8},{3,9},{4,10},{5,11},{6,12},{7,13},{8,22},{9,23... | collective-permute-start | bytes 196616 | tf_op jit(solution)/shard_map/ppermute | solution.py:50
  189.6 4.2 %collective-permute-done.56 = bf16[16,2048]{1,0:T(8,128)(2,1)S(1)} collective-permute-done((bf16[16,2048]{1,0:T(8,128)(2,1)S(1)}, bf16[16,2048]{1,0:T(8,128)(2,1)S(1)}, u32[]{:S(2)}, u32[]{:S(2)}) %collective-permute-start.56) | collective-permute-done | bytes 65568 | tf_op jit(solution)/shard_map/ppermute | solution.py:22
  195.5 3.8 %fusion.75 = f32[2,128,768]{2,1,0:T(8,128)S(1)} fusion(bf16[128,2048,1]{1,0,2:T(8,128)(2,1)S(1)} %bitcast.520, bf16[1,2,2048,768]{3,2,1,0:T(8,128)(2,1)} %param.9), kind=kOutput, calls=%fused_computation.53 | convolution fusion | flops 805306368 | bytes 7602176 | tf_op jit(solution)/shard_map/td,edf->etf/dot_general | solution.py:97
  199.3 6.7 %fusion.54 = f32[128,2048]{1,0:T(8,128)S(1)} fusion(bf16[1,2,768,2048]{3,2,1,0:T(8,128)(2,1)} %param.11, bf16[128,2048,1]{1,0,2:T(8,128)(2,1)S(1)} %bitcast.521, bf16[1,2,2048,768]{3,2,1,0:T(8,128)(2,1)} %param.10, f32[2,128,768]{2,1,0:T(8,128)S(1)} %fusion.75, f32[2,128]{1,0:T(2,128)S(1)} %get-tuple-element.70), kind=kOutput, calls=%fused_computation.46 | convolution fusion | flops 1611988992 | bytes 14943232 | tf_op jit(solution)/shard_map/etf,efd->td/dot_general | solution.py:100
  207.7 3.0 collective-permute-start.61
  211.3 4.3 %collective-permute-start.64 = (bf16[16,2048]{1,0:T(8,128)(2,1)S(1)}, bf16[16,2048]{1,0:T(8,128)(2,1)S(1)}, u32[]{:S(2)}, u32[]{:S(2)}) collective-permute-start(bf16[16,2048]{1,0:T(8,128)(2,1)S(1)} %get-tuple-element.10), channel_id=1, source_target_pairs={{0,8},{8,16},{16,24},{1,9},{9,17},{17,25},{2,10},{10,18},{18,26},{... | collective-permute-start | bytes 196616 | tf_op jit(solution)/shard_map/ppermute | solution.py:15
  215.5 4.8 %collective-permute-start.66 = (bf16[16,2048]{1,0:T(8,128)(2,1)S(1)}, bf16[16,2048]{1,0:T(8,128)(2,1)S(1)}, u32[]{:S(2)}, u32[]{:S(2)}) collective-permute-start(bf16[16,2048]{1,0:T(8,128)(2,1)S(1)} %get-tuple-element.33), channel_id=1, source_target_pairs={{0,14},{1,15},{2,8},{3,9},{4,10},{5,11},{6,12},{7,13},{8,22},{9,23... | collective-permute-start | bytes 196616 | tf_op jit(solution)/shard_map/ppermute | solution.py:50
  238.5 3.8 %fusion.78 = f32[2,128,768]{2,1,0:T(8,128)S(1)} fusion(bf16[128,2048,1]{1,0,2:T(8,128)(2,1)S(1)} %bitcast.522, bf16[1,2,2048,768]{3,2,1,0:T(8,128)(2,1)} %param.9), kind=kOutput, calls=%fused_computation.54 | convolution fusion | flops 805306368 | bytes 7602176 | tf_op jit(solution)/shard_map/td,edf->etf/dot_general | solution.py:97
  242.3 6.7 %fusion.57 = f32[128,2048]{1,0:T(8,128)S(1)} fusion(bf16[1,2,768,2048]{3,2,1,0:T(8,128)(2,1)} %param.11, bf16[128,2048,1]{1,0,2:T(8,128)(2,1)S(1)} %bitcast.523, bf16[1,2,2048,768]{3,2,1,0:T(8,128)(2,1)} %param.10, f32[2,128,768]{2,1,0:T(8,128)S(1)} %fusion.78, f32[2,128]{1,0:T(2,128)S(1)} %get-tuple-element.69), kind=kOutput, calls=%fused_computation.47 | convolution fusion | flops 1611988992 | bytes 14943232 | tf_op jit(solution)/shard_map/etf,efd->td/dot_general | solution.py:100
  253.8 4.3 %collective-permute-start.77 = (bf16[16,2048]{1,0:T(8,128)(2,1)S(1)}, bf16[16,2048]{1,0:T(8,128)(2,1)S(1)}, u32[]{:S(2)}, u32[]{:S(2)}) collective-permute-start(bf16[16,2048]{1,0:T(8,128)(2,1)S(1)} %get-tuple-element.8), channel_id=1, source_target_pairs={{0,8},{8,16},{16,24},{1,9},{9,17},{17,25},{2,10},{10,18},{18,26},{... | collective-permute-start | bytes 196616 | tf_op jit(solution)/shard_map/ppermute | solution.py:15
  258.2 5.9 %collective-permute-start.79 = (bf16[16,2048]{1,0:T(8,128)(2,1)S(1)}, bf16[16,2048]{1,0:T(8,128)(2,1)S(1)}, u32[]{:S(2)}, u32[]{:S(2)}) collective-permute-start(bf16[16,2048]{1,0:T(8,128)(2,1)S(1)} %get-tuple-element.26), channel_id=1, source_target_pairs={{0,14},{1,15},{2,8},{3,9},{4,10},{5,11},{6,12},{7,13},{8,22},{9,23... | collective-permute-start | bytes 196616 | tf_op jit(solution)/shard_map/ppermute | solution.py:50
  281.7 3.8 %fusion.81 = f32[2,128,768]{2,1,0:T(8,128)S(1)} fusion(bf16[128,2048,1]{1,0,2:T(8,128)(2,1)S(1)} %bitcast.510, bf16[1,2,2048,768]{3,2,1,0:T(8,128)(2,1)} %param.9), kind=kOutput, calls=%fused_computation.55 | convolution fusion | flops 805306368 | bytes 7602176 | tf_op jit(solution)/shard_map/td,edf->etf/dot_general | solution.py:97
  285.5 6.7 %fusion.60 = f32[128,2048]{1,0:T(8,128)S(1)} fusion(bf16[1,2,768,2048]{3,2,1,0:T(8,128)(2,1)} %param.11, bf16[128,2048,1]{1,0,2:T(8,128)(2,1)S(1)} %bitcast.511, bf16[1,2,2048,768]{3,2,1,0:T(8,128)(2,1)} %param.10, f32[2,128,768]{2,1,0:T(8,128)S(1)} %fusion.81, f32[2,128]{1,0:T(2,128)S(1)} %get-tuple-element.68), kind=kOutput, calls=%fused_computation.48 | convolution fusion | flops 1611988992 | bytes 14943232 | tf_op jit(solution)/shard_map/etf,efd->td/dot_general | solution.py:100
  299.1 4.2 %collective-permute-done.88 = bf16[16,2048]{1,0:T(8,128)(2,1)S(1)} collective-permute-done((bf16[16,2048]{1,0:T(8,128)(2,1)S(1)}, bf16[16,2048]{1,0:T(8,128)(2,1)S(1)}, u32[]{:S(2)}, u32[]{:S(2)}) %collective-permute-start.88) | collective-permute-done | bytes 65568 | tf_op jit(solution)/shard_map/ppermute | solution.py:22
  (255 shorter events, 152.0 us)
Async XLA Ops:
  1.8 11.6 %collective-permute-start = (bf16[16,2048]{1,0:T(8,128)(2,1)S(1)}, bf16[16,2048]{1,0:T(8,128)(2,1)S(1)}, u32[]{:S(2)}, u32[]{:S(2)}) collective-permute-start(bf16[16,2048]{1,0:T(8,128)(2,1)S(1)} %fusion.220), channel_id=1, source_target_pairs={{0,2},{1,3},{2,4},{3,5},{4,6},{5,7},{6,0},{7,1},{8,10},{9,11},{10,... | collective-permute-start | bytes 196616 | tf_op jit(solution)/shard_map/ppermute | solution.py:22
  4.8 11.4 %collective-permute-start.1 = (bf16[16,2048]{1,0:T(8,128)(2,1)S(1)}, bf16[16,2048]{1,0:T(8,128)(2,1)S(1)}, u32[]{:S(2)}, u32[]{:S(2)}) collective-permute-start(bf16[16,2048]{1,0:T(8,128)(2,1)S(1)} %fusion.220), channel_id=1, source_target_pairs={{0,4},{1,5},{2,6},{3,7},{4,0},{5,1},{6,2},{7,3},{8,12},{9,13},{10,... | collective-permute-start | bytes 196616 | tf_op jit(solution)/shard_map/ppermute | solution.py:22
  32.9 12.7 %collective-permute-start.10 = (bf16[16,2048]{1,0:T(8,128)(2,1)S(1)}, bf16[16,2048]{1,0:T(8,128)(2,1)S(1)}, u32[]{:S(2)}, u32[]{:S(2)}) collective-permute-start(bf16[16,2048]{1,0:T(8,128)(2,1)S(1)} %get-tuple-element.63), channel_id=1, source_target_pairs={{0,4},{1,5},{2,6},{3,7},{4,0},{5,1},{6,2},{7,3},{8,12},{9,13},{10,... | collective-permute-start | bytes 196616 | tf_op jit(solution)/shard_map/ppermute | solution.py:22
  34.3 15.2 %collective-permute-start.11 = (bf16[16,2048]{1,0:T(8,128)(2,1)S(1)}, bf16[16,2048]{1,0:T(8,128)(2,1)S(1)}, u32[]{:S(2)}, u32[]{:S(2)}) collective-permute-start(bf16[16,2048]{1,0:T(8,128)(2,1)S(1)} %get-tuple-element.62), channel_id=1, source_target_pairs={{0,2},{1,3},{2,4},{3,5},{4,6},{5,7},{6,0},{7,1},{8,10},{9,11},{10,... | collective-permute-start | bytes 196616 | tf_op jit(solution)/shard_map/ppermute | solution.py:22
  36.8 14.3 %collective-permute-start.9 = (bf16[16,2048]{1,0:T(8,128)(2,1)S(1)}, bf16[16,2048]{1,0:T(8,128)(2,1)S(1)}, u32[]{:S(2)}, u32[]{:S(2)}) collective-permute-start(bf16[16,2048]{1,0:T(8,128)(2,1)S(1)} %get-tuple-element.61), channel_id=1, source_target_pairs={{0,6},{1,7},{2,0},{3,1},{4,2},{5,3},{6,4},{7,5},{8,14},{9,15},{10,... | collective-permute-start | bytes 196616 | tf_op jit(solution)/shard_map/ppermute | solution.py:22
  38.1 15.0 %collective-permute-start.12 = (bf16[16,2048]{1,0:T(8,128)(2,1)S(1)}, bf16[16,2048]{1,0:T(8,128)(2,1)S(1)}, u32[]{:S(2)}, u32[]{:S(2)}) collective-permute-start(bf16[16,2048]{1,0:T(8,128)(2,1)S(1)} %get-tuple-element.18), channel_id=1, source_target_pairs={{0,8},{8,16},{16,24},{1,9},{9,17},{17,25},{2,10},{10,18},{18,26},{... | collective-permute-start | bytes 196616 | tf_op jit(solution)/shard_map/ppermute | solution.py:15
  41.5 11.6 %collective-permute-start.14 = (bf16[16,2048]{1,0:T(8,128)(2,1)S(1)}, bf16[16,2048]{1,0:T(8,128)(2,1)S(1)}, u32[]{:S(2)}, u32[]{:S(2)}) collective-permute-start(bf16[16,2048]{1,0:T(8,128)(2,1)S(1)} %get-tuple-element.61), channel_id=1, source_target_pairs={{0,14},{1,15},{2,8},{3,9},{4,10},{5,11},{6,12},{7,13},{8,22},{9,23... | collective-permute-start | bytes 196616 | tf_op jit(solution)/shard_map/ppermute | solution.py:50
  77.1 13.3 %collective-permute-start.22 = (bf16[16,2048]{1,0:T(8,128)(2,1)S(1)}, bf16[16,2048]{1,0:T(8,128)(2,1)S(1)}, u32[]{:S(2)}, u32[]{:S(2)}) collective-permute-start(bf16[16,2048]{1,0:T(8,128)(2,1)S(1)} %get-tuple-element.54), channel_id=1, source_target_pairs={{0,6},{1,7},{2,0},{3,1},{4,2},{5,3},{6,4},{7,5},{8,14},{9,15},{10,... | collective-permute-start | bytes 196616 | tf_op jit(solution)/shard_map/ppermute | solution.py:22
  79.9 13.0 %collective-permute-start.23 = (bf16[16,2048]{1,0:T(8,128)(2,1)S(1)}, bf16[16,2048]{1,0:T(8,128)(2,1)S(1)}, u32[]{:S(2)}, u32[]{:S(2)}) collective-permute-start(bf16[16,2048]{1,0:T(8,128)(2,1)S(1)} %get-tuple-element.56), channel_id=1, source_target_pairs={{0,4},{1,5},{2,6},{3,7},{4,0},{5,1},{6,2},{7,3},{8,12},{9,13},{10,... | collective-permute-start | bytes 196616 | tf_op jit(solution)/shard_map/ppermute | solution.py:22
  79.9 14.4 %collective-permute-start.24 = (bf16[16,2048]{1,0:T(8,128)(2,1)S(1)}, bf16[16,2048]{1,0:T(8,128)(2,1)S(1)}, u32[]{:S(2)}, u32[]{:S(2)}) collective-permute-start(bf16[16,2048]{1,0:T(8,128)(2,1)S(1)} %get-tuple-element.55), channel_id=1, source_target_pairs={{0,2},{1,3},{2,4},{3,5},{4,6},{5,7},{6,0},{7,1},{8,10},{9,11},{10,... | collective-permute-start | bytes 196616 | tf_op jit(solution)/shard_map/ppermute | solution.py:22
  80.5 15.8 %collective-permute-start.25 = (bf16[16,2048]{1,0:T(8,128)(2,1)S(1)}, bf16[16,2048]{1,0:T(8,128)(2,1)S(1)}, u32[]{:S(2)}, u32[]{:S(2)}) collective-permute-start(bf16[16,2048]{1,0:T(8,128)(2,1)S(1)} %get-tuple-element.16), channel_id=1, source_target_pairs={{0,8},{8,16},{16,24},{1,9},{9,17},{17,25},{2,10},{10,18},{18,26},{... | collective-permute-start | bytes 196616 | tf_op jit(solution)/shard_map/ppermute | solution.py:15
  84.8 11.5 %collective-permute-start.27 = (bf16[16,2048]{1,0:T(8,128)(2,1)S(1)}, bf16[16,2048]{1,0:T(8,128)(2,1)S(1)}, u32[]{:S(2)}, u32[]{:S(2)}) collective-permute-start(bf16[16,2048]{1,0:T(8,128)(2,1)S(1)} %get-tuple-element.54), channel_id=1, source_target_pairs={{0,14},{1,15},{2,8},{3,9},{4,10},{5,11},{6,12},{7,13},{8,22},{9,23... | collective-permute-start | bytes 196616 | tf_op jit(solution)/shard_map/ppermute | solution.py:50
  120.8 13.4 %collective-permute-start.35 = (bf16[16,2048]{1,0:T(8,128)(2,1)S(1)}, bf16[16,2048]{1,0:T(8,128)(2,1)S(1)}, u32[]{:S(2)}, u32[]{:S(2)}) collective-permute-start(bf16[16,2048]{1,0:T(8,128)(2,1)S(1)} %get-tuple-element.47), channel_id=1, source_target_pairs={{0,6},{1,7},{2,0},{3,1},{4,2},{5,3},{6,4},{7,5},{8,14},{9,15},{10,... | collective-permute-start | bytes 196616 | tf_op jit(solution)/shard_map/ppermute | solution.py:22
  123.2 12.6 %collective-permute-start.36 = (bf16[16,2048]{1,0:T(8,128)(2,1)S(1)}, bf16[16,2048]{1,0:T(8,128)(2,1)S(1)}, u32[]{:S(2)}, u32[]{:S(2)}) collective-permute-start(bf16[16,2048]{1,0:T(8,128)(2,1)S(1)} %get-tuple-element.49), channel_id=1, source_target_pairs={{0,4},{1,5},{2,6},{3,7},{4,0},{5,1},{6,2},{7,3},{8,12},{9,13},{10,... | collective-permute-start | bytes 196616 | tf_op jit(solution)/shard_map/ppermute | solution.py:22
  123.6 14.4 %collective-permute-start.37 = (bf16[16,2048]{1,0:T(8,128)(2,1)S(1)}, bf16[16,2048]{1,0:T(8,128)(2,1)S(1)}, u32[]{:S(2)}, u32[]{:S(2)}) collective-permute-start(bf16[16,2048]{1,0:T(8,128)(2,1)S(1)} %get-tuple-element.48), channel_id=1, source_target_pairs={{0,2},{1,3},{2,4},{3,5},{4,6},{5,7},{6,0},{7,1},{8,10},{9,11},{10,... | collective-permute-start | bytes 196616 | tf_op jit(solution)/shard_map/ppermute | solution.py:22
  123.9 16.2 %collective-permute-start.38 = (bf16[16,2048]{1,0:T(8,128)(2,1)S(1)}, bf16[16,2048]{1,0:T(8,128)(2,1)S(1)}, u32[]{:S(2)}, u32[]{:S(2)}) collective-permute-start(bf16[16,2048]{1,0:T(8,128)(2,1)S(1)} %get-tuple-element.14), channel_id=1, source_target_pairs={{0,8},{8,16},{16,24},{1,9},{9,17},{17,25},{2,10},{10,18},{18,26},{... | collective-permute-start | bytes 196616 | tf_op jit(solution)/shard_map/ppermute | solution.py:15
  128.2 11.8 %collective-permute-start.40 = (bf16[16,2048]{1,0:T(8,128)(2,1)S(1)}, bf16[16,2048]{1,0:T(8,128)(2,1)S(1)}, u32[]{:S(2)}, u32[]{:S(2)}) collective-permute-start(bf16[16,2048]{1,0:T(8,128)(2,1)S(1)} %get-tuple-element.47), channel_id=1, source_target_pairs={{0,14},{1,15},{2,8},{3,9},{4,10},{5,11},{6,12},{7,13},{8,22},{9,23... | collective-permute-start | bytes 196616 | tf_op jit(solution)/shard_map/ppermute | solution.py:50
  163.9 13.0 %collective-permute-start.48 = (bf16[16,2048]{1,0:T(8,128)(2,1)S(1)}, bf16[16,2048]{1,0:T(8,128)(2,1)S(1)}, u32[]{:S(2)}, u32[]{:S(2)}) collective-permute-start(bf16[16,2048]{1,0:T(8,128)(2,1)S(1)} %get-tuple-element.40), channel_id=1, source_target_pairs={{0,6},{1,7},{2,0},{3,1},{4,2},{5,3},{6,4},{7,5},{8,14},{9,15},{10,... | collective-permute-start | bytes 196616 | tf_op jit(solution)/shard_map/ppermute | solution.py:22
  166.7 12.7 %collective-permute-start.49 = (bf16[16,2048]{1,0:T(8,128)(2,1)S(1)}, bf16[16,2048]{1,0:T(8,128)(2,1)S(1)}, u32[]{:S(2)}, u32[]{:S(2)}) collective-permute-start(bf16[16,2048]{1,0:T(8,128)(2,1)S(1)} %get-tuple-element.42), channel_id=1, source_target_pairs={{0,4},{1,5},{2,6},{3,7},{4,0},{5,1},{6,2},{7,3},{8,12},{9,13},{10,... | collective-permute-start | bytes 196616 | tf_op jit(solution)/shard_map/ppermute | solution.py:22
  166.8 14.1 %collective-permute-start.50 = (bf16[16,2048]{1,0:T(8,128)(2,1)S(1)}, bf16[16,2048]{1,0:T(8,128)(2,1)S(1)}, u32[]{:S(2)}, u32[]{:S(2)}) collective-permute-start(bf16[16,2048]{1,0:T(8,128)(2,1)S(1)} %get-tuple-element.41), channel_id=1, source_target_pairs={{0,2},{1,3},{2,4},{3,5},{4,6},{5,7},{6,0},{7,1},{8,10},{9,11},{10,... | collective-permute-start | bytes 196616 | tf_op jit(solution)/shard_map/ppermute | solution.py:22
  167.3 15.5 %collective-permute-start.51 = (bf16[16,2048]{1,0:T(8,128)(2,1)S(1)}, bf16[16,2048]{1,0:T(8,128)(2,1)S(1)}, u32[]{:S(2)}, u32[]{:S(2)}) collective-permute-start(bf16[16,2048]{1,0:T(8,128)(2,1)S(1)} %get-tuple-element.12), channel_id=1, source_target_pairs={{0,8},{8,16},{16,24},{1,9},{9,17},{17,25},{2,10},{10,18},{18,26},{... | collective-permute-start | bytes 196616 | tf_op jit(solution)/shard_map/ppermute | solution.py:15
  171.8 11.1 %collective-permute-start.53 = (bf16[16,2048]{1,0:T(8,128)(2,1)S(1)}, bf16[16,2048]{1,0:T(8,128)(2,1)S(1)}, u32[]{:S(2)}, u32[]{:S(2)}) collective-permute-start(bf16[16,2048]{1,0:T(8,128)(2,1)S(1)} %get-tuple-element.40), channel_id=1, source_target_pairs={{0,14},{1,15},{2,8},{3,9},{4,10},{5,11},{6,12},{7,13},{8,22},{9,23... | collective-permute-start | bytes 196616 | tf_op jit(solution)/shard_map/ppermute | solution.py:50
  207.7 12.7 %collective-permute-start.61 = (bf16[16,2048]{1,0:T(8,128)(2,1)S(1)}, bf16[16,2048]{1,0:T(8,128)(2,1)S(1)}, u32[]{:S(2)}, u32[]{:S(2)}) collective-permute-start(bf16[16,2048]{1,0:T(8,128)(2,1)S(1)} %get-tuple-element.33), channel_id=1, source_target_pairs={{0,6},{1,7},{2,0},{3,1},{4,2},{5,3},{6,4},{7,5},{8,14},{9,15},{10,... | collective-permute-start | bytes 196616 | tf_op jit(solution)/shard_map/ppermute | solution.py:22
  210.6 12.2 %collective-permute-start.62 = (bf16[16,2048]{1,0:T(8,128)(2,1)S(1)}, bf16[16,2048]{1,0:T(8,128)(2,1)S(1)}, u32[]{:S(2)}, u32[]{:S(2)}) collective-permute-start(bf16[16,2048]{1,0:T(8,128)(2,1)S(1)} %get-tuple-element.35), channel_id=1, source_target_pairs={{0,4},{1,5},{2,6},{3,7},{4,0},{5,1},{6,2},{7,3},{8,12},{9,13},{10,... | collective-permute-start | bytes 196616 | tf_op jit(solution)/shard_map/ppermute | solution.py:22
  210.6 13.6 %collective-permute-start.63 = (bf16[16,2048]{1,0:T(8,128)(2,1)S(1)}, bf16[16,2048]{1,0:T(8,128)(2,1)S(1)}, u32[]{:S(2)}, u32[]{:S(2)}) collective-permute-start(bf16[16,2048]{1,0:T(8,128)(2,1)S(1)} %get-tuple-element.34), channel_id=1, source_target_pairs={{0,2},{1,3},{2,4},{3,5},{4,6},{5,7},{6,0},{7,1},{8,10},{9,11},{10,... | collective-permute-start | bytes 196616 | tf_op jit(solution)/shard_map/ppermute | solution.py:22
  211.3 14.9 %collective-permute-start.64 = (bf16[16,2048]{1,0:T(8,128)(2,1)S(1)}, bf16[16,2048]{1,0:T(8,128)(2,1)S(1)}, u32[]{:S(2)}, u32[]{:S(2)}) collective-permute-start(bf16[16,2048]{1,0:T(8,128)(2,1)S(1)} %get-tuple-element.10), channel_id=1, source_target_pairs={{0,8},{8,16},{16,24},{1,9},{9,17},{17,25},{2,10},{10,18},{18,26},{... | collective-permute-start | bytes 196616 | tf_op jit(solution)/shard_map/ppermute | solution.py:15
  215.5 10.7 %collective-permute-start.66 = (bf16[16,2048]{1,0:T(8,128)(2,1)S(1)}, bf16[16,2048]{1,0:T(8,128)(2,1)S(1)}, u32[]{:S(2)}, u32[]{:S(2)}) collective-permute-start(bf16[16,2048]{1,0:T(8,128)(2,1)S(1)} %get-tuple-element.33), channel_id=1, source_target_pairs={{0,14},{1,15},{2,8},{3,9},{4,10},{5,11},{6,12},{7,13},{8,22},{9,23... | collective-permute-start | bytes 196616 | tf_op jit(solution)/shard_map/ppermute | solution.py:50
  250.7 13.4 %collective-permute-start.74 = (bf16[16,2048]{1,0:T(8,128)(2,1)S(1)}, bf16[16,2048]{1,0:T(8,128)(2,1)S(1)}, u32[]{:S(2)}, u32[]{:S(2)}) collective-permute-start(bf16[16,2048]{1,0:T(8,128)(2,1)S(1)} %get-tuple-element.26), channel_id=1, source_target_pairs={{0,6},{1,7},{2,0},{3,1},{4,2},{5,3},{6,4},{7,5},{8,14},{9,15},{10,... | collective-permute-start | bytes 196616 | tf_op jit(solution)/shard_map/ppermute | solution.py:22
  253.2 12.6 %collective-permute-start.75 = (bf16[16,2048]{1,0:T(8,128)(2,1)S(1)}, bf16[16,2048]{1,0:T(8,128)(2,1)S(1)}, u32[]{:S(2)}, u32[]{:S(2)}) collective-permute-start(bf16[16,2048]{1,0:T(8,128)(2,1)S(1)} %get-tuple-element.28), channel_id=1, source_target_pairs={{0,4},{1,5},{2,6},{3,7},{4,0},{5,1},{6,2},{7,3},{8,12},{9,13},{10,... | collective-permute-start | bytes 196616 | tf_op jit(solution)/shard_map/ppermute | solution.py:22
  253.6 14.4 %collective-permute-start.76 = (bf16[16,2048]{1,0:T(8,128)(2,1)S(1)}, bf16[16,2048]{1,0:T(8,128)(2,1)S(1)}, u32[]{:S(2)}, u32[]{:S(2)}) collective-permute-start(bf16[16,2048]{1,0:T(8,128)(2,1)S(1)} %get-tuple-element.27), channel_id=1, source_target_pairs={{0,2},{1,3},{2,4},{3,5},{4,6},{5,7},{6,0},{7,1},{8,10},{9,11},{10,... | collective-permute-start | bytes 196616 | tf_op jit(solution)/shard_map/ppermute | solution.py:22
  253.8 16.2 %collective-permute-start.77 = (bf16[16,2048]{1,0:T(8,128)(2,1)S(1)}, bf16[16,2048]{1,0:T(8,128)(2,1)S(1)}, u32[]{:S(2)}, u32[]{:S(2)}) collective-permute-start(bf16[16,2048]{1,0:T(8,128)(2,1)S(1)} %get-tuple-element.8), channel_id=1, source_target_pairs={{0,8},{8,16},{16,24},{1,9},{9,17},{17,25},{2,10},{10,18},{18,26},{... | collective-permute-start | bytes 196616 | tf_op jit(solution)/shard_map/ppermute | solution.py:15
  258.2 11.8 %collective-permute-start.79 = (bf16[16,2048]{1,0:T(8,128)(2,1)S(1)}, bf16[16,2048]{1,0:T(8,128)(2,1)S(1)}, u32[]{:S(2)}, u32[]{:S(2)}) collective-permute-start(bf16[16,2048]{1,0:T(8,128)(2,1)S(1)} %get-tuple-element.26), channel_id=1, source_target_pairs={{0,14},{1,15},{2,8},{3,9},{4,10},{5,11},{6,12},{7,13},{8,22},{9,23... | collective-permute-start | bytes 196616 | tf_op jit(solution)/shard_map/ppermute | solution.py:50
  (60 other events, 324.2 us)

commit v5 on v3

--- a/solution.py
+++ b/solution.py
@@ -15,32 +15,33 @@
     return lax.ppermute(array, axis, pairs)
 
 
-def chip_shift(array, axis, by):
-    count = lax.axis_size(axis)
-    chips = count // 2
-    pairs = [(i, ((i // 2 + by) % chips) * 2 + i % 2) for i in range(count)]
-    return lax.ppermute(array, axis, pairs)
+def exchange_masks(count):
+    masks = []
+    bit = 1
+    while bit < count:
+        masks.append(bit)
+        bit *= 2
+    return masks[1:][::-1] + masks[:1]
 
 
-def core_swap(array, axis):
+def swap(array, axis, mask):
     count = lax.axis_size(axis)
-    return lax.ppermute(array, axis, [(i, i ^ 1) for i in range(count)])
+    return lax.ppermute(array, axis, [(i, i ^ mask) for i in range(count)])
 
 
 def gather_blocks(array, axis):
-    chips = lax.axis_size(axis) // 2
-    own = jnp.stack([array] + [chip_shift(array, axis, k) for k in range(1, chips)])
-    return jnp.stack([own, core_swap(own, axis)])
+    blocks = array[None]
+    for mask in exchange_masks(lax.axis_size(axis)):
+        blocks = jnp.concatenate([blocks, swap(blocks, axis, mask)])
+    return blocks
 
 
 def scatter_blocks(partial, axis):
-    chips = lax.axis_size(axis) // 2
-    swapped = core_swap(partial[1].astype(jnp.bfloat16), axis)
-    chip_sum = partial[0] + swapped.astype(jnp.float32)
-    total = chip_sum[0]
-    for k in range(1, chips):
-        total = total + chip_shift(chip_sum[k].astype(jnp.bfloat16), axis, -k).astype(jnp.float32)
-    return total
+    blocks = partial
+    for mask in exchange_masks(lax.axis_size(axis))[::-1]:
+        half = blocks.shape[0] // 2
+        blocks = blocks[:half] + swap(blocks[half:].astype(jnp.bfloat16), axis, mask).astype(jnp.float32)
+    return blocks[0]
 
 
 def rms_normed(hidden, gain):
@@ -62,7 +63,6 @@
     expert_index = lax.axis_index("expert")
     local_experts = gate_weight.shape[1]
     experts = local_experts * devices
-    chips = devices // 2
     gain = norm_gain[0]
     w_gate = gate_weight[0]
     w_up = up_weight[0]
@@ -71,8 +71,8 @@
     width = tokens.shape[2]
     table = route_table(routes[0], gates[0], experts)
     table = gather_blocks(table, "expert")
-    mine = lax.dynamic_slice_in_dim(table, expert_index * local_experts, local_experts, axis=4)
-    mixing = jnp.transpose(mine, (2, 4, 0, 1, 3)).reshape(MB, local_experts, 2 * chips * tok_rows)
+    mine = lax.dynamic_slice_in_dim(table, expert_index * local_experts, local_experts, axis=3)
+    mixing = jnp.transpose(mine, (1, 3, 0, 2)).reshape(MB, local_experts, devices * tok_rows)
     held = jnp.zeros((tok_rows, width), jnp.bfloat16)
     collected = jnp.zeros((MB, tok_rows, width), jnp.bfloat16)
     for moment in range(MB + sections - 1):
@@ -87,12 +87,12 @@
         incoming = jnp.where(section_index == 0, first_rows, arrived)
         weight = lax.dynamic_index_in_dim(mixing, clipped, 0, keepdims=False)
         values, normed = rms_normed(incoming, gain)
-        rows = gather_blocks(normed, "expert").reshape(2 * chips * tok_rows, width)
+        rows = gather_blocks(normed, "expert").reshape(devices * tok_rows, width)
         gate_part = jnp.einsum("td,edf->etf", rows, w_gate, preferred_element_type=jnp.float32)
         up_part = jnp.einsum("td,edf->etf", rows, w_up, preferred_element_type=jnp.float32)
         inner = (jax.nn.silu(gate_part) * up_part * weight[:, :, None]).astype(jnp.bfloat16)
         partial = jnp.einsum("etf,efd->td", inner, w_down, preferred_element_type=jnp.float32)
-        mixed = scatter_blocks(partial.reshape(2, chips, tok_rows, width), "expert")
+        mixed = scatter_blocks(partial.reshape(devices, tok_rows, width), "expert")
         produced = (values + mixed).astype(jnp.bfloat16)
         held = jnp.where(active, produced, incoming)
         updated = lax.dynamic_update_index_in_dim(collected, held, clipped, 0)

time: 275 us -> 302 us (1.098)
  waiting for transfers between devices: 89.5 us -> 139 us
  starting transfers between devices: 98 us -> 77.4 us
    ppermute x60 -> x45, waiting for transfers between devices: 78.2 us -> 128 us  [swap(): return lax.ppermute(array, axis, [(i, i ^ mask) for i in range(count)])]
    ppermute x60 -> x45, starting transfers between devices: 70.6 us -> 52.1 us  [swap(): return lax.ppermute(array, axis, [(i, i ^ mask) for i in range(count)])]
  transfers between devices with their start and end apart: 66 -> 51, of which waited for: 49 -> 49; matrix products, arithmetic and copies ran while one was open for 2% -> 1% of each run, Pallas kernels for 0% -> 0%
where the time goes in v5:
time: 302 us; the launch traced here: 300 us
  waiting for transfers between devices  139 us (46%)
  starting transfers between devices  77.4 us (26%)
  matrix products  72.9 us (24%)
  other arithmetic  7.31 us (2%)
    ppermute x45, waiting for transfers between devices, swap(): return lax.ppermute(array, axis, [(i, i ^ mask) for i in range(count)])  128 us
    ppermute x45, starting transfers between devices, swap(): return lax.ppermute(array, axis, [(i, i ^ mask) for i in range(count)])  52.1 us
    dot_general x7, matrix products, on_device(): jnp.einsum('etf,efd->td', inner, w_down, preferred_element_type=jnp.float32)  46.4 us
    dot_general x7, matrix products, on_device(): jnp.einsum('td,edf->etf', rows, w_gate, preferred_element_type=jnp.float32)  26.4 us
    ppermute x6, starting transfers between devices, shifted(): return lax.ppermute(array, axis, pairs)  25.3 us
    ppermute x6, waiting for transfers between devices, shifted(): return lax.ppermute(array, axis, pairs)  10.9 us
  transfers between devices with their start and end apart: 51, of which 49 were waited for; matrix products, arithmetic and copies ran while one was open for 1% of the time, Pallas kernels for 0%

profile of v5, /device:TPU:0, one launch (start us, length us, event | category | flops | bytes accessed | tf_op | source)
XLA Modules:
  0.0 300.4 jit_solution(11122878875216249817)
XLA Ops:
  1.9 4.1 %collective-permute-start = (bf16[1,16,2048]{2,1,0:T(8,128)(2,1)S(1)}, bf16[1,16,2048]{2,1,0:T(8,128)(2,1)S(1)}, u32[]{:S(2)}, u32[]{:S(2)}) collective-permute-start(bf16[1,16,2048]{2,1,0:T(8,128)(2,1)S(1)} %fusion.149), channel_id=1, source_target_pairs={{0,4},{1,5},{2,6},{3,7},{4,0},{5,1},{6,2},{7,3},{8,12},{9,13},{10,... | collective-permute-start | bytes 196616 | tf_op jit(solution)/shard_map/ppermute | solution.py:29
  22.6 3.8 %fusion.63 = f32[2,128,768]{2,1,0:T(8,128)S(1)} fusion(bf16[128,2048,1]{1,0,2:T(8,128)(2,1)S(1)} %bitcast.378, bf16[1,2,2048,768]{3,2,1,0:T(8,128)(2,1)} %param.9), kind=kOutput, calls=%fused_computation.49 | convolution fusion | flops 805306368 | bytes 7602176 | tf_op jit(solution)/shard_map/td,edf->etf/dot_general | solution.py:91
  26.4 6.7 %fusion.42 = f32[128,2048]{1,0:T(8,128)S(1)} fusion(bf16[1,2,768,2048]{3,2,1,0:T(8,128)(2,1)} %param.11, f32[2,128,768]{2,1,0:T(8,128)S(1)} %fusion.63, bf16[128,2048,1]{1,0,2:T(8,128)(2,1)S(1)} %bitcast.379, bf16[1,2,2048,768]{3,2,1,0:T(8,128)(2,1)} %param.10, f32[2,128]{1,0:T(2,128)S(1)} %get-tuple-element.33), kind=kOutput, calls=%fused_computation.42 | convolution fusion | flops 1611988992 | bytes 14943232 | tf_op jit(solution)/shard_map/etf,efd->td/dot_general | solution.py:94
  36.4 4.0 %collective-permute-done.7 = bf16[2,16,2048]{2,1,0:T(8,128)(2,1)S(1)} collective-permute-done((bf16[2,16,2048]{2,1,0:T(8,128)(2,1)S(1)}, bf16[2,16,2048]{2,1,0:T(8,128)(2,1)S(1)}, u32[]{:S(2)}, u32[]{:S(2)}) %collective-permute-start.7) | collective-permute-done | bytes 131104 | tf_op jit(solution)/shard_map/ppermute | solution.py:29
  63.4 3.8 %fusion.66 = f32[2,128,768]{2,1,0:T(8,128)S(1)} fusion(bf16[128,2048,1]{1,0,2:T(8,128)(2,1)S(1)} %bitcast.380, bf16[1,2,2048,768]{3,2,1,0:T(8,128)(2,1)} %param.9), kind=kOutput, calls=%fused_computation.50 | convolution fusion | flops 805306368 | bytes 7602176 | tf_op jit(solution)/shard_map/td,edf->etf/dot_general | solution.py:91
  67.1 6.6 %fusion.45 = f32[128,2048]{1,0:T(8,128)S(1)} fusion(bf16[1,2,768,2048]{3,2,1,0:T(8,128)(2,1)} %param.11, f32[2,128,768]{2,1,0:T(8,128)S(1)} %fusion.66, bf16[128,2048,1]{1,0,2:T(8,128)(2,1)S(1)} %bitcast.381, bf16[1,2,2048,768]{3,2,1,0:T(8,128)(2,1)} %param.10, f32[2,128]{1,0:T(2,128)S(1)} %get-tuple-element.32), kind=kOutput, calls=%fused_computation.43 | convolution fusion | flops 1611988992 | bytes 14943232 | tf_op jit(solution)/shard_map/etf,efd->td/dot_general | solution.py:94
  77.1 4.0 %collective-permute-done.14 = bf16[2,16,2048]{2,1,0:T(8,128)(2,1)S(1)} collective-permute-done((bf16[2,16,2048]{2,1,0:T(8,128)(2,1)S(1)}, bf16[2,16,2048]{2,1,0:T(8,128)(2,1)S(1)}, u32[]{:S(2)}, u32[]{:S(2)}) %collective-permute-start.14) | collective-permute-done | bytes 131104 | tf_op jit(solution)/shard_map/ppermute | solution.py:29
  86.7 4.5 %collective-permute-start.16 = (bf16[16,2048]{1,0:T(8,128)(2,1)S(1)}, bf16[16,2048]{1,0:T(8,128)(2,1)S(1)}, u32[]{:S(2)}, u32[]{:S(2)}) collective-permute-start(bf16[16,2048]{1,0:T(8,128)(2,1)S(1)} %get-tuple-element.24), channel_id=1, source_target_pairs={{0,8},{8,16},{16,24},{1,9},{9,17},{17,25},{2,10},{10,18},{18,26},{... | collective-permute-start | bytes 196616 | tf_op jit(solution)/shard_map/ppermute | solution.py:15
  105.2 3.8 %fusion.69 = f32[2,128,768]{2,1,0:T(8,128)S(1)} fusion(bf16[128,2048,1]{1,0,2:T(8,128)(2,1)S(1)} %bitcast.382, bf16[1,2,2048,768]{3,2,1,0:T(8,128)(2,1)} %param.9), kind=kOutput, calls=%fused_computation.51 | convolution fusion | flops 805306368 | bytes 7602176 | tf_op jit(solution)/shard_map/td,edf->etf/dot_general | solution.py:91
  108.9 6.6 %fusion.48 = f32[128,2048]{1,0:T(8,128)S(1)} fusion(bf16[1,2,768,2048]{3,2,1,0:T(8,128)(2,1)} %param.11, f32[2,128,768]{2,1,0:T(8,128)S(1)} %fusion.69, bf16[128,2048,1]{1,0,2:T(8,128)(2,1)S(1)} %bitcast.383, bf16[1,2,2048,768]{3,2,1,0:T(8,128)(2,1)} %param.10, f32[2,128]{1,0:T(2,128)S(1)} %get-tuple-element.31), kind=kOutput, calls=%fused_computation.44 | convolution fusion | flops 1611988992 | bytes 14943232 | tf_op jit(solution)/shard_map/etf,efd->td/dot_general | solution.py:94
  118.8 4.1 %collective-permute-done.21 = bf16[2,16,2048]{2,1,0:T(8,128)(2,1)S(1)} collective-permute-done((bf16[2,16,2048]{2,1,0:T(8,128)(2,1)S(1)}, bf16[2,16,2048]{2,1,0:T(8,128)(2,1)S(1)}, u32[]{:S(2)}, u32[]{:S(2)}) %collective-permute-start.21) | collective-permute-done | bytes 131104 | tf_op jit(solution)/shard_map/ppermute | solution.py:29
  129.3 4.3 %collective-permute-start.23 = (bf16[16,2048]{1,0:T(8,128)(2,1)S(1)}, bf16[16,2048]{1,0:T(8,128)(2,1)S(1)}, u32[]{:S(2)}, u32[]{:S(2)}) collective-permute-start(bf16[16,2048]{1,0:T(8,128)(2,1)S(1)} %get-tuple-element.20), channel_id=1, source_target_pairs={{0,8},{8,16},{16,24},{1,9},{9,17},{17,25},{2,10},{10,18},{18,26},{... | collective-permute-start | bytes 196616 | tf_op jit(solution)/shard_map/ppermute | solution.py:15
  141.8 5.0 %collective-permute-done.25 = bf16[2,16,2048]{2,1,0:T(8,128)(2,1)S(1)} collective-permute-done((bf16[2,16,2048]{2,1,0:T(8,128)(2,1)S(1)}, bf16[2,16,2048]{2,1,0:T(8,128)(2,1)S(1)}, u32[]{:S(2)}, u32[]{:S(2)}) %collective-permute-start.25) | collective-permute-done | bytes 131104 | tf_op jit(solution)/shard_map/ppermute | solution.py:29
  148.4 3.8 %fusion.72 = f32[2,128,768]{2,1,0:T(8,128)S(1)} fusion(bf16[128,2048,1]{1,0,2:T(8,128)(2,1)S(1)} %bitcast.384, bf16[1,2,2048,768]{3,2,1,0:T(8,128)(2,1)} %param.9), kind=kOutput, calls=%fused_computation.52 | convolution fusion | flops 805306368 | bytes 7602176 | tf_op jit(solution)/shard_map/td,edf->etf/dot_general | solution.py:91
  152.2 6.7 %fusion.51 = f32[128,2048]{1,0:T(8,128)S(1)} fusion(bf16[1,2,768,2048]{3,2,1,0:T(8,128)(2,1)} %param.11, f32[2,128,768]{2,1,0:T(8,128)S(1)} %fusion.72, bf16[128,2048,1]{1,0,2:T(8,128)(2,1)S(1)} %bitcast.385, bf16[1,2,2048,768]{3,2,1,0:T(8,128)(2,1)} %param.10, f32[2,128]{1,0:T(2,128)S(1)} %get-tuple-element.30), kind=kOutput, calls=%fused_computation.45 | convolution fusion | flops 1611988992 | bytes 14943232 | tf_op jit(solution)/shard_map/etf,efd->td/dot_general | solution.py:94
  160.7 5.5 %collective-permute-done.28 = bf16[2,16,2048]{2,1,0:T(8,128)(2,1)S(1)} collective-permute-done((bf16[2,16,2048]{2,1,0:T(8,128)(2,1)S(1)}, bf16[2,16,2048]{2,1,0:T(8,128)(2,1)S(1)}, u32[]{:S(2)}, u32[]{:S(2)}) %collective-permute-start.28) | collective-permute-done | bytes 131104 | tf_op jit(solution)/shard_map/ppermute | solution.py:29
  172.0 4.3 %collective-permute-start.30 = (bf16[16,2048]{1,0:T(8,128)(2,1)S(1)}, bf16[16,2048]{1,0:T(8,128)(2,1)S(1)}, u32[]{:S(2)}, u32[]{:S(2)}) collective-permute-start(bf16[16,2048]{1,0:T(8,128)(2,1)S(1)} %get-tuple-element.16), channel_id=1, source_target_pairs={{0,8},{8,16},{16,24},{1,9},{9,17},{17,25},{2,10},{10,18},{18,26},{... | collective-permute-start | bytes 196616 | tf_op jit(solution)/shard_map/ppermute | solution.py:15
  180.7 3.7 %collective-permute-done.31 = bf16[1,16,2048]{2,1,0:T(8,128)(2,1)S(1)} collective-permute-done((bf16[1,16,2048]{2,1,0:T(8,128)(2,1)S(1)}, bf16[1,16,2048]{2,1,0:T(8,128)(2,1)S(1)}, u32[]{:S(2)}, u32[]{:S(2)}) %collective-permute-start.31) | collective-permute-done | bytes 65568 | tf_op jit(solution)/shard_map/ppermute | solution.py:29
  184.5 5.0 %collective-permute-done.32 = bf16[2,16,2048]{2,1,0:T(8,128)(2,1)S(1)} collective-permute-done((bf16[2,16,2048]{2,1,0:T(8,128)(2,1)S(1)}, bf16[2,16,2048]{2,1,0:T(8,128)(2,1)S(1)}, u32[]{:S(2)}, u32[]{:S(2)}) %collective-permute-start.32) | collective-permute-done | bytes 131104 | tf_op jit(solution)/shard_map/ppermute | solution.py:29
  191.1 3.8 %fusion.75 = f32[2,128,768]{2,1,0:T(8,128)S(1)} fusion(bf16[128,2048,1]{1,0,2:T(8,128)(2,1)S(1)} %bitcast.386, bf16[1,2,2048,768]{3,2,1,0:T(8,128)(2,1)} %param.9), kind=kOutput, calls=%fused_computation.53 | convolution fusion | flops 805306368 | bytes 7602176 | tf_op jit(solution)/shard_map/td,edf->etf/dot_general | solution.py:91
  194.9 6.7 %fusion.54 = f32[128,2048]{1,0:T(8,128)S(1)} fusion(bf16[1,2,768,2048]{3,2,1,0:T(8,128)(2,1)} %param.11, f32[2,128,768]{2,1,0:T(8,128)S(1)} %fusion.75, bf16[128,2048,1]{1,0,2:T(8,128)(2,1)S(1)} %bitcast.387, bf16[1,2,2048,768]{3,2,1,0:T(8,128)(2,1)} %param.10, f32[2,128]{1,0:T(2,128)S(1)} %get-tuple-element.29), kind=kOutput, calls=%fused_computation.46 | convolution fusion | flops 1611988992 | bytes 14943232 | tf_op jit(solution)/shard_map/etf,efd->td/dot_general | solution.py:94
  203.4 5.5 %collective-permute-done.35 = bf16[2,16,2048]{2,1,0:T(8,128)(2,1)S(1)} collective-permute-done((bf16[2,16,2048]{2,1,0:T(8,128)(2,1)S(1)}, bf16[2,16,2048]{2,1,0:T(8,128)(2,1)S(1)}, u32[]{:S(2)}, u32[]{:S(2)}) %collective-permute-start.35) | collective-permute-done | bytes 131104 | tf_op jit(solution)/shard_map/ppermute | solution.py:29
  214.7 4.5 %collective-permute-start.37 = (bf16[16,2048]{1,0:T(8,128)(2,1)S(1)}, bf16[16,2048]{1,0:T(8,128)(2,1)S(1)}, u32[]{:S(2)}, u32[]{:S(2)}) collective-permute-start(bf16[16,2048]{1,0:T(8,128)(2,1)S(1)} %get-tuple-element.12), channel_id=1, source_target_pairs={{0,8},{8,16},{16,24},{1,9},{9,17},{17,25},{2,10},{10,18},{18,26},{... | collective-permute-start | bytes 196616 | tf_op jit(solution)/shard_map/ppermute | solution.py:15
  227.1 5.0 %collective-permute-done.39 = bf16[2,16,2048]{2,1,0:T(8,128)(2,1)S(1)} collective-permute-done((bf16[2,16,2048]{2,1,0:T(8,128)(2,1)S(1)}, bf16[2,16,2048]{2,1,0:T(8,128)(2,1)S(1)}, u32[]{:S(2)}, u32[]{:S(2)}) %collective-permute-start.39) | collective-permute-done | bytes 131104 | tf_op jit(solution)/shard_map/ppermute | solution.py:29
  233.7 3.8 %fusion.78 = f32[2,128,768]{2,1,0:T(8,128)S(1)} fusion(bf16[128,2048,1]{1,0,2:T(8,128)(2,1)S(1)} %bitcast.388, bf16[1,2,2048,768]{3,2,1,0:T(8,128)(2,1)} %param.9), kind=kOutput, calls=%fused_computation.54 | convolution fusion | flops 805306368 | bytes 7602176 | tf_op jit(solution)/shard_map/td,edf->etf/dot_general | solution.py:91
  237.5 6.6 %fusion.57 = f32[128,2048]{1,0:T(8,128)S(1)} fusion(bf16[1,2,768,2048]{3,2,1,0:T(8,128)(2,1)} %param.11, f32[2,128,768]{2,1,0:T(8,128)S(1)} %fusion.78, bf16[128,2048,1]{1,0,2:T(8,128)(2,1)S(1)} %bitcast.389, bf16[1,2,2048,768]{3,2,1,0:T(8,128)(2,1)} %param.10, f32[2,128]{1,0:T(2,128)S(1)} %get-tuple-element.28), kind=kOutput, calls=%fused_computation.47 | convolution fusion | flops 1611988992 | bytes 14943232 | tf_op jit(solution)/shard_map/etf,efd->td/dot_general | solution.py:94
  245.9 5.5 %collective-permute-done.42 = bf16[2,16,2048]{2,1,0:T(8,128)(2,1)S(1)} collective-permute-done((bf16[2,16,2048]{2,1,0:T(8,128)(2,1)S(1)}, bf16[2,16,2048]{2,1,0:T(8,128)(2,1)S(1)}, u32[]{:S(2)}, u32[]{:S(2)}) %collective-permute-start.42) | collective-permute-done | bytes 131104 | tf_op jit(solution)/shard_map/ppermute | solution.py:29
  257.2 4.2 %collective-permute-start.44 = (bf16[16,2048]{1,0:T(8,128)(2,1)S(1)}, bf16[16,2048]{1,0:T(8,128)(2,1)S(1)}, u32[]{:S(2)}, u32[]{:S(2)}) collective-permute-start(bf16[16,2048]{1,0:T(8,128)(2,1)S(1)} %get-tuple-element.8), channel_id=1, source_target_pairs={{0,8},{8,16},{16,24},{1,9},{9,17},{17,25},{2,10},{10,18},{18,26},{... | collective-permute-start | bytes 196616 | tf_op jit(solution)/shard_map/ppermute | solution.py:15
  269.6 5.0 %collective-permute-done.46 = bf16[2,16,2048]{2,1,0:T(8,128)(2,1)S(1)} collective-permute-done((bf16[2,16,2048]{2,1,0:T(8,128)(2,1)S(1)}, bf16[2,16,2048]{2,1,0:T(8,128)(2,1)S(1)}, u32[]{:S(2)}, u32[]{:S(2)}) %collective-permute-start.46) | collective-permute-done | bytes 131104 | tf_op jit(solution)/shard_map/ppermute | solution.py:29
  276.3 3.8 %fusion.81 = f32[2,128,768]{2,1,0:T(8,128)S(1)} fusion(bf16[128,2048,1]{1,0,2:T(8,128)(2,1)S(1)} %bitcast.376, bf16[1,2,2048,768]{3,2,1,0:T(8,128)(2,1)} %param.9), kind=kOutput, calls=%fused_computation.55 | convolution fusion | flops 805306368 | bytes 7602176 | tf_op jit(solution)/shard_map/td,edf->etf/dot_general | solution.py:91
  280.0 6.6 %fusion.60 = f32[128,2048]{1,0:T(8,128)S(1)} fusion(bf16[1,2,768,2048]{3,2,1,0:T(8,128)(2,1)} %param.11, f32[2,128,768]{2,1,0:T(8,128)S(1)} %fusion.81, bf16[128,2048,1]{1,0,2:T(8,128)(2,1)S(1)} %bitcast.377, bf16[1,2,2048,768]{3,2,1,0:T(8,128)(2,1)} %param.10, f32[2,128]{1,0:T(2,128)S(1)} %get-tuple-element.27), kind=kOutput, calls=%fused_computation.48 | convolution fusion | flops 1611988992 | bytes 14943232 | tf_op jit(solution)/shard_map/etf,efd->td/dot_general | solution.py:94
  288.4 5.5 %collective-permute-done.49 = bf16[2,16,2048]{2,1,0:T(8,128)(2,1)S(1)} collective-permute-done((bf16[2,16,2048]{2,1,0:T(8,128)(2,1)S(1)}, bf16[2,16,2048]{2,1,0:T(8,128)(2,1)S(1)}, u32[]{:S(2)}, u32[]{:S(2)}) %collective-permute-start.49) | collective-permute-done | bytes 131104 | tf_op jit(solution)/shard_map/ppermute | solution.py:29
  (193 shorter events, 143.0 us)
Async XLA Ops:
  1.9 7.8 %collective-permute-start = (bf16[1,16,2048]{2,1,0:T(8,128)(2,1)S(1)}, bf16[1,16,2048]{2,1,0:T(8,128)(2,1)S(1)}, u32[]{:S(2)}, u32[]{:S(2)}) collective-permute-start(bf16[1,16,2048]{2,1,0:T(8,128)(2,1)S(1)} %fusion.149), channel_id=1, source_target_pairs={{0,4},{1,5},{2,6},{3,7},{4,0},{5,1},{6,2},{7,3},{8,12},{9,13},{10,... | collective-permute-start | bytes 196616 | tf_op jit(solution)/shard_map/ppermute | solution.py:29
  9.7 8.1 %collective-permute-start.1 = (bf16[2,16,2048]{2,1,0:T(8,128)(2,1)S(1)}, bf16[2,16,2048]{2,1,0:T(8,128)(2,1)S(1)}, u32[]{:S(2)}, u32[]{:S(2)}) collective-permute-start(bf16[2,16,2048]{2,1,0:T(8,128)(2,1)S(1)} %pad_maximum_fusion.14), channel_id=1, source_target_pairs={{0,2},{1,3},{2,0},{3,1},{4,6},{5,7},{6,4},{7,5},{8,10},{9,11},{10,... | collective-permute-start | bytes 393224 | tf_op jit(solution)/shard_map/ppermute | solution.py:29
  10.5 5.6 %collective-permute-start.3 = (f32[1,4,16,16]{3,2,1,0:T(8,128)S(1)}, f32[1,4,16,16]{3,2,1,0:T(8,128)S(1)}, u32[]{:S(2)}, u32[]{:S(2)}) collective-permute-start(f32[1,4,16,16]{3,2,1,0:T(8,128)S(1)} %bitcast.398), channel_id=1, source_target_pairs={{0,4},{1,5},{2,6},{3,7},{4,0},{5,1},{6,2},{7,3},{8,12},{9,13},{10,... | collective-permute-start | bytes 12296 | tf_op jit(solution)/shard_map/ppermute | solution.py:29
  34.8 5.6 %collective-permute-start.7 = (bf16[2,16,2048]{2,1,0:T(8,128)(2,1)S(1)}, bf16[2,16,2048]{2,1,0:T(8,128)(2,1)S(1)}, u32[]{:S(2)}, u32[]{:S(2)}) collective-permute-start(bf16[2,16,2048]{2,1,0:T(8,128)(2,1)S(1)} %slice.366), channel_id=1, source_target_pairs={{0,2},{1,3},{2,0},{3,1},{4,6},{5,7},{6,4},{7,5},{8,10},{9,11},{10,... | collective-permute-start | bytes 393224 | tf_op jit(solution)/shard_map/ppermute | solution.py:29
  40.4 5.3 %collective-permute-start.8 = (bf16[1,16,2048]{2,1,0:T(8,128)(2,1)S(1)}, bf16[1,16,2048]{2,1,0:T(8,128)(2,1)S(1)}, u32[]{:S(2)}, u32[]{:S(2)}) collective-permute-start(bf16[1,16,2048]{2,1,0:T(8,128)(2,1)S(1)} %slice.373), channel_id=1, source_target_pairs={{0,4},{1,5},{2,6},{3,7},{4,0},{5,1},{6,2},{7,3},{8,12},{9,13},{10,... | collective-permute-start | bytes 196616 | tf_op jit(solution)/shard_map/ppermute | solution.py:29
  45.7 5.3 %collective-permute-start.9 = (bf16[16,2048]{1,0:T(8,128)(2,1)S(1)}, bf16[16,2048]{1,0:T(8,128)(2,1)S(1)}, u32[]{:S(2)}, u32[]{:S(2)}) collective-permute-start(bf16[16,2048]{1,0:T(8,128)(2,1)S(1)} %fusion.189), channel_id=1, source_target_pairs={{0,8},{8,16},{16,24},{1,9},{9,17},{17,25},{2,10},{10,18},{18,26},{... | collective-permute-start | bytes 196616 | tf_op jit(solution)/shard_map/ppermute | solution.py:15
  51.3 5.3 %collective-permute-start.10 = (bf16[1,16,2048]{2,1,0:T(8,128)(2,1)S(1)}, bf16[1,16,2048]{2,1,0:T(8,128)(2,1)S(1)}, u32[]{:S(2)}, u32[]{:S(2)}) collective-permute-start(bf16[1,16,2048]{2,1,0:T(8,128)(2,1)S(1)} %fusion.202), channel_id=1, source_target_pairs={{0,4},{1,5},{2,6},{3,7},{4,0},{5,1},{6,2},{7,3},{8,12},{9,13},{10,... | collective-permute-start | bytes 196616 | tf_op jit(solution)/shard_map/ppermute | solution.py:29
  75.5 5.6 %collective-permute-start.14 = (bf16[2,16,2048]{2,1,0:T(8,128)(2,1)S(1)}, bf16[2,16,2048]{2,1,0:T(8,128)(2,1)S(1)}, u32[]{:S(2)}, u32[]{:S(2)}) collective-permute-start(bf16[2,16,2048]{2,1,0:T(8,128)(2,1)S(1)} %slice.365), channel_id=1, source_target_pairs={{0,2},{1,3},{2,0},{3,1},{4,6},{5,7},{6,4},{7,5},{8,10},{9,11},{10,... | collective-permute-start | bytes 393224 | tf_op jit(solution)/shard_map/ppermute | solution.py:29
  81.2 5.5 %collective-permute-start.15 = (bf16[1,16,2048]{2,1,0:T(8,128)(2,1)S(1)}, bf16[1,16,2048]{2,1,0:T(8,128)(2,1)S(1)}, u32[]{:S(2)}, u32[]{:S(2)}) collective-permute-start(bf16[1,16,2048]{2,1,0:T(8,128)(2,1)S(1)} %slice.372), channel_id=1, source_target_pairs={{0,4},{1,5},{2,6},{3,7},{4,0},{5,1},{6,2},{7,3},{8,12},{9,13},{10,... | collective-permute-start | bytes 196616 | tf_op jit(solution)/shard_map/ppermute | solution.py:29
  86.7 6.2 %collective-permute-start.16 = (bf16[16,2048]{1,0:T(8,128)(2,1)S(1)}, bf16[16,2048]{1,0:T(8,128)(2,1)S(1)}, u32[]{:S(2)}, u32[]{:S(2)}) collective-permute-start(bf16[16,2048]{1,0:T(8,128)(2,1)S(1)} %get-tuple-element.24), channel_id=1, source_target_pairs={{0,8},{8,16},{16,24},{1,9},{9,17},{17,25},{2,10},{10,18},{18,26},{... | collective-permute-start | bytes 196616 | tf_op jit(solution)/shard_map/ppermute | solution.py:15
  93.1 5.3 %collective-permute-start.17 = (bf16[1,16,2048]{2,1,0:T(8,128)(2,1)S(1)}, bf16[1,16,2048]{2,1,0:T(8,128)(2,1)S(1)}, u32[]{:S(2)}, u32[]{:S(2)}) collective-permute-start(bf16[1,16,2048]{2,1,0:T(8,128)(2,1)S(1)} %fusion.201), channel_id=1, source_target_pairs={{0,4},{1,5},{2,6},{3,7},{4,0},{5,1},{6,2},{7,3},{8,12},{9,13},{10,... | collective-permute-start | bytes 196616 | tf_op jit(solution)/shard_map/ppermute | solution.py:29
  98.4 5.0 %collective-permute-start.18 = (bf16[2,16,2048]{2,1,0:T(8,128)(2,1)S(1)}, bf16[2,16,2048]{2,1,0:T(8,128)(2,1)S(1)}, u32[]{:S(2)}, u32[]{:S(2)}) collective-permute-start(bf16[2,16,2048]{2,1,0:T(8,128)(2,1)S(1)} %pad_maximum_fusion.17), channel_id=1, source_target_pairs={{0,2},{1,3},{2,0},{3,1},{4,6},{5,7},{6,4},{7,5},{8,10},{9,11},{10,... | collective-permute-start | bytes 393224 | tf_op jit(solution)/shard_map/ppermute | solution.py:29
  117.3 5.6 %collective-permute-start.21 = (bf16[2,16,2048]{2,1,0:T(8,128)(2,1)S(1)}, bf16[2,16,2048]{2,1,0:T(8,128)(2,1)S(1)}, u32[]{:S(2)}, u32[]{:S(2)}) collective-permute-start(bf16[2,16,2048]{2,1,0:T(8,128)(2,1)S(1)} %slice.364), channel_id=1, source_target_pairs={{0,2},{1,3},{2,0},{3,1},{4,6},{5,7},{6,4},{7,5},{8,10},{9,11},{10,... | collective-permute-start | bytes 393224 | tf_op jit(solution)/shard_map/ppermute | solution.py:29
  123.0 6.3 %collective-permute-start.22 = (bf16[1,16,2048]{2,1,0:T(8,128)(2,1)S(1)}, bf16[1,16,2048]{2,1,0:T(8,128)(2,1)S(1)}, u32[]{:S(2)}, u32[]{:S(2)}) collective-permute-start(bf16[1,16,2048]{2,1,0:T(8,128)(2,1)S(1)} %slice.371), channel_id=1, source_target_pairs={{0,4},{1,5},{2,6},{3,7},{4,0},{5,1},{6,2},{7,3},{8,12},{9,13},{10,... | collective-permute-start | bytes 196616 | tf_op jit(solution)/shard_map/ppermute | solution.py:29
  129.3 6.2 %collective-permute-start.23 = (bf16[16,2048]{1,0:T(8,128)(2,1)S(1)}, bf16[16,2048]{1,0:T(8,128)(2,1)S(1)}, u32[]{:S(2)}, u32[]{:S(2)}) collective-permute-start(bf16[16,2048]{1,0:T(8,128)(2,1)S(1)} %get-tuple-element.20), channel_id=1, source_target_pairs={{0,8},{8,16},{16,24},{1,9},{9,17},{17,25},{2,10},{10,18},{18,26},{... | collective-permute-start | bytes 196616 | tf_op jit(solution)/shard_map/ppermute | solution.py:15
  135.7 5.9 %collective-permute-start.24 = (bf16[1,16,2048]{2,1,0:T(8,128)(2,1)S(1)}, bf16[1,16,2048]{2,1,0:T(8,128)(2,1)S(1)}, u32[]{:S(2)}, u32[]{:S(2)}) collective-permute-start(bf16[1,16,2048]{2,1,0:T(8,128)(2,1)S(1)} %fusion.200), channel_id=1, source_target_pairs={{0,4},{1,5},{2,6},{3,7},{4,0},{5,1},{6,2},{7,3},{8,12},{9,13},{10,... | collective-permute-start | bytes 196616 | tf_op jit(solution)/shard_map/ppermute | solution.py:29
  141.7 5.0 %collective-permute-start.25 = (bf16[2,16,2048]{2,1,0:T(8,128)(2,1)S(1)}, bf16[2,16,2048]{2,1,0:T(8,128)(2,1)S(1)}, u32[]{:S(2)}, u32[]{:S(2)}) collective-permute-start(bf16[2,16,2048]{2,1,0:T(8,128)(2,1)S(1)} %pad_maximum_fusion.18), channel_id=1, source_target_pairs={{0,2},{1,3},{2,0},{3,1},{4,6},{5,7},{6,4},{7,5},{8,10},{9,11},{10,... | collective-permute-start | bytes 393224 | tf_op jit(solution)/shard_map/ppermute | solution.py:29
  160.6 5.6 %collective-permute-start.28 = (bf16[2,16,2048]{2,1,0:T(8,128)(2,1)S(1)}, bf16[2,16,2048]{2,1,0:T(8,128)(2,1)S(1)}, u32[]{:S(2)}, u32[]{:S(2)}) collective-permute-start(bf16[2,16,2048]{2,1,0:T(8,128)(2,1)S(1)} %slice.363), channel_id=1, source_target_pairs={{0,2},{1,3},{2,0},{3,1},{4,6},{5,7},{6,4},{7,5},{8,10},{9,11},{10,... | collective-permute-start | bytes 393224 | tf_op jit(solution)/shard_map/ppermute | solution.py:29
  166.2 5.7 %collective-permute-start.29 = (bf16[1,16,2048]{2,1,0:T(8,128)(2,1)S(1)}, bf16[1,16,2048]{2,1,0:T(8,128)(2,1)S(1)}, u32[]{:S(2)}, u32[]{:S(2)}) collective-permute-start(bf16[1,16,2048]{2,1,0:T(8,128)(2,1)S(1)} %slice.370), channel_id=1, source_target_pairs={{0,4},{1,5},{2,6},{3,7},{4,0},{5,1},{6,2},{7,3},{8,12},{9,13},{10,... | collective-permute-start | bytes 196616 | tf_op jit(solution)/shard_map/ppermute | solution.py:29
  172.0 6.2 %collective-permute-start.30 = (bf16[16,2048]{1,0:T(8,128)(2,1)S(1)}, bf16[16,2048]{1,0:T(8,128)(2,1)S(1)}, u32[]{:S(2)}, u32[]{:S(2)}) collective-permute-start(bf16[16,2048]{1,0:T(8,128)(2,1)S(1)} %get-tuple-element.16), channel_id=1, source_target_pairs={{0,8},{8,16},{16,24},{1,9},{9,17},{17,25},{2,10},{10,18},{18,26},{... | collective-permute-start | bytes 196616 | tf_op jit(solution)/shard_map/ppermute | solution.py:15
  178.5 5.9 %collective-permute-start.31 = (bf16[1,16,2048]{2,1,0:T(8,128)(2,1)S(1)}, bf16[1,16,2048]{2,1,0:T(8,128)(2,1)S(1)}, u32[]{:S(2)}, u32[]{:S(2)}) collective-permute-start(bf16[1,16,2048]{2,1,0:T(8,128)(2,1)S(1)} %fusion.199), channel_id=1, source_target_pairs={{0,4},{1,5},{2,6},{3,7},{4,0},{5,1},{6,2},{7,3},{8,12},{9,13},{10,... | collective-permute-start | bytes 196616 | tf_op jit(solution)/shard_map/ppermute | solution.py:29
  203.3 5.6 %collective-permute-start.35 = (bf16[2,16,2048]{2,1,0:T(8,128)(2,1)S(1)}, bf16[2,16,2048]{2,1,0:T(8,128)(2,1)S(1)}, u32[]{:S(2)}, u32[]{:S(2)}) collective-permute-start(bf16[2,16,2048]{2,1,0:T(8,128)(2,1)S(1)} %slice.362), channel_id=1, source_target_pairs={{0,2},{1,3},{2,0},{3,1},{4,6},{5,7},{6,4},{7,5},{8,10},{9,11},{10,... | collective-permute-start | bytes 393224 | tf_op jit(solution)/shard_map/ppermute | solution.py:29
  208.9 5.7 %collective-permute-start.36 = (bf16[1,16,2048]{2,1,0:T(8,128)(2,1)S(1)}, bf16[1,16,2048]{2,1,0:T(8,128)(2,1)S(1)}, u32[]{:S(2)}, u32[]{:S(2)}) collective-permute-start(bf16[1,16,2048]{2,1,0:T(8,128)(2,1)S(1)} %slice.369), channel_id=1, source_target_pairs={{0,4},{1,5},{2,6},{3,7},{4,0},{5,1},{6,2},{7,3},{8,12},{9,13},{10,... | collective-permute-start | bytes 196616 | tf_op jit(solution)/shard_map/ppermute | solution.py:29
  214.7 6.2 %collective-permute-start.37 = (bf16[16,2048]{1,0:T(8,128)(2,1)S(1)}, bf16[16,2048]{1,0:T(8,128)(2,1)S(1)}, u32[]{:S(2)}, u32[]{:S(2)}) collective-permute-start(bf16[16,2048]{1,0:T(8,128)(2,1)S(1)} %get-tuple-element.12), channel_id=1, source_target_pairs={{0,8},{8,16},{16,24},{1,9},{9,17},{17,25},{2,10},{10,18},{18,26},{... | collective-permute-start | bytes 196616 | tf_op jit(solution)/shard_map/ppermute | solution.py:15
  221.1 5.9 %collective-permute-start.38 = (bf16[1,16,2048]{2,1,0:T(8,128)(2,1)S(1)}, bf16[1,16,2048]{2,1,0:T(8,128)(2,1)S(1)}, u32[]{:S(2)}, u32[]{:S(2)}) collective-permute-start(bf16[1,16,2048]{2,1,0:T(8,128)(2,1)S(1)} %fusion.198), channel_id=1, source_target_pairs={{0,4},{1,5},{2,6},{3,7},{4,0},{5,1},{6,2},{7,3},{8,12},{9,13},{10,... | collective-permute-start | bytes 196616 | tf_op jit(solution)/shard_map/ppermute | solution.py:29
  227.0 5.0 %collective-permute-start.39 = (bf16[2,16,2048]{2,1,0:T(8,128)(2,1)S(1)}, bf16[2,16,2048]{2,1,0:T(8,128)(2,1)S(1)}, u32[]{:S(2)}, u32[]{:S(2)}) collective-permute-start(bf16[2,16,2048]{2,1,0:T(8,128)(2,1)S(1)} %pad_maximum_fusion.20), channel_id=1, source_target_pairs={{0,2},{1,3},{2,0},{3,1},{4,6},{5,7},{6,4},{7,5},{8,10},{9,11},{10,... | collective-permute-start | bytes 393224 | tf_op jit(solution)/shard_map/ppermute | solution.py:29
  245.8 5.6 %collective-permute-start.42 = (bf16[2,16,2048]{2,1,0:T(8,128)(2,1)S(1)}, bf16[2,16,2048]{2,1,0:T(8,128)(2,1)S(1)}, u32[]{:S(2)}, u32[]{:S(2)}) collective-permute-start(bf16[2,16,2048]{2,1,0:T(8,128)(2,1)S(1)} %slice.361), channel_id=1, source_target_pairs={{0,2},{1,3},{2,0},{3,1},{4,6},{5,7},{6,4},{7,5},{8,10},{9,11},{10,... | collective-permute-start | bytes 393224 | tf_op jit(solution)/shard_map/ppermute | solution.py:29
  251.5 5.7 %collective-permute-start.43 = (bf16[1,16,2048]{2,1,0:T(8,128)(2,1)S(1)}, bf16[1,16,2048]{2,1,0:T(8,128)(2,1)S(1)}, u32[]{:S(2)}, u32[]{:S(2)}) collective-permute-start(bf16[1,16,2048]{2,1,0:T(8,128)(2,1)S(1)} %slice.368), channel_id=1, source_target_pairs={{0,4},{1,5},{2,6},{3,7},{4,0},{5,1},{6,2},{7,3},{8,12},{9,13},{10,... | collective-permute-start | bytes 196616 | tf_op jit(solution)/shard_map/ppermute | solution.py:29
  257.2 6.1 %collective-permute-start.44 = (bf16[16,2048]{1,0:T(8,128)(2,1)S(1)}, bf16[16,2048]{1,0:T(8,128)(2,1)S(1)}, u32[]{:S(2)}, u32[]{:S(2)}) collective-permute-start(bf16[16,2048]{1,0:T(8,128)(2,1)S(1)} %get-tuple-element.8), channel_id=1, source_target_pairs={{0,8},{8,16},{16,24},{1,9},{9,17},{17,25},{2,10},{10,18},{18,26},{... | collective-permute-start | bytes 196616 | tf_op jit(solution)/shard_map/ppermute | solution.py:15
  263.6 5.9 %collective-permute-start.45 = (bf16[1,16,2048]{2,1,0:T(8,128)(2,1)S(1)}, bf16[1,16,2048]{2,1,0:T(8,128)(2,1)S(1)}, u32[]{:S(2)}, u32[]{:S(2)}) collective-permute-start(bf16[1,16,2048]{2,1,0:T(8,128)(2,1)S(1)} %fusion.197), channel_id=1, source_target_pairs={{0,4},{1,5},{2,6},{3,7},{4,0},{5,1},{6,2},{7,3},{8,12},{9,13},{10,... | collective-permute-start | bytes 196616 | tf_op jit(solution)/shard_map/ppermute | solution.py:29
  288.4 5.6 %collective-permute-start.49 = (bf16[2,16,2048]{2,1,0:T(8,128)(2,1)S(1)}, bf16[2,16,2048]{2,1,0:T(8,128)(2,1)S(1)}, u32[]{:S(2)}, u32[]{:S(2)}) collective-permute-start(bf16[2,16,2048]{2,1,0:T(8,128)(2,1)S(1)} %slice.360), channel_id=1, source_target_pairs={{0,2},{1,3},{2,0},{3,1},{4,6},{5,7},{6,4},{7,5},{8,10},{9,11},{10,... | collective-permute-start | bytes 393224 | tf_op jit(solution)/shard_map/ppermute | solution.py:29
  294.0 5.7 %collective-permute-start.50 = (bf16[1,16,2048]{2,1,0:T(8,128)(2,1)S(1)}, bf16[1,16,2048]{2,1,0:T(8,128)(2,1)S(1)}, u32[]{:S(2)}, u32[]{:S(2)}) collective-permute-start(bf16[1,16,2048]{2,1,0:T(8,128)(2,1)S(1)} %slice.367), channel_id=1, source_target_pairs={{0,4},{1,5},{2,6},{3,7},{4,0},{5,1},{6,2},{7,3},{8,12},{9,13},{10,... | collective-permute-start | bytes 196616 | tf_op jit(solution)/shard_map/ppermute | solution.py:29
  (21 other events, 90.5 us)

commit v6 on v3

--- a/solution.py
+++ b/solution.py
@@ -4,6 +4,7 @@
 from jax.sharding import PartitionSpec as P
 
 MB = 4
+GROUP = 2
 
 
 EPSILON = 1e-06
@@ -72,30 +73,32 @@
     table = route_table(routes[0], gates[0], experts)
     table = gather_blocks(table, "expert")
     mine = lax.dynamic_slice_in_dim(table, expert_index * local_experts, local_experts, axis=4)
-    mixing = jnp.transpose(mine, (2, 4, 0, 1, 3)).reshape(MB, local_experts, 2 * chips * tok_rows)
-    held = jnp.zeros((tok_rows, width), jnp.bfloat16)
+    mixing = jnp.transpose(mine, (2, 4, 0, 1, 3))
+    held = jnp.zeros((GROUP, tok_rows, width), jnp.bfloat16)
     collected = jnp.zeros((MB, tok_rows, width), jnp.bfloat16)
-    for moment in range(MB + sections - 1):
+    groups = MB // GROUP
+    for moment in range(groups + sections - 1):
         if moment > 0:
             arrived = shifted(held, "section", 1)
         else:
             arrived = held
-        batch_index = moment - section_index
-        active = (batch_index >= 0) & (batch_index < MB)
-        clipped = jnp.clip(batch_index, 0, MB - 1)
-        first_rows = lax.dynamic_index_in_dim(tokens, clipped, 0, keepdims=False)
+        group_index = moment - section_index
+        active = (group_index >= 0) & (group_index < groups)
+        start = jnp.clip(group_index, 0, groups - 1) * GROUP
+        first_rows = lax.dynamic_slice_in_dim(tokens, start, GROUP, axis=0)
         incoming = jnp.where(section_index == 0, first_rows, arrived)
-        weight = lax.dynamic_index_in_dim(mixing, clipped, 0, keepdims=False)
+        weight = lax.dynamic_slice_in_dim(mixing, start, GROUP, axis=0)
+        weight = jnp.transpose(weight, (1, 2, 3, 0, 4)).reshape(local_experts, -1)
         values, normed = rms_normed(incoming, gain)
-        rows = gather_blocks(normed, "expert").reshape(2 * chips * tok_rows, width)
+        rows = gather_blocks(normed, "expert").reshape(-1, width)
         gate_part = jnp.einsum("td,edf->etf", rows, w_gate, preferred_element_type=jnp.float32)
         up_part = jnp.einsum("td,edf->etf", rows, w_up, preferred_element_type=jnp.float32)
         inner = (jax.nn.silu(gate_part) * up_part * weight[:, :, None]).astype(jnp.bfloat16)
         partial = jnp.einsum("etf,efd->td", inner, w_down, preferred_element_type=jnp.float32)
-        mixed = scatter_blocks(partial.reshape(2, chips, tok_rows, width), "expert")
+        mixed = scatter_blocks(partial.reshape(2, chips, GROUP, tok_rows, width), "expert")
         produced = (values + mixed).astype(jnp.bfloat16)
         held = jnp.where(active, produced, incoming)
-        updated = lax.dynamic_update_index_in_dim(collected, held, clipped, 0)
+        updated = lax.dynamic_update_slice_in_dim(collected, held, start, axis=0)
         collected = jnp.where(active, updated, collected)
     return collected[None]
 

time: 275 us -> 282 us (1.025)
  waiting for transfers between devices: 89.5 us -> 122 us
  starting transfers between devices: 98 us -> 68 us
  other arithmetic: 8.72 us -> 13.1 us
    ppermute x45 -> x33, waiting for transfers between devices: 58.2 us -> 94.6 us  [chip_shift(): return lax.ppermute(array, axis, pairs)]
    ppermute x45 -> x33, starting transfers between devices: 68.6 us -> 49 us  [chip_shift(): return lax.ppermute(array, axis, pairs)]
    ppermute x6 -> x4, starting transfers between devices: 27.5 us -> 17.5 us  [shifted(): return lax.ppermute(array, axis, pairs)]
    another operation x15 -> x11, other arithmetic: 0.69 us -> 5.73 us  [gather_blocks(): return jnp.stack([own, core_swap(own, axis)])]
    dot_general x7 -> x5, matrix products: 26.4 us -> 30.1 us  [on_device(): jnp.einsum('td,edf->etf', rows, w_gate, preferred_element_type=jnp.float32)]
    ppermute x15 -> x11, waiting for transfers between devices: 20 us -> 16.9 us  [core_swap(): return lax.ppermute(array, axis, [(i, i ^ 1) for i in range(count)])]
    dot_general x7 -> x5, matrix products: 46.4 us -> 43.8 us  [on_device(): jnp.einsum('etf,efd->td', inner, w_down, preferred_element_type=jnp.float32)]
    ppermute x6 -> x4, waiting for transfers between devices: 11.3 us -> 10.2 us  [shifted(): return lax.ppermute(array, axis, pairs)]
  transfers between devices with their start and end apart: 66 -> 48, of which waited for: 49 -> 41; matrix products, arithmetic and copies ran while one was open for 2% -> 2% of each run, Pallas kernels for 0% -> 0%
where the time goes in v6:
time: 282 us; the launch traced here: 279 us
  waiting for transfers between devices  122 us (43%)
  matrix products  73.9 us (26%)
  starting transfers between devices  68 us (24%)
  other arithmetic  13.1 us (5%)
    ppermute x33, waiting for transfers between devices, chip_shift(): return lax.ppermute(array, axis, pairs)  94.6 us
    ppermute x33, starting transfers between devices, chip_shift(): return lax.ppermute(array, axis, pairs)  49 us
    dot_general x5, matrix products, on_device(): jnp.einsum('etf,efd->td', inner, w_down, preferred_element_type=jnp.float32)  43.8 us
    dot_general x5, matrix products, on_device(): jnp.einsum('td,edf->etf', rows, w_gate, preferred_element_type=jnp.float32)  30.1 us
    ppermute x4, starting transfers between devices, shifted(): return lax.ppermute(array, axis, pairs)  17.5 us
    ppermute x11, waiting for transfers between devices, core_swap(): return lax.ppermute(array, axis, [(i, i ^ 1) for i in range(count)])  16.9 us
    ppermute x4, waiting for transfers between devices, shifted(): return lax.ppermute(array, axis, pairs)  10.2 us
    another operation x11, other arithmetic, gather_blocks(): return jnp.stack([own, core_swap(own, axis)])  5.73 us
  transfers between devices with their start and end apart: 48, of which 41 were waited for; matrix products, arithmetic and copies ran while one was open for 2% of the time, Pallas kernels for 0%

profile of v6, /device:TPU:0, one launch (start us, length us, event | category | flops | bytes accessed | tf_op | source)
XLA Modules:
  0.0 279.5 jit_solution(12018055384646421195)
XLA Ops:
  2.1 4.1 %collective-permute-start.1 = (bf16[2,16,2048]{2,1,0:T(8,128)(2,1)S(1)}, bf16[2,16,2048]{2,1,0:T(8,128)(2,1)S(1)}, u32[]{:S(2)}, u32[]{:S(2)}) collective-permute-start(bf16[2,16,2048]{2,1,0:T(8,128)(2,1)S(1)} %fusion.102), channel_id=1, source_target_pairs={{0,4},{1,5},{2,6},{3,7},{4,0},{5,1},{6,2},{7,3},{8,12},{9,13},{10,... | collective-permute-start | bytes 393224 | tf_op jit(solution)/shard_map/ppermute | solution.py:23
  11.8 4.4 %collective-permute-done.1 = bf16[2,16,2048]{2,1,0:T(8,128)(2,1)S(1)} collective-permute-done((bf16[2,16,2048]{2,1,0:T(8,128)(2,1)S(1)}, bf16[2,16,2048]{2,1,0:T(8,128)(2,1)S(1)}, u32[]{:S(2)}, u32[]{:S(2)}) %collective-permute-start.1) | collective-permute-done | bytes 131104 | tf_op jit(solution)/shard_map/ppermute | solution.py:23
  29.7 5.8 %fusion.28 = f32[256,2,768]{2,0,1:T(8,128)} fusion(bf16[256,2048,1]{1,0,2:T(8,128)(2,1)S(1)} %bitcast.400, bf16[1,2,2048,768]{3,2,1,0:T(8,128)(2,1)} %param.9), kind=kOutput, calls=%fused_computation.28 | convolution fusion | flops 1610612736 | bytes 8912896 | tf_op jit(solution)/shard_map/td,edf->etf/dot_general | solution.py:94
  35.4 8.5 %fusion.30 = f32[256,2048]{1,0:T(8,128)S(1)} fusion(bf16[1,2,768,2048]{3,2,1,0:T(8,128)(2,1)} %param.11, f32[256,2,768]{2,0,1:T(8,128)} %fusion.28, bf16[256,2048,1]{1,0,2:T(8,128)(2,1)S(1)} %bitcast.401, bf16[1,2,2048,768]{3,2,1,0:T(8,128)(2,1)} %param.10, f32[2,256]{1,0:T(2,128)S(1)} %copy.16), kind=kOutput, calls=%fused_computation.30 | convolution fusion | flops 3223977984 | bytes 17303552 | tf_op jit(solution)/shard_map/etf,efd->td/dot_general | solution.py:97
  48.7 5.8 %collective-permute-done.9 = bf16[2,16,2048]{2,1,0:T(8,128)(2,1)S(1)} collective-permute-done((bf16[2,16,2048]{2,1,0:T(8,128)(2,1)S(1)}, bf16[2,16,2048]{2,1,0:T(8,128)(2,1)S(1)}, u32[]{:S(2)}, u32[]{:S(2)}) %collective-permute-start.9) | collective-permute-done | bytes 131104 | tf_op jit(solution)/shard_map/ppermute | solution.py:23
  55.4 4.4 %collective-permute-done.10 = bf16[2,16,2048]{2,1,0:T(8,128)(2,1)S(1)} collective-permute-done((bf16[2,16,2048]{2,1,0:T(8,128)(2,1)S(1)}, bf16[2,16,2048]{2,1,0:T(8,128)(2,1)S(1)}, u32[]{:S(2)}, u32[]{:S(2)}) %collective-permute-start.10) | collective-permute-done | bytes 131104 | tf_op jit(solution)/shard_map/ppermute | solution.py:23
  60.0 3.4 %collective-permute-start.12 = (bf16[2,16,2048]{2,1,0:T(8,128)(2,1)S(1)}, bf16[2,16,2048]{2,1,0:T(8,128)(2,1)S(1)}, u32[]{:S(2)}, u32[]{:S(2)}) collective-permute-start(bf16[2,16,2048]{2,1,0:T(8,128)(2,1)S(1)} %get-tuple-element.28), channel_id=1, source_target_pairs={{0,8},{8,16},{16,24},{1,9},{9,17},{17,25},{2,10},{10,18},{18,26},{... | collective-permute-start | bytes 393224 | tf_op jit(solution)/shard_map/ppermute | solution.py:16
  66.5 3.2 %collective-permute-start.13 = (bf16[2,16,2048]{2,1,0:T(8,128)(2,1)S(1)}, bf16[2,16,2048]{2,1,0:T(8,128)(2,1)S(1)}, u32[]{:S(2)}, u32[]{:S(2)}) collective-permute-start(bf16[2,16,2048]{2,1,0:T(8,128)(2,1)S(1)} %fusion.106), channel_id=1, source_target_pairs={{0,2},{1,3},{2,4},{3,5},{4,6},{5,7},{6,0},{7,1},{8,10},{9,11},{10,... | collective-permute-start | bytes 393224 | tf_op jit(solution)/shard_map/ppermute | solution.py:23
  70.4 6.8 %collective-permute-done.14 = bf16[2,16,2048]{2,1,0:T(8,128)(2,1)S(1)} collective-permute-done((bf16[2,16,2048]{2,1,0:T(8,128)(2,1)S(1)}, bf16[2,16,2048]{2,1,0:T(8,128)(2,1)S(1)}, u32[]{:S(2)}, u32[]{:S(2)}) %collective-permute-start.14) | collective-permute-done | bytes 131104 | tf_op jit(solution)/shard_map/ppermute | solution.py:23
  81.7 6.1 %fusion.26 = f32[256,2,768]{2,0,1:T(8,128)} fusion(bf16[256,2048,1]{1,0,2:T(8,128)(2,1)} %bitcast.39, bf16[1,2,2048,768]{3,2,1,0:T(8,128)(2,1)} %param.9), kind=kOutput, calls=%fused_computation.26 | convolution fusion | flops 1610612736 | bytes 8912896 | tf_op jit(solution)/shard_map/td,edf->etf/dot_general | solution.py:94
  87.8 8.8 %fusion.33 = f32[256,2048]{1,0:T(8,128)S(1)} fusion(bf16[1,2,768,2048]{3,2,1,0:T(8,128)(2,1)} %param.11, f32[256,2,768]{2,0,1:T(8,128)} %fusion.26, bf16[256,2048,1]{1,0,2:T(8,128)(2,1)} %bitcast.39, bf16[1,2,2048,768]{3,2,1,0:T(8,128)(2,1)} %param.10, f32[2,256]{1,0:T(2,128)S(1)} %copy.17), kind=kOutput, calls=%fused_computation.31 | convolution fusion | flops 3223977984 | bytes 17303552 | tf_op jit(solution)/shard_map/etf,efd->td/dot_general | solution.py:97
  104.7 4.7 %collective-permute-done.20 = bf16[2,16,2048]{2,1,0:T(8,128)(2,1)S(1)} collective-permute-done((bf16[2,16,2048]{2,1,0:T(8,128)(2,1)S(1)}, bf16[2,16,2048]{2,1,0:T(8,128)(2,1)S(1)}, u32[]{:S(2)}, u32[]{:S(2)}) %collective-permute-start.20) | collective-permute-done | bytes 131104 | tf_op jit(solution)/shard_map/ppermute | solution.py:23
  109.4 4.9 %collective-permute-done.19 = bf16[2,16,2048]{2,1,0:T(8,128)(2,1)S(1)} collective-permute-done((bf16[2,16,2048]{2,1,0:T(8,128)(2,1)S(1)}, bf16[2,16,2048]{2,1,0:T(8,128)(2,1)S(1)}, u32[]{:S(2)}, u32[]{:S(2)}) %collective-permute-start.19) | collective-permute-done | bytes 131104 | tf_op jit(solution)/shard_map/ppermute | solution.py:23
  114.4 4.6 %collective-permute-start.21 = (bf16[2,16,2048]{2,1,0:T(8,128)(2,1)S(1)}, bf16[2,16,2048]{2,1,0:T(8,128)(2,1)S(1)}, u32[]{:S(2)}, u32[]{:S(2)}) collective-permute-start(bf16[2,16,2048]{2,1,0:T(8,128)(2,1)S(1)} %get-tuple-element.22), channel_id=1, source_target_pairs={{0,8},{8,16},{16,24},{1,9},{9,17},{17,25},{2,10},{10,18},{18,26},{... | collective-permute-start | bytes 393224 | tf_op jit(solution)/shard_map/ppermute | solution.py:16
  125.7 6.0 %collective-permute-done.23 = bf16[2,16,2048]{2,1,0:T(8,128)(2,1)S(1)} collective-permute-done((bf16[2,16,2048]{2,1,0:T(8,128)(2,1)S(1)}, bf16[2,16,2048]{2,1,0:T(8,128)(2,1)S(1)}, u32[]{:S(2)}, u32[]{:S(2)}) %collective-permute-start.23) | collective-permute-done | bytes 131104 | tf_op jit(solution)/shard_map/ppermute | solution.py:23
  135.9 6.1 %fusion.24 = f32[256,2,768]{2,0,1:T(8,128)} fusion(bf16[256,2048,1]{1,0,2:T(8,128)(2,1)} %bitcast.59, bf16[1,2,2048,768]{3,2,1,0:T(8,128)(2,1)} %param.9), kind=kOutput, calls=%fused_computation.24 | convolution fusion | flops 1610612736 | bytes 8912896 | tf_op jit(solution)/shard_map/td,edf->etf/dot_general | solution.py:94
  141.9 8.8 %fusion.36 = f32[256,2048]{1,0:T(8,128)S(1)} fusion(bf16[1,2,768,2048]{3,2,1,0:T(8,128)(2,1)} %param.11, f32[256,2,768]{2,0,1:T(8,128)} %fusion.24, bf16[256,2048,1]{1,0,2:T(8,128)(2,1)} %bitcast.59, bf16[1,2,2048,768]{3,2,1,0:T(8,128)(2,1)} %param.10, f32[2,256]{1,0:T(2,128)S(1)} %copy.18), kind=kOutput, calls=%fused_computation.32 | convolution fusion | flops 3223977984 | bytes 17303552 | tf_op jit(solution)/shard_map/etf,efd->td/dot_general | solution.py:97
  158.8 5.4 %collective-permute-done.29 = bf16[2,16,2048]{2,1,0:T(8,128)(2,1)S(1)} collective-permute-done((bf16[2,16,2048]{2,1,0:T(8,128)(2,1)S(1)}, bf16[2,16,2048]{2,1,0:T(8,128)(2,1)S(1)}, u32[]{:S(2)}, u32[]{:S(2)}) %collective-permute-start.29) | collective-permute-done | bytes 131104 | tf_op jit(solution)/shard_map/ppermute | solution.py:23
  164.3 4.2 %collective-permute-done.28 = bf16[2,16,2048]{2,1,0:T(8,128)(2,1)S(1)} collective-permute-done((bf16[2,16,2048]{2,1,0:T(8,128)(2,1)S(1)}, bf16[2,16,2048]{2,1,0:T(8,128)(2,1)S(1)}, u32[]{:S(2)}, u32[]{:S(2)}) %collective-permute-start.28) | collective-permute-done | bytes 131104 | tf_op jit(solution)/shard_map/ppermute | solution.py:23
  168.6 4.4 %collective-permute-start.30 = (bf16[2,16,2048]{2,1,0:T(8,128)(2,1)S(1)}, bf16[2,16,2048]{2,1,0:T(8,128)(2,1)S(1)}, u32[]{:S(2)}, u32[]{:S(2)}) collective-permute-start(bf16[2,16,2048]{2,1,0:T(8,128)(2,1)S(1)} %get-tuple-element.16), channel_id=1, source_target_pairs={{0,8},{8,16},{16,24},{1,9},{9,17},{17,25},{2,10},{10,18},{18,26},{... | collective-permute-start | bytes 393224 | tf_op jit(solution)/shard_map/ppermute | solution.py:16
  175.8 3.0 %collective-permute-start.31 = (bf16[2,16,2048]{2,1,0:T(8,128)(2,1)S(1)}, bf16[2,16,2048]{2,1,0:T(8,128)(2,1)S(1)}, u32[]{:S(2)}, u32[]{:S(2)}) collective-permute-start(bf16[2,16,2048]{2,1,0:T(8,128)(2,1)S(1)} %fusion.114), channel_id=1, source_target_pairs={{0,2},{1,3},{2,4},{3,5},{4,6},{5,7},{6,0},{7,1},{8,10},{9,11},{10,... | collective-permute-start | bytes 393224 | tf_op jit(solution)/shard_map/ppermute | solution.py:23
  179.8 7.1 %collective-permute-done.32 = bf16[2,16,2048]{2,1,0:T(8,128)(2,1)S(1)} collective-permute-done((bf16[2,16,2048]{2,1,0:T(8,128)(2,1)S(1)}, bf16[2,16,2048]{2,1,0:T(8,128)(2,1)S(1)}, u32[]{:S(2)}, u32[]{:S(2)}) %collective-permute-start.32) | collective-permute-done | bytes 131104 | tf_op jit(solution)/shard_map/ppermute | solution.py:23
  190.8 6.1 %fusion.22 = f32[256,2,768]{2,0,1:T(8,128)} fusion(bf16[256,2048,1]{1,0,2:T(8,128)(2,1)} %bitcast.79, bf16[1,2,2048,768]{3,2,1,0:T(8,128)(2,1)} %param.9), kind=kOutput, calls=%fused_computation.22 | convolution fusion | flops 1610612736 | bytes 8912896 | tf_op jit(solution)/shard_map/td,edf->etf/dot_general | solution.py:94
  196.8 8.8 %fusion.39 = f32[256,2048]{1,0:T(8,128)S(1)} fusion(bf16[1,2,768,2048]{3,2,1,0:T(8,128)(2,1)} %param.11, f32[256,2,768]{2,0,1:T(8,128)} %fusion.22, bf16[256,2048,1]{1,0,2:T(8,128)(2,1)} %bitcast.79, bf16[1,2,2048,768]{3,2,1,0:T(8,128)(2,1)} %param.10, f32[2,256]{1,0:T(2,128)S(1)} %copy.19), kind=kOutput, calls=%fused_computation.33 | convolution fusion | flops 3223977984 | bytes 17303552 | tf_op jit(solution)/shard_map/etf,efd->td/dot_general | solution.py:97
  213.7 5.2 %collective-permute-done.38 = bf16[2,16,2048]{2,1,0:T(8,128)(2,1)S(1)} collective-permute-done((bf16[2,16,2048]{2,1,0:T(8,128)(2,1)S(1)}, bf16[2,16,2048]{2,1,0:T(8,128)(2,1)S(1)}, u32[]{:S(2)}, u32[]{:S(2)}) %collective-permute-start.38) | collective-permute-done | bytes 131104 | tf_op jit(solution)/shard_map/ppermute | solution.py:23
  218.9 4.4 %collective-permute-done.37 = bf16[2,16,2048]{2,1,0:T(8,128)(2,1)S(1)} collective-permute-done((bf16[2,16,2048]{2,1,0:T(8,128)(2,1)S(1)}, bf16[2,16,2048]{2,1,0:T(8,128)(2,1)S(1)}, u32[]{:S(2)}, u32[]{:S(2)}) %collective-permute-start.37) | collective-permute-done | bytes 131104 | tf_op jit(solution)/shard_map/ppermute | solution.py:23
  223.4 5.2 %collective-permute-start.39 = (bf16[2,16,2048]{2,1,0:T(8,128)(2,1)S(1)}, bf16[2,16,2048]{2,1,0:T(8,128)(2,1)S(1)}, u32[]{:S(2)}, u32[]{:S(2)}) collective-permute-start(bf16[2,16,2048]{2,1,0:T(8,128)(2,1)S(1)} %get-tuple-element.10), channel_id=1, source_target_pairs={{0,8},{8,16},{16,24},{1,9},{9,17},{17,25},{2,10},{10,18},{18,26},{... | collective-permute-start | bytes 393224 | tf_op jit(solution)/shard_map/ppermute | solution.py:16
  235.5 6.2 %collective-permute-done.41 = bf16[2,16,2048]{2,1,0:T(8,128)(2,1)S(1)} collective-permute-done((bf16[2,16,2048]{2,1,0:T(8,128)(2,1)S(1)}, bf16[2,16,2048]{2,1,0:T(8,128)(2,1)S(1)}, u32[]{:S(2)}, u32[]{:S(2)}) %collective-permute-start.41) | collective-permute-done | bytes 131104 | tf_op jit(solution)/shard_map/ppermute | solution.py:23
  246.1 6.1 %fusion.20 = f32[256,2,768]{2,0,1:T(8,128)} fusion(bf16[256,2048,1]{1,0,2:T(8,128)(2,1)} %bitcast.100, bf16[1,2,2048,768]{3,2,1,0:T(8,128)(2,1)} %param.9), kind=kOutput, calls=%fused_computation.20 | convolution fusion | flops 1610612736 | bytes 8912896 | tf_op jit(solution)/shard_map/td,edf->etf/dot_general | solution.py:94
  252.2 8.8 %fusion.42 = f32[256,2048]{1,0:T(8,128)S(1)} fusion(bf16[1,2,768,2048]{3,2,1,0:T(8,128)(2,1)} %param.11, f32[256,2,768]{2,0,1:T(8,128)} %fusion.20, bf16[256,2048,1]{1,0,2:T(8,128)(2,1)} %bitcast.100, bf16[1,2,2048,768]{3,2,1,0:T(8,128)(2,1)} %param.10, f32[2,256]{1,0:T(2,128)S(1)} %copy.20), kind=kOutput, calls=%fused_computation.34 | convolution fusion | flops 3223977984 | bytes 17303552 | tf_op jit(solution)/shard_map/etf,efd->td/dot_general | solution.py:97
  269.1 4.9 %collective-permute-done.47 = bf16[2,16,2048]{2,1,0:T(8,128)(2,1)S(1)} collective-permute-done((bf16[2,16,2048]{2,1,0:T(8,128)(2,1)S(1)}, bf16[2,16,2048]{2,1,0:T(8,128)(2,1)S(1)}, u32[]{:S(2)}, u32[]{:S(2)}) %collective-permute-start.47) | collective-permute-done | bytes 131104 | tf_op jit(solution)/shard_map/ppermute | solution.py:23
  274.0 4.7 %collective-permute-done.46 = bf16[2,16,2048]{2,1,0:T(8,128)(2,1)S(1)} collective-permute-done((bf16[2,16,2048]{2,1,0:T(8,128)(2,1)S(1)}, bf16[2,16,2048]{2,1,0:T(8,128)(2,1)S(1)}, u32[]{:S(2)}, u32[]{:S(2)}) %collective-permute-start.46) | collective-permute-done | bytes 131104 | tf_op jit(solution)/shard_map/ppermute | solution.py:23
  (153 shorter events, 97.9 us)
Async XLA Ops:
  2.1 14.1 %collective-permute-start.1 = (bf16[2,16,2048]{2,1,0:T(8,128)(2,1)S(1)}, bf16[2,16,2048]{2,1,0:T(8,128)(2,1)S(1)}, u32[]{:S(2)}, u32[]{:S(2)}) collective-permute-start(bf16[2,16,2048]{2,1,0:T(8,128)(2,1)S(1)} %fusion.102), channel_id=1, source_target_pairs={{0,4},{1,5},{2,6},{3,7},{4,0},{5,1},{6,2},{7,3},{8,12},{9,13},{10,... | collective-permute-start | bytes 393224 | tf_op jit(solution)/shard_map/ppermute | solution.py:23
  6.2 10.0 %collective-permute-start = (bf16[2,16,2048]{2,1,0:T(8,128)(2,1)S(1)}, bf16[2,16,2048]{2,1,0:T(8,128)(2,1)S(1)}, u32[]{:S(2)}, u32[]{:S(2)}) collective-permute-start(bf16[2,16,2048]{2,1,0:T(8,128)(2,1)S(1)} %fusion.102), channel_id=1, source_target_pairs={{0,2},{1,3},{2,4},{3,5},{4,6},{5,7},{6,0},{7,1},{8,10},{9,11},{10,... | collective-permute-start | bytes 393224 | tf_op jit(solution)/shard_map/ppermute | solution.py:23
  7.8 9.1 %collective-permute-start.2 = (bf16[2,16,2048]{2,1,0:T(8,128)(2,1)S(1)}, bf16[2,16,2048]{2,1,0:T(8,128)(2,1)S(1)}, u32[]{:S(2)}, u32[]{:S(2)}) collective-permute-start(bf16[2,16,2048]{2,1,0:T(8,128)(2,1)S(1)} %fusion.102), channel_id=1, source_target_pairs={{0,6},{1,7},{2,0},{3,1},{4,2},{5,3},{6,4},{7,5},{8,14},{9,15},{10,... | collective-permute-start | bytes 393224 | tf_op jit(solution)/shard_map/ppermute | solution.py:23
  17.0 12.6 %collective-permute-start.3 = (bf16[4,2,16,2048]{3,2,1,0:T(8,128)(2,1)S(1)}, bf16[4,2,16,2048]{3,2,1,0:T(8,128)(2,1)S(1)}, u32[]{:S(2)}, u32[]{:S(2)}) collective-permute-start(bf16[4,2,16,2048]{3,2,1,0:T(8,128)(2,1)S(1)} %get-tuple-element.55), channel_id=1, source_target_pairs={{0,1},{1,0},{2,3},{3,2},{4,5},{5,4},{6,7},{7,6},{8,9},{9,8},{10,11... | collective-permute-start | bytes 1572872 | tf_op jit(solution)/shard_map/ppermute | solution.py:28
  17.5 5.9 %collective-permute-start.6 = (f32[4,16,16]{2,1,0:T(8,128)S(1)}, f32[4,16,16]{2,1,0:T(8,128)S(1)}, u32[]{:S(2)}, u32[]{:S(2)}) collective-permute-start(f32[4,16,16]{2,1,0:T(8,128)S(1)} %select_reduce_fusion), channel_id=1, source_target_pairs={{0,6},{1,7},{2,0},{3,1},{4,2},{5,3},{6,4},{7,5},{8,14},{9,15},{10,... | collective-permute-start | bytes 12296 | tf_op jit(solution)/shard_map/ppermute | solution.py:23
  46.2 8.3 %collective-permute-start.9 = (bf16[2,16,2048]{2,1,0:T(8,128)(2,1)S(1)}, bf16[2,16,2048]{2,1,0:T(8,128)(2,1)S(1)}, u32[]{:S(2)}, u32[]{:S(2)}) collective-permute-start(bf16[2,16,2048]{2,1,0:T(8,128)(2,1)S(1)} %get-tuple-element.51), channel_id=1, source_target_pairs={{0,6},{1,7},{2,0},{3,1},{4,2},{5,3},{6,4},{7,5},{8,14},{9,15},{10,... | collective-permute-start | bytes 393224 | tf_op jit(solution)/shard_map/ppermute | solution.py:23
  47.1 8.3 %collective-permute-start.11 = (bf16[2,16,2048]{2,1,0:T(8,128)(2,1)S(1)}, bf16[2,16,2048]{2,1,0:T(8,128)(2,1)S(1)}, u32[]{:S(2)}, u32[]{:S(2)}) collective-permute-start(bf16[2,16,2048]{2,1,0:T(8,128)(2,1)S(1)} %get-tuple-element.52), channel_id=1, source_target_pairs={{0,2},{1,3},{2,4},{3,5},{4,6},{5,7},{6,0},{7,1},{8,10},{9,11},{10,... | collective-permute-start | bytes 393224 | tf_op jit(solution)/shard_map/ppermute | solution.py:23
  48.3 11.6 %collective-permute-start.10 = (bf16[2,16,2048]{2,1,0:T(8,128)(2,1)S(1)}, bf16[2,16,2048]{2,1,0:T(8,128)(2,1)S(1)}, u32[]{:S(2)}, u32[]{:S(2)}) collective-permute-start(bf16[2,16,2048]{2,1,0:T(8,128)(2,1)S(1)} %get-tuple-element.53), channel_id=1, source_target_pairs={{0,4},{1,5},{2,6},{3,7},{4,0},{5,1},{6,2},{7,3},{8,12},{9,13},{10,... | collective-permute-start | bytes 393224 | tf_op jit(solution)/shard_map/ppermute | solution.py:23
  60.0 6.1 %collective-permute-start.12 = (bf16[2,16,2048]{2,1,0:T(8,128)(2,1)S(1)}, bf16[2,16,2048]{2,1,0:T(8,128)(2,1)S(1)}, u32[]{:S(2)}, u32[]{:S(2)}) collective-permute-start(bf16[2,16,2048]{2,1,0:T(8,128)(2,1)S(1)} %get-tuple-element.28), channel_id=1, source_target_pairs={{0,8},{8,16},{16,24},{1,9},{9,17},{17,25},{2,10},{10,18},{18,26},{... | collective-permute-start | bytes 393224 | tf_op jit(solution)/shard_map/ppermute | solution.py:16
  66.4 10.9 %collective-permute-start.14 = (bf16[2,16,2048]{2,1,0:T(8,128)(2,1)S(1)}, bf16[2,16,2048]{2,1,0:T(8,128)(2,1)S(1)}, u32[]{:S(2)}, u32[]{:S(2)}) collective-permute-start(bf16[2,16,2048]{2,1,0:T(8,128)(2,1)S(1)} %fusion.106), channel_id=1, source_target_pairs={{0,4},{1,5},{2,6},{3,7},{4,0},{5,1},{6,2},{7,3},{8,12},{9,13},{10,... | collective-permute-start | bytes 393224 | tf_op jit(solution)/shard_map/ppermute | solution.py:23
  66.5 10.8 %collective-permute-start.13 = (bf16[2,16,2048]{2,1,0:T(8,128)(2,1)S(1)}, bf16[2,16,2048]{2,1,0:T(8,128)(2,1)S(1)}, u32[]{:S(2)}, u32[]{:S(2)}) collective-permute-start(bf16[2,16,2048]{2,1,0:T(8,128)(2,1)S(1)} %fusion.106), channel_id=1, source_target_pairs={{0,2},{1,3},{2,4},{3,5},{4,6},{5,7},{6,0},{7,1},{8,10},{9,11},{10,... | collective-permute-start | bytes 393224 | tf_op jit(solution)/shard_map/ppermute | solution.py:23
  69.7 8.8 %collective-permute-start.15 = (bf16[2,16,2048]{2,1,0:T(8,128)(2,1)S(1)}, bf16[2,16,2048]{2,1,0:T(8,128)(2,1)S(1)}, u32[]{:S(2)}, u32[]{:S(2)}) collective-permute-start(bf16[2,16,2048]{2,1,0:T(8,128)(2,1)S(1)} %fusion.106), channel_id=1, source_target_pairs={{0,6},{1,7},{2,0},{3,1},{4,2},{5,3},{6,4},{7,5},{8,14},{9,15},{10,... | collective-permute-start | bytes 393224 | tf_op jit(solution)/shard_map/ppermute | solution.py:23
  99.8 9.6 %collective-permute-start.20 = (bf16[2,16,2048]{2,1,0:T(8,128)(2,1)S(1)}, bf16[2,16,2048]{2,1,0:T(8,128)(2,1)S(1)}, u32[]{:S(2)}, u32[]{:S(2)}) collective-permute-start(bf16[2,16,2048]{2,1,0:T(8,128)(2,1)S(1)} %get-tuple-element.47), channel_id=1, source_target_pairs={{0,2},{1,3},{2,4},{3,5},{4,6},{5,7},{6,0},{7,1},{8,10},{9,11},{10,... | collective-permute-start | bytes 393224 | tf_op jit(solution)/shard_map/ppermute | solution.py:23
  101.1 13.2 %collective-permute-start.19 = (bf16[2,16,2048]{2,1,0:T(8,128)(2,1)S(1)}, bf16[2,16,2048]{2,1,0:T(8,128)(2,1)S(1)}, u32[]{:S(2)}, u32[]{:S(2)}) collective-permute-start(bf16[2,16,2048]{2,1,0:T(8,128)(2,1)S(1)} %get-tuple-element.48), channel_id=1, source_target_pairs={{0,4},{1,5},{2,6},{3,7},{4,0},{5,1},{6,2},{7,3},{8,12},{9,13},{10,... | collective-permute-start | bytes 393224 | tf_op jit(solution)/shard_map/ppermute | solution.py:23
  114.4 7.1 %collective-permute-start.21 = (bf16[2,16,2048]{2,1,0:T(8,128)(2,1)S(1)}, bf16[2,16,2048]{2,1,0:T(8,128)(2,1)S(1)}, u32[]{:S(2)}, u32[]{:S(2)}) collective-permute-start(bf16[2,16,2048]{2,1,0:T(8,128)(2,1)S(1)} %get-tuple-element.22), channel_id=1, source_target_pairs={{0,8},{8,16},{16,24},{1,9},{9,17},{17,25},{2,10},{10,18},{18,26},{... | collective-permute-start | bytes 393224 | tf_op jit(solution)/shard_map/ppermute | solution.py:16
  121.7 10.0 %collective-permute-start.23 = (bf16[2,16,2048]{2,1,0:T(8,128)(2,1)S(1)}, bf16[2,16,2048]{2,1,0:T(8,128)(2,1)S(1)}, u32[]{:S(2)}, u32[]{:S(2)}) collective-permute-start(bf16[2,16,2048]{2,1,0:T(8,128)(2,1)S(1)} %fusion.110), channel_id=1, source_target_pairs={{0,4},{1,5},{2,6},{3,7},{4,0},{5,1},{6,2},{7,3},{8,12},{9,13},{10,... | collective-permute-start | bytes 393224 | tf_op jit(solution)/shard_map/ppermute | solution.py:23
  121.8 10.0 %collective-permute-start.22 = (bf16[2,16,2048]{2,1,0:T(8,128)(2,1)S(1)}, bf16[2,16,2048]{2,1,0:T(8,128)(2,1)S(1)}, u32[]{:S(2)}, u32[]{:S(2)}) collective-permute-start(bf16[2,16,2048]{2,1,0:T(8,128)(2,1)S(1)} %fusion.110), channel_id=1, source_target_pairs={{0,2},{1,3},{2,4},{3,5},{4,6},{5,7},{6,0},{7,1},{8,10},{9,11},{10,... | collective-permute-start | bytes 393224 | tf_op jit(solution)/shard_map/ppermute | solution.py:23
  123.7 9.1 %collective-permute-start.24 = (bf16[2,16,2048]{2,1,0:T(8,128)(2,1)S(1)}, bf16[2,16,2048]{2,1,0:T(8,128)(2,1)S(1)}, u32[]{:S(2)}, u32[]{:S(2)}) collective-permute-start(bf16[2,16,2048]{2,1,0:T(8,128)(2,1)S(1)} %fusion.110), channel_id=1, source_target_pairs={{0,6},{1,7},{2,0},{3,1},{4,2},{5,3},{6,4},{7,5},{8,14},{9,15},{10,... | collective-permute-start | bytes 393224 | tf_op jit(solution)/shard_map/ppermute | solution.py:23
  154.8 9.5 %collective-permute-start.29 = (bf16[2,16,2048]{2,1,0:T(8,128)(2,1)S(1)}, bf16[2,16,2048]{2,1,0:T(8,128)(2,1)S(1)}, u32[]{:S(2)}, u32[]{:S(2)}) collective-permute-start(bf16[2,16,2048]{2,1,0:T(8,128)(2,1)S(1)} %get-tuple-element.42), channel_id=1, source_target_pairs={{0,2},{1,3},{2,4},{3,5},{4,6},{5,7},{6,0},{7,1},{8,10},{9,11},{10,... | collective-permute-start | bytes 393224 | tf_op jit(solution)/shard_map/ppermute | solution.py:23
  155.1 13.3 %collective-permute-start.28 = (bf16[2,16,2048]{2,1,0:T(8,128)(2,1)S(1)}, bf16[2,16,2048]{2,1,0:T(8,128)(2,1)S(1)}, u32[]{:S(2)}, u32[]{:S(2)}) collective-permute-start(bf16[2,16,2048]{2,1,0:T(8,128)(2,1)S(1)} %get-tuple-element.43), channel_id=1, source_target_pairs={{0,4},{1,5},{2,6},{3,7},{4,0},{5,1},{6,2},{7,3},{8,12},{9,13},{10,... | collective-permute-start | bytes 393224 | tf_op jit(solution)/shard_map/ppermute | solution.py:23
  168.6 6.9 %collective-permute-start.30 = (bf16[2,16,2048]{2,1,0:T(8,128)(2,1)S(1)}, bf16[2,16,2048]{2,1,0:T(8,128)(2,1)S(1)}, u32[]{:S(2)}, u32[]{:S(2)}) collective-permute-start(bf16[2,16,2048]{2,1,0:T(8,128)(2,1)S(1)} %get-tuple-element.16), channel_id=1, source_target_pairs={{0,8},{8,16},{16,24},{1,9},{9,17},{17,25},{2,10},{10,18},{18,26},{... | collective-permute-start | bytes 393224 | tf_op jit(solution)/shard_map/ppermute | solution.py:16
  175.7 11.2 %collective-permute-start.32 = (bf16[2,16,2048]{2,1,0:T(8,128)(2,1)S(1)}, bf16[2,16,2048]{2,1,0:T(8,128)(2,1)S(1)}, u32[]{:S(2)}, u32[]{:S(2)}) collective-permute-start(bf16[2,16,2048]{2,1,0:T(8,128)(2,1)S(1)} %fusion.114), channel_id=1, source_target_pairs={{0,4},{1,5},{2,6},{3,7},{4,0},{5,1},{6,2},{7,3},{8,12},{9,13},{10,... | collective-permute-start | bytes 393224 | tf_op jit(solution)/shard_map/ppermute | solution.py:23
  175.8 11.1 %collective-permute-start.31 = (bf16[2,16,2048]{2,1,0:T(8,128)(2,1)S(1)}, bf16[2,16,2048]{2,1,0:T(8,128)(2,1)S(1)}, u32[]{:S(2)}, u32[]{:S(2)}) collective-permute-start(bf16[2,16,2048]{2,1,0:T(8,128)(2,1)S(1)} %fusion.114), channel_id=1, source_target_pairs={{0,2},{1,3},{2,4},{3,5},{4,6},{5,7},{6,0},{7,1},{8,10},{9,11},{10,... | collective-permute-start | bytes 393224 | tf_op jit(solution)/shard_map/ppermute | solution.py:23
  178.8 8.8 %collective-permute-start.33 = (bf16[2,16,2048]{2,1,0:T(8,128)(2,1)S(1)}, bf16[2,16,2048]{2,1,0:T(8,128)(2,1)S(1)}, u32[]{:S(2)}, u32[]{:S(2)}) collective-permute-start(bf16[2,16,2048]{2,1,0:T(8,128)(2,1)S(1)} %fusion.114), channel_id=1, source_target_pairs={{0,6},{1,7},{2,0},{3,1},{4,2},{5,3},{6,4},{7,5},{8,14},{9,15},{10,... | collective-permute-start | bytes 393224 | tf_op jit(solution)/shard_map/ppermute | solution.py:23
  209.0 10.0 %collective-permute-start.38 = (bf16[2,16,2048]{2,1,0:T(8,128)(2,1)S(1)}, bf16[2,16,2048]{2,1,0:T(8,128)(2,1)S(1)}, u32[]{:S(2)}, u32[]{:S(2)}) collective-permute-start(bf16[2,16,2048]{2,1,0:T(8,128)(2,1)S(1)} %get-tuple-element.37), channel_id=1, source_target_pairs={{0,2},{1,3},{2,4},{3,5},{4,6},{5,7},{6,0},{7,1},{8,10},{9,11},{10,... | collective-permute-start | bytes 393224 | tf_op jit(solution)/shard_map/ppermute | solution.py:23
  210.0 13.3 %collective-permute-start.37 = (bf16[2,16,2048]{2,1,0:T(8,128)(2,1)S(1)}, bf16[2,16,2048]{2,1,0:T(8,128)(2,1)S(1)}, u32[]{:S(2)}, u32[]{:S(2)}) collective-permute-start(bf16[2,16,2048]{2,1,0:T(8,128)(2,1)S(1)} %get-tuple-element.38), channel_id=1, source_target_pairs={{0,4},{1,5},{2,6},{3,7},{4,0},{5,1},{6,2},{7,3},{8,12},{9,13},{10,... | collective-permute-start | bytes 393224 | tf_op jit(solution)/shard_map/ppermute | solution.py:23
  223.4 7.7 %collective-permute-start.39 = (bf16[2,16,2048]{2,1,0:T(8,128)(2,1)S(1)}, bf16[2,16,2048]{2,1,0:T(8,128)(2,1)S(1)}, u32[]{:S(2)}, u32[]{:S(2)}) collective-permute-start(bf16[2,16,2048]{2,1,0:T(8,128)(2,1)S(1)} %get-tuple-element.10), channel_id=1, source_target_pairs={{0,8},{8,16},{16,24},{1,9},{9,17},{17,25},{2,10},{10,18},{18,26},{... | collective-permute-start | bytes 393224 | tf_op jit(solution)/shard_map/ppermute | solution.py:16
  231.4 10.3 %collective-permute-start.41 = (bf16[2,16,2048]{2,1,0:T(8,128)(2,1)S(1)}, bf16[2,16,2048]{2,1,0:T(8,128)(2,1)S(1)}, u32[]{:S(2)}, u32[]{:S(2)}) collective-permute-start(bf16[2,16,2048]{2,1,0:T(8,128)(2,1)S(1)} %fusion.118), channel_id=1, source_target_pairs={{0,4},{1,5},{2,6},{3,7},{4,0},{5,1},{6,2},{7,3},{8,12},{9,13},{10,... | collective-permute-start | bytes 393224 | tf_op jit(solution)/shard_map/ppermute | solution.py:23
  231.5 10.2 %collective-permute-start.40 = (bf16[2,16,2048]{2,1,0:T(8,128)(2,1)S(1)}, bf16[2,16,2048]{2,1,0:T(8,128)(2,1)S(1)}, u32[]{:S(2)}, u32[]{:S(2)}) collective-permute-start(bf16[2,16,2048]{2,1,0:T(8,128)(2,1)S(1)} %fusion.118), channel_id=1, source_target_pairs={{0,2},{1,3},{2,4},{3,5},{4,6},{5,7},{6,0},{7,1},{8,10},{9,11},{10,... | collective-permute-start | bytes 393224 | tf_op jit(solution)/shard_map/ppermute | solution.py:23
  233.8 9.2 %collective-permute-start.42 = (bf16[2,16,2048]{2,1,0:T(8,128)(2,1)S(1)}, bf16[2,16,2048]{2,1,0:T(8,128)(2,1)S(1)}, u32[]{:S(2)}, u32[]{:S(2)}) collective-permute-start(bf16[2,16,2048]{2,1,0:T(8,128)(2,1)S(1)} %fusion.118), channel_id=1, source_target_pairs={{0,6},{1,7},{2,0},{3,1},{4,2},{5,3},{6,4},{7,5},{8,14},{9,15},{10,... | collective-permute-start | bytes 393224 | tf_op jit(solution)/shard_map/ppermute | solution.py:23
  264.6 9.3 %collective-permute-start.47 = (bf16[2,16,2048]{2,1,0:T(8,128)(2,1)S(1)}, bf16[2,16,2048]{2,1,0:T(8,128)(2,1)S(1)}, u32[]{:S(2)}, u32[]{:S(2)}) collective-permute-start(bf16[2,16,2048]{2,1,0:T(8,128)(2,1)S(1)} %get-tuple-element.32), channel_id=1, source_target_pairs={{0,2},{1,3},{2,4},{3,5},{4,6},{5,7},{6,0},{7,1},{8,10},{9,11},{10,... | collective-permute-start | bytes 393224 | tf_op jit(solution)/shard_map/ppermute | solution.py:23
  265.4 13.3 %collective-permute-start.46 = (bf16[2,16,2048]{2,1,0:T(8,128)(2,1)S(1)}, bf16[2,16,2048]{2,1,0:T(8,128)(2,1)S(1)}, u32[]{:S(2)}, u32[]{:S(2)}) collective-permute-start(bf16[2,16,2048]{2,1,0:T(8,128)(2,1)S(1)} %get-tuple-element.33), channel_id=1, source_target_pairs={{0,4},{1,5},{2,6},{3,7},{4,0},{5,1},{6,2},{7,3},{8,12},{9,13},{10,... | collective-permute-start | bytes 393224 | tf_op jit(solution)/shard_map/ppermute | solution.py:23
  (21 other events, 140.1 us)

commit v7 on v3

--- a/solution.py
+++ b/solution.py
@@ -2,6 +2,8 @@
 import jax.numpy as jnp
 from jax import lax
 from jax.sharding import PartitionSpec as P
+from jax.experimental import pallas as pl
+from jax.experimental.pallas import tpu as pltpu
 
 MB = 4
 
@@ -41,6 +43,40 @@
     for k in range(1, chips):
         total = total + chip_shift(chip_sum[k].astype(jnp.bfloat16), axis, -k).astype(jnp.float32)
     return total
+
+
+def expert_kernel(rows_ref, gate_ref, up_ref, down_ref, weight_ref, out_ref):
+    first = (pl.program_id(0) == 0) & (pl.program_id(1) == 0)
+
+    @pl.when(first)
+    def _():
+        out_ref[...] = jnp.zeros_like(out_ref)
+
+    rows = rows_ref[...]
+    gate_part = jnp.dot(rows, gate_ref[...], preferred_element_type=jnp.float32)
+    up_part = jnp.dot(rows, up_ref[...], preferred_element_type=jnp.float32)
+    inner = (jax.nn.silu(gate_part) * up_part * weight_ref[...]).astype(jnp.bfloat16)
+    out_ref[...] += jnp.dot(inner, down_ref[...], preferred_element_type=jnp.float32)
+
+
+def experts_mixed(rows, w_gate, w_up, w_down, weight, chunk=256):
+    count, width = rows.shape
+    local, _, hidden = w_gate.shape
+    chunks = hidden // chunk
+    return pl.pallas_call(
+        expert_kernel,
+        grid=(local, chunks),
+        in_specs=[
+            pl.BlockSpec((count, width), lambda e, f: (0, 0)),
+            pl.BlockSpec((None, width, chunk), lambda e, f: (e, 0, f)),
+            pl.BlockSpec((None, width, chunk), lambda e, f: (e, 0, f)),
+            pl.BlockSpec((None, chunk, width), lambda e, f: (e, f, 0)),
+            pl.BlockSpec((None, count, 1), lambda e, f: (e, 0, 0)),
+        ],
+        out_specs=pl.BlockSpec((count, width), lambda e, f: (0, 0)),
+        out_shape=jax.ShapeDtypeStruct((count, width), jnp.float32),
+        compiler_params=pltpu.CompilerParams(dimension_semantics=("arbitrary", "arbitrary")),
+    )(rows, w_gate, w_up, w_down, weight[:, :, None])
 
 
 def rms_normed(hidden, gain):
@@ -88,10 +124,7 @@
         weight = lax.dynamic_index_in_dim(mixing, clipped, 0, keepdims=False)
         values, normed = rms_normed(incoming, gain)
         rows = gather_blocks(normed, "expert").reshape(2 * chips * tok_rows, width)
-        gate_part = jnp.einsum("td,edf->etf", rows, w_gate, preferred_element_type=jnp.float32)
-        up_part = jnp.einsum("td,edf->etf", rows, w_up, preferred_element_type=jnp.float32)
-        inner = (jax.nn.silu(gate_part) * up_part * weight[:, :, None]).astype(jnp.bfloat16)
-        partial = jnp.einsum("etf,efd->td", inner, w_down, preferred_element_type=jnp.float32)
+        partial = experts_mixed(rows, w_gate, w_up, w_down, weight)
         mixed = scatter_blocks(partial.reshape(2, chips, tok_rows, width), "expert")
         produced = (values + mixed).astype(jnp.bfloat16)
         held = jnp.where(active, produced, incoming)

time: 275 us -> 294 us (1.069)
  Pallas kernels: 0 us -> 77.4 us
  matrix products: 72.8 us -> 0 us
  local copies, waits for them, and re-layouts: 2.55 us -> 22.7 us
  waiting for transfers between devices: 89.5 us -> 75.8 us
  other arithmetic: 8.72 us -> 14.4 us
    pallas_call x0 -> x7, Pallas kernels: none -> 77.4 us  [experts_mixed(): pl.pallas_call(expert_kernel, grid=(local, chunks), in_specs=[pl.BlockSpe...]
    dot_general x14 -> x0, matrix products: 72.8 us -> none  [the longest x7 46.4 us: on_device(): jnp.einsum('etf,efd->td', inner, w_down, preferred_element_type=jnp.float32)]
    ppermute x15, waiting for transfers between devices: 20 us -> 7.86 us  [core_swap(): return lax.ppermute(array, axis, [(i, i ^ 1) for i in range(count)])]
    slice x7, local copies, waits for them, and re-layouts: 0.24 us -> 7.53 us  [scatter_blocks(): chip_sum = partial[0] + swapped.astype(jnp.float32)]
    slice x7, local copies, waits for them, and re-layouts: 0.21 us -> 7.48 us  [scatter_blocks(): swapped = core_swap(partial[1].astype(jnp.bfloat16), axis)]
    another operation x15, other arithmetic: 0.69 us -> 6.34 us  [gather_blocks(): return jnp.stack([own, core_swap(own, axis)])]
    broadcast_in_dim x0 -> x8, local copies, waits for them, and re-layouts: none -> 5.63 us  [experts_mixed(): weight[:, :, None]]
  transfers between devices with their start and end apart: 66 -> 66, of which waited for: 49 -> 49; matrix products, arithmetic and copies ran while one was open for 2% -> 6% of each run, Pallas kernels for 0% -> 0%
where the time goes in v7:
time: 294 us; the launch traced here: 290 us
  starting transfers between devices  99.4 us (34%)
  Pallas kernels  77.4 us (26%)
  waiting for transfers between devices  75.8 us (26%)
  local copies, waits for them, and re-layouts  22.7 us (8%)
  other arithmetic  14.4 us (5%)
    pallas_call x7, Pallas kernels, experts_mixed(): pl.pallas_call(expert_kernel, grid=(local, chunks), in_specs=[pl.BlockSpe...  77.4 us
    ppermute x45, starting transfers between devices, chip_shift(): return lax.ppermute(array, axis, pairs)  70 us
    ppermute x45, waiting for transfers between devices, chip_shift(): return lax.ppermute(array, axis, pairs)  56.7 us
    ppermute x6, starting transfers between devices, shifted(): return lax.ppermute(array, axis, pairs)  27.5 us
    ppermute x6, waiting for transfers between devices, shifted(): return lax.ppermute(array, axis, pairs)  11.3 us
    ppermute x15, waiting for transfers between devices, core_swap(): return lax.ppermute(array, axis, [(i, i ^ 1) for i in range(count)])  7.86 us
    slice x7, local copies, waits for them, and re-layouts, scatter_blocks(): chip_sum = partial[0] + swapped.astype(jnp.float32)  7.53 us
    slice x7, local copies, waits for them, and re-layouts, scatter_blocks(): swapped = core_swap(partial[1].astype(jnp.bfloat16), axis)  7.48 us
  transfers between devices with their start and end apart: 66, of which 49 were waited for; matrix products, arithmetic and copies ran while one was open for 6% of the time, Pallas kernels for 0%

profile of v7, /device:TPU:0, one launch (start us, length us, event | category | flops | bytes accessed | tf_op | source)
XLA Modules:
  0.0 290.4 jit_solution(13623062002734057467)
XLA Ops:
  1.9 3.1 %collective-permute-start = (bf16[16,2048]{1,0:T(8,128)(2,1)S(1)}, bf16[16,2048]{1,0:T(8,128)(2,1)S(1)}, u32[]{:S(2)}, u32[]{:S(2)}) collective-permute-start(bf16[16,2048]{1,0:T(8,128)(2,1)S(1)} %fusion.3), channel_id=1, source_target_pairs={{0,2},{1,3},{2,4},{3,5},{4,6},{5,7},{6,0},{7,1},{8,10},{9,11},{10,... | collective-permute-start | bytes 196616 | tf_op jit(solution)/shard_map/ppermute | solution.py:24
  5.0 2.6 collective-permute-start.1
  13.5 2.9 collective-permute-start.6
  22.5 11.1 %shard_map.73 = f32[128,2048]{1,0:T(8,128)} custom-call(bf16[128,2048]{1,0:T(8,128)(2,1)} %bitcast.332, bf16[2,2048,768]{2,1,0:T(8,128)(2,1)} %bitcast.303, bf16[2,2048,768]{2,1,0:T(8,128)(2,1)} %bitcast.310, bf16[2,768,2048]{2,1,0:T(8,128)(2,1)} %bitcast.317, f32[2,128,1]{2,1,0:T(8,128)} %copy.39.weight_ref), custom_call_target="tpu_custom_call" | custom-call | tf_op jit(solution)/shard_map/pallas_call | solution.py:66
  37.6 2.6 collective-permute-start.11
  41.6 3.6 %collective-permute-done.11 = bf16[16,2048]{1,0:T(8,128)(2,1)S(1)} collective-permute-done((bf16[16,2048]{1,0:T(8,128)(2,1)S(1)}, bf16[16,2048]{1,0:T(8,128)(2,1)S(1)}, u32[]{:S(2)}, u32[]{:S(2)}) %collective-permute-start.11) | collective-permute-done | bytes 65568 | tf_op jit(solution)/shard_map/ppermute | solution.py:24
  45.3 3.4 %collective-permute-start.12 = (bf16[16,2048]{1,0:T(8,128)(2,1)S(1)}, bf16[16,2048]{1,0:T(8,128)(2,1)S(1)}, u32[]{:S(2)}, u32[]{:S(2)}) collective-permute-start(bf16[16,2048]{1,0:T(8,128)(2,1)S(1)} %get-tuple-element.40), channel_id=1, source_target_pairs={{0,8},{8,16},{16,24},{1,9},{9,17},{17,25},{2,10},{10,18},{18,26},{... | collective-permute-start | bytes 196616 | tf_op jit(solution)/shard_map/ppermute | solution.py:17
  61.2 11.1 %shard_map.74 = f32[128,2048]{1,0:T(8,128)} custom-call(bf16[128,2048]{1,0:T(8,128)(2,1)} %bitcast.333, bf16[2,2048,768]{2,1,0:T(8,128)(2,1)} %bitcast.304, bf16[2,2048,768]{2,1,0:T(8,128)(2,1)} %bitcast.311, bf16[2,768,2048]{2,1,0:T(8,128)(2,1)} %bitcast.318, f32[2,128,1]{2,1,0:T(8,128)} %copy.40.weight_ref), custom_call_target="tpu_custom_call" | custom-call | tf_op jit(solution)/shard_map/pallas_call | solution.py:66
  75.0 3.1 %collective-permute-start.18 = (bf16[16,2048]{1,0:T(8,128)(2,1)S(1)}, bf16[16,2048]{1,0:T(8,128)(2,1)S(1)}, u32[]{:S(2)}, u32[]{:S(2)}) collective-permute-start(bf16[16,2048]{1,0:T(8,128)(2,1)S(1)} %get-tuple-element.68), channel_id=1, source_target_pairs={{0,6},{1,7},{2,0},{3,1},{4,2},{5,3},{6,4},{7,5},{8,14},{9,15},{10,... | collective-permute-start | bytes 196616 | tf_op jit(solution)/shard_map/ppermute | solution.py:24
  80.6 4.1 %collective-permute-done.19 = bf16[16,2048]{1,0:T(8,128)(2,1)S(1)} collective-permute-done((bf16[16,2048]{1,0:T(8,128)(2,1)S(1)}, bf16[16,2048]{1,0:T(8,128)(2,1)S(1)}, u32[]{:S(2)}, u32[]{:S(2)}) %collective-permute-start.19) | collective-permute-done | bytes 65568 | tf_op jit(solution)/shard_map/ppermute | solution.py:24
  84.8 4.3 %collective-permute-start.21 = (bf16[16,2048]{1,0:T(8,128)(2,1)S(1)}, bf16[16,2048]{1,0:T(8,128)(2,1)S(1)}, u32[]{:S(2)}, u32[]{:S(2)}) collective-permute-start(bf16[16,2048]{1,0:T(8,128)(2,1)S(1)} %get-tuple-element.34), channel_id=1, source_target_pairs={{0,8},{8,16},{16,24},{1,9},{9,17},{17,25},{2,10},{10,18},{18,26},{... | collective-permute-start | bytes 196616 | tf_op jit(solution)/shard_map/ppermute | solution.py:17
  93.9 2.3 collective-permute-start.24
  101.2 11.1 %shard_map.75 = f32[128,2048]{1,0:T(8,128)} custom-call(bf16[128,2048]{1,0:T(8,128)(2,1)} %bitcast.334, bf16[2,2048,768]{2,1,0:T(8,128)(2,1)} %bitcast.305, bf16[2,2048,768]{2,1,0:T(8,128)(2,1)} %bitcast.312, bf16[2,768,2048]{2,1,0:T(8,128)(2,1)} %bitcast.319, f32[2,128,1]{2,1,0:T(8,128)} %copy.41.weight_ref), custom_call_target="tpu_custom_call" | custom-call | tf_op jit(solution)/shard_map/pallas_call | solution.py:66
  115.1 3.5 %collective-permute-start.27 = (bf16[16,2048]{1,0:T(8,128)(2,1)S(1)}, bf16[16,2048]{1,0:T(8,128)(2,1)S(1)}, u32[]{:S(2)}, u32[]{:S(2)}) collective-permute-start(bf16[16,2048]{1,0:T(8,128)(2,1)S(1)} %get-tuple-element.63), channel_id=1, source_target_pairs={{0,6},{1,7},{2,0},{3,1},{4,2},{5,3},{6,4},{7,5},{8,14},{9,15},{10,... | collective-permute-start | bytes 196616 | tf_op jit(solution)/shard_map/ppermute | solution.py:24
  121.1 4.1 %collective-permute-done.28 = bf16[16,2048]{1,0:T(8,128)(2,1)S(1)} collective-permute-done((bf16[16,2048]{1,0:T(8,128)(2,1)S(1)}, bf16[16,2048]{1,0:T(8,128)(2,1)S(1)}, u32[]{:S(2)}, u32[]{:S(2)}) %collective-permute-start.28) | collective-permute-done | bytes 65568 | tf_op jit(solution)/shard_map/ppermute | solution.py:24
  125.3 4.3 %collective-permute-start.30 = (bf16[16,2048]{1,0:T(8,128)(2,1)S(1)}, bf16[16,2048]{1,0:T(8,128)(2,1)S(1)}, u32[]{:S(2)}, u32[]{:S(2)}) collective-permute-start(bf16[16,2048]{1,0:T(8,128)(2,1)S(1)} %get-tuple-element.28), channel_id=1, source_target_pairs={{0,8},{8,16},{16,24},{1,9},{9,17},{17,25},{2,10},{10,18},{18,26},{... | collective-permute-start | bytes 196616 | tf_op jit(solution)/shard_map/ppermute | solution.py:17
  141.7 11.1 %shard_map.76 = f32[128,2048]{1,0:T(8,128)} custom-call(bf16[128,2048]{1,0:T(8,128)(2,1)} %bitcast.335, bf16[2,2048,768]{2,1,0:T(8,128)(2,1)} %bitcast.306, bf16[2,2048,768]{2,1,0:T(8,128)(2,1)} %bitcast.313, bf16[2,768,2048]{2,1,0:T(8,128)(2,1)} %bitcast.320, f32[2,128,1]{2,1,0:T(8,128)} %copy.42.weight_ref), custom_call_target="tpu_custom_call" | custom-call | tf_op jit(solution)/shard_map/pallas_call | solution.py:66
  155.5 3.5 %collective-permute-start.36 = (bf16[16,2048]{1,0:T(8,128)(2,1)S(1)}, bf16[16,2048]{1,0:T(8,128)(2,1)S(1)}, u32[]{:S(2)}, u32[]{:S(2)}) collective-permute-start(bf16[16,2048]{1,0:T(8,128)(2,1)S(1)} %get-tuple-element.58), channel_id=1, source_target_pairs={{0,6},{1,7},{2,0},{3,1},{4,2},{5,3},{6,4},{7,5},{8,14},{9,15},{10,... | collective-permute-start | bytes 196616 | tf_op jit(solution)/shard_map/ppermute | solution.py:24
  161.5 4.1 %collective-permute-done.37 = bf16[16,2048]{1,0:T(8,128)(2,1)S(1)} collective-permute-done((bf16[16,2048]{1,0:T(8,128)(2,1)S(1)}, bf16[16,2048]{1,0:T(8,128)(2,1)S(1)}, u32[]{:S(2)}, u32[]{:S(2)}) %collective-permute-start.37) | collective-permute-done | bytes 65568 | tf_op jit(solution)/shard_map/ppermute | solution.py:24
  165.7 5.2 %collective-permute-start.39 = (bf16[16,2048]{1,0:T(8,128)(2,1)S(1)}, bf16[16,2048]{1,0:T(8,128)(2,1)S(1)}, u32[]{:S(2)}, u32[]{:S(2)}) collective-permute-start(bf16[16,2048]{1,0:T(8,128)(2,1)S(1)} %get-tuple-element.22), channel_id=1, source_target_pairs={{0,8},{8,16},{16,24},{1,9},{9,17},{17,25},{2,10},{10,18},{18,26},{... | collective-permute-start | bytes 196616 | tf_op jit(solution)/shard_map/ppermute | solution.py:17
  183.0 11.1 %shard_map.77 = f32[128,2048]{1,0:T(8,128)} custom-call(bf16[128,2048]{1,0:T(8,128)(2,1)} %bitcast.336, bf16[2,2048,768]{2,1,0:T(8,128)(2,1)} %bitcast.307, bf16[2,2048,768]{2,1,0:T(8,128)(2,1)} %bitcast.314, bf16[2,768,2048]{2,1,0:T(8,128)(2,1)} %bitcast.321, f32[2,128,1]{2,1,0:T(8,128)} %copy.43.weight_ref), custom_call_target="tpu_custom_call" | custom-call | tf_op jit(solution)/shard_map/pallas_call | solution.py:66
  196.9 3.5 %collective-permute-start.45 = (bf16[16,2048]{1,0:T(8,128)(2,1)S(1)}, bf16[16,2048]{1,0:T(8,128)(2,1)S(1)}, u32[]{:S(2)}, u32[]{:S(2)}) collective-permute-start(bf16[16,2048]{1,0:T(8,128)(2,1)S(1)} %get-tuple-element.53), channel_id=1, source_target_pairs={{0,6},{1,7},{2,0},{3,1},{4,2},{5,3},{6,4},{7,5},{8,14},{9,15},{10,... | collective-permute-start | bytes 196616 | tf_op jit(solution)/shard_map/ppermute | solution.py:24
  202.9 4.1 %collective-permute-done.46 = bf16[16,2048]{1,0:T(8,128)(2,1)S(1)} collective-permute-done((bf16[16,2048]{1,0:T(8,128)(2,1)S(1)}, bf16[16,2048]{1,0:T(8,128)(2,1)S(1)}, u32[]{:S(2)}, u32[]{:S(2)}) %collective-permute-start.46) | collective-permute-done | bytes 65568 | tf_op jit(solution)/shard_map/ppermute | solution.py:24
  207.1 5.2 %collective-permute-start.48 = (bf16[16,2048]{1,0:T(8,128)(2,1)S(1)}, bf16[16,2048]{1,0:T(8,128)(2,1)S(1)}, u32[]{:S(2)}, u32[]{:S(2)}) collective-permute-start(bf16[16,2048]{1,0:T(8,128)(2,1)S(1)} %get-tuple-element.16), channel_id=1, source_target_pairs={{0,8},{8,16},{16,24},{1,9},{9,17},{17,25},{2,10},{10,18},{18,26},{... | collective-permute-start | bytes 196616 | tf_op jit(solution)/shard_map/ppermute | solution.py:17
  217.0 2.3 collective-permute-start.51
  224.4 11.1 %shard_map.78 = f32[128,2048]{1,0:T(8,128)} custom-call(bf16[128,2048]{1,0:T(8,128)(2,1)} %bitcast.337, bf16[2,2048,768]{2,1,0:T(8,128)(2,1)} %bitcast.308, bf16[2,2048,768]{2,1,0:T(8,128)(2,1)} %bitcast.315, bf16[2,768,2048]{2,1,0:T(8,128)(2,1)} %bitcast.322, f32[2,128,1]{2,1,0:T(8,128)} %copy.44.weight_ref), custom_call_target="tpu_custom_call" | custom-call | tf_op jit(solution)/shard_map/pallas_call | solution.py:66
  238.2 3.5 %collective-permute-start.54 = (bf16[16,2048]{1,0:T(8,128)(2,1)S(1)}, bf16[16,2048]{1,0:T(8,128)(2,1)S(1)}, u32[]{:S(2)}, u32[]{:S(2)}) collective-permute-start(bf16[16,2048]{1,0:T(8,128)(2,1)S(1)} %get-tuple-element.48), channel_id=1, source_target_pairs={{0,6},{1,7},{2,0},{3,1},{4,2},{5,3},{6,4},{7,5},{8,14},{9,15},{10,... | collective-permute-start | bytes 196616 | tf_op jit(solution)/shard_map/ppermute | solution.py:24
  244.2 4.1 %collective-permute-done.55 = bf16[16,2048]{1,0:T(8,128)(2,1)S(1)} collective-permute-done((bf16[16,2048]{1,0:T(8,128)(2,1)S(1)}, bf16[16,2048]{1,0:T(8,128)(2,1)S(1)}, u32[]{:S(2)}, u32[]{:S(2)}) %collective-permute-start.55) | collective-permute-done | bytes 65568 | tf_op jit(solution)/shard_map/ppermute | solution.py:24
  248.4 5.2 %collective-permute-start.57 = (bf16[16,2048]{1,0:T(8,128)(2,1)S(1)}, bf16[16,2048]{1,0:T(8,128)(2,1)S(1)}, u32[]{:S(2)}, u32[]{:S(2)}) collective-permute-start(bf16[16,2048]{1,0:T(8,128)(2,1)S(1)} %get-tuple-element.10), channel_id=1, source_target_pairs={{0,8},{8,16},{16,24},{1,9},{9,17},{17,25},{2,10},{10,18},{18,26},{... | collective-permute-start | bytes 196616 | tf_op jit(solution)/shard_map/ppermute | solution.py:17
  265.7 11.1 %shard_map.79 = f32[128,2048]{1,0:T(8,128)} custom-call(bf16[128,2048]{1,0:T(8,128)(2,1)} %bitcast.338, bf16[2,2048,768]{2,1,0:T(8,128)(2,1)} %bitcast.309, bf16[2,2048,768]{2,1,0:T(8,128)(2,1)} %bitcast.316, bf16[2,768,2048]{2,1,0:T(8,128)(2,1)} %bitcast.323, f32[2,128,1]{2,1,0:T(8,128)} %copy.45.weight_ref), custom_call_target="tpu_custom_call" | custom-call | tf_op jit(solution)/shard_map/pallas_call | solution.py:66
  279.6 3.5 %collective-permute-start.63 = (bf16[16,2048]{1,0:T(8,128)(2,1)S(1)}, bf16[16,2048]{1,0:T(8,128)(2,1)S(1)}, u32[]{:S(2)}, u32[]{:S(2)}) collective-permute-start(bf16[16,2048]{1,0:T(8,128)(2,1)S(1)} %get-tuple-element.43), channel_id=1, source_target_pairs={{0,6},{1,7},{2,0},{3,1},{4,2},{5,3},{6,4},{7,5},{8,14},{9,15},{10,... | collective-permute-start | bytes 196616 | tf_op jit(solution)/shard_map/ppermute | solution.py:24
  285.6 4.1 %collective-permute-done.64 = bf16[16,2048]{1,0:T(8,128)(2,1)S(1)} collective-permute-done((bf16[16,2048]{1,0:T(8,128)(2,1)S(1)}, bf16[16,2048]{1,0:T(8,128)(2,1)S(1)}, u32[]{:S(2)}, u32[]{:S(2)}) %collective-permute-start.64) | collective-permute-done | bytes 65568 | tf_op jit(solution)/shard_map/ppermute | solution.py:24
  (207 shorter events, 120.4 us)
Async XLA Ops:
  1.9 11.6 %collective-permute-start = (bf16[16,2048]{1,0:T(8,128)(2,1)S(1)}, bf16[16,2048]{1,0:T(8,128)(2,1)S(1)}, u32[]{:S(2)}, u32[]{:S(2)}) collective-permute-start(bf16[16,2048]{1,0:T(8,128)(2,1)S(1)} %fusion.3), channel_id=1, source_target_pairs={{0,2},{1,3},{2,4},{3,5},{4,6},{5,7},{6,0},{7,1},{8,10},{9,11},{10,... | collective-permute-start | bytes 196616 | tf_op jit(solution)/shard_map/ppermute | solution.py:24
  5.0 11.4 %collective-permute-start.1 = (bf16[16,2048]{1,0:T(8,128)(2,1)S(1)}, bf16[16,2048]{1,0:T(8,128)(2,1)S(1)}, u32[]{:S(2)}, u32[]{:S(2)}) collective-permute-start(bf16[16,2048]{1,0:T(8,128)(2,1)S(1)} %fusion.3), channel_id=1, source_target_pairs={{0,4},{1,5},{2,6},{3,7},{4,0},{5,1},{6,2},{7,3},{8,12},{9,13},{10,... | collective-permute-start | bytes 196616 | tf_op jit(solution)/shard_map/ppermute | solution.py:24
  7.6 8.8 %collective-permute-start.2 = (bf16[16,2048]{1,0:T(8,128)(2,1)S(1)}, bf16[16,2048]{1,0:T(8,128)(2,1)S(1)}, u32[]{:S(2)}, u32[]{:S(2)}) collective-permute-start(bf16[16,2048]{1,0:T(8,128)(2,1)S(1)} %fusion.3), channel_id=1, source_target_pairs={{0,6},{1,7},{2,0},{3,1},{4,2},{5,3},{6,4},{7,5},{8,14},{9,15},{10,... | collective-permute-start | bytes 196616 | tf_op jit(solution)/shard_map/ppermute | solution.py:24
  37.6 7.5 %collective-permute-start.11 = (bf16[16,2048]{1,0:T(8,128)(2,1)S(1)}, bf16[16,2048]{1,0:T(8,128)(2,1)S(1)}, u32[]{:S(2)}, u32[]{:S(2)}) collective-permute-start(bf16[16,2048]{1,0:T(8,128)(2,1)S(1)} %get-tuple-element.74), channel_id=1, source_target_pairs={{0,2},{1,3},{2,4},{3,5},{4,6},{5,7},{6,0},{7,1},{8,10},{9,11},{10,... | collective-permute-start | bytes 196616 | tf_op jit(solution)/shard_map/ppermute | solution.py:24
  50.8 6.3 %collective-permute-start.13 = (bf16[16,2048]{1,0:T(8,128)(2,1)S(1)}, bf16[16,2048]{1,0:T(8,128)(2,1)S(1)}, u32[]{:S(2)}, u32[]{:S(2)}) collective-permute-start(bf16[16,2048]{1,0:T(8,128)(2,1)S(1)} %fusion.7), channel_id=1, source_target_pairs={{0,2},{1,3},{2,4},{3,5},{4,6},{5,7},{6,0},{7,1},{8,10},{9,11},{10,... | collective-permute-start | bytes 196616 | tf_op jit(solution)/shard_map/ppermute | solution.py:24
  52.1 6.6 %collective-permute-start.14 = (bf16[16,2048]{1,0:T(8,128)(2,1)S(1)}, bf16[16,2048]{1,0:T(8,128)(2,1)S(1)}, u32[]{:S(2)}, u32[]{:S(2)}) collective-permute-start(bf16[16,2048]{1,0:T(8,128)(2,1)S(1)} %fusion.7), channel_id=1, source_target_pairs={{0,4},{1,5},{2,6},{3,7},{4,0},{5,1},{6,2},{7,3},{8,12},{9,13},{10,... | collective-permute-start | bytes 196616 | tf_op jit(solution)/shard_map/ppermute | solution.py:24
  78.1 6.6 %collective-permute-start.19 = (bf16[16,2048]{1,0:T(8,128)(2,1)S(1)}, bf16[16,2048]{1,0:T(8,128)(2,1)S(1)}, u32[]{:S(2)}, u32[]{:S(2)}) collective-permute-start(bf16[16,2048]{1,0:T(8,128)(2,1)S(1)} %get-tuple-element.70), channel_id=1, source_target_pairs={{0,4},{1,5},{2,6},{3,7},{4,0},{5,1},{6,2},{7,3},{8,12},{9,13},{10,... | collective-permute-start | bytes 196616 | tf_op jit(solution)/shard_map/ppermute | solution.py:24
  78.1 6.6 %collective-permute-start.20 = (bf16[16,2048]{1,0:T(8,128)(2,1)S(1)}, bf16[16,2048]{1,0:T(8,128)(2,1)S(1)}, u32[]{:S(2)}, u32[]{:S(2)}) collective-permute-start(bf16[16,2048]{1,0:T(8,128)(2,1)S(1)} %get-tuple-element.69), channel_id=1, source_target_pairs={{0,2},{1,3},{2,4},{3,5},{4,6},{5,7},{6,0},{7,1},{8,10},{9,11},{10,... | collective-permute-start | bytes 196616 | tf_op jit(solution)/shard_map/ppermute | solution.py:24
  91.2 6.2 %collective-permute-start.22 = (bf16[16,2048]{1,0:T(8,128)(2,1)S(1)}, bf16[16,2048]{1,0:T(8,128)(2,1)S(1)}, u32[]{:S(2)}, u32[]{:S(2)}) collective-permute-start(bf16[16,2048]{1,0:T(8,128)(2,1)S(1)} %fusion.11), channel_id=1, source_target_pairs={{0,2},{1,3},{2,4},{3,5},{4,6},{5,7},{6,0},{7,1},{8,10},{9,11},{10,... | collective-permute-start | bytes 196616 | tf_op jit(solution)/shard_map/ppermute | solution.py:24
  91.6 7.1 %collective-permute-start.23 = (bf16[16,2048]{1,0:T(8,128)(2,1)S(1)}, bf16[16,2048]{1,0:T(8,128)(2,1)S(1)}, u32[]{:S(2)}, u32[]{:S(2)}) collective-permute-start(bf16[16,2048]{1,0:T(8,128)(2,1)S(1)} %fusion.11), channel_id=1, source_target_pairs={{0,4},{1,5},{2,6},{3,7},{4,0},{5,1},{6,2},{7,3},{8,12},{9,13},{10,... | collective-permute-start | bytes 196616 | tf_op jit(solution)/shard_map/ppermute | solution.py:24
  118.6 6.6 %collective-permute-start.28 = (bf16[16,2048]{1,0:T(8,128)(2,1)S(1)}, bf16[16,2048]{1,0:T(8,128)(2,1)S(1)}, u32[]{:S(2)}, u32[]{:S(2)}) collective-permute-start(bf16[16,2048]{1,0:T(8,128)(2,1)S(1)} %get-tuple-element.65), channel_id=1, source_target_pairs={{0,4},{1,5},{2,6},{3,7},{4,0},{5,1},{6,2},{7,3},{8,12},{9,13},{10,... | collective-permute-start | bytes 196616 | tf_op jit(solution)/shard_map/ppermute | solution.py:24
  118.6 6.6 %collective-permute-start.29 = (bf16[16,2048]{1,0:T(8,128)(2,1)S(1)}, bf16[16,2048]{1,0:T(8,128)(2,1)S(1)}, u32[]{:S(2)}, u32[]{:S(2)}) collective-permute-start(bf16[16,2048]{1,0:T(8,128)(2,1)S(1)} %get-tuple-element.64), channel_id=1, source_target_pairs={{0,2},{1,3},{2,4},{3,5},{4,6},{5,7},{6,0},{7,1},{8,10},{9,11},{10,... | collective-permute-start | bytes 196616 | tf_op jit(solution)/shard_map/ppermute | solution.py:24
  125.3 6.2 %collective-permute-start.30 = (bf16[16,2048]{1,0:T(8,128)(2,1)S(1)}, bf16[16,2048]{1,0:T(8,128)(2,1)S(1)}, u32[]{:S(2)}, u32[]{:S(2)}) collective-permute-start(bf16[16,2048]{1,0:T(8,128)(2,1)S(1)} %get-tuple-element.28), channel_id=1, source_target_pairs={{0,8},{8,16},{16,24},{1,9},{9,17},{17,25},{2,10},{10,18},{18,26},{... | collective-permute-start | bytes 196616 | tf_op jit(solution)/shard_map/ppermute | solution.py:17
  131.7 6.2 %collective-permute-start.31 = (bf16[16,2048]{1,0:T(8,128)(2,1)S(1)}, bf16[16,2048]{1,0:T(8,128)(2,1)S(1)}, u32[]{:S(2)}, u32[]{:S(2)}) collective-permute-start(bf16[16,2048]{1,0:T(8,128)(2,1)S(1)} %fusion.15), channel_id=1, source_target_pairs={{0,2},{1,3},{2,4},{3,5},{4,6},{5,7},{6,0},{7,1},{8,10},{9,11},{10,... | collective-permute-start | bytes 196616 | tf_op jit(solution)/shard_map/ppermute | solution.py:24
  132.1 7.1 %collective-permute-start.32 = (bf16[16,2048]{1,0:T(8,128)(2,1)S(1)}, bf16[16,2048]{1,0:T(8,128)(2,1)S(1)}, u32[]{:S(2)}, u32[]{:S(2)}) collective-permute-start(bf16[16,2048]{1,0:T(8,128)(2,1)S(1)} %fusion.15), channel_id=1, source_target_pairs={{0,4},{1,5},{2,6},{3,7},{4,0},{5,1},{6,2},{7,3},{8,12},{9,13},{10,... | collective-permute-start | bytes 196616 | tf_op jit(solution)/shard_map/ppermute | solution.py:24
  159.0 6.6 %collective-permute-start.37 = (bf16[16,2048]{1,0:T(8,128)(2,1)S(1)}, bf16[16,2048]{1,0:T(8,128)(2,1)S(1)}, u32[]{:S(2)}, u32[]{:S(2)}) collective-permute-start(bf16[16,2048]{1,0:T(8,128)(2,1)S(1)} %get-tuple-element.60), channel_id=1, source_target_pairs={{0,4},{1,5},{2,6},{3,7},{4,0},{5,1},{6,2},{7,3},{8,12},{9,13},{10,... | collective-permute-start | bytes 196616 | tf_op jit(solution)/shard_map/ppermute | solution.py:24
  159.0 6.6 %collective-permute-start.38 = (bf16[16,2048]{1,0:T(8,128)(2,1)S(1)}, bf16[16,2048]{1,0:T(8,128)(2,1)S(1)}, u32[]{:S(2)}, u32[]{:S(2)}) collective-permute-start(bf16[16,2048]{1,0:T(8,128)(2,1)S(1)} %get-tuple-element.59), channel_id=1, source_target_pairs={{0,2},{1,3},{2,4},{3,5},{4,6},{5,7},{6,0},{7,1},{8,10},{9,11},{10,... | collective-permute-start | bytes 196616 | tf_op jit(solution)/shard_map/ppermute | solution.py:24
  165.7 7.1 %collective-permute-start.39 = (bf16[16,2048]{1,0:T(8,128)(2,1)S(1)}, bf16[16,2048]{1,0:T(8,128)(2,1)S(1)}, u32[]{:S(2)}, u32[]{:S(2)}) collective-permute-start(bf16[16,2048]{1,0:T(8,128)(2,1)S(1)} %get-tuple-element.22), channel_id=1, source_target_pairs={{0,8},{8,16},{16,24},{1,9},{9,17},{17,25},{2,10},{10,18},{18,26},{... | collective-permute-start | bytes 196616 | tf_op jit(solution)/shard_map/ppermute | solution.py:17
  173.0 6.2 %collective-permute-start.40 = (bf16[16,2048]{1,0:T(8,128)(2,1)S(1)}, bf16[16,2048]{1,0:T(8,128)(2,1)S(1)}, u32[]{:S(2)}, u32[]{:S(2)}) collective-permute-start(bf16[16,2048]{1,0:T(8,128)(2,1)S(1)} %fusion.19), channel_id=1, source_target_pairs={{0,2},{1,3},{2,4},{3,5},{4,6},{5,7},{6,0},{7,1},{8,10},{9,11},{10,... | collective-permute-start | bytes 196616 | tf_op jit(solution)/shard_map/ppermute | solution.py:24
  173.4 7.1 %collective-permute-start.41 = (bf16[16,2048]{1,0:T(8,128)(2,1)S(1)}, bf16[16,2048]{1,0:T(8,128)(2,1)S(1)}, u32[]{:S(2)}, u32[]{:S(2)}) collective-permute-start(bf16[16,2048]{1,0:T(8,128)(2,1)S(1)} %fusion.19), channel_id=1, source_target_pairs={{0,4},{1,5},{2,6},{3,7},{4,0},{5,1},{6,2},{7,3},{8,12},{9,13},{10,... | collective-permute-start | bytes 196616 | tf_op jit(solution)/shard_map/ppermute | solution.py:24
  200.4 6.6 %collective-permute-start.46 = (bf16[16,2048]{1,0:T(8,128)(2,1)S(1)}, bf16[16,2048]{1,0:T(8,128)(2,1)S(1)}, u32[]{:S(2)}, u32[]{:S(2)}) collective-permute-start(bf16[16,2048]{1,0:T(8,128)(2,1)S(1)} %get-tuple-element.55), channel_id=1, source_target_pairs={{0,4},{1,5},{2,6},{3,7},{4,0},{5,1},{6,2},{7,3},{8,12},{9,13},{10,... | collective-permute-start | bytes 196616 | tf_op jit(solution)/shard_map/ppermute | solution.py:24
  200.4 6.6 %collective-permute-start.47 = (bf16[16,2048]{1,0:T(8,128)(2,1)S(1)}, bf16[16,2048]{1,0:T(8,128)(2,1)S(1)}, u32[]{:S(2)}, u32[]{:S(2)}) collective-permute-start(bf16[16,2048]{1,0:T(8,128)(2,1)S(1)} %get-tuple-element.54), channel_id=1, source_target_pairs={{0,2},{1,3},{2,4},{3,5},{4,6},{5,7},{6,0},{7,1},{8,10},{9,11},{10,... | collective-permute-start | bytes 196616 | tf_op jit(solution)/shard_map/ppermute | solution.py:24
  207.1 7.1 %collective-permute-start.48 = (bf16[16,2048]{1,0:T(8,128)(2,1)S(1)}, bf16[16,2048]{1,0:T(8,128)(2,1)S(1)}, u32[]{:S(2)}, u32[]{:S(2)}) collective-permute-start(bf16[16,2048]{1,0:T(8,128)(2,1)S(1)} %get-tuple-element.16), channel_id=1, source_target_pairs={{0,8},{8,16},{16,24},{1,9},{9,17},{17,25},{2,10},{10,18},{18,26},{... | collective-permute-start | bytes 196616 | tf_op jit(solution)/shard_map/ppermute | solution.py:17
  214.4 6.2 %collective-permute-start.49 = (bf16[16,2048]{1,0:T(8,128)(2,1)S(1)}, bf16[16,2048]{1,0:T(8,128)(2,1)S(1)}, u32[]{:S(2)}, u32[]{:S(2)}) collective-permute-start(bf16[16,2048]{1,0:T(8,128)(2,1)S(1)} %fusion.23), channel_id=1, source_target_pairs={{0,2},{1,3},{2,4},{3,5},{4,6},{5,7},{6,0},{7,1},{8,10},{9,11},{10,... | collective-permute-start | bytes 196616 | tf_op jit(solution)/shard_map/ppermute | solution.py:24
  214.8 7.1 %collective-permute-start.50 = (bf16[16,2048]{1,0:T(8,128)(2,1)S(1)}, bf16[16,2048]{1,0:T(8,128)(2,1)S(1)}, u32[]{:S(2)}, u32[]{:S(2)}) collective-permute-start(bf16[16,2048]{1,0:T(8,128)(2,1)S(1)} %fusion.23), channel_id=1, source_target_pairs={{0,4},{1,5},{2,6},{3,7},{4,0},{5,1},{6,2},{7,3},{8,12},{9,13},{10,... | collective-permute-start | bytes 196616 | tf_op jit(solution)/shard_map/ppermute | solution.py:24
  241.7 6.6 %collective-permute-start.55 = (bf16[16,2048]{1,0:T(8,128)(2,1)S(1)}, bf16[16,2048]{1,0:T(8,128)(2,1)S(1)}, u32[]{:S(2)}, u32[]{:S(2)}) collective-permute-start(bf16[16,2048]{1,0:T(8,128)(2,1)S(1)} %get-tuple-element.50), channel_id=1, source_target_pairs={{0,4},{1,5},{2,6},{3,7},{4,0},{5,1},{6,2},{7,3},{8,12},{9,13},{10,... | collective-permute-start | bytes 196616 | tf_op jit(solution)/shard_map/ppermute | solution.py:24
  241.7 6.6 %collective-permute-start.56 = (bf16[16,2048]{1,0:T(8,128)(2,1)S(1)}, bf16[16,2048]{1,0:T(8,128)(2,1)S(1)}, u32[]{:S(2)}, u32[]{:S(2)}) collective-permute-start(bf16[16,2048]{1,0:T(8,128)(2,1)S(1)} %get-tuple-element.49), channel_id=1, source_target_pairs={{0,2},{1,3},{2,4},{3,5},{4,6},{5,7},{6,0},{7,1},{8,10},{9,11},{10,... | collective-permute-start | bytes 196616 | tf_op jit(solution)/shard_map/ppermute | solution.py:24
  248.4 7.1 %collective-permute-start.57 = (bf16[16,2048]{1,0:T(8,128)(2,1)S(1)}, bf16[16,2048]{1,0:T(8,128)(2,1)S(1)}, u32[]{:S(2)}, u32[]{:S(2)}) collective-permute-start(bf16[16,2048]{1,0:T(8,128)(2,1)S(1)} %get-tuple-element.10), channel_id=1, source_target_pairs={{0,8},{8,16},{16,24},{1,9},{9,17},{17,25},{2,10},{10,18},{18,26},{... | collective-permute-start | bytes 196616 | tf_op jit(solution)/shard_map/ppermute | solution.py:17
  255.7 6.2 %collective-permute-start.58 = (bf16[16,2048]{1,0:T(8,128)(2,1)S(1)}, bf16[16,2048]{1,0:T(8,128)(2,1)S(1)}, u32[]{:S(2)}, u32[]{:S(2)}) collective-permute-start(bf16[16,2048]{1,0:T(8,128)(2,1)S(1)} %fusion.27), channel_id=1, source_target_pairs={{0,2},{1,3},{2,4},{3,5},{4,6},{5,7},{6,0},{7,1},{8,10},{9,11},{10,... | collective-permute-start | bytes 196616 | tf_op jit(solution)/shard_map/ppermute | solution.py:24
  256.1 7.1 %collective-permute-start.59 = (bf16[16,2048]{1,0:T(8,128)(2,1)S(1)}, bf16[16,2048]{1,0:T(8,128)(2,1)S(1)}, u32[]{:S(2)}, u32[]{:S(2)}) collective-permute-start(bf16[16,2048]{1,0:T(8,128)(2,1)S(1)} %fusion.27), channel_id=1, source_target_pairs={{0,4},{1,5},{2,6},{3,7},{4,0},{5,1},{6,2},{7,3},{8,12},{9,13},{10,... | collective-permute-start | bytes 196616 | tf_op jit(solution)/shard_map/ppermute | solution.py:24
  283.1 6.6 %collective-permute-start.64 = (bf16[16,2048]{1,0:T(8,128)(2,1)S(1)}, bf16[16,2048]{1,0:T(8,128)(2,1)S(1)}, u32[]{:S(2)}, u32[]{:S(2)}) collective-permute-start(bf16[16,2048]{1,0:T(8,128)(2,1)S(1)} %get-tuple-element.45), channel_id=1, source_target_pairs={{0,4},{1,5},{2,6},{3,7},{4,0},{5,1},{6,2},{7,3},{8,12},{9,13},{10,... | collective-permute-start | bytes 196616 | tf_op jit(solution)/shard_map/ppermute | solution.py:24
  283.1 6.6 %collective-permute-start.65 = (bf16[16,2048]{1,0:T(8,128)(2,1)S(1)}, bf16[16,2048]{1,0:T(8,128)(2,1)S(1)}, u32[]{:S(2)}, u32[]{:S(2)}) collective-permute-start(bf16[16,2048]{1,0:T(8,128)(2,1)S(1)} %get-tuple-element.44), channel_id=1, source_target_pairs={{0,2},{1,3},{2,4},{3,5},{4,6},{5,7},{6,0},{7,1},{8,10},{9,11},{10,... | collective-permute-start | bytes 196616 | tf_op jit(solution)/shard_map/ppermute | solution.py:24
  (36 other events, 181.2 us)

commit v8 on v7

--- a/solution.py
+++ b/solution.py
@@ -59,7 +59,7 @@
     out_ref[...] += jnp.dot(inner, down_ref[...], preferred_element_type=jnp.float32)
 
 
-def experts_mixed(rows, w_gate, w_up, w_down, weight, chunk=256):
+def experts_mixed(rows, w_gate, w_up, w_down, weight, chunk=768):
     count, width = rows.shape
     local, _, hidden = w_gate.shape
     chunks = hidden // chunk

time: 294 us -> 290 us (0.986)
  Pallas kernels: 77.4 us -> 74.1 us
    pallas_call x7, Pallas kernels: 77.4 us -> 74.1 us  [experts_mixed(): pl.pallas_call(expert_kernel, grid=(local, chunks), in_specs=[pl.BlockSpe...]
  transfers between devices with their start and end apart: 66 -> 66, of which waited for: 49 -> 50; matrix products, arithmetic and copies ran while one was open for 6% -> 6% of each run, Pallas kernels for 0% -> 0%
where the time goes in v8:
time: 290 us; the launch traced here: 287 us
  starting transfers between devices  99.6 us (34%)
  waiting for transfers between devices  75.9 us (26%)
  Pallas kernels  74.1 us (26%)
  local copies, waits for them, and re-layouts  22.7 us (8%)
  other arithmetic  14.4 us (5%)
    pallas_call x7, Pallas kernels, experts_mixed(): pl.pallas_call(expert_kernel, grid=(local, chunks), in_specs=[pl.BlockSpe...  74.1 us
    ppermute x45, starting transfers between devices, chip_shift(): return lax.ppermute(array, axis, pairs)  70.1 us
    ppermute x45, waiting for transfers between devices, chip_shift(): return lax.ppermute(array, axis, pairs)  56.7 us
    ppermute x6, starting transfers between devices, shifted(): return lax.ppermute(array, axis, pairs)  27.5 us
    ppermute x6, waiting for transfers between devices, shifted(): return lax.ppermute(array, axis, pairs)  11.3 us
    ppermute x15, waiting for transfers between devices, core_swap(): return lax.ppermute(array, axis, [(i, i ^ 1) for i in range(count)])  7.87 us
    slice x7, local copies, waits for them, and re-layouts, scatter_blocks(): chip_sum = partial[0] + swapped.astype(jnp.float32)  7.53 us
    slice x7, local copies, waits for them, and re-layouts, scatter_blocks(): swapped = core_swap(partial[1].astype(jnp.bfloat16), axis)  7.48 us
  transfers between devices with their start and end apart: 66, of which 50 were waited for; matrix products, arithmetic and copies ran while one was open for 6% of the time, Pallas kernels for 0%

profile of v8, /device:TPU:0, one launch (start us, length us, event | category | flops | bytes accessed | tf_op | source)
XLA Modules:
  0.0 287.2 jit_solution(14296318198231946508)
XLA Ops:
  1.9 3.1 %collective-permute-start = (bf16[16,2048]{1,0:T(8,128)(2,1)S(1)}, bf16[16,2048]{1,0:T(8,128)(2,1)S(1)}, u32[]{:S(2)}, u32[]{:S(2)}) collective-permute-start(bf16[16,2048]{1,0:T(8,128)(2,1)S(1)} %fusion.3), channel_id=1, source_target_pairs={{0,2},{1,3},{2,4},{3,5},{4,6},{5,7},{6,0},{7,1},{8,10},{9,11},{10,... | collective-permute-start | bytes 196616 | tf_op jit(solution)/shard_map/ppermute | solution.py:24
  5.0 2.6 collective-permute-start.1
  13.5 2.9 collective-permute-start.6
  22.5 10.6 %shard_map.73 = f32[128,2048]{1,0:T(8,128)} custom-call(bf16[128,2048]{1,0:T(8,128)(2,1)} %bitcast.332, bf16[2,2048,768]{2,1,0:T(8,128)(2,1)} %bitcast.303, bf16[2,2048,768]{2,1,0:T(8,128)(2,1)} %bitcast.310, bf16[2,768,2048]{2,1,0:T(8,128)(2,1)} %bitcast.317, f32[2,128,1]{2,1,0:T(8,128)} %copy.39.weight_ref), custom_call_target="tpu_custom_call" | custom-call | tf_op jit(solution)/shard_map/pallas_call | solution.py:66
  37.2 2.6 collective-permute-start.11
  41.1 3.5 %collective-permute-done.11 = bf16[16,2048]{1,0:T(8,128)(2,1)S(1)} collective-permute-done((bf16[16,2048]{1,0:T(8,128)(2,1)S(1)}, bf16[16,2048]{1,0:T(8,128)(2,1)S(1)}, u32[]{:S(2)}, u32[]{:S(2)}) %collective-permute-start.11) | collective-permute-done | bytes 65568 | tf_op jit(solution)/shard_map/ppermute | solution.py:24
  44.8 3.4 %collective-permute-start.12 = (bf16[16,2048]{1,0:T(8,128)(2,1)S(1)}, bf16[16,2048]{1,0:T(8,128)(2,1)S(1)}, u32[]{:S(2)}, u32[]{:S(2)}) collective-permute-start(bf16[16,2048]{1,0:T(8,128)(2,1)S(1)} %get-tuple-element.40), channel_id=1, source_target_pairs={{0,8},{8,16},{16,24},{1,9},{9,17},{17,25},{2,10},{10,18},{18,26},{... | collective-permute-start | bytes 196616 | tf_op jit(solution)/shard_map/ppermute | solution.py:17
  60.8 10.6 %shard_map.74 = f32[128,2048]{1,0:T(8,128)} custom-call(bf16[128,2048]{1,0:T(8,128)(2,1)} %bitcast.333, bf16[2,2048,768]{2,1,0:T(8,128)(2,1)} %bitcast.304, bf16[2,2048,768]{2,1,0:T(8,128)(2,1)} %bitcast.311, bf16[2,768,2048]{2,1,0:T(8,128)(2,1)} %bitcast.318, f32[2,128,1]{2,1,0:T(8,128)} %copy.40.weight_ref), custom_call_target="tpu_custom_call" | custom-call | tf_op jit(solution)/shard_map/pallas_call | solution.py:66
  74.1 3.1 %collective-permute-start.18 = (bf16[16,2048]{1,0:T(8,128)(2,1)S(1)}, bf16[16,2048]{1,0:T(8,128)(2,1)S(1)}, u32[]{:S(2)}, u32[]{:S(2)}) collective-permute-start(bf16[16,2048]{1,0:T(8,128)(2,1)S(1)} %get-tuple-element.68), channel_id=1, source_target_pairs={{0,6},{1,7},{2,0},{3,1},{4,2},{5,3},{6,4},{7,5},{8,14},{9,15},{10,... | collective-permute-start | bytes 196616 | tf_op jit(solution)/shard_map/ppermute | solution.py:24
  79.7 4.1 %collective-permute-done.19 = bf16[16,2048]{1,0:T(8,128)(2,1)S(1)} collective-permute-done((bf16[16,2048]{1,0:T(8,128)(2,1)S(1)}, bf16[16,2048]{1,0:T(8,128)(2,1)S(1)}, u32[]{:S(2)}, u32[]{:S(2)}) %collective-permute-start.19) | collective-permute-done | bytes 65568 | tf_op jit(solution)/shard_map/ppermute | solution.py:24
  83.9 4.3 %collective-permute-start.21 = (bf16[16,2048]{1,0:T(8,128)(2,1)S(1)}, bf16[16,2048]{1,0:T(8,128)(2,1)S(1)}, u32[]{:S(2)}, u32[]{:S(2)}) collective-permute-start(bf16[16,2048]{1,0:T(8,128)(2,1)S(1)} %get-tuple-element.34), channel_id=1, source_target_pairs={{0,8},{8,16},{16,24},{1,9},{9,17},{17,25},{2,10},{10,18},{18,26},{... | collective-permute-start | bytes 196616 | tf_op jit(solution)/shard_map/ppermute | solution.py:17
  92.9 2.3 collective-permute-start.24
  100.3 10.6 %shard_map.75 = f32[128,2048]{1,0:T(8,128)} custom-call(bf16[128,2048]{1,0:T(8,128)(2,1)} %bitcast.334, bf16[2,2048,768]{2,1,0:T(8,128)(2,1)} %bitcast.305, bf16[2,2048,768]{2,1,0:T(8,128)(2,1)} %bitcast.312, bf16[2,768,2048]{2,1,0:T(8,128)(2,1)} %bitcast.319, f32[2,128,1]{2,1,0:T(8,128)} %copy.41.weight_ref), custom_call_target="tpu_custom_call" | custom-call | tf_op jit(solution)/shard_map/pallas_call | solution.py:66
  113.6 3.5 %collective-permute-start.27 = (bf16[16,2048]{1,0:T(8,128)(2,1)S(1)}, bf16[16,2048]{1,0:T(8,128)(2,1)S(1)}, u32[]{:S(2)}, u32[]{:S(2)}) collective-permute-start(bf16[16,2048]{1,0:T(8,128)(2,1)S(1)} %get-tuple-element.63), channel_id=1, source_target_pairs={{0,6},{1,7},{2,0},{3,1},{4,2},{5,3},{6,4},{7,5},{8,14},{9,15},{10,... | collective-permute-start | bytes 196616 | tf_op jit(solution)/shard_map/ppermute | solution.py:24
  119.7 4.1 %collective-permute-done.28 = bf16[16,2048]{1,0:T(8,128)(2,1)S(1)} collective-permute-done((bf16[16,2048]{1,0:T(8,128)(2,1)S(1)}, bf16[16,2048]{1,0:T(8,128)(2,1)S(1)}, u32[]{:S(2)}, u32[]{:S(2)}) %collective-permute-start.28) | collective-permute-done | bytes 65568 | tf_op jit(solution)/shard_map/ppermute | solution.py:24
  123.8 4.3 %collective-permute-start.30 = (bf16[16,2048]{1,0:T(8,128)(2,1)S(1)}, bf16[16,2048]{1,0:T(8,128)(2,1)S(1)}, u32[]{:S(2)}, u32[]{:S(2)}) collective-permute-start(bf16[16,2048]{1,0:T(8,128)(2,1)S(1)} %get-tuple-element.28), channel_id=1, source_target_pairs={{0,8},{8,16},{16,24},{1,9},{9,17},{17,25},{2,10},{10,18},{18,26},{... | collective-permute-start | bytes 196616 | tf_op jit(solution)/shard_map/ppermute | solution.py:17
  132.9 2.3 collective-permute-start.33
  140.3 10.6 %shard_map.76 = f32[128,2048]{1,0:T(8,128)} custom-call(bf16[128,2048]{1,0:T(8,128)(2,1)} %bitcast.335, bf16[2,2048,768]{2,1,0:T(8,128)(2,1)} %bitcast.306, bf16[2,2048,768]{2,1,0:T(8,128)(2,1)} %bitcast.313, bf16[2,768,2048]{2,1,0:T(8,128)(2,1)} %bitcast.320, f32[2,128,1]{2,1,0:T(8,128)} %copy.42.weight_ref), custom_call_target="tpu_custom_call" | custom-call | tf_op jit(solution)/shard_map/pallas_call | solution.py:66
  153.6 3.7 %collective-permute-start.36 = (bf16[16,2048]{1,0:T(8,128)(2,1)S(1)}, bf16[16,2048]{1,0:T(8,128)(2,1)S(1)}, u32[]{:S(2)}, u32[]{:S(2)}) collective-permute-start(bf16[16,2048]{1,0:T(8,128)(2,1)S(1)} %get-tuple-element.58), channel_id=1, source_target_pairs={{0,6},{1,7},{2,0},{3,1},{4,2},{5,3},{6,4},{7,5},{8,14},{9,15},{10,... | collective-permute-start | bytes 196616 | tf_op jit(solution)/shard_map/ppermute | solution.py:24
  159.8 4.1 %collective-permute-done.37 = bf16[16,2048]{1,0:T(8,128)(2,1)S(1)} collective-permute-done((bf16[16,2048]{1,0:T(8,128)(2,1)S(1)}, bf16[16,2048]{1,0:T(8,128)(2,1)S(1)}, u32[]{:S(2)}, u32[]{:S(2)}) %collective-permute-start.37) | collective-permute-done | bytes 65568 | tf_op jit(solution)/shard_map/ppermute | solution.py:24
  164.0 5.2 %collective-permute-start.39 = (bf16[16,2048]{1,0:T(8,128)(2,1)S(1)}, bf16[16,2048]{1,0:T(8,128)(2,1)S(1)}, u32[]{:S(2)}, u32[]{:S(2)}) collective-permute-start(bf16[16,2048]{1,0:T(8,128)(2,1)S(1)} %get-tuple-element.22), channel_id=1, source_target_pairs={{0,8},{8,16},{16,24},{1,9},{9,17},{17,25},{2,10},{10,18},{18,26},{... | collective-permute-start | bytes 196616 | tf_op jit(solution)/shard_map/ppermute | solution.py:17
  181.3 10.6 %shard_map.77 = f32[128,2048]{1,0:T(8,128)} custom-call(bf16[128,2048]{1,0:T(8,128)(2,1)} %bitcast.336, bf16[2,2048,768]{2,1,0:T(8,128)(2,1)} %bitcast.307, bf16[2,2048,768]{2,1,0:T(8,128)(2,1)} %bitcast.314, bf16[2,768,2048]{2,1,0:T(8,128)(2,1)} %bitcast.321, f32[2,128,1]{2,1,0:T(8,128)} %copy.43.weight_ref), custom_call_target="tpu_custom_call" | custom-call | tf_op jit(solution)/shard_map/pallas_call | solution.py:66
  194.7 3.5 %collective-permute-start.45 = (bf16[16,2048]{1,0:T(8,128)(2,1)S(1)}, bf16[16,2048]{1,0:T(8,128)(2,1)S(1)}, u32[]{:S(2)}, u32[]{:S(2)}) collective-permute-start(bf16[16,2048]{1,0:T(8,128)(2,1)S(1)} %get-tuple-element.53), channel_id=1, source_target_pairs={{0,6},{1,7},{2,0},{3,1},{4,2},{5,3},{6,4},{7,5},{8,14},{9,15},{10,... | collective-permute-start | bytes 196616 | tf_op jit(solution)/shard_map/ppermute | solution.py:24
  200.7 4.1 %collective-permute-done.46 = bf16[16,2048]{1,0:T(8,128)(2,1)S(1)} collective-permute-done((bf16[16,2048]{1,0:T(8,128)(2,1)S(1)}, bf16[16,2048]{1,0:T(8,128)(2,1)S(1)}, u32[]{:S(2)}, u32[]{:S(2)}) %collective-permute-start.46) | collective-permute-done | bytes 65568 | tf_op jit(solution)/shard_map/ppermute | solution.py:24
  204.9 5.2 %collective-permute-start.48 = (bf16[16,2048]{1,0:T(8,128)(2,1)S(1)}, bf16[16,2048]{1,0:T(8,128)(2,1)S(1)}, u32[]{:S(2)}, u32[]{:S(2)}) collective-permute-start(bf16[16,2048]{1,0:T(8,128)(2,1)S(1)} %get-tuple-element.16), channel_id=1, source_target_pairs={{0,8},{8,16},{16,24},{1,9},{9,17},{17,25},{2,10},{10,18},{18,26},{... | collective-permute-start | bytes 196616 | tf_op jit(solution)/shard_map/ppermute | solution.py:17
  222.2 10.6 %shard_map.78 = f32[128,2048]{1,0:T(8,128)} custom-call(bf16[128,2048]{1,0:T(8,128)(2,1)} %bitcast.337, bf16[2,2048,768]{2,1,0:T(8,128)(2,1)} %bitcast.308, bf16[2,2048,768]{2,1,0:T(8,128)(2,1)} %bitcast.315, bf16[2,768,2048]{2,1,0:T(8,128)(2,1)} %bitcast.322, f32[2,128,1]{2,1,0:T(8,128)} %copy.44.weight_ref), custom_call_target="tpu_custom_call" | custom-call | tf_op jit(solution)/shard_map/pallas_call | solution.py:66
  235.5 3.5 %collective-permute-start.54 = (bf16[16,2048]{1,0:T(8,128)(2,1)S(1)}, bf16[16,2048]{1,0:T(8,128)(2,1)S(1)}, u32[]{:S(2)}, u32[]{:S(2)}) collective-permute-start(bf16[16,2048]{1,0:T(8,128)(2,1)S(1)} %get-tuple-element.48), channel_id=1, source_target_pairs={{0,6},{1,7},{2,0},{3,1},{4,2},{5,3},{6,4},{7,5},{8,14},{9,15},{10,... | collective-permute-start | bytes 196616 | tf_op jit(solution)/shard_map/ppermute | solution.py:24
  241.5 4.1 %collective-permute-done.55 = bf16[16,2048]{1,0:T(8,128)(2,1)S(1)} collective-permute-done((bf16[16,2048]{1,0:T(8,128)(2,1)S(1)}, bf16[16,2048]{1,0:T(8,128)(2,1)S(1)}, u32[]{:S(2)}, u32[]{:S(2)}) %collective-permute-start.55) | collective-permute-done | bytes 65568 | tf_op jit(solution)/shard_map/ppermute | solution.py:24
  245.7 5.2 %collective-permute-start.57 = (bf16[16,2048]{1,0:T(8,128)(2,1)S(1)}, bf16[16,2048]{1,0:T(8,128)(2,1)S(1)}, u32[]{:S(2)}, u32[]{:S(2)}) collective-permute-start(bf16[16,2048]{1,0:T(8,128)(2,1)S(1)} %get-tuple-element.10), channel_id=1, source_target_pairs={{0,8},{8,16},{16,24},{1,9},{9,17},{17,25},{2,10},{10,18},{18,26},{... | collective-permute-start | bytes 196616 | tf_op jit(solution)/shard_map/ppermute | solution.py:17
  263.1 10.6 %shard_map.79 = f32[128,2048]{1,0:T(8,128)} custom-call(bf16[128,2048]{1,0:T(8,128)(2,1)} %bitcast.338, bf16[2,2048,768]{2,1,0:T(8,128)(2,1)} %bitcast.309, bf16[2,2048,768]{2,1,0:T(8,128)(2,1)} %bitcast.316, bf16[2,768,2048]{2,1,0:T(8,128)(2,1)} %bitcast.323, f32[2,128,1]{2,1,0:T(8,128)} %copy.45.weight_ref), custom_call_target="tpu_custom_call" | custom-call | tf_op jit(solution)/shard_map/pallas_call | solution.py:66
  276.4 3.5 %collective-permute-start.63 = (bf16[16,2048]{1,0:T(8,128)(2,1)S(1)}, bf16[16,2048]{1,0:T(8,128)(2,1)S(1)}, u32[]{:S(2)}, u32[]{:S(2)}) collective-permute-start(bf16[16,2048]{1,0:T(8,128)(2,1)S(1)} %get-tuple-element.43), channel_id=1, source_target_pairs={{0,6},{1,7},{2,0},{3,1},{4,2},{5,3},{6,4},{7,5},{8,14},{9,15},{10,... | collective-permute-start | bytes 196616 | tf_op jit(solution)/shard_map/ppermute | solution.py:24
  282.4 4.1 %collective-permute-done.64 = bf16[16,2048]{1,0:T(8,128)(2,1)S(1)} collective-permute-done((bf16[16,2048]{1,0:T(8,128)(2,1)S(1)}, bf16[16,2048]{1,0:T(8,128)(2,1)S(1)}, u32[]{:S(2)}, u32[]{:S(2)}) %collective-permute-start.64) | collective-permute-done | bytes 65568 | tf_op jit(solution)/shard_map/ppermute | solution.py:24
  (207 shorter events, 120.5 us)
Async XLA Ops:
  1.9 11.6 %collective-permute-start = (bf16[16,2048]{1,0:T(8,128)(2,1)S(1)}, bf16[16,2048]{1,0:T(8,128)(2,1)S(1)}, u32[]{:S(2)}, u32[]{:S(2)}) collective-permute-start(bf16[16,2048]{1,0:T(8,128)(2,1)S(1)} %fusion.3), channel_id=1, source_target_pairs={{0,2},{1,3},{2,4},{3,5},{4,6},{5,7},{6,0},{7,1},{8,10},{9,11},{10,... | collective-permute-start | bytes 196616 | tf_op jit(solution)/shard_map/ppermute | solution.py:24
  5.0 11.4 %collective-permute-start.1 = (bf16[16,2048]{1,0:T(8,128)(2,1)S(1)}, bf16[16,2048]{1,0:T(8,128)(2,1)S(1)}, u32[]{:S(2)}, u32[]{:S(2)}) collective-permute-start(bf16[16,2048]{1,0:T(8,128)(2,1)S(1)} %fusion.3), channel_id=1, source_target_pairs={{0,4},{1,5},{2,6},{3,7},{4,0},{5,1},{6,2},{7,3},{8,12},{9,13},{10,... | collective-permute-start | bytes 196616 | tf_op jit(solution)/shard_map/ppermute | solution.py:24
  7.6 8.8 %collective-permute-start.2 = (bf16[16,2048]{1,0:T(8,128)(2,1)S(1)}, bf16[16,2048]{1,0:T(8,128)(2,1)S(1)}, u32[]{:S(2)}, u32[]{:S(2)}) collective-permute-start(bf16[16,2048]{1,0:T(8,128)(2,1)S(1)} %fusion.3), channel_id=1, source_target_pairs={{0,6},{1,7},{2,0},{3,1},{4,2},{5,3},{6,4},{7,5},{8,14},{9,15},{10,... | collective-permute-start | bytes 196616 | tf_op jit(solution)/shard_map/ppermute | solution.py:24
  37.2 7.4 %collective-permute-start.11 = (bf16[16,2048]{1,0:T(8,128)(2,1)S(1)}, bf16[16,2048]{1,0:T(8,128)(2,1)S(1)}, u32[]{:S(2)}, u32[]{:S(2)}) collective-permute-start(bf16[16,2048]{1,0:T(8,128)(2,1)S(1)} %get-tuple-element.74), channel_id=1, source_target_pairs={{0,2},{1,3},{2,4},{3,5},{4,6},{5,7},{6,0},{7,1},{8,10},{9,11},{10,... | collective-permute-start | bytes 196616 | tf_op jit(solution)/shard_map/ppermute | solution.py:24
  50.3 6.3 %collective-permute-start.13 = (bf16[16,2048]{1,0:T(8,128)(2,1)S(1)}, bf16[16,2048]{1,0:T(8,128)(2,1)S(1)}, u32[]{:S(2)}, u32[]{:S(2)}) collective-permute-start(bf16[16,2048]{1,0:T(8,128)(2,1)S(1)} %fusion.7), channel_id=1, source_target_pairs={{0,2},{1,3},{2,4},{3,5},{4,6},{5,7},{6,0},{7,1},{8,10},{9,11},{10,... | collective-permute-start | bytes 196616 | tf_op jit(solution)/shard_map/ppermute | solution.py:24
  51.6 6.6 %collective-permute-start.14 = (bf16[16,2048]{1,0:T(8,128)(2,1)S(1)}, bf16[16,2048]{1,0:T(8,128)(2,1)S(1)}, u32[]{:S(2)}, u32[]{:S(2)}) collective-permute-start(bf16[16,2048]{1,0:T(8,128)(2,1)S(1)} %fusion.7), channel_id=1, source_target_pairs={{0,4},{1,5},{2,6},{3,7},{4,0},{5,1},{6,2},{7,3},{8,12},{9,13},{10,... | collective-permute-start | bytes 196616 | tf_op jit(solution)/shard_map/ppermute | solution.py:24
  77.2 6.6 %collective-permute-start.19 = (bf16[16,2048]{1,0:T(8,128)(2,1)S(1)}, bf16[16,2048]{1,0:T(8,128)(2,1)S(1)}, u32[]{:S(2)}, u32[]{:S(2)}) collective-permute-start(bf16[16,2048]{1,0:T(8,128)(2,1)S(1)} %get-tuple-element.70), channel_id=1, source_target_pairs={{0,4},{1,5},{2,6},{3,7},{4,0},{5,1},{6,2},{7,3},{8,12},{9,13},{10,... | collective-permute-start | bytes 196616 | tf_op jit(solution)/shard_map/ppermute | solution.py:24
  77.2 6.6 %collective-permute-start.20 = (bf16[16,2048]{1,0:T(8,128)(2,1)S(1)}, bf16[16,2048]{1,0:T(8,128)(2,1)S(1)}, u32[]{:S(2)}, u32[]{:S(2)}) collective-permute-start(bf16[16,2048]{1,0:T(8,128)(2,1)S(1)} %get-tuple-element.69), channel_id=1, source_target_pairs={{0,2},{1,3},{2,4},{3,5},{4,6},{5,7},{6,0},{7,1},{8,10},{9,11},{10,... | collective-permute-start | bytes 196616 | tf_op jit(solution)/shard_map/ppermute | solution.py:24
  90.3 6.2 %collective-permute-start.22 = (bf16[16,2048]{1,0:T(8,128)(2,1)S(1)}, bf16[16,2048]{1,0:T(8,128)(2,1)S(1)}, u32[]{:S(2)}, u32[]{:S(2)}) collective-permute-start(bf16[16,2048]{1,0:T(8,128)(2,1)S(1)} %fusion.11), channel_id=1, source_target_pairs={{0,2},{1,3},{2,4},{3,5},{4,6},{5,7},{6,0},{7,1},{8,10},{9,11},{10,... | collective-permute-start | bytes 196616 | tf_op jit(solution)/shard_map/ppermute | solution.py:24
  90.7 7.1 %collective-permute-start.23 = (bf16[16,2048]{1,0:T(8,128)(2,1)S(1)}, bf16[16,2048]{1,0:T(8,128)(2,1)S(1)}, u32[]{:S(2)}, u32[]{:S(2)}) collective-permute-start(bf16[16,2048]{1,0:T(8,128)(2,1)S(1)} %fusion.11), channel_id=1, source_target_pairs={{0,4},{1,5},{2,6},{3,7},{4,0},{5,1},{6,2},{7,3},{8,12},{9,13},{10,... | collective-permute-start | bytes 196616 | tf_op jit(solution)/shard_map/ppermute | solution.py:24
  117.2 6.6 %collective-permute-start.28 = (bf16[16,2048]{1,0:T(8,128)(2,1)S(1)}, bf16[16,2048]{1,0:T(8,128)(2,1)S(1)}, u32[]{:S(2)}, u32[]{:S(2)}) collective-permute-start(bf16[16,2048]{1,0:T(8,128)(2,1)S(1)} %get-tuple-element.65), channel_id=1, source_target_pairs={{0,4},{1,5},{2,6},{3,7},{4,0},{5,1},{6,2},{7,3},{8,12},{9,13},{10,... | collective-permute-start | bytes 196616 | tf_op jit(solution)/shard_map/ppermute | solution.py:24
  117.2 6.6 %collective-permute-start.29 = (bf16[16,2048]{1,0:T(8,128)(2,1)S(1)}, bf16[16,2048]{1,0:T(8,128)(2,1)S(1)}, u32[]{:S(2)}, u32[]{:S(2)}) collective-permute-start(bf16[16,2048]{1,0:T(8,128)(2,1)S(1)} %get-tuple-element.64), channel_id=1, source_target_pairs={{0,2},{1,3},{2,4},{3,5},{4,6},{5,7},{6,0},{7,1},{8,10},{9,11},{10,... | collective-permute-start | bytes 196616 | tf_op jit(solution)/shard_map/ppermute | solution.py:24
  130.3 6.2 %collective-permute-start.31 = (bf16[16,2048]{1,0:T(8,128)(2,1)S(1)}, bf16[16,2048]{1,0:T(8,128)(2,1)S(1)}, u32[]{:S(2)}, u32[]{:S(2)}) collective-permute-start(bf16[16,2048]{1,0:T(8,128)(2,1)S(1)} %fusion.15), channel_id=1, source_target_pairs={{0,2},{1,3},{2,4},{3,5},{4,6},{5,7},{6,0},{7,1},{8,10},{9,11},{10,... | collective-permute-start | bytes 196616 | tf_op jit(solution)/shard_map/ppermute | solution.py:24
  130.7 7.1 %collective-permute-start.32 = (bf16[16,2048]{1,0:T(8,128)(2,1)S(1)}, bf16[16,2048]{1,0:T(8,128)(2,1)S(1)}, u32[]{:S(2)}, u32[]{:S(2)}) collective-permute-start(bf16[16,2048]{1,0:T(8,128)(2,1)S(1)} %fusion.15), channel_id=1, source_target_pairs={{0,4},{1,5},{2,6},{3,7},{4,0},{5,1},{6,2},{7,3},{8,12},{9,13},{10,... | collective-permute-start | bytes 196616 | tf_op jit(solution)/shard_map/ppermute | solution.py:24
  153.6 6.2 %collective-permute-start.36 = (bf16[16,2048]{1,0:T(8,128)(2,1)S(1)}, bf16[16,2048]{1,0:T(8,128)(2,1)S(1)}, u32[]{:S(2)}, u32[]{:S(2)}) collective-permute-start(bf16[16,2048]{1,0:T(8,128)(2,1)S(1)} %get-tuple-element.58), channel_id=1, source_target_pairs={{0,6},{1,7},{2,0},{3,1},{4,2},{5,3},{6,4},{7,5},{8,14},{9,15},{10,... | collective-permute-start | bytes 196616 | tf_op jit(solution)/shard_map/ppermute | solution.py:24
  157.3 6.6 %collective-permute-start.37 = (bf16[16,2048]{1,0:T(8,128)(2,1)S(1)}, bf16[16,2048]{1,0:T(8,128)(2,1)S(1)}, u32[]{:S(2)}, u32[]{:S(2)}) collective-permute-start(bf16[16,2048]{1,0:T(8,128)(2,1)S(1)} %get-tuple-element.60), channel_id=1, source_target_pairs={{0,4},{1,5},{2,6},{3,7},{4,0},{5,1},{6,2},{7,3},{8,12},{9,13},{10,... | collective-permute-start | bytes 196616 | tf_op jit(solution)/shard_map/ppermute | solution.py:24
  157.3 6.6 %collective-permute-start.38 = (bf16[16,2048]{1,0:T(8,128)(2,1)S(1)}, bf16[16,2048]{1,0:T(8,128)(2,1)S(1)}, u32[]{:S(2)}, u32[]{:S(2)}) collective-permute-start(bf16[16,2048]{1,0:T(8,128)(2,1)S(1)} %get-tuple-element.59), channel_id=1, source_target_pairs={{0,2},{1,3},{2,4},{3,5},{4,6},{5,7},{6,0},{7,1},{8,10},{9,11},{10,... | collective-permute-start | bytes 196616 | tf_op jit(solution)/shard_map/ppermute | solution.py:24
  164.0 7.1 %collective-permute-start.39 = (bf16[16,2048]{1,0:T(8,128)(2,1)S(1)}, bf16[16,2048]{1,0:T(8,128)(2,1)S(1)}, u32[]{:S(2)}, u32[]{:S(2)}) collective-permute-start(bf16[16,2048]{1,0:T(8,128)(2,1)S(1)} %get-tuple-element.22), channel_id=1, source_target_pairs={{0,8},{8,16},{16,24},{1,9},{9,17},{17,25},{2,10},{10,18},{18,26},{... | collective-permute-start | bytes 196616 | tf_op jit(solution)/shard_map/ppermute | solution.py:17
  171.3 6.2 %collective-permute-start.40 = (bf16[16,2048]{1,0:T(8,128)(2,1)S(1)}, bf16[16,2048]{1,0:T(8,128)(2,1)S(1)}, u32[]{:S(2)}, u32[]{:S(2)}) collective-permute-start(bf16[16,2048]{1,0:T(8,128)(2,1)S(1)} %fusion.19), channel_id=1, source_target_pairs={{0,2},{1,3},{2,4},{3,5},{4,6},{5,7},{6,0},{7,1},{8,10},{9,11},{10,... | collective-permute-start | bytes 196616 | tf_op jit(solution)/shard_map/ppermute | solution.py:24
  171.7 7.1 %collective-permute-start.41 = (bf16[16,2048]{1,0:T(8,128)(2,1)S(1)}, bf16[16,2048]{1,0:T(8,128)(2,1)S(1)}, u32[]{:S(2)}, u32[]{:S(2)}) collective-permute-start(bf16[16,2048]{1,0:T(8,128)(2,1)S(1)} %fusion.19), channel_id=1, source_target_pairs={{0,4},{1,5},{2,6},{3,7},{4,0},{5,1},{6,2},{7,3},{8,12},{9,13},{10,... | collective-permute-start | bytes 196616 | tf_op jit(solution)/shard_map/ppermute | solution.py:24
  198.2 6.6 %collective-permute-start.46 = (bf16[16,2048]{1,0:T(8,128)(2,1)S(1)}, bf16[16,2048]{1,0:T(8,128)(2,1)S(1)}, u32[]{:S(2)}, u32[]{:S(2)}) collective-permute-start(bf16[16,2048]{1,0:T(8,128)(2,1)S(1)} %get-tuple-element.55), channel_id=1, source_target_pairs={{0,4},{1,5},{2,6},{3,7},{4,0},{5,1},{6,2},{7,3},{8,12},{9,13},{10,... | collective-permute-start | bytes 196616 | tf_op jit(solution)/shard_map/ppermute | solution.py:24
  198.2 6.6 %collective-permute-start.47 = (bf16[16,2048]{1,0:T(8,128)(2,1)S(1)}, bf16[16,2048]{1,0:T(8,128)(2,1)S(1)}, u32[]{:S(2)}, u32[]{:S(2)}) collective-permute-start(bf16[16,2048]{1,0:T(8,128)(2,1)S(1)} %get-tuple-element.54), channel_id=1, source_target_pairs={{0,2},{1,3},{2,4},{3,5},{4,6},{5,7},{6,0},{7,1},{8,10},{9,11},{10,... | collective-permute-start | bytes 196616 | tf_op jit(solution)/shard_map/ppermute | solution.py:24
  204.9 7.1 %collective-permute-start.48 = (bf16[16,2048]{1,0:T(8,128)(2,1)S(1)}, bf16[16,2048]{1,0:T(8,128)(2,1)S(1)}, u32[]{:S(2)}, u32[]{:S(2)}) collective-permute-start(bf16[16,2048]{1,0:T(8,128)(2,1)S(1)} %get-tuple-element.16), channel_id=1, source_target_pairs={{0,8},{8,16},{16,24},{1,9},{9,17},{17,25},{2,10},{10,18},{18,26},{... | collective-permute-start | bytes 196616 | tf_op jit(solution)/shard_map/ppermute | solution.py:17
  212.2 6.2 %collective-permute-start.49 = (bf16[16,2048]{1,0:T(8,128)(2,1)S(1)}, bf16[16,2048]{1,0:T(8,128)(2,1)S(1)}, u32[]{:S(2)}, u32[]{:S(2)}) collective-permute-start(bf16[16,2048]{1,0:T(8,128)(2,1)S(1)} %fusion.23), channel_id=1, source_target_pairs={{0,2},{1,3},{2,4},{3,5},{4,6},{5,7},{6,0},{7,1},{8,10},{9,11},{10,... | collective-permute-start | bytes 196616 | tf_op jit(solution)/shard_map/ppermute | solution.py:24
  212.6 7.1 %collective-permute-start.50 = (bf16[16,2048]{1,0:T(8,128)(2,1)S(1)}, bf16[16,2048]{1,0:T(8,128)(2,1)S(1)}, u32[]{:S(2)}, u32[]{:S(2)}) collective-permute-start(bf16[16,2048]{1,0:T(8,128)(2,1)S(1)} %fusion.23), channel_id=1, source_target_pairs={{0,4},{1,5},{2,6},{3,7},{4,0},{5,1},{6,2},{7,3},{8,12},{9,13},{10,... | collective-permute-start | bytes 196616 | tf_op jit(solution)/shard_map/ppermute | solution.py:24
  239.0 6.6 %collective-permute-start.55 = (bf16[16,2048]{1,0:T(8,128)(2,1)S(1)}, bf16[16,2048]{1,0:T(8,128)(2,1)S(1)}, u32[]{:S(2)}, u32[]{:S(2)}) collective-permute-start(bf16[16,2048]{1,0:T(8,128)(2,1)S(1)} %get-tuple-element.50), channel_id=1, source_target_pairs={{0,4},{1,5},{2,6},{3,7},{4,0},{5,1},{6,2},{7,3},{8,12},{9,13},{10,... | collective-permute-start | bytes 196616 | tf_op jit(solution)/shard_map/ppermute | solution.py:24
  239.0 6.6 %collective-permute-start.56 = (bf16[16,2048]{1,0:T(8,128)(2,1)S(1)}, bf16[16,2048]{1,0:T(8,128)(2,1)S(1)}, u32[]{:S(2)}, u32[]{:S(2)}) collective-permute-start(bf16[16,2048]{1,0:T(8,128)(2,1)S(1)} %get-tuple-element.49), channel_id=1, source_target_pairs={{0,2},{1,3},{2,4},{3,5},{4,6},{5,7},{6,0},{7,1},{8,10},{9,11},{10,... | collective-permute-start | bytes 196616 | tf_op jit(solution)/shard_map/ppermute | solution.py:24
  245.7 7.1 %collective-permute-start.57 = (bf16[16,2048]{1,0:T(8,128)(2,1)S(1)}, bf16[16,2048]{1,0:T(8,128)(2,1)S(1)}, u32[]{:S(2)}, u32[]{:S(2)}) collective-permute-start(bf16[16,2048]{1,0:T(8,128)(2,1)S(1)} %get-tuple-element.10), channel_id=1, source_target_pairs={{0,8},{8,16},{16,24},{1,9},{9,17},{17,25},{2,10},{10,18},{18,26},{... | collective-permute-start | bytes 196616 | tf_op jit(solution)/shard_map/ppermute | solution.py:17
  253.0 6.2 %collective-permute-start.58 = (bf16[16,2048]{1,0:T(8,128)(2,1)S(1)}, bf16[16,2048]{1,0:T(8,128)(2,1)S(1)}, u32[]{:S(2)}, u32[]{:S(2)}) collective-permute-start(bf16[16,2048]{1,0:T(8,128)(2,1)S(1)} %fusion.27), channel_id=1, source_target_pairs={{0,2},{1,3},{2,4},{3,5},{4,6},{5,7},{6,0},{7,1},{8,10},{9,11},{10,... | collective-permute-start | bytes 196616 | tf_op jit(solution)/shard_map/ppermute | solution.py:24
  253.5 7.1 %collective-permute-start.59 = (bf16[16,2048]{1,0:T(8,128)(2,1)S(1)}, bf16[16,2048]{1,0:T(8,128)(2,1)S(1)}, u32[]{:S(2)}, u32[]{:S(2)}) collective-permute-start(bf16[16,2048]{1,0:T(8,128)(2,1)S(1)} %fusion.27), channel_id=1, source_target_pairs={{0,4},{1,5},{2,6},{3,7},{4,0},{5,1},{6,2},{7,3},{8,12},{9,13},{10,... | collective-permute-start | bytes 196616 | tf_op jit(solution)/shard_map/ppermute | solution.py:24
  279.9 6.6 %collective-permute-start.64 = (bf16[16,2048]{1,0:T(8,128)(2,1)S(1)}, bf16[16,2048]{1,0:T(8,128)(2,1)S(1)}, u32[]{:S(2)}, u32[]{:S(2)}) collective-permute-start(bf16[16,2048]{1,0:T(8,128)(2,1)S(1)} %get-tuple-element.45), channel_id=1, source_target_pairs={{0,4},{1,5},{2,6},{3,7},{4,0},{5,1},{6,2},{7,3},{8,12},{9,13},{10,... | collective-permute-start | bytes 196616 | tf_op jit(solution)/shard_map/ppermute | solution.py:24
  279.9 6.6 %collective-permute-start.65 = (bf16[16,2048]{1,0:T(8,128)(2,1)S(1)}, bf16[16,2048]{1,0:T(8,128)(2,1)S(1)}, u32[]{:S(2)}, u32[]{:S(2)}) collective-permute-start(bf16[16,2048]{1,0:T(8,128)(2,1)S(1)} %get-tuple-element.44), channel_id=1, source_target_pairs={{0,2},{1,3},{2,4},{3,5},{4,6},{5,7},{6,0},{7,1},{8,10},{9,11},{10,... | collective-permute-start | bytes 196616 | tf_op jit(solution)/shard_map/ppermute | solution.py:24
  (36 other events, 180.5 us)

commit v9 on v3

--- a/solution.py
+++ b/solution.py
@@ -43,6 +43,18 @@
     return total
 
 
+def to_next_section(array, by):
+    sections = lax.axis_size("section")
+    count = lax.axis_size("expert")
+    chips = count // 2
+    pairs = [
+        (s * count + i, ((s + 1) % sections) * count + ((i // 2 + by) % chips) * 2 + i % 2)
+        for s in range(sections)
+        for i in range(count)
+    ]
+    return lax.ppermute(array, ("section", "expert"), pairs)
+
+
 def rms_normed(hidden, gain):
     values = hidden.astype(jnp.float32)
     scale = lax.rsqrt(jnp.mean(values * values, axis=-1, keepdims=True) + EPSILON)
@@ -73,30 +85,29 @@
     table = gather_blocks(table, "expert")
     mine = lax.dynamic_slice_in_dim(table, expert_index * local_experts, local_experts, axis=4)
     mixing = jnp.transpose(mine, (2, 4, 0, 1, 3)).reshape(MB, local_experts, 2 * chips * tok_rows)
-    held = jnp.zeros((tok_rows, width), jnp.bfloat16)
     collected = jnp.zeros((MB, tok_rows, width), jnp.bfloat16)
+    blocks = gather_blocks(tokens[0], "expert")[0]
+    last = MB + sections - 2
     for moment in range(MB + sections - 1):
-        if moment > 0:
-            arrived = shifted(held, "section", 1)
-        else:
-            arrived = held
         batch_index = moment - section_index
         active = (batch_index >= 0) & (batch_index < MB)
         clipped = jnp.clip(batch_index, 0, MB - 1)
-        first_rows = lax.dynamic_index_in_dim(tokens, clipped, 0, keepdims=False)
-        incoming = jnp.where(section_index == 0, first_rows, arrived)
         weight = lax.dynamic_index_in_dim(mixing, clipped, 0, keepdims=False)
-        values, normed = rms_normed(incoming, gain)
-        rows = gather_blocks(normed, "expert").reshape(2 * chips * tok_rows, width)
+        rows = jnp.stack([blocks, core_swap(blocks, "expert")])
+        values, normed = rms_normed(rows, gain)
+        rows = normed.reshape(2 * chips * tok_rows, width)
         gate_part = jnp.einsum("td,edf->etf", rows, w_gate, preferred_element_type=jnp.float32)
         up_part = jnp.einsum("td,edf->etf", rows, w_up, preferred_element_type=jnp.float32)
         inner = (jax.nn.silu(gate_part) * up_part * weight[:, :, None]).astype(jnp.bfloat16)
         partial = jnp.einsum("etf,efd->td", inner, w_down, preferred_element_type=jnp.float32)
         mixed = scatter_blocks(partial.reshape(2, chips, tok_rows, width), "expert")
-        produced = (values + mixed).astype(jnp.bfloat16)
-        held = jnp.where(active, produced, incoming)
-        updated = lax.dynamic_update_index_in_dim(collected, held, clipped, 0)
+        produced = (values[0, 0] + mixed).astype(jnp.bfloat16)
+        updated = lax.dynamic_update_index_in_dim(collected, produced, clipped, 0)
         collected = jnp.where(active, updated, collected)
+        if moment < last:
+            upcoming = lax.dynamic_index_in_dim(tokens, min(moment + 1, MB - 1), 0, keepdims=False)
+            outgoing = jnp.where(section_index == sections - 1, upcoming, produced)
+            blocks = jnp.stack([to_next_section(outgoing, k) for k in range(chips)])
     return collected[None]
 
 

time: 275 us -> 257 us (0.935)
  starting transfers between devices: 98 us -> 75.8 us
  waiting for transfers between devices: 89.5 us -> 93.2 us
    ppermute x45 -> x27, starting transfers between devices: 68.6 us -> 37.7 us  [chip_shift(): return lax.ppermute(array, axis, pairs)]
    ppermute x6 -> x24, waiting for transfers between devices: 11.3 us -> 35.4 us  [to_next_section(): return lax.ppermute(array, ('section', 'expert'), pairs)]
    ppermute x45 -> x27, waiting for transfers between devices: 58.2 us -> 38.7 us  [chip_shift(): return lax.ppermute(array, axis, pairs)]
    ppermute x6 -> x24, starting transfers between devices: 27.5 us -> 36 us  [to_next_section(): return lax.ppermute(array, ('section', 'expert'), pairs)]
  transfers between devices with their start and end apart: 66 -> 66, of which waited for: 49 -> 46; matrix products, arithmetic and copies ran while one was open for 2% -> 2% of each run, Pallas kernels for 0% -> 0%
where the time goes in v9:
time: 257 us
  waiting for transfers between devices  93.2 us (36%)
  starting transfers between devices  75.8 us (29%)
  matrix products  72.6 us (28%)
  other arithmetic  10.3 us (4%)
  local copies, waits for them, and re-layouts  4.02 us (2%)
    dot_general x7, matrix products, on_device(): jnp.einsum('etf,efd->td', inner, w_down, preferred_element_type=jnp.float32)  46.2 us
    ppermute x27, waiting for transfers between devices, chip_shift(): return lax.ppermute(array, axis, pairs)  38.7 us
    ppermute x27, starting transfers between devices, chip_shift(): return lax.ppermute(array, axis, pairs)  37.7 us
    ppermute x24, starting transfers between devices, to_next_section(): return lax.ppermute(array, ('section', 'expert'), pairs)  36 us
    ppermute x24, waiting for transfers between devices, to_next_section(): return lax.ppermute(array, ('section', 'expert'), pairs)  35.4 us
    dot_general x7, matrix products, on_device(): jnp.einsum('td,edf->etf', rows, w_gate, preferred_element_type=jnp.float32)  26.4 us
    ppermute x15, waiting for transfers between devices, core_swap(): return lax.ppermute(array, axis, [(i, i ^ 1) for i in range(count)])  19.1 us
  transfers between devices with their start and end apart: 66, of which 46 were waited for; matrix products, arithmetic and copies ran while one was open for 2% of the time, Pallas kernels for 0%

profile of v9, /device:TPU:0, one launch (start us, length us, event | category | flops | bytes accessed | tf_op | source)
XLA Modules:
  0.0 256.7 jit_solution(2255458944596753205)
XLA Ops:
  0.9 5.1 %collective-permute-start.2 = (bf16[16,2048]{1,0:T(8,128)(2,1)S(1)}, bf16[16,2048]{1,0:T(8,128)(2,1)S(1)}, u32[]{:S(2)}, u32[]{:S(2)}) collective-permute-start(bf16[16,2048]{1,0:T(8,128)(2,1)S(1)} %get-tuple-element.67), channel_id=1, source_target_pairs={{0,6},{1,7},{2,0},{3,1},{4,2},{5,3},{6,4},{7,5},{8,14},{9,15},{10,... | collective-permute-start | bytes 196616 | tf_op jit(solution)/shard_map/ppermute | solution.py:22
  9.5 2.9 %collective-permute-start.6 = (f32[4,16,16]{2,1,0:T(8,128)S(1)}, f32[4,16,16]{2,1,0:T(8,128)S(1)}, u32[]{:S(2)}, u32[]{:S(2)}) collective-permute-start(f32[4,16,16]{2,1,0:T(8,128)S(1)} %select_reduce_fusion), channel_id=1, source_target_pairs={{0,6},{1,7},{2,0},{3,1},{4,2},{5,3},{6,4},{7,5},{8,14},{9,15},{10,... | collective-permute-start | bytes 12296 | tf_op jit(solution)/shard_map/ppermute | solution.py:22
  14.0 3.2 %collective-permute-done.5 = f32[4,16,16]{2,1,0:T(8,128)S(1)} collective-permute-done((f32[4,16,16]{2,1,0:T(8,128)S(1)}, f32[4,16,16]{2,1,0:T(8,128)S(1)}, u32[]{:S(2)}, u32[]{:S(2)}) %collective-permute-start.5) | collective-permute-done | bytes 4128 | tf_op jit(solution)/shard_map/ppermute | solution.py:22
  22.9 3.8 %fusion.63 = f32[2,128,768]{2,1,0:T(8,128)S(1)} fusion(bf16[128,2048,1]{1,0,2:T(8,128)(2,1)S(1)} %bitcast.595, bf16[1,2,2048,768]{3,2,1,0:T(8,128)(2,1)} %param.9), kind=kOutput, calls=%fused_computation.49 | convolution fusion | flops 805306368 | bytes 7602176 | tf_op jit(solution)/shard_map/td,edf->etf/dot_general | solution.py:99
  26.7 6.6 %fusion.42 = f32[128,2048]{1,0:T(8,128)S(1)} fusion(bf16[1,2,768,2048]{3,2,1,0:T(8,128)(2,1)} %param.11, bf16[128,2048,1]{1,0,2:T(8,128)(2,1)S(1)} %bitcast.596, bf16[1,2,2048,768]{3,2,1,0:T(8,128)(2,1)} %param.10, f32[2,128,768]{2,1,0:T(8,128)S(1)} %fusion.63, f32[2,128]{1,0:T(2,128)S(1)} %get-tuple-element.76), kind=kOutput, calls=%fused_computation.42 | convolution fusion | flops 1611988992 | bytes 14943232 | tf_op jit(solution)/shard_map/etf,efd->td/dot_general | solution.py:102
  35.4 3.6 %collective-permute-start.9 = (bf16[16,2048]{1,0:T(8,128)(2,1)S(1)}, bf16[16,2048]{1,0:T(8,128)(2,1)S(1)}, u32[]{:S(2)}, u32[]{:S(2)}) collective-permute-start(bf16[16,2048]{1,0:T(8,128)(2,1)S(1)} %get-tuple-element.61), channel_id=1, source_target_pairs={{0,6},{1,7},{2,0},{3,1},{4,2},{5,3},{6,4},{7,5},{8,14},{9,15},{10,... | collective-permute-start | bytes 196616 | tf_op jit(solution)/shard_map/ppermute | solution.py:22
  39.0 2.9 %collective-permute-done.11 = bf16[16,2048]{1,0:T(8,128)(2,1)S(1)} collective-permute-done((bf16[16,2048]{1,0:T(8,128)(2,1)S(1)}, bf16[16,2048]{1,0:T(8,128)(2,1)S(1)}, u32[]{:S(2)}, u32[]{:S(2)}) %collective-permute-start.11) | collective-permute-done | bytes 65568 | tf_op jit(solution)/shard_map/ppermute | solution.py:22
  50.6 4.7 %collective-permute-done.14 = bf16[16,2048]{1,0:T(8,128)(2,1)S(1)} collective-permute-done((bf16[16,2048]{1,0:T(8,128)(2,1)S(1)}, bf16[16,2048]{1,0:T(8,128)(2,1)S(1)}, u32[]{:S(2)}, u32[]{:S(2)}) %collective-permute-start.14) | collective-permute-done | bytes 65568 | tf_op jit(solution)/shard_map/ppermute | solution.py:55
  59.0 3.8 %fusion.66 = f32[2,128,768]{2,1,0:T(8,128)S(1)} fusion(bf16[128,2048,1]{1,0,2:T(8,128)(2,1)S(1)} %bitcast.597, bf16[1,2,2048,768]{3,2,1,0:T(8,128)(2,1)} %param.9), kind=kOutput, calls=%fused_computation.50 | convolution fusion | flops 805306368 | bytes 7602176 | tf_op jit(solution)/shard_map/td,edf->etf/dot_general | solution.py:99
  62.8 6.6 %fusion.45 = f32[128,2048]{1,0:T(8,128)S(1)} fusion(bf16[1,2,768,2048]{3,2,1,0:T(8,128)(2,1)} %param.11, bf16[128,2048,1]{1,0,2:T(8,128)(2,1)S(1)} %bitcast.598, bf16[1,2,2048,768]{3,2,1,0:T(8,128)(2,1)} %param.10, f32[2,128,768]{2,1,0:T(8,128)S(1)} %fusion.66, f32[2,128]{1,0:T(2,128)S(1)} %get-tuple-element.75), kind=kOutput, calls=%fused_computation.43 | convolution fusion | flops 1611988992 | bytes 14943232 | tf_op jit(solution)/shard_map/etf,efd->td/dot_general | solution.py:102
  75.1 2.9 %collective-permute-done.20 = bf16[16,2048]{1,0:T(8,128)(2,1)S(1)} collective-permute-done((bf16[16,2048]{1,0:T(8,128)(2,1)S(1)}, bf16[16,2048]{1,0:T(8,128)(2,1)S(1)}, u32[]{:S(2)}, u32[]{:S(2)}) %collective-permute-start.20) | collective-permute-done | bytes 65568 | tf_op jit(solution)/shard_map/ppermute | solution.py:22
  86.2 4.1 %collective-permute-done.23 = bf16[16,2048]{1,0:T(8,128)(2,1)S(1)} collective-permute-done((bf16[16,2048]{1,0:T(8,128)(2,1)S(1)}, bf16[16,2048]{1,0:T(8,128)(2,1)S(1)}, u32[]{:S(2)}, u32[]{:S(2)}) %collective-permute-start.23) | collective-permute-done | bytes 65568 | tf_op jit(solution)/shard_map/ppermute | solution.py:55
  93.8 3.8 %fusion.69 = f32[2,128,768]{2,1,0:T(8,128)S(1)} fusion(bf16[128,2048,1]{1,0,2:T(8,128)(2,1)S(1)} %bitcast.599, bf16[1,2,2048,768]{3,2,1,0:T(8,128)(2,1)} %param.9), kind=kOutput, calls=%fused_computation.51 | convolution fusion | flops 805306368 | bytes 7602176 | tf_op jit(solution)/shard_map/td,edf->etf/dot_general | solution.py:99
  97.5 6.6 %fusion.48 = f32[128,2048]{1,0:T(8,128)S(1)} fusion(bf16[1,2,768,2048]{3,2,1,0:T(8,128)(2,1)} %param.11, bf16[128,2048,1]{1,0,2:T(8,128)(2,1)S(1)} %bitcast.600, bf16[1,2,2048,768]{3,2,1,0:T(8,128)(2,1)} %param.10, f32[2,128,768]{2,1,0:T(8,128)S(1)} %fusion.69, f32[2,128]{1,0:T(2,128)S(1)} %get-tuple-element.74), kind=kOutput, calls=%fused_computation.44 | convolution fusion | flops 1611988992 | bytes 14943232 | tf_op jit(solution)/shard_map/etf,efd->td/dot_general | solution.py:102
  120.7 3.7 %collective-permute-done.32 = bf16[16,2048]{1,0:T(8,128)(2,1)S(1)} collective-permute-done((bf16[16,2048]{1,0:T(8,128)(2,1)S(1)}, bf16[16,2048]{1,0:T(8,128)(2,1)S(1)}, u32[]{:S(2)}, u32[]{:S(2)}) %collective-permute-start.32) | collective-permute-done | bytes 65568 | tf_op jit(solution)/shard_map/ppermute | solution.py:55
  124.4 2.8 %collective-permute-done.31 = bf16[16,2048]{1,0:T(8,128)(2,1)S(1)} collective-permute-done((bf16[16,2048]{1,0:T(8,128)(2,1)S(1)}, bf16[16,2048]{1,0:T(8,128)(2,1)S(1)}, u32[]{:S(2)}, u32[]{:S(2)}) %collective-permute-start.31) | collective-permute-done | bytes 65568 | tf_op jit(solution)/shard_map/ppermute | solution.py:55
  129.3 3.8 %fusion.72 = f32[2,128,768]{2,1,0:T(8,128)S(1)} fusion(bf16[128,2048,1]{1,0,2:T(8,128)(2,1)S(1)} %bitcast.601, bf16[1,2,2048,768]{3,2,1,0:T(8,128)(2,1)} %param.9), kind=kOutput, calls=%fused_computation.52 | convolution fusion | flops 805306368 | bytes 7602176 | tf_op jit(solution)/shard_map/td,edf->etf/dot_general | solution.py:99
  133.1 6.6 %fusion.51 = f32[128,2048]{1,0:T(8,128)S(1)} fusion(bf16[1,2,768,2048]{3,2,1,0:T(8,128)(2,1)} %param.11, bf16[128,2048,1]{1,0,2:T(8,128)(2,1)S(1)} %bitcast.602, bf16[1,2,2048,768]{3,2,1,0:T(8,128)(2,1)} %param.10, f32[2,128,768]{2,1,0:T(8,128)S(1)} %fusion.72, f32[2,128]{1,0:T(2,128)S(1)} %copy-done.5), kind=kOutput, calls=%fused_computation.45 | convolution fusion | flops 1611988992 | bytes 14943232 | tf_op jit(solution)/shard_map/etf,efd->td/dot_general | solution.py:102
  145.4 2.9 %collective-permute-done.38 = bf16[16,2048]{1,0:T(8,128)(2,1)S(1)} collective-permute-done((bf16[16,2048]{1,0:T(8,128)(2,1)S(1)}, bf16[16,2048]{1,0:T(8,128)(2,1)S(1)}, u32[]{:S(2)}, u32[]{:S(2)}) %collective-permute-start.38) | collective-permute-done | bytes 65568 | tf_op jit(solution)/shard_map/ppermute | solution.py:22
  156.8 4.1 %collective-permute-done.41 = bf16[16,2048]{1,0:T(8,128)(2,1)S(1)} collective-permute-done((bf16[16,2048]{1,0:T(8,128)(2,1)S(1)}, bf16[16,2048]{1,0:T(8,128)(2,1)S(1)}, u32[]{:S(2)}, u32[]{:S(2)}) %collective-permute-start.41) | collective-permute-done | bytes 65568 | tf_op jit(solution)/shard_map/ppermute | solution.py:55
  164.4 3.8 %fusion.75 = f32[2,128,768]{2,1,0:T(8,128)S(1)} fusion(bf16[128,2048,1]{1,0,2:T(8,128)(2,1)S(1)} %bitcast.603, bf16[1,2,2048,768]{3,2,1,0:T(8,128)(2,1)} %param.9), kind=kOutput, calls=%fused_computation.53 | convolution fusion | flops 805306368 | bytes 7602176 | tf_op jit(solution)/shard_map/td,edf->etf/dot_general | solution.py:99
  168.2 6.6 %fusion.54 = f32[128,2048]{1,0:T(8,128)S(1)} fusion(bf16[1,2,768,2048]{3,2,1,0:T(8,128)(2,1)} %param.11, bf16[128,2048,1]{1,0,2:T(8,128)(2,1)S(1)} %bitcast.604, bf16[1,2,2048,768]{3,2,1,0:T(8,128)(2,1)} %param.10, f32[2,128,768]{2,1,0:T(8,128)S(1)} %fusion.75, f32[2,128]{1,0:T(2,128)S(1)} %copy-done.4), kind=kOutput, calls=%fused_computation.46 | convolution fusion | flops 1611988992 | bytes 14943232 | tf_op jit(solution)/shard_map/etf,efd->td/dot_general | solution.py:102
  180.7 2.9 %collective-permute-done.47 = bf16[16,2048]{1,0:T(8,128)(2,1)S(1)} collective-permute-done((bf16[16,2048]{1,0:T(8,128)(2,1)S(1)}, bf16[16,2048]{1,0:T(8,128)(2,1)S(1)}, u32[]{:S(2)}, u32[]{:S(2)}) %collective-permute-start.47) | collective-permute-done | bytes 65568 | tf_op jit(solution)/shard_map/ppermute | solution.py:22
  193.0 2.7 %collective-permute-done.50 = bf16[16,2048]{1,0:T(8,128)(2,1)S(1)} collective-permute-done((bf16[16,2048]{1,0:T(8,128)(2,1)S(1)}, bf16[16,2048]{1,0:T(8,128)(2,1)S(1)}, u32[]{:S(2)}, u32[]{:S(2)}) %collective-permute-start.50) | collective-permute-done | bytes 65568 | tf_op jit(solution)/shard_map/ppermute | solution.py:55
  195.7 2.9 %collective-permute-done.49 = bf16[16,2048]{1,0:T(8,128)(2,1)S(1)} collective-permute-done((bf16[16,2048]{1,0:T(8,128)(2,1)S(1)}, bf16[16,2048]{1,0:T(8,128)(2,1)S(1)}, u32[]{:S(2)}, u32[]{:S(2)}) %collective-permute-start.49) | collective-permute-done | bytes 65568 | tf_op jit(solution)/shard_map/ppermute | solution.py:55
  200.7 3.8 %fusion.78 = f32[2,128,768]{2,1,0:T(8,128)S(1)} fusion(bf16[128,2048,1]{1,0,2:T(8,128)(2,1)S(1)} %bitcast.605, bf16[1,2,2048,768]{3,2,1,0:T(8,128)(2,1)} %param.9), kind=kOutput, calls=%fused_computation.54 | convolution fusion | flops 805306368 | bytes 7602176 | tf_op jit(solution)/shard_map/td,edf->etf/dot_general | solution.py:99
  204.5 6.6 %fusion.57 = f32[128,2048]{1,0:T(8,128)S(1)} fusion(bf16[1,2,768,2048]{3,2,1,0:T(8,128)(2,1)} %param.11, bf16[128,2048,1]{1,0,2:T(8,128)(2,1)S(1)} %bitcast.606, bf16[1,2,2048,768]{3,2,1,0:T(8,128)(2,1)} %param.10, f32[2,128,768]{2,1,0:T(8,128)S(1)} %fusion.78, f32[2,128]{1,0:T(2,128)S(1)} %get-tuple-element.71), kind=kOutput, calls=%fused_computation.47 | convolution fusion | flops 1611988992 | bytes 14943232 | tf_op jit(solution)/shard_map/etf,efd->td/dot_general | solution.py:102
  216.8 2.9 %collective-permute-done.56 = bf16[16,2048]{1,0:T(8,128)(2,1)S(1)} collective-permute-done((bf16[16,2048]{1,0:T(8,128)(2,1)S(1)}, bf16[16,2048]{1,0:T(8,128)(2,1)S(1)}, u32[]{:S(2)}, u32[]{:S(2)}) %collective-permute-start.56) | collective-permute-done | bytes 65568 | tf_op jit(solution)/shard_map/ppermute | solution.py:22
  227.7 4.2 %collective-permute-done.59 = bf16[16,2048]{1,0:T(8,128)(2,1)S(1)} collective-permute-done((bf16[16,2048]{1,0:T(8,128)(2,1)S(1)}, bf16[16,2048]{1,0:T(8,128)(2,1)S(1)}, u32[]{:S(2)}, u32[]{:S(2)}) %collective-permute-start.59) | collective-permute-done | bytes 65568 | tf_op jit(solution)/shard_map/ppermute | solution.py:55
  235.2 3.8 %fusion.81 = f32[2,128,768]{2,1,0:T(8,128)S(1)} fusion(bf16[128,2048,1]{1,0,2:T(8,128)(2,1)S(1)} %bitcast.593, bf16[1,2,2048,768]{3,2,1,0:T(8,128)(2,1)} %param.9), kind=kOutput, calls=%fused_computation.55 | convolution fusion | flops 805306368 | bytes 7602176 | tf_op jit(solution)/shard_map/td,edf->etf/dot_general | solution.py:99
  239.0 6.6 %fusion.60 = f32[128,2048]{1,0:T(8,128)S(1)} fusion(bf16[1,2,768,2048]{3,2,1,0:T(8,128)(2,1)} %param.11, bf16[128,2048,1]{1,0,2:T(8,128)(2,1)S(1)} %bitcast.594, bf16[1,2,2048,768]{3,2,1,0:T(8,128)(2,1)} %param.10, f32[2,128,768]{2,1,0:T(8,128)S(1)} %fusion.81, f32[2,128]{1,0:T(2,128)S(1)} %get-tuple-element.70), kind=kOutput, calls=%fused_computation.48 | convolution fusion | flops 1611988992 | bytes 14943232 | tf_op jit(solution)/shard_map/etf,efd->td/dot_general | solution.py:102
  251.3 2.9 %collective-permute-done.65 = bf16[16,2048]{1,0:T(8,128)(2,1)S(1)} collective-permute-done((bf16[16,2048]{1,0:T(8,128)(2,1)S(1)}, bf16[16,2048]{1,0:T(8,128)(2,1)S(1)}, u32[]{:S(2)}, u32[]{:S(2)}) %collective-permute-start.65) | collective-permute-done | bytes 65568 | tf_op jit(solution)/shard_map/ppermute | solution.py:22
  (215 shorter events, 122.2 us)
Async XLA Ops:
  0.9 12.7 %collective-permute-start.2 = (bf16[16,2048]{1,0:T(8,128)(2,1)S(1)}, bf16[16,2048]{1,0:T(8,128)(2,1)S(1)}, u32[]{:S(2)}, u32[]{:S(2)}) collective-permute-start(bf16[16,2048]{1,0:T(8,128)(2,1)S(1)} %get-tuple-element.67), channel_id=1, source_target_pairs={{0,6},{1,7},{2,0},{3,1},{4,2},{5,3},{6,4},{7,5},{8,14},{9,15},{10,... | collective-permute-start | bytes 196616 | tf_op jit(solution)/shard_map/ppermute | solution.py:22
  6.0 7.6 %collective-permute-start.1 = (bf16[16,2048]{1,0:T(8,128)(2,1)S(1)}, bf16[16,2048]{1,0:T(8,128)(2,1)S(1)}, u32[]{:S(2)}, u32[]{:S(2)}) collective-permute-start(bf16[16,2048]{1,0:T(8,128)(2,1)S(1)} %get-tuple-element.67), channel_id=1, source_target_pairs={{0,4},{1,5},{2,6},{3,7},{4,0},{5,1},{6,2},{7,3},{8,12},{9,13},{10,... | collective-permute-start | bytes 196616 | tf_op jit(solution)/shard_map/ppermute | solution.py:22
  6.0 7.6 %collective-permute-start = (bf16[16,2048]{1,0:T(8,128)(2,1)S(1)}, bf16[16,2048]{1,0:T(8,128)(2,1)S(1)}, u32[]{:S(2)}, u32[]{:S(2)}) collective-permute-start(bf16[16,2048]{1,0:T(8,128)(2,1)S(1)} %get-tuple-element.67), channel_id=1, source_target_pairs={{0,2},{1,3},{2,4},{3,5},{4,6},{5,7},{6,0},{7,1},{8,10},{9,11},{10,... | collective-permute-start | bytes 196616 | tf_op jit(solution)/shard_map/ppermute | solution.py:22
  13.6 8.2 %collective-permute-start.3 = (bf16[4,16,2048]{2,1,0:T(8,128)(2,1)S(1)}, bf16[4,16,2048]{2,1,0:T(8,128)(2,1)S(1)}, u32[]{:S(2)}, u32[]{:S(2)}) collective-permute-start(bf16[4,16,2048]{2,1,0:T(8,128)(2,1)S(1)} %get-tuple-element.65), channel_id=1, source_target_pairs={{0,1},{1,0},{2,3},{3,2},{4,5},{5,4},{6,7},{7,6},{8,9},{9,8},{10,11... | collective-permute-start | bytes 786440 | tf_op jit(solution)/shard_map/ppermute | solution.py:27
  35.1 8.6 %collective-permute-start.10 = (bf16[16,2048]{1,0:T(8,128)(2,1)S(1)}, bf16[16,2048]{1,0:T(8,128)(2,1)S(1)}, u32[]{:S(2)}, u32[]{:S(2)}) collective-permute-start(bf16[16,2048]{1,0:T(8,128)(2,1)S(1)} %get-tuple-element.63), channel_id=1, source_target_pairs={{0,4},{1,5},{2,6},{3,7},{4,0},{5,1},{6,2},{7,3},{8,12},{9,13},{10,... | collective-permute-start | bytes 196616 | tf_op jit(solution)/shard_map/ppermute | solution.py:22
  35.4 8.4 %collective-permute-start.9 = (bf16[16,2048]{1,0:T(8,128)(2,1)S(1)}, bf16[16,2048]{1,0:T(8,128)(2,1)S(1)}, u32[]{:S(2)}, u32[]{:S(2)}) collective-permute-start(bf16[16,2048]{1,0:T(8,128)(2,1)S(1)} %get-tuple-element.61), channel_id=1, source_target_pairs={{0,6},{1,7},{2,0},{3,1},{4,2},{5,3},{6,4},{7,5},{8,14},{9,15},{10,... | collective-permute-start | bytes 196616 | tf_op jit(solution)/shard_map/ppermute | solution.py:22
  47.2 8.1 %collective-permute-start.14 = (bf16[16,2048]{1,0:T(8,128)(2,1)S(1)}, bf16[16,2048]{1,0:T(8,128)(2,1)S(1)}, u32[]{:S(2)}, u32[]{:S(2)}) collective-permute-start(bf16[16,2048]{1,0:T(8,128)(2,1)S(1)} %get-tuple-element.27), channel_id=1, source_target_pairs={{0,12},{1,13},{2,14},{3,15},{4,8},{5,9},{6,10},{7,11},{8,20},{9,21... | collective-permute-start | bytes 196616 | tf_op jit(solution)/shard_map/ppermute | solution.py:55
  49.1 7.9 %collective-permute-start.13 = (bf16[16,2048]{1,0:T(8,128)(2,1)S(1)}, bf16[16,2048]{1,0:T(8,128)(2,1)S(1)}, u32[]{:S(2)}, u32[]{:S(2)}) collective-permute-start(bf16[16,2048]{1,0:T(8,128)(2,1)S(1)} %get-tuple-element.27), channel_id=1, source_target_pairs={{0,10},{1,11},{2,12},{3,13},{4,14},{5,15},{6,8},{7,9},{8,18},{9,19... | collective-permute-start | bytes 196616 | tf_op jit(solution)/shard_map/ppermute | solution.py:55
  71.9 8.2 %collective-permute-start.19 = (bf16[16,2048]{1,0:T(8,128)(2,1)S(1)}, bf16[16,2048]{1,0:T(8,128)(2,1)S(1)}, u32[]{:S(2)}, u32[]{:S(2)}) collective-permute-start(bf16[16,2048]{1,0:T(8,128)(2,1)S(1)} %get-tuple-element.58), channel_id=1, source_target_pairs={{0,4},{1,5},{2,6},{3,7},{4,0},{5,1},{6,2},{7,3},{8,12},{9,13},{10,... | collective-permute-start | bytes 196616 | tf_op jit(solution)/shard_map/ppermute | solution.py:22
  81.8 8.5 %collective-permute-start.23 = (bf16[16,2048]{1,0:T(8,128)(2,1)S(1)}, bf16[16,2048]{1,0:T(8,128)(2,1)S(1)}, u32[]{:S(2)}, u32[]{:S(2)}) collective-permute-start(bf16[16,2048]{1,0:T(8,128)(2,1)S(1)} %get-tuple-element.23), channel_id=1, source_target_pairs={{0,12},{1,13},{2,14},{3,15},{4,8},{5,9},{6,10},{7,11},{8,20},{9,21... | collective-permute-start | bytes 196616 | tf_op jit(solution)/shard_map/ppermute | solution.py:55
  83.8 7.9 %collective-permute-start.22 = (bf16[16,2048]{1,0:T(8,128)(2,1)S(1)}, bf16[16,2048]{1,0:T(8,128)(2,1)S(1)}, u32[]{:S(2)}, u32[]{:S(2)}) collective-permute-start(bf16[16,2048]{1,0:T(8,128)(2,1)S(1)} %get-tuple-element.23), channel_id=1, source_target_pairs={{0,10},{1,11},{2,12},{3,13},{4,14},{5,15},{6,8},{7,9},{8,18},{9,19... | collective-permute-start | bytes 196616 | tf_op jit(solution)/shard_map/ppermute | solution.py:55
  83.9 7.8 %collective-permute-start.21 = (bf16[16,2048]{1,0:T(8,128)(2,1)S(1)}, bf16[16,2048]{1,0:T(8,128)(2,1)S(1)}, u32[]{:S(2)}, u32[]{:S(2)}) collective-permute-start(bf16[16,2048]{1,0:T(8,128)(2,1)S(1)} %get-tuple-element.23), channel_id=1, source_target_pairs={{0,8},{1,9},{2,10},{3,11},{4,12},{5,13},{6,14},{7,15},{8,16},{9,17... | collective-permute-start | bytes 196616 | tf_op jit(solution)/shard_map/ppermute | solution.py:55
  106.2 8.4 %collective-permute-start.28 = (bf16[16,2048]{1,0:T(8,128)(2,1)S(1)}, bf16[16,2048]{1,0:T(8,128)(2,1)S(1)}, u32[]{:S(2)}, u32[]{:S(2)}) collective-permute-start(bf16[16,2048]{1,0:T(8,128)(2,1)S(1)} %get-tuple-element.53), channel_id=1, source_target_pairs={{0,4},{1,5},{2,6},{3,7},{4,0},{5,1},{6,2},{7,3},{8,12},{9,13},{10,... | collective-permute-start | bytes 196616 | tf_op jit(solution)/shard_map/ppermute | solution.py:22
  117.0 7.4 %collective-permute-start.32 = (bf16[16,2048]{1,0:T(8,128)(2,1)S(1)}, bf16[16,2048]{1,0:T(8,128)(2,1)S(1)}, u32[]{:S(2)}, u32[]{:S(2)}) collective-permute-start(bf16[16,2048]{1,0:T(8,128)(2,1)S(1)} %get-tuple-element.19), channel_id=1, source_target_pairs={{0,12},{1,13},{2,14},{3,15},{4,8},{5,9},{6,10},{7,11},{8,20},{9,21... | collective-permute-start | bytes 196616 | tf_op jit(solution)/shard_map/ppermute | solution.py:55
  119.4 7.9 %collective-permute-start.31 = (bf16[16,2048]{1,0:T(8,128)(2,1)S(1)}, bf16[16,2048]{1,0:T(8,128)(2,1)S(1)}, u32[]{:S(2)}, u32[]{:S(2)}) collective-permute-start(bf16[16,2048]{1,0:T(8,128)(2,1)S(1)} %get-tuple-element.19), channel_id=1, source_target_pairs={{0,10},{1,11},{2,12},{3,13},{4,14},{5,15},{6,8},{7,9},{8,18},{9,19... | collective-permute-start | bytes 196616 | tf_op jit(solution)/shard_map/ppermute | solution.py:55
  119.4 7.9 %collective-permute-start.30 = (bf16[16,2048]{1,0:T(8,128)(2,1)S(1)}, bf16[16,2048]{1,0:T(8,128)(2,1)S(1)}, u32[]{:S(2)}, u32[]{:S(2)}) collective-permute-start(bf16[16,2048]{1,0:T(8,128)(2,1)S(1)} %get-tuple-element.19), channel_id=1, source_target_pairs={{0,8},{1,9},{2,10},{3,11},{4,12},{5,13},{6,14},{7,15},{8,16},{9,17... | collective-permute-start | bytes 196616 | tf_op jit(solution)/shard_map/ppermute | solution.py:55
  141.5 8.6 %collective-permute-start.37 = (bf16[16,2048]{1,0:T(8,128)(2,1)S(1)}, bf16[16,2048]{1,0:T(8,128)(2,1)S(1)}, u32[]{:S(2)}, u32[]{:S(2)}) collective-permute-start(bf16[16,2048]{1,0:T(8,128)(2,1)S(1)} %get-tuple-element.48), channel_id=1, source_target_pairs={{0,4},{1,5},{2,6},{3,7},{4,0},{5,1},{6,2},{7,3},{8,12},{9,13},{10,... | collective-permute-start | bytes 196616 | tf_op jit(solution)/shard_map/ppermute | solution.py:22
  142.8 7.3 %collective-permute-start.36 = (bf16[16,2048]{1,0:T(8,128)(2,1)S(1)}, bf16[16,2048]{1,0:T(8,128)(2,1)S(1)}, u32[]{:S(2)}, u32[]{:S(2)}) collective-permute-start(bf16[16,2048]{1,0:T(8,128)(2,1)S(1)} %get-tuple-element.46), channel_id=1, source_target_pairs={{0,6},{1,7},{2,0},{3,1},{4,2},{5,3},{6,4},{7,5},{8,14},{9,15},{10,... | collective-permute-start | bytes 196616 | tf_op jit(solution)/shard_map/ppermute | solution.py:22
  152.4 8.6 %collective-permute-start.41 = (bf16[16,2048]{1,0:T(8,128)(2,1)S(1)}, bf16[16,2048]{1,0:T(8,128)(2,1)S(1)}, u32[]{:S(2)}, u32[]{:S(2)}) collective-permute-start(bf16[16,2048]{1,0:T(8,128)(2,1)S(1)} %get-tuple-element.15), channel_id=1, source_target_pairs={{0,12},{1,13},{2,14},{3,15},{4,8},{5,9},{6,10},{7,11},{8,20},{9,21... | collective-permute-start | bytes 196616 | tf_op jit(solution)/shard_map/ppermute | solution.py:55
  154.4 7.9 %collective-permute-start.40 = (bf16[16,2048]{1,0:T(8,128)(2,1)S(1)}, bf16[16,2048]{1,0:T(8,128)(2,1)S(1)}, u32[]{:S(2)}, u32[]{:S(2)}) collective-permute-start(bf16[16,2048]{1,0:T(8,128)(2,1)S(1)} %get-tuple-element.15), channel_id=1, source_target_pairs={{0,10},{1,11},{2,12},{3,13},{4,14},{5,15},{6,8},{7,9},{8,18},{9,19... | collective-permute-start | bytes 196616 | tf_op jit(solution)/shard_map/ppermute | solution.py:55
  154.4 7.9 %collective-permute-start.39 = (bf16[16,2048]{1,0:T(8,128)(2,1)S(1)}, bf16[16,2048]{1,0:T(8,128)(2,1)S(1)}, u32[]{:S(2)}, u32[]{:S(2)}) collective-permute-start(bf16[16,2048]{1,0:T(8,128)(2,1)S(1)} %get-tuple-element.15), channel_id=1, source_target_pairs={{0,8},{1,9},{2,10},{3,11},{4,12},{5,13},{6,14},{7,15},{8,16},{9,17... | collective-permute-start | bytes 196616 | tf_op jit(solution)/shard_map/ppermute | solution.py:55
  176.5 7.0 %collective-permute-start.47 = (bf16[16,2048]{1,0:T(8,128)(2,1)S(1)}, bf16[16,2048]{1,0:T(8,128)(2,1)S(1)}, u32[]{:S(2)}, u32[]{:S(2)}) collective-permute-start(bf16[16,2048]{1,0:T(8,128)(2,1)S(1)} %get-tuple-element.42), channel_id=1, source_target_pairs={{0,2},{1,3},{2,4},{3,5},{4,6},{5,7},{6,0},{7,1},{8,10},{9,11},{10,... | collective-permute-start | bytes 196616 | tf_op jit(solution)/shard_map/ppermute | solution.py:22
  177.1 8.3 %collective-permute-start.46 = (bf16[16,2048]{1,0:T(8,128)(2,1)S(1)}, bf16[16,2048]{1,0:T(8,128)(2,1)S(1)}, u32[]{:S(2)}, u32[]{:S(2)}) collective-permute-start(bf16[16,2048]{1,0:T(8,128)(2,1)S(1)} %get-tuple-element.43), channel_id=1, source_target_pairs={{0,4},{1,5},{2,6},{3,7},{4,0},{5,1},{6,2},{7,3},{8,12},{9,13},{10,... | collective-permute-start | bytes 196616 | tf_op jit(solution)/shard_map/ppermute | solution.py:22
  188.5 7.2 %collective-permute-start.50 = (bf16[16,2048]{1,0:T(8,128)(2,1)S(1)}, bf16[16,2048]{1,0:T(8,128)(2,1)S(1)}, u32[]{:S(2)}, u32[]{:S(2)}) collective-permute-start(bf16[16,2048]{1,0:T(8,128)(2,1)S(1)} %get-tuple-element.11), channel_id=1, source_target_pairs={{0,12},{1,13},{2,14},{3,15},{4,8},{5,9},{6,10},{7,11},{8,20},{9,21... | collective-permute-start | bytes 196616 | tf_op jit(solution)/shard_map/ppermute | solution.py:55
  190.8 7.9 %collective-permute-start.49 = (bf16[16,2048]{1,0:T(8,128)(2,1)S(1)}, bf16[16,2048]{1,0:T(8,128)(2,1)S(1)}, u32[]{:S(2)}, u32[]{:S(2)}) collective-permute-start(bf16[16,2048]{1,0:T(8,128)(2,1)S(1)} %get-tuple-element.11), channel_id=1, source_target_pairs={{0,10},{1,11},{2,12},{3,13},{4,14},{5,15},{6,8},{7,9},{8,18},{9,19... | collective-permute-start | bytes 196616 | tf_op jit(solution)/shard_map/ppermute | solution.py:55
  190.8 7.9 %collective-permute-start.48 = (bf16[16,2048]{1,0:T(8,128)(2,1)S(1)}, bf16[16,2048]{1,0:T(8,128)(2,1)S(1)}, u32[]{:S(2)}, u32[]{:S(2)}) collective-permute-start(bf16[16,2048]{1,0:T(8,128)(2,1)S(1)} %get-tuple-element.11), channel_id=1, source_target_pairs={{0,8},{1,9},{2,10},{3,11},{4,12},{5,13},{6,14},{7,15},{8,16},{9,17... | collective-permute-start | bytes 196616 | tf_op jit(solution)/shard_map/ppermute | solution.py:55
  212.9 8.6 %collective-permute-start.55 = (bf16[16,2048]{1,0:T(8,128)(2,1)S(1)}, bf16[16,2048]{1,0:T(8,128)(2,1)S(1)}, u32[]{:S(2)}, u32[]{:S(2)}) collective-permute-start(bf16[16,2048]{1,0:T(8,128)(2,1)S(1)} %get-tuple-element.38), channel_id=1, source_target_pairs={{0,4},{1,5},{2,6},{3,7},{4,0},{5,1},{6,2},{7,3},{8,12},{9,13},{10,... | collective-permute-start | bytes 196616 | tf_op jit(solution)/shard_map/ppermute | solution.py:22
  214.1 7.5 %collective-permute-start.54 = (bf16[16,2048]{1,0:T(8,128)(2,1)S(1)}, bf16[16,2048]{1,0:T(8,128)(2,1)S(1)}, u32[]{:S(2)}, u32[]{:S(2)}) collective-permute-start(bf16[16,2048]{1,0:T(8,128)(2,1)S(1)} %get-tuple-element.36), channel_id=1, source_target_pairs={{0,6},{1,7},{2,0},{3,1},{4,2},{5,3},{6,4},{7,5},{8,14},{9,15},{10,... | collective-permute-start | bytes 196616 | tf_op jit(solution)/shard_map/ppermute | solution.py:22
  223.2 8.6 %collective-permute-start.59 = (bf16[16,2048]{1,0:T(8,128)(2,1)S(1)}, bf16[16,2048]{1,0:T(8,128)(2,1)S(1)}, u32[]{:S(2)}, u32[]{:S(2)}) collective-permute-start(bf16[16,2048]{1,0:T(8,128)(2,1)S(1)} %get-tuple-element.7), channel_id=1, source_target_pairs={{0,12},{1,13},{2,14},{3,15},{4,8},{5,9},{6,10},{7,11},{8,20},{9,21... | collective-permute-start | bytes 196616 | tf_op jit(solution)/shard_map/ppermute | solution.py:55
  225.3 7.9 %collective-permute-start.58 = (bf16[16,2048]{1,0:T(8,128)(2,1)S(1)}, bf16[16,2048]{1,0:T(8,128)(2,1)S(1)}, u32[]{:S(2)}, u32[]{:S(2)}) collective-permute-start(bf16[16,2048]{1,0:T(8,128)(2,1)S(1)} %get-tuple-element.7), channel_id=1, source_target_pairs={{0,10},{1,11},{2,12},{3,13},{4,14},{5,15},{6,8},{7,9},{8,18},{9,19... | collective-permute-start | bytes 196616 | tf_op jit(solution)/shard_map/ppermute | solution.py:55
  225.3 7.9 %collective-permute-start.57 = (bf16[16,2048]{1,0:T(8,128)(2,1)S(1)}, bf16[16,2048]{1,0:T(8,128)(2,1)S(1)}, u32[]{:S(2)}, u32[]{:S(2)}) collective-permute-start(bf16[16,2048]{1,0:T(8,128)(2,1)S(1)} %get-tuple-element.7), channel_id=1, source_target_pairs={{0,8},{1,9},{2,10},{3,11},{4,12},{5,13},{6,14},{7,15},{8,16},{9,17... | collective-permute-start | bytes 196616 | tf_op jit(solution)/shard_map/ppermute | solution.py:55
  247.8 8.3 %collective-permute-start.64 = (bf16[16,2048]{1,0:T(8,128)(2,1)S(1)}, bf16[16,2048]{1,0:T(8,128)(2,1)S(1)}, u32[]{:S(2)}, u32[]{:S(2)}) collective-permute-start(bf16[16,2048]{1,0:T(8,128)(2,1)S(1)} %get-tuple-element.33), channel_id=1, source_target_pairs={{0,4},{1,5},{2,6},{3,7},{4,0},{5,1},{6,2},{7,3},{8,12},{9,13},{10,... | collective-permute-start | bytes 196616 | tf_op jit(solution)/shard_map/ppermute | solution.py:22
  (40 other events, 244.6 us)

commit v10 on v9

--- a/solution.py
+++ b/solution.py
@@ -82,18 +82,29 @@
     tok_rows = tokens.shape[1]
     width = tokens.shape[2]
     table = route_table(routes[0], gates[0], experts)
-    table = gather_blocks(table, "expert")
+    high = table.astype(jnp.bfloat16)
+    low = (table - high.astype(jnp.float32)).astype(jnp.bfloat16)
+    packed = jnp.concatenate([high.reshape(-1), low.reshape(-1)])
+    extra = -(-packed.shape[0] // width)
+    packed = jnp.pad(packed, (0, extra * width - packed.shape[0])).reshape(extra, width)
+    first = gather_blocks(jnp.concatenate([tokens[0], packed]), "expert")
+    first_rows = first[:, :, :tok_rows]
+    packed = first[:, :, tok_rows:].reshape(2, chips, extra * width)[:, :, : 2 * table.size]
+    table = packed[:, :, : table.size].astype(jnp.float32) + packed[:, :, table.size :].astype(jnp.float32)
+    table = table.reshape((2, chips) + high.shape)
     mine = lax.dynamic_slice_in_dim(table, expert_index * local_experts, local_experts, axis=4)
     mixing = jnp.transpose(mine, (2, 4, 0, 1, 3)).reshape(MB, local_experts, 2 * chips * tok_rows)
     collected = jnp.zeros((MB, tok_rows, width), jnp.bfloat16)
-    blocks = gather_blocks(tokens[0], "expert")[0]
     last = MB + sections - 2
     for moment in range(MB + sections - 1):
         batch_index = moment - section_index
         active = (batch_index >= 0) & (batch_index < MB)
         clipped = jnp.clip(batch_index, 0, MB - 1)
         weight = lax.dynamic_index_in_dim(mixing, clipped, 0, keepdims=False)
-        rows = jnp.stack([blocks, core_swap(blocks, "expert")])
+        if moment == 0:
+            rows = first_rows
+        else:
+            rows = jnp.stack([blocks, core_swap(blocks, "expert")])
         values, normed = rms_normed(rows, gain)
         rows = normed.reshape(2 * chips * tok_rows, width)
         gate_part = jnp.einsum("td,edf->etf", rows, w_gate, preferred_element_type=jnp.float32)

time: 257 us -> 257 us (level)
    ppermute x27 -> x24, starting transfers between devices: 37.7 us -> 35.3 us  [chip_shift(): return lax.ppermute(array, axis, pairs)]
    ppermute x27 -> x24, waiting for transfers between devices: 38.7 us -> 39.3 us  [chip_shift(): return lax.ppermute(array, axis, pairs)]
    ppermute x15 -> x14, waiting for transfers between devices: 19.1 us -> 19.5 us  [core_swap(): return lax.ppermute(array, axis, [(i, i ^ 1) for i in range(count)])]
  transfers between devices with their start and end apart: 66 -> 62, of which waited for: 46 -> 44; matrix products, arithmetic and copies ran while one was open for 2% -> 1% of each run, Pallas kernels for 0% -> 0%
where the time goes in v10:
time: 257 us; the launch traced here: 256 us
  waiting for transfers between devices  93.9 us (37%)
  starting transfers between devices  74.4 us (29%)
  matrix products  72.6 us (28%)
  other arithmetic  10.3 us (4%)
  local copies, waits for them, and re-layouts  4.38 us (2%)
    dot_general x7, matrix products, on_device(): jnp.einsum('etf,efd->td', inner, w_down, preferred_element_type=jnp.float32)  46.2 us
    ppermute x24, waiting for transfers between devices, chip_shift(): return lax.ppermute(array, axis, pairs)  39.3 us
    ppermute x24, starting transfers between devices, to_next_section(): return lax.ppermute(array, ('section', 'expert'), pairs)  37.2 us
    ppermute x24, starting transfers between devices, chip_shift(): return lax.ppermute(array, axis, pairs)  35.3 us
    ppermute x24, waiting for transfers between devices, to_next_section(): return lax.ppermute(array, ('section', 'expert'), pairs)  35.1 us
    dot_general x7, matrix products, on_device(): jnp.einsum('td,edf->etf', rows, w_gate, preferred_element_type=jnp.float32)  26.4 us
    ppermute x14, waiting for transfers between devices, core_swap(): return lax.ppermute(array, axis, [(i, i ^ 1) for i in range(count)])  19.5 us
  transfers between devices with their start and end apart: 62, of which 44 were waited for; matrix products, arithmetic and copies ran while one was open for 1% of the time, Pallas kernels for 0%

profile of v10, /device:TPU:0, one launch (start us, length us, event | category | flops | bytes accessed | tf_op | source)
XLA Modules:
  0.0 256.3 jit_solution(6367427393202345758)
XLA Ops:
  3.5 5.1 %collective-permute-start.2 = (bf16[17,2048]{1,0:T(8,128)(2,1)S(1)}, bf16[17,2048]{1,0:T(8,128)(2,1)S(1)}, u32[]{:S(2)}, u32[]{:S(2)}) collective-permute-start(bf16[17,2048]{1,0:T(8,128)(2,1)S(1)} %get-tuple-element.69), channel_id=1, source_target_pairs={{0,6},{1,7},{2,0},{3,1},{4,2},{5,3},{6,4},{7,5},{8,14},{9,15},{10,... | collective-permute-start | bytes 208904 | tf_op jit(solution)/shard_map/ppermute | solution.py:22
  11.8 5.5 %collective-permute-done.1 = bf16[17,2048]{1,0:T(8,128)(2,1)S(1)} collective-permute-done((bf16[17,2048]{1,0:T(8,128)(2,1)S(1)}, bf16[17,2048]{1,0:T(8,128)(2,1)S(1)}, u32[]{:S(2)}, u32[]{:S(2)}) %collective-permute-start.1) | collective-permute-done | bytes 69664 | tf_op jit(solution)/shard_map/ppermute | solution.py:22
  21.1 3.8 %fusion.63 = f32[2,128,768]{2,1,0:T(8,128)S(1)} fusion(bf16[128,2048,1]{1,0,2:T(8,128)(2,1)S(1)} %bitcast.594, bf16[1,2,2048,768]{3,2,1,0:T(8,128)(2,1)} %param.9), kind=kOutput, calls=%fused_computation.49 | convolution fusion | flops 805306368 | bytes 7602176 | tf_op jit(solution)/shard_map/td,edf->etf/dot_general | solution.py:110
  25.5 6.6 %fusion.42 = f32[128,2048]{1,0:T(8,128)S(1)} fusion(bf16[1,2,768,2048]{3,2,1,0:T(8,128)(2,1)} %param.11, bf16[128,2048,1]{1,0,2:T(8,128)(2,1)S(1)} %bitcast.595, bf16[1,2,2048,768]{3,2,1,0:T(8,128)(2,1)} %param.10, f32[2,128,768]{2,1,0:T(8,128)S(1)} %fusion.63, f32[2,128]{1,0:T(2,128)S(1)} %get-tuple-element.76), kind=kOutput, calls=%fused_computation.42 | convolution fusion | flops 1611988992 | bytes 14943232 | tf_op jit(solution)/shard_map/etf,efd->td/dot_general | solution.py:113
  36.4 2.7 %collective-permute-start.5 = (bf16[16,2048]{1,0:T(8,128)(2,1)S(1)}, bf16[16,2048]{1,0:T(8,128)(2,1)S(1)}, u32[]{:S(2)}, u32[]{:S(2)}) collective-permute-start(bf16[16,2048]{1,0:T(8,128)(2,1)S(1)} %get-tuple-element.65), channel_id=1, source_target_pairs={{0,6},{1,7},{2,0},{3,1},{4,2},{5,3},{6,4},{7,5},{8,14},{9,15},{10,... | collective-permute-start | bytes 196616 | tf_op jit(solution)/shard_map/ppermute | solution.py:22
  43.2 4.0 %collective-permute-start.11 = (bf16[16,2048]{1,0:T(8,128)(2,1)S(1)}, bf16[16,2048]{1,0:T(8,128)(2,1)S(1)}, u32[]{:S(2)}, u32[]{:S(2)}) collective-permute-start(bf16[16,2048]{1,0:T(8,128)(2,1)S(1)} %get-tuple-element.27), channel_id=1, source_target_pairs={{0,14},{1,15},{2,8},{3,9},{4,10},{5,11},{6,12},{7,13},{8,22},{9,23... | collective-permute-start | bytes 196616 | tf_op jit(solution)/shard_map/ppermute | solution.py:55
  50.2 4.4 %collective-permute-done.10 = bf16[16,2048]{1,0:T(8,128)(2,1)S(1)} collective-permute-done((bf16[16,2048]{1,0:T(8,128)(2,1)S(1)}, bf16[16,2048]{1,0:T(8,128)(2,1)S(1)}, u32[]{:S(2)}, u32[]{:S(2)}) %collective-permute-start.10) | collective-permute-done | bytes 65568 | tf_op jit(solution)/shard_map/ppermute | solution.py:55
  58.0 3.8 %fusion.66 = f32[2,128,768]{2,1,0:T(8,128)S(1)} fusion(bf16[128,2048,1]{1,0,2:T(8,128)(2,1)S(1)} %bitcast.598, bf16[1,2,2048,768]{3,2,1,0:T(8,128)(2,1)} %param.9), kind=kOutput, calls=%fused_computation.50 | convolution fusion | flops 805306368 | bytes 7602176 | tf_op jit(solution)/shard_map/td,edf->etf/dot_general | solution.py:110
  61.7 6.6 %fusion.45 = f32[128,2048]{1,0:T(8,128)S(1)} fusion(bf16[1,2,768,2048]{3,2,1,0:T(8,128)(2,1)} %param.11, bf16[128,2048,1]{1,0,2:T(8,128)(2,1)S(1)} %bitcast.599, bf16[1,2,2048,768]{3,2,1,0:T(8,128)(2,1)} %param.10, f32[2,128,768]{2,1,0:T(8,128)S(1)} %fusion.66, f32[2,128]{1,0:T(2,128)S(1)} %get-tuple-element.75), kind=kOutput, calls=%fused_computation.43 | convolution fusion | flops 1611988992 | bytes 14943232 | tf_op jit(solution)/shard_map/etf,efd->td/dot_general | solution.py:113
  85.2 4.8 %collective-permute-done.19 = bf16[16,2048]{1,0:T(8,128)(2,1)S(1)} collective-permute-done((bf16[16,2048]{1,0:T(8,128)(2,1)S(1)}, bf16[16,2048]{1,0:T(8,128)(2,1)S(1)}, u32[]{:S(2)}, u32[]{:S(2)}) %collective-permute-start.19) | collective-permute-done | bytes 65568 | tf_op jit(solution)/shard_map/ppermute | solution.py:55
  93.3 3.8 %fusion.69 = f32[2,128,768]{2,1,0:T(8,128)S(1)} fusion(bf16[128,2048,1]{1,0,2:T(8,128)(2,1)S(1)} %bitcast.600, bf16[1,2,2048,768]{3,2,1,0:T(8,128)(2,1)} %param.9), kind=kOutput, calls=%fused_computation.51 | convolution fusion | flops 805306368 | bytes 7602176 | tf_op jit(solution)/shard_map/td,edf->etf/dot_general | solution.py:110
  97.1 6.6 %fusion.48 = f32[128,2048]{1,0:T(8,128)S(1)} fusion(bf16[1,2,768,2048]{3,2,1,0:T(8,128)(2,1)} %param.11, bf16[128,2048,1]{1,0,2:T(8,128)(2,1)S(1)} %bitcast.601, bf16[1,2,2048,768]{3,2,1,0:T(8,128)(2,1)} %param.10, f32[2,128,768]{2,1,0:T(8,128)S(1)} %fusion.69, f32[2,128]{1,0:T(2,128)S(1)} %get-tuple-element.74), kind=kOutput, calls=%fused_computation.44 | convolution fusion | flops 1611988992 | bytes 14943232 | tf_op jit(solution)/shard_map/etf,efd->td/dot_general | solution.py:113
  109.4 2.9 %collective-permute-done.25 = bf16[16,2048]{1,0:T(8,128)(2,1)S(1)} collective-permute-done((bf16[16,2048]{1,0:T(8,128)(2,1)S(1)}, bf16[16,2048]{1,0:T(8,128)(2,1)S(1)}, u32[]{:S(2)}, u32[]{:S(2)}) %collective-permute-start.25) | collective-permute-done | bytes 65568 | tf_op jit(solution)/shard_map/ppermute | solution.py:22
  120.3 3.5 %collective-permute-done.28 = bf16[16,2048]{1,0:T(8,128)(2,1)S(1)} collective-permute-done((bf16[16,2048]{1,0:T(8,128)(2,1)S(1)}, bf16[16,2048]{1,0:T(8,128)(2,1)S(1)}, u32[]{:S(2)}, u32[]{:S(2)}) %collective-permute-start.28) | collective-permute-done | bytes 65568 | tf_op jit(solution)/shard_map/ppermute | solution.py:55
  123.8 2.8 %collective-permute-done.27 = bf16[16,2048]{1,0:T(8,128)(2,1)S(1)} collective-permute-done((bf16[16,2048]{1,0:T(8,128)(2,1)S(1)}, bf16[16,2048]{1,0:T(8,128)(2,1)S(1)}, u32[]{:S(2)}, u32[]{:S(2)}) %collective-permute-start.27) | collective-permute-done | bytes 65568 | tf_op jit(solution)/shard_map/ppermute | solution.py:55
  128.7 3.8 %fusion.72 = f32[2,128,768]{2,1,0:T(8,128)S(1)} fusion(bf16[128,2048,1]{1,0,2:T(8,128)(2,1)S(1)} %bitcast.602, bf16[1,2,2048,768]{3,2,1,0:T(8,128)(2,1)} %param.9), kind=kOutput, calls=%fused_computation.52 | convolution fusion | flops 805306368 | bytes 7602176 | tf_op jit(solution)/shard_map/td,edf->etf/dot_general | solution.py:110
  132.5 6.6 %fusion.51 = f32[128,2048]{1,0:T(8,128)S(1)} fusion(bf16[1,2,768,2048]{3,2,1,0:T(8,128)(2,1)} %param.11, bf16[128,2048,1]{1,0,2:T(8,128)(2,1)S(1)} %bitcast.603, bf16[1,2,2048,768]{3,2,1,0:T(8,128)(2,1)} %param.10, f32[2,128,768]{2,1,0:T(8,128)S(1)} %fusion.72, f32[2,128]{1,0:T(2,128)S(1)} %copy-done.5), kind=kOutput, calls=%fused_computation.45 | convolution fusion | flops 1611988992 | bytes 14943232 | tf_op jit(solution)/shard_map/etf,efd->td/dot_general | solution.py:113
  142.0 2.7 %collective-permute-start.32 = (bf16[16,2048]{1,0:T(8,128)(2,1)S(1)}, bf16[16,2048]{1,0:T(8,128)(2,1)S(1)}, u32[]{:S(2)}, u32[]{:S(2)}) collective-permute-start(bf16[16,2048]{1,0:T(8,128)(2,1)S(1)} %get-tuple-element.50), channel_id=1, source_target_pairs={{0,6},{1,7},{2,0},{3,1},{4,2},{5,3},{6,4},{7,5},{8,14},{9,15},{10,... | collective-permute-start | bytes 196616 | tf_op jit(solution)/shard_map/ppermute | solution.py:22
  144.8 2.9 %collective-permute-done.34 = bf16[16,2048]{1,0:T(8,128)(2,1)S(1)} collective-permute-done((bf16[16,2048]{1,0:T(8,128)(2,1)S(1)}, bf16[16,2048]{1,0:T(8,128)(2,1)S(1)}, u32[]{:S(2)}, u32[]{:S(2)}) %collective-permute-start.34) | collective-permute-done | bytes 65568 | tf_op jit(solution)/shard_map/ppermute | solution.py:22
  156.2 4.1 %collective-permute-done.37 = bf16[16,2048]{1,0:T(8,128)(2,1)S(1)} collective-permute-done((bf16[16,2048]{1,0:T(8,128)(2,1)S(1)}, bf16[16,2048]{1,0:T(8,128)(2,1)S(1)}, u32[]{:S(2)}, u32[]{:S(2)}) %collective-permute-start.37) | collective-permute-done | bytes 65568 | tf_op jit(solution)/shard_map/ppermute | solution.py:55
  164.0 3.8 %fusion.75 = f32[2,128,768]{2,1,0:T(8,128)S(1)} fusion(bf16[128,2048,1]{1,0,2:T(8,128)(2,1)S(1)} %bitcast.604, bf16[1,2,2048,768]{3,2,1,0:T(8,128)(2,1)} %param.9), kind=kOutput, calls=%fused_computation.53 | convolution fusion | flops 805306368 | bytes 7602176 | tf_op jit(solution)/shard_map/td,edf->etf/dot_general | solution.py:110
  167.7 6.6 %fusion.54 = f32[128,2048]{1,0:T(8,128)S(1)} fusion(bf16[1,2,768,2048]{3,2,1,0:T(8,128)(2,1)} %param.11, bf16[128,2048,1]{1,0,2:T(8,128)(2,1)S(1)} %bitcast.605, bf16[1,2,2048,768]{3,2,1,0:T(8,128)(2,1)} %param.10, f32[2,128,768]{2,1,0:T(8,128)S(1)} %fusion.75, f32[2,128]{1,0:T(2,128)S(1)} %copy-done.4), kind=kOutput, calls=%fused_computation.46 | convolution fusion | flops 1611988992 | bytes 14943232 | tf_op jit(solution)/shard_map/etf,efd->td/dot_general | solution.py:113
  180.2 2.9 %collective-permute-done.43 = bf16[16,2048]{1,0:T(8,128)(2,1)S(1)} collective-permute-done((bf16[16,2048]{1,0:T(8,128)(2,1)S(1)}, bf16[16,2048]{1,0:T(8,128)(2,1)S(1)}, u32[]{:S(2)}, u32[]{:S(2)}) %collective-permute-start.43) | collective-permute-done | bytes 65568 | tf_op jit(solution)/shard_map/ppermute | solution.py:22
  195.1 2.9 %collective-permute-done.45 = bf16[16,2048]{1,0:T(8,128)(2,1)S(1)} collective-permute-done((bf16[16,2048]{1,0:T(8,128)(2,1)S(1)}, bf16[16,2048]{1,0:T(8,128)(2,1)S(1)}, u32[]{:S(2)}, u32[]{:S(2)}) %collective-permute-start.45) | collective-permute-done | bytes 65568 | tf_op jit(solution)/shard_map/ppermute | solution.py:55
  200.1 3.8 %fusion.78 = f32[2,128,768]{2,1,0:T(8,128)S(1)} fusion(bf16[128,2048,1]{1,0,2:T(8,128)(2,1)S(1)} %bitcast.606, bf16[1,2,2048,768]{3,2,1,0:T(8,128)(2,1)} %param.9), kind=kOutput, calls=%fused_computation.54 | convolution fusion | flops 805306368 | bytes 7602176 | tf_op jit(solution)/shard_map/td,edf->etf/dot_general | solution.py:110
  203.9 6.6 %fusion.57 = f32[128,2048]{1,0:T(8,128)S(1)} fusion(bf16[1,2,768,2048]{3,2,1,0:T(8,128)(2,1)} %param.11, bf16[128,2048,1]{1,0,2:T(8,128)(2,1)S(1)} %bitcast.607, bf16[1,2,2048,768]{3,2,1,0:T(8,128)(2,1)} %param.10, f32[2,128,768]{2,1,0:T(8,128)S(1)} %fusion.78, f32[2,128]{1,0:T(2,128)S(1)} %get-tuple-element.71), kind=kOutput, calls=%fused_computation.47 | convolution fusion | flops 1611988992 | bytes 14943232 | tf_op jit(solution)/shard_map/etf,efd->td/dot_general | solution.py:113
  213.5 2.6 %collective-permute-start.50 = (bf16[16,2048]{1,0:T(8,128)(2,1)S(1)}, bf16[16,2048]{1,0:T(8,128)(2,1)S(1)}, u32[]{:S(2)}, u32[]{:S(2)}) collective-permute-start(bf16[16,2048]{1,0:T(8,128)(2,1)S(1)} %get-tuple-element.40), channel_id=1, source_target_pairs={{0,6},{1,7},{2,0},{3,1},{4,2},{5,3},{6,4},{7,5},{8,14},{9,15},{10,... | collective-permute-start | bytes 196616 | tf_op jit(solution)/shard_map/ppermute | solution.py:22
  216.2 2.9 %collective-permute-done.52 = bf16[16,2048]{1,0:T(8,128)(2,1)S(1)} collective-permute-done((bf16[16,2048]{1,0:T(8,128)(2,1)S(1)}, bf16[16,2048]{1,0:T(8,128)(2,1)S(1)}, u32[]{:S(2)}, u32[]{:S(2)}) %collective-permute-start.52) | collective-permute-done | bytes 65568 | tf_op jit(solution)/shard_map/ppermute | solution.py:22
  227.1 4.2 %collective-permute-done.55 = bf16[16,2048]{1,0:T(8,128)(2,1)S(1)} collective-permute-done((bf16[16,2048]{1,0:T(8,128)(2,1)S(1)}, bf16[16,2048]{1,0:T(8,128)(2,1)S(1)}, u32[]{:S(2)}, u32[]{:S(2)}) %collective-permute-start.55) | collective-permute-done | bytes 65568 | tf_op jit(solution)/shard_map/ppermute | solution.py:55
  234.8 3.8 %fusion.81 = f32[2,128,768]{2,1,0:T(8,128)S(1)} fusion(bf16[128,2048,1]{1,0,2:T(8,128)(2,1)S(1)} %bitcast.596, bf16[1,2,2048,768]{3,2,1,0:T(8,128)(2,1)} %param.9), kind=kOutput, calls=%fused_computation.55 | convolution fusion | flops 805306368 | bytes 7602176 | tf_op jit(solution)/shard_map/td,edf->etf/dot_general | solution.py:110
  238.6 6.6 %fusion.60 = f32[128,2048]{1,0:T(8,128)S(1)} fusion(bf16[1,2,768,2048]{3,2,1,0:T(8,128)(2,1)} %param.11, bf16[128,2048,1]{1,0,2:T(8,128)(2,1)S(1)} %bitcast.597, bf16[1,2,2048,768]{3,2,1,0:T(8,128)(2,1)} %param.10, f32[2,128,768]{2,1,0:T(8,128)S(1)} %fusion.81, f32[2,128]{1,0:T(2,128)S(1)} %get-tuple-element.70), kind=kOutput, calls=%fused_computation.48 | convolution fusion | flops 1611988992 | bytes 14943232 | tf_op jit(solution)/shard_map/etf,efd->td/dot_general | solution.py:113
  250.9 2.9 %collective-permute-done.61 = bf16[16,2048]{1,0:T(8,128)(2,1)S(1)} collective-permute-done((bf16[16,2048]{1,0:T(8,128)(2,1)S(1)}, bf16[16,2048]{1,0:T(8,128)(2,1)S(1)}, u32[]{:S(2)}, u32[]{:S(2)}) %collective-permute-start.61) | collective-permute-done | bytes 65568 | tf_op jit(solution)/shard_map/ppermute | solution.py:22
  (215 shorter events, 119.2 us)
Async XLA Ops:
  3.5 8.3 %collective-permute-start.2 = (bf16[17,2048]{1,0:T(8,128)(2,1)S(1)}, bf16[17,2048]{1,0:T(8,128)(2,1)S(1)}, u32[]{:S(2)}, u32[]{:S(2)}) collective-permute-start(bf16[17,2048]{1,0:T(8,128)(2,1)S(1)} %get-tuple-element.69), channel_id=1, source_target_pairs={{0,6},{1,7},{2,0},{3,1},{4,2},{5,3},{6,4},{7,5},{8,14},{9,15},{10,... | collective-permute-start | bytes 208904 | tf_op jit(solution)/shard_map/ppermute | solution.py:22
  8.6 8.7 %collective-permute-start.1 = (bf16[17,2048]{1,0:T(8,128)(2,1)S(1)}, bf16[17,2048]{1,0:T(8,128)(2,1)S(1)}, u32[]{:S(2)}, u32[]{:S(2)}) collective-permute-start(bf16[17,2048]{1,0:T(8,128)(2,1)S(1)} %get-tuple-element.69), channel_id=1, source_target_pairs={{0,4},{1,5},{2,6},{3,7},{4,0},{5,1},{6,2},{7,3},{8,12},{9,13},{10,... | collective-permute-start | bytes 208904 | tf_op jit(solution)/shard_map/ppermute | solution.py:22
  8.6 8.7 %collective-permute-start = (bf16[17,2048]{1,0:T(8,128)(2,1)S(1)}, bf16[17,2048]{1,0:T(8,128)(2,1)S(1)}, u32[]{:S(2)}, u32[]{:S(2)}) collective-permute-start(bf16[17,2048]{1,0:T(8,128)(2,1)S(1)} %get-tuple-element.69), channel_id=1, source_target_pairs={{0,2},{1,3},{2,4},{3,5},{4,6},{5,7},{6,0},{7,1},{8,10},{9,11},{10,... | collective-permute-start | bytes 208904 | tf_op jit(solution)/shard_map/ppermute | solution.py:22
  34.3 8.3 %collective-permute-start.6 = (bf16[16,2048]{1,0:T(8,128)(2,1)S(1)}, bf16[16,2048]{1,0:T(8,128)(2,1)S(1)}, u32[]{:S(2)}, u32[]{:S(2)}) collective-permute-start(bf16[16,2048]{1,0:T(8,128)(2,1)S(1)} %get-tuple-element.67), channel_id=1, source_target_pairs={{0,4},{1,5},{2,6},{3,7},{4,0},{5,1},{6,2},{7,3},{8,12},{9,13},{10,... | collective-permute-start | bytes 196616 | tf_op jit(solution)/shard_map/ppermute | solution.py:22
  43.2 7.0 %collective-permute-start.11 = (bf16[16,2048]{1,0:T(8,128)(2,1)S(1)}, bf16[16,2048]{1,0:T(8,128)(2,1)S(1)}, u32[]{:S(2)}, u32[]{:S(2)}) collective-permute-start(bf16[16,2048]{1,0:T(8,128)(2,1)S(1)} %get-tuple-element.27), channel_id=1, source_target_pairs={{0,14},{1,15},{2,8},{3,9},{4,10},{5,11},{6,12},{7,13},{8,22},{9,23... | collective-permute-start | bytes 196616 | tf_op jit(solution)/shard_map/ppermute | solution.py:55
  47.2 7.4 %collective-permute-start.10 = (bf16[16,2048]{1,0:T(8,128)(2,1)S(1)}, bf16[16,2048]{1,0:T(8,128)(2,1)S(1)}, u32[]{:S(2)}, u32[]{:S(2)}) collective-permute-start(bf16[16,2048]{1,0:T(8,128)(2,1)S(1)} %get-tuple-element.27), channel_id=1, source_target_pairs={{0,12},{1,13},{2,14},{3,15},{4,8},{5,9},{6,10},{7,11},{8,20},{9,21... | collective-permute-start | bytes 196616 | tf_op jit(solution)/shard_map/ppermute | solution.py:55
  47.9 8.0 %collective-permute-start.9 = (bf16[16,2048]{1,0:T(8,128)(2,1)S(1)}, bf16[16,2048]{1,0:T(8,128)(2,1)S(1)}, u32[]{:S(2)}, u32[]{:S(2)}) collective-permute-start(bf16[16,2048]{1,0:T(8,128)(2,1)S(1)} %get-tuple-element.27), channel_id=1, source_target_pairs={{0,10},{1,11},{2,12},{3,13},{4,14},{5,15},{6,8},{7,9},{8,18},{9,19... | collective-permute-start | bytes 196616 | tf_op jit(solution)/shard_map/ppermute | solution.py:55
  48.9 7.0 %collective-permute-start.8 = (bf16[16,2048]{1,0:T(8,128)(2,1)S(1)}, bf16[16,2048]{1,0:T(8,128)(2,1)S(1)}, u32[]{:S(2)}, u32[]{:S(2)}) collective-permute-start(bf16[16,2048]{1,0:T(8,128)(2,1)S(1)} %get-tuple-element.27), channel_id=1, source_target_pairs={{0,8},{1,9},{2,10},{3,11},{4,12},{5,13},{6,14},{7,15},{8,16},{9,17... | collective-permute-start | bytes 196616 | tf_op jit(solution)/shard_map/ppermute | solution.py:55
  71.9 7.0 %collective-permute-start.15 = (bf16[16,2048]{1,0:T(8,128)(2,1)S(1)}, bf16[16,2048]{1,0:T(8,128)(2,1)S(1)}, u32[]{:S(2)}, u32[]{:S(2)}) collective-permute-start(bf16[16,2048]{1,0:T(8,128)(2,1)S(1)} %get-tuple-element.62), channel_id=1, source_target_pairs={{0,4},{1,5},{2,6},{3,7},{4,0},{5,1},{6,2},{7,3},{8,12},{9,13},{10,... | collective-permute-start | bytes 196616 | tf_op jit(solution)/shard_map/ppermute | solution.py:22
  81.0 9.0 %collective-permute-start.19 = (bf16[16,2048]{1,0:T(8,128)(2,1)S(1)}, bf16[16,2048]{1,0:T(8,128)(2,1)S(1)}, u32[]{:S(2)}, u32[]{:S(2)}) collective-permute-start(bf16[16,2048]{1,0:T(8,128)(2,1)S(1)} %get-tuple-element.23), channel_id=1, source_target_pairs={{0,12},{1,13},{2,14},{3,15},{4,8},{5,9},{6,10},{7,11},{8,20},{9,21... | collective-permute-start | bytes 196616 | tf_op jit(solution)/shard_map/ppermute | solution.py:55
  83.4 7.9 %collective-permute-start.18 = (bf16[16,2048]{1,0:T(8,128)(2,1)S(1)}, bf16[16,2048]{1,0:T(8,128)(2,1)S(1)}, u32[]{:S(2)}, u32[]{:S(2)}) collective-permute-start(bf16[16,2048]{1,0:T(8,128)(2,1)S(1)} %get-tuple-element.23), channel_id=1, source_target_pairs={{0,10},{1,11},{2,12},{3,13},{4,14},{5,15},{6,8},{7,9},{8,18},{9,19... | collective-permute-start | bytes 196616 | tf_op jit(solution)/shard_map/ppermute | solution.py:55
  83.4 7.9 %collective-permute-start.17 = (bf16[16,2048]{1,0:T(8,128)(2,1)S(1)}, bf16[16,2048]{1,0:T(8,128)(2,1)S(1)}, u32[]{:S(2)}, u32[]{:S(2)}) collective-permute-start(bf16[16,2048]{1,0:T(8,128)(2,1)S(1)} %get-tuple-element.23), channel_id=1, source_target_pairs={{0,8},{1,9},{2,10},{3,11},{4,12},{5,13},{6,14},{7,15},{8,16},{9,17... | collective-permute-start | bytes 196616 | tf_op jit(solution)/shard_map/ppermute | solution.py:55
  105.5 8.6 %collective-permute-start.24 = (bf16[16,2048]{1,0:T(8,128)(2,1)S(1)}, bf16[16,2048]{1,0:T(8,128)(2,1)S(1)}, u32[]{:S(2)}, u32[]{:S(2)}) collective-permute-start(bf16[16,2048]{1,0:T(8,128)(2,1)S(1)} %get-tuple-element.57), channel_id=1, source_target_pairs={{0,4},{1,5},{2,6},{3,7},{4,0},{5,1},{6,2},{7,3},{8,12},{9,13},{10,... | collective-permute-start | bytes 196616 | tf_op jit(solution)/shard_map/ppermute | solution.py:22
  116.3 7.5 %collective-permute-start.28 = (bf16[16,2048]{1,0:T(8,128)(2,1)S(1)}, bf16[16,2048]{1,0:T(8,128)(2,1)S(1)}, u32[]{:S(2)}, u32[]{:S(2)}) collective-permute-start(bf16[16,2048]{1,0:T(8,128)(2,1)S(1)} %get-tuple-element.19), channel_id=1, source_target_pairs={{0,12},{1,13},{2,14},{3,15},{4,8},{5,9},{6,10},{7,11},{8,20},{9,21... | collective-permute-start | bytes 196616 | tf_op jit(solution)/shard_map/ppermute | solution.py:55
  118.8 7.9 %collective-permute-start.27 = (bf16[16,2048]{1,0:T(8,128)(2,1)S(1)}, bf16[16,2048]{1,0:T(8,128)(2,1)S(1)}, u32[]{:S(2)}, u32[]{:S(2)}) collective-permute-start(bf16[16,2048]{1,0:T(8,128)(2,1)S(1)} %get-tuple-element.19), channel_id=1, source_target_pairs={{0,10},{1,11},{2,12},{3,13},{4,14},{5,15},{6,8},{7,9},{8,18},{9,19... | collective-permute-start | bytes 196616 | tf_op jit(solution)/shard_map/ppermute | solution.py:55
  118.8 7.9 %collective-permute-start.26 = (bf16[16,2048]{1,0:T(8,128)(2,1)S(1)}, bf16[16,2048]{1,0:T(8,128)(2,1)S(1)}, u32[]{:S(2)}, u32[]{:S(2)}) collective-permute-start(bf16[16,2048]{1,0:T(8,128)(2,1)S(1)} %get-tuple-element.19), channel_id=1, source_target_pairs={{0,8},{1,9},{2,10},{3,11},{4,12},{5,13},{6,14},{7,15},{8,16},{9,17... | collective-permute-start | bytes 196616 | tf_op jit(solution)/shard_map/ppermute | solution.py:55
  140.9 8.6 %collective-permute-start.33 = (bf16[16,2048]{1,0:T(8,128)(2,1)S(1)}, bf16[16,2048]{1,0:T(8,128)(2,1)S(1)}, u32[]{:S(2)}, u32[]{:S(2)}) collective-permute-start(bf16[16,2048]{1,0:T(8,128)(2,1)S(1)} %get-tuple-element.52), channel_id=1, source_target_pairs={{0,4},{1,5},{2,6},{3,7},{4,0},{5,1},{6,2},{7,3},{8,12},{9,13},{10,... | collective-permute-start | bytes 196616 | tf_op jit(solution)/shard_map/ppermute | solution.py:22
  142.0 7.5 %collective-permute-start.32 = (bf16[16,2048]{1,0:T(8,128)(2,1)S(1)}, bf16[16,2048]{1,0:T(8,128)(2,1)S(1)}, u32[]{:S(2)}, u32[]{:S(2)}) collective-permute-start(bf16[16,2048]{1,0:T(8,128)(2,1)S(1)} %get-tuple-element.50), channel_id=1, source_target_pairs={{0,6},{1,7},{2,0},{3,1},{4,2},{5,3},{6,4},{7,5},{8,14},{9,15},{10,... | collective-permute-start | bytes 196616 | tf_op jit(solution)/shard_map/ppermute | solution.py:22
  151.8 8.6 %collective-permute-start.37 = (bf16[16,2048]{1,0:T(8,128)(2,1)S(1)}, bf16[16,2048]{1,0:T(8,128)(2,1)S(1)}, u32[]{:S(2)}, u32[]{:S(2)}) collective-permute-start(bf16[16,2048]{1,0:T(8,128)(2,1)S(1)} %get-tuple-element.15), channel_id=1, source_target_pairs={{0,12},{1,13},{2,14},{3,15},{4,8},{5,9},{6,10},{7,11},{8,20},{9,21... | collective-permute-start | bytes 196616 | tf_op jit(solution)/shard_map/ppermute | solution.py:55
  154.0 7.9 %collective-permute-start.36 = (bf16[16,2048]{1,0:T(8,128)(2,1)S(1)}, bf16[16,2048]{1,0:T(8,128)(2,1)S(1)}, u32[]{:S(2)}, u32[]{:S(2)}) collective-permute-start(bf16[16,2048]{1,0:T(8,128)(2,1)S(1)} %get-tuple-element.15), channel_id=1, source_target_pairs={{0,10},{1,11},{2,12},{3,13},{4,14},{5,15},{6,8},{7,9},{8,18},{9,19... | collective-permute-start | bytes 196616 | tf_op jit(solution)/shard_map/ppermute | solution.py:55
  154.0 7.9 %collective-permute-start.35 = (bf16[16,2048]{1,0:T(8,128)(2,1)S(1)}, bf16[16,2048]{1,0:T(8,128)(2,1)S(1)}, u32[]{:S(2)}, u32[]{:S(2)}) collective-permute-start(bf16[16,2048]{1,0:T(8,128)(2,1)S(1)} %get-tuple-element.15), channel_id=1, source_target_pairs={{0,8},{1,9},{2,10},{3,11},{4,12},{5,13},{6,14},{7,15},{8,16},{9,17... | collective-permute-start | bytes 196616 | tf_op jit(solution)/shard_map/ppermute | solution.py:55
  176.1 7.0 %collective-permute-start.43 = (bf16[16,2048]{1,0:T(8,128)(2,1)S(1)}, bf16[16,2048]{1,0:T(8,128)(2,1)S(1)}, u32[]{:S(2)}, u32[]{:S(2)}) collective-permute-start(bf16[16,2048]{1,0:T(8,128)(2,1)S(1)} %get-tuple-element.46), channel_id=1, source_target_pairs={{0,2},{1,3},{2,4},{3,5},{4,6},{5,7},{6,0},{7,1},{8,10},{9,11},{10,... | collective-permute-start | bytes 196616 | tf_op jit(solution)/shard_map/ppermute | solution.py:22
  176.6 8.4 %collective-permute-start.42 = (bf16[16,2048]{1,0:T(8,128)(2,1)S(1)}, bf16[16,2048]{1,0:T(8,128)(2,1)S(1)}, u32[]{:S(2)}, u32[]{:S(2)}) collective-permute-start(bf16[16,2048]{1,0:T(8,128)(2,1)S(1)} %get-tuple-element.47), channel_id=1, source_target_pairs={{0,4},{1,5},{2,6},{3,7},{4,0},{5,1},{6,2},{7,3},{8,12},{9,13},{10,... | collective-permute-start | bytes 196616 | tf_op jit(solution)/shard_map/ppermute | solution.py:22
  188.0 7.1 %collective-permute-start.46 = (bf16[16,2048]{1,0:T(8,128)(2,1)S(1)}, bf16[16,2048]{1,0:T(8,128)(2,1)S(1)}, u32[]{:S(2)}, u32[]{:S(2)}) collective-permute-start(bf16[16,2048]{1,0:T(8,128)(2,1)S(1)} %get-tuple-element.11), channel_id=1, source_target_pairs={{0,12},{1,13},{2,14},{3,15},{4,8},{5,9},{6,10},{7,11},{8,20},{9,21... | collective-permute-start | bytes 196616 | tf_op jit(solution)/shard_map/ppermute | solution.py:55
  190.2 7.9 %collective-permute-start.45 = (bf16[16,2048]{1,0:T(8,128)(2,1)S(1)}, bf16[16,2048]{1,0:T(8,128)(2,1)S(1)}, u32[]{:S(2)}, u32[]{:S(2)}) collective-permute-start(bf16[16,2048]{1,0:T(8,128)(2,1)S(1)} %get-tuple-element.11), channel_id=1, source_target_pairs={{0,10},{1,11},{2,12},{3,13},{4,14},{5,15},{6,8},{7,9},{8,18},{9,19... | collective-permute-start | bytes 196616 | tf_op jit(solution)/shard_map/ppermute | solution.py:55
  190.2 7.9 %collective-permute-start.44 = (bf16[16,2048]{1,0:T(8,128)(2,1)S(1)}, bf16[16,2048]{1,0:T(8,128)(2,1)S(1)}, u32[]{:S(2)}, u32[]{:S(2)}) collective-permute-start(bf16[16,2048]{1,0:T(8,128)(2,1)S(1)} %get-tuple-element.11), channel_id=1, source_target_pairs={{0,8},{1,9},{2,10},{3,11},{4,12},{5,13},{6,14},{7,15},{8,16},{9,17... | collective-permute-start | bytes 196616 | tf_op jit(solution)/shard_map/ppermute | solution.py:55
  212.3 8.6 %collective-permute-start.51 = (bf16[16,2048]{1,0:T(8,128)(2,1)S(1)}, bf16[16,2048]{1,0:T(8,128)(2,1)S(1)}, u32[]{:S(2)}, u32[]{:S(2)}) collective-permute-start(bf16[16,2048]{1,0:T(8,128)(2,1)S(1)} %get-tuple-element.42), channel_id=1, source_target_pairs={{0,4},{1,5},{2,6},{3,7},{4,0},{5,1},{6,2},{7,3},{8,12},{9,13},{10,... | collective-permute-start | bytes 196616 | tf_op jit(solution)/shard_map/ppermute | solution.py:22
  213.5 7.4 %collective-permute-start.50 = (bf16[16,2048]{1,0:T(8,128)(2,1)S(1)}, bf16[16,2048]{1,0:T(8,128)(2,1)S(1)}, u32[]{:S(2)}, u32[]{:S(2)}) collective-permute-start(bf16[16,2048]{1,0:T(8,128)(2,1)S(1)} %get-tuple-element.40), channel_id=1, source_target_pairs={{0,6},{1,7},{2,0},{3,1},{4,2},{5,3},{6,4},{7,5},{8,14},{9,15},{10,... | collective-permute-start | bytes 196616 | tf_op jit(solution)/shard_map/ppermute | solution.py:22
  222.8 8.5 %collective-permute-start.55 = (bf16[16,2048]{1,0:T(8,128)(2,1)S(1)}, bf16[16,2048]{1,0:T(8,128)(2,1)S(1)}, u32[]{:S(2)}, u32[]{:S(2)}) collective-permute-start(bf16[16,2048]{1,0:T(8,128)(2,1)S(1)} %get-tuple-element.7), channel_id=1, source_target_pairs={{0,12},{1,13},{2,14},{3,15},{4,8},{5,9},{6,10},{7,11},{8,20},{9,21... | collective-permute-start | bytes 196616 | tf_op jit(solution)/shard_map/ppermute | solution.py:55
  224.9 7.9 %collective-permute-start.54 = (bf16[16,2048]{1,0:T(8,128)(2,1)S(1)}, bf16[16,2048]{1,0:T(8,128)(2,1)S(1)}, u32[]{:S(2)}, u32[]{:S(2)}) collective-permute-start(bf16[16,2048]{1,0:T(8,128)(2,1)S(1)} %get-tuple-element.7), channel_id=1, source_target_pairs={{0,10},{1,11},{2,12},{3,13},{4,14},{5,15},{6,8},{7,9},{8,18},{9,19... | collective-permute-start | bytes 196616 | tf_op jit(solution)/shard_map/ppermute | solution.py:55
  224.9 7.9 %collective-permute-start.53 = (bf16[16,2048]{1,0:T(8,128)(2,1)S(1)}, bf16[16,2048]{1,0:T(8,128)(2,1)S(1)}, u32[]{:S(2)}, u32[]{:S(2)}) collective-permute-start(bf16[16,2048]{1,0:T(8,128)(2,1)S(1)} %get-tuple-element.7), channel_id=1, source_target_pairs={{0,8},{1,9},{2,10},{3,11},{4,12},{5,13},{6,14},{7,15},{8,16},{9,17... | collective-permute-start | bytes 196616 | tf_op jit(solution)/shard_map/ppermute | solution.py:55
  247.2 8.4 %collective-permute-start.60 = (bf16[16,2048]{1,0:T(8,128)(2,1)S(1)}, bf16[16,2048]{1,0:T(8,128)(2,1)S(1)}, u32[]{:S(2)}, u32[]{:S(2)}) collective-permute-start(bf16[16,2048]{1,0:T(8,128)(2,1)S(1)} %get-tuple-element.37), channel_id=1, source_target_pairs={{0,4},{1,5},{2,6},{3,7},{4,0},{5,1},{6,2},{7,3},{8,12},{9,13},{10,... | collective-permute-start | bytes 196616 | tf_op jit(solution)/shard_map/ppermute | solution.py:22
  (36 other events, 223.7 us)

commit v11 on v10

--- a/solution.py
+++ b/solution.py
@@ -118,7 +118,8 @@
         if moment < last:
             upcoming = lax.dynamic_index_in_dim(tokens, min(moment + 1, MB - 1), 0, keepdims=False)
             outgoing = jnp.where(section_index == sections - 1, upcoming, produced)
-            blocks = jnp.stack([to_next_section(outgoing, k) for k in range(chips)])
+            sent = {k: to_next_section(outgoing, k) for k in range(chips - 1, -1, -1)}
+            blocks = jnp.stack([sent[k] for k in range(chips)])
     return collected[None]
 
 

time: 257 us -> 257 us (level)
  no operation moved by 1% of the time
where the time goes in v11:
time: 257 us; the launch traced here: 256 us
  waiting for transfers between devices  93.9 us (37%)
  starting transfers between devices  74.4 us (29%)
  matrix products  72.6 us (28%)
  other arithmetic  10.3 us (4%)
  local copies, waits for them, and re-layouts  4.38 us (2%)
    dot_general x7, matrix products, on_device(): jnp.einsum('etf,efd->td', inner, w_down, preferred_element_type=jnp.float32)  46.2 us
    ppermute x24, waiting for transfers between devices, chip_shift(): return lax.ppermute(array, axis, pairs)  39.3 us
    ppermute x24, starting transfers between devices, to_next_section(): return lax.ppermute(array, ('section', 'expert'), pairs)  37.2 us
    ppermute x24, starting transfers between devices, chip_shift(): return lax.ppermute(array, axis, pairs)  35.3 us
    ppermute x24, waiting for transfers between devices, to_next_section(): return lax.ppermute(array, ('section', 'expert'), pairs)  35.1 us
    dot_general x7, matrix products, on_device(): jnp.einsum('td,edf->etf', rows, w_gate, preferred_element_type=jnp.float32)  26.4 us
    ppermute x14, waiting for transfers between devices, core_swap(): return lax.ppermute(array, axis, [(i, i ^ 1) for i in range(count)])  19.5 us
  transfers between devices with their start and end apart: 62, of which 44 were waited for; matrix products, arithmetic and copies ran while one was open for 1% of the time, Pallas kernels for 0%

profile of v11, /device:TPU:0, one launch (start us, length us, event | category | flops | bytes accessed | tf_op | source)
XLA Modules:
  0.0 256.3 jit_solution(6367427393202345758)
XLA Ops:
  3.5 5.1 %collective-permute-start.2 = (bf16[17,2048]{1,0:T(8,128)(2,1)S(1)}, bf16[17,2048]{1,0:T(8,128)(2,1)S(1)}, u32[]{:S(2)}, u32[]{:S(2)}) collective-permute-start(bf16[17,2048]{1,0:T(8,128)(2,1)S(1)} %get-tuple-element.69), channel_id=1, source_target_pairs={{0,6},{1,7},{2,0},{3,1},{4,2},{5,3},{6,4},{7,5},{8,14},{9,15},{10,... | collective-permute-start | bytes 208904 | tf_op jit(solution)/shard_map/ppermute | solution.py:22
  11.8 5.5 %collective-permute-done.1 = bf16[17,2048]{1,0:T(8,128)(2,1)S(1)} collective-permute-done((bf16[17,2048]{1,0:T(8,128)(2,1)S(1)}, bf16[17,2048]{1,0:T(8,128)(2,1)S(1)}, u32[]{:S(2)}, u32[]{:S(2)}) %collective-permute-start.1) | collective-permute-done | bytes 69664 | tf_op jit(solution)/shard_map/ppermute | solution.py:22
  21.1 3.8 %fusion.63 = f32[2,128,768]{2,1,0:T(8,128)S(1)} fusion(bf16[128,2048,1]{1,0,2:T(8,128)(2,1)S(1)} %bitcast.594, bf16[1,2,2048,768]{3,2,1,0:T(8,128)(2,1)} %param.9), kind=kOutput, calls=%fused_computation.49 | convolution fusion | flops 805306368 | bytes 7602176 | tf_op jit(solution)/shard_map/td,edf->etf/dot_general | solution.py:110
  25.5 6.6 %fusion.42 = f32[128,2048]{1,0:T(8,128)S(1)} fusion(bf16[1,2,768,2048]{3,2,1,0:T(8,128)(2,1)} %param.11, bf16[128,2048,1]{1,0,2:T(8,128)(2,1)S(1)} %bitcast.595, bf16[1,2,2048,768]{3,2,1,0:T(8,128)(2,1)} %param.10, f32[2,128,768]{2,1,0:T(8,128)S(1)} %fusion.63, f32[2,128]{1,0:T(2,128)S(1)} %get-tuple-element.76), kind=kOutput, calls=%fused_computation.42 | convolution fusion | flops 1611988992 | bytes 14943232 | tf_op jit(solution)/shard_map/etf,efd->td/dot_general | solution.py:113
  36.4 2.7 %collective-permute-start.5 = (bf16[16,2048]{1,0:T(8,128)(2,1)S(1)}, bf16[16,2048]{1,0:T(8,128)(2,1)S(1)}, u32[]{:S(2)}, u32[]{:S(2)}) collective-permute-start(bf16[16,2048]{1,0:T(8,128)(2,1)S(1)} %get-tuple-element.65), channel_id=1, source_target_pairs={{0,6},{1,7},{2,0},{3,1},{4,2},{5,3},{6,4},{7,5},{8,14},{9,15},{10,... | collective-permute-start | bytes 196616 | tf_op jit(solution)/shard_map/ppermute | solution.py:22
  43.2 4.0 %collective-permute-start.11 = (bf16[16,2048]{1,0:T(8,128)(2,1)S(1)}, bf16[16,2048]{1,0:T(8,128)(2,1)S(1)}, u32[]{:S(2)}, u32[]{:S(2)}) collective-permute-start(bf16[16,2048]{1,0:T(8,128)(2,1)S(1)} %get-tuple-element.27), channel_id=1, source_target_pairs={{0,14},{1,15},{2,8},{3,9},{4,10},{5,11},{6,12},{7,13},{8,22},{9,23... | collective-permute-start | bytes 196616 | tf_op jit(solution)/shard_map/ppermute | solution.py:55
  50.2 4.4 %collective-permute-done.10 = bf16[16,2048]{1,0:T(8,128)(2,1)S(1)} collective-permute-done((bf16[16,2048]{1,0:T(8,128)(2,1)S(1)}, bf16[16,2048]{1,0:T(8,128)(2,1)S(1)}, u32[]{:S(2)}, u32[]{:S(2)}) %collective-permute-start.10) | collective-permute-done | bytes 65568 | tf_op jit(solution)/shard_map/ppermute | solution.py:55
  58.0 3.8 %fusion.66 = f32[2,128,768]{2,1,0:T(8,128)S(1)} fusion(bf16[128,2048,1]{1,0,2:T(8,128)(2,1)S(1)} %bitcast.598, bf16[1,2,2048,768]{3,2,1,0:T(8,128)(2,1)} %param.9), kind=kOutput, calls=%fused_computation.50 | convolution fusion | flops 805306368 | bytes 7602176 | tf_op jit(solution)/shard_map/td,edf->etf/dot_general | solution.py:110
  61.7 6.6 %fusion.45 = f32[128,2048]{1,0:T(8,128)S(1)} fusion(bf16[1,2,768,2048]{3,2,1,0:T(8,128)(2,1)} %param.11, bf16[128,2048,1]{1,0,2:T(8,128)(2,1)S(1)} %bitcast.599, bf16[1,2,2048,768]{3,2,1,0:T(8,128)(2,1)} %param.10, f32[2,128,768]{2,1,0:T(8,128)S(1)} %fusion.66, f32[2,128]{1,0:T(2,128)S(1)} %get-tuple-element.75), kind=kOutput, calls=%fused_computation.43 | convolution fusion | flops 1611988992 | bytes 14943232 | tf_op jit(solution)/shard_map/etf,efd->td/dot_general | solution.py:113
  85.2 4.8 %collective-permute-done.19 = bf16[16,2048]{1,0:T(8,128)(2,1)S(1)} collective-permute-done((bf16[16,2048]{1,0:T(8,128)(2,1)S(1)}, bf16[16,2048]{1,0:T(8,128)(2,1)S(1)}, u32[]{:S(2)}, u32[]{:S(2)}) %collective-permute-start.19) | collective-permute-done | bytes 65568 | tf_op jit(solution)/shard_map/ppermute | solution.py:55
  93.3 3.8 %fusion.69 = f32[2,128,768]{2,1,0:T(8,128)S(1)} fusion(bf16[128,2048,1]{1,0,2:T(8,128)(2,1)S(1)} %bitcast.600, bf16[1,2,2048,768]{3,2,1,0:T(8,128)(2,1)} %param.9), kind=kOutput, calls=%fused_computation.51 | convolution fusion | flops 805306368 | bytes 7602176 | tf_op jit(solution)/shard_map/td,edf->etf/dot_general | solution.py:110
  97.1 6.6 %fusion.48 = f32[128,2048]{1,0:T(8,128)S(1)} fusion(bf16[1,2,768,2048]{3,2,1,0:T(8,128)(2,1)} %param.11, bf16[128,2048,1]{1,0,2:T(8,128)(2,1)S(1)} %bitcast.601, bf16[1,2,2048,768]{3,2,1,0:T(8,128)(2,1)} %param.10, f32[2,128,768]{2,1,0:T(8,128)S(1)} %fusion.69, f32[2,128]{1,0:T(2,128)S(1)} %get-tuple-element.74), kind=kOutput, calls=%fused_computation.44 | convolution fusion | flops 1611988992 | bytes 14943232 | tf_op jit(solution)/shard_map/etf,efd->td/dot_general | solution.py:113
  109.4 2.9 %collective-permute-done.25 = bf16[16,2048]{1,0:T(8,128)(2,1)S(1)} collective-permute-done((bf16[16,2048]{1,0:T(8,128)(2,1)S(1)}, bf16[16,2048]{1,0:T(8,128)(2,1)S(1)}, u32[]{:S(2)}, u32[]{:S(2)}) %collective-permute-start.25) | collective-permute-done | bytes 65568 | tf_op jit(solution)/shard_map/ppermute | solution.py:22
  120.3 3.5 %collective-permute-done.28 = bf16[16,2048]{1,0:T(8,128)(2,1)S(1)} collective-permute-done((bf16[16,2048]{1,0:T(8,128)(2,1)S(1)}, bf16[16,2048]{1,0:T(8,128)(2,1)S(1)}, u32[]{:S(2)}, u32[]{:S(2)}) %collective-permute-start.28) | collective-permute-done | bytes 65568 | tf_op jit(solution)/shard_map/ppermute | solution.py:55
  123.8 2.8 %collective-permute-done.27 = bf16[16,2048]{1,0:T(8,128)(2,1)S(1)} collective-permute-done((bf16[16,2048]{1,0:T(8,128)(2,1)S(1)}, bf16[16,2048]{1,0:T(8,128)(2,1)S(1)}, u32[]{:S(2)}, u32[]{:S(2)}) %collective-permute-start.27) | collective-permute-done | bytes 65568 | tf_op jit(solution)/shard_map/ppermute | solution.py:55
  128.7 3.8 %fusion.72 = f32[2,128,768]{2,1,0:T(8,128)S(1)} fusion(bf16[128,2048,1]{1,0,2:T(8,128)(2,1)S(1)} %bitcast.602, bf16[1,2,2048,768]{3,2,1,0:T(8,128)(2,1)} %param.9), kind=kOutput, calls=%fused_computation.52 | convolution fusion | flops 805306368 | bytes 7602176 | tf_op jit(solution)/shard_map/td,edf->etf/dot_general | solution.py:110
  132.5 6.6 %fusion.51 = f32[128,2048]{1,0:T(8,128)S(1)} fusion(bf16[1,2,768,2048]{3,2,1,0:T(8,128)(2,1)} %param.11, bf16[128,2048,1]{1,0,2:T(8,128)(2,1)S(1)} %bitcast.603, bf16[1,2,2048,768]{3,2,1,0:T(8,128)(2,1)} %param.10, f32[2,128,768]{2,1,0:T(8,128)S(1)} %fusion.72, f32[2,128]{1,0:T(2,128)S(1)} %copy-done.5), kind=kOutput, calls=%fused_computation.45 | convolution fusion | flops 1611988992 | bytes 14943232 | tf_op jit(solution)/shard_map/etf,efd->td/dot_general | solution.py:113
  142.0 2.7 %collective-permute-start.32 = (bf16[16,2048]{1,0:T(8,128)(2,1)S(1)}, bf16[16,2048]{1,0:T(8,128)(2,1)S(1)}, u32[]{:S(2)}, u32[]{:S(2)}) collective-permute-start(bf16[16,2048]{1,0:T(8,128)(2,1)S(1)} %get-tuple-element.50), channel_id=1, source_target_pairs={{0,6},{1,7},{2,0},{3,1},{4,2},{5,3},{6,4},{7,5},{8,14},{9,15},{10,... | collective-permute-start | bytes 196616 | tf_op jit(solution)/shard_map/ppermute | solution.py:22
  144.8 2.9 %collective-permute-done.34 = bf16[16,2048]{1,0:T(8,128)(2,1)S(1)} collective-permute-done((bf16[16,2048]{1,0:T(8,128)(2,1)S(1)}, bf16[16,2048]{1,0:T(8,128)(2,1)S(1)}, u32[]{:S(2)}, u32[]{:S(2)}) %collective-permute-start.34) | collective-permute-done | bytes 65568 | tf_op jit(solution)/shard_map/ppermute | solution.py:22
  156.2 4.1 %collective-permute-done.37 = bf16[16,2048]{1,0:T(8,128)(2,1)S(1)} collective-permute-done((bf16[16,2048]{1,0:T(8,128)(2,1)S(1)}, bf16[16,2048]{1,0:T(8,128)(2,1)S(1)}, u32[]{:S(2)}, u32[]{:S(2)}) %collective-permute-start.37) | collective-permute-done | bytes 65568 | tf_op jit(solution)/shard_map/ppermute | solution.py:55
  164.0 3.8 %fusion.75 = f32[2,128,768]{2,1,0:T(8,128)S(1)} fusion(bf16[128,2048,1]{1,0,2:T(8,128)(2,1)S(1)} %bitcast.604, bf16[1,2,2048,768]{3,2,1,0:T(8,128)(2,1)} %param.9), kind=kOutput, calls=%fused_computation.53 | convolution fusion | flops 805306368 | bytes 7602176 | tf_op jit(solution)/shard_map/td,edf->etf/dot_general | solution.py:110
  167.7 6.6 %fusion.54 = f32[128,2048]{1,0:T(8,128)S(1)} fusion(bf16[1,2,768,2048]{3,2,1,0:T(8,128)(2,1)} %param.11, bf16[128,2048,1]{1,0,2:T(8,128)(2,1)S(1)} %bitcast.605, bf16[1,2,2048,768]{3,2,1,0:T(8,128)(2,1)} %param.10, f32[2,128,768]{2,1,0:T(8,128)S(1)} %fusion.75, f32[2,128]{1,0:T(2,128)S(1)} %copy-done.4), kind=kOutput, calls=%fused_computation.46 | convolution fusion | flops 1611988992 | bytes 14943232 | tf_op jit(solution)/shard_map/etf,efd->td/dot_general | solution.py:113
  180.2 2.9 %collective-permute-done.43 = bf16[16,2048]{1,0:T(8,128)(2,1)S(1)} collective-permute-done((bf16[16,2048]{1,0:T(8,128)(2,1)S(1)}, bf16[16,2048]{1,0:T(8,128)(2,1)S(1)}, u32[]{:S(2)}, u32[]{:S(2)}) %collective-permute-start.43) | collective-permute-done | bytes 65568 | tf_op jit(solution)/shard_map/ppermute | solution.py:22
  195.1 2.9 %collective-permute-done.45 = bf16[16,2048]{1,0:T(8,128)(2,1)S(1)} collective-permute-done((bf16[16,2048]{1,0:T(8,128)(2,1)S(1)}, bf16[16,2048]{1,0:T(8,128)(2,1)S(1)}, u32[]{:S(2)}, u32[]{:S(2)}) %collective-permute-start.45) | collective-permute-done | bytes 65568 | tf_op jit(solution)/shard_map/ppermute | solution.py:55
  200.1 3.8 %fusion.78 = f32[2,128,768]{2,1,0:T(8,128)S(1)} fusion(bf16[128,2048,1]{1,0,2:T(8,128)(2,1)S(1)} %bitcast.606, bf16[1,2,2048,768]{3,2,1,0:T(8,128)(2,1)} %param.9), kind=kOutput, calls=%fused_computation.54 | convolution fusion | flops 805306368 | bytes 7602176 | tf_op jit(solution)/shard_map/td,edf->etf/dot_general | solution.py:110
  203.9 6.6 %fusion.57 = f32[128,2048]{1,0:T(8,128)S(1)} fusion(bf16[1,2,768,2048]{3,2,1,0:T(8,128)(2,1)} %param.11, bf16[128,2048,1]{1,0,2:T(8,128)(2,1)S(1)} %bitcast.607, bf16[1,2,2048,768]{3,2,1,0:T(8,128)(2,1)} %param.10, f32[2,128,768]{2,1,0:T(8,128)S(1)} %fusion.78, f32[2,128]{1,0:T(2,128)S(1)} %get-tuple-element.71), kind=kOutput, calls=%fused_computation.47 | convolution fusion | flops 1611988992 | bytes 14943232 | tf_op jit(solution)/shard_map/etf,efd->td/dot_general | solution.py:113
  213.5 2.6 %collective-permute-start.50 = (bf16[16,2048]{1,0:T(8,128)(2,1)S(1)}, bf16[16,2048]{1,0:T(8,128)(2,1)S(1)}, u32[]{:S(2)}, u32[]{:S(2)}) collective-permute-start(bf16[16,2048]{1,0:T(8,128)(2,1)S(1)} %get-tuple-element.40), channel_id=1, source_target_pairs={{0,6},{1,7},{2,0},{3,1},{4,2},{5,3},{6,4},{7,5},{8,14},{9,15},{10,... | collective-permute-start | bytes 196616 | tf_op jit(solution)/shard_map/ppermute | solution.py:22
  216.2 2.9 %collective-permute-done.52 = bf16[16,2048]{1,0:T(8,128)(2,1)S(1)} collective-permute-done((bf16[16,2048]{1,0:T(8,128)(2,1)S(1)}, bf16[16,2048]{1,0:T(8,128)(2,1)S(1)}, u32[]{:S(2)}, u32[]{:S(2)}) %collective-permute-start.52) | collective-permute-done | bytes 65568 | tf_op jit(solution)/shard_map/ppermute | solution.py:22
  227.1 4.2 %collective-permute-done.55 = bf16[16,2048]{1,0:T(8,128)(2,1)S(1)} collective-permute-done((bf16[16,2048]{1,0:T(8,128)(2,1)S(1)}, bf16[16,2048]{1,0:T(8,128)(2,1)S(1)}, u32[]{:S(2)}, u32[]{:S(2)}) %collective-permute-start.55) | collective-permute-done | bytes 65568 | tf_op jit(solution)/shard_map/ppermute | solution.py:55
  234.8 3.8 %fusion.81 = f32[2,128,768]{2,1,0:T(8,128)S(1)} fusion(bf16[128,2048,1]{1,0,2:T(8,128)(2,1)S(1)} %bitcast.596, bf16[1,2,2048,768]{3,2,1,0:T(8,128)(2,1)} %param.9), kind=kOutput, calls=%fused_computation.55 | convolution fusion | flops 805306368 | bytes 7602176 | tf_op jit(solution)/shard_map/td,edf->etf/dot_general | solution.py:110
  238.6 6.6 %fusion.60 = f32[128,2048]{1,0:T(8,128)S(1)} fusion(bf16[1,2,768,2048]{3,2,1,0:T(8,128)(2,1)} %param.11, bf16[128,2048,1]{1,0,2:T(8,128)(2,1)S(1)} %bitcast.597, bf16[1,2,2048,768]{3,2,1,0:T(8,128)(2,1)} %param.10, f32[2,128,768]{2,1,0:T(8,128)S(1)} %fusion.81, f32[2,128]{1,0:T(2,128)S(1)} %get-tuple-element.70), kind=kOutput, calls=%fused_computation.48 | convolution fusion | flops 1611988992 | bytes 14943232 | tf_op jit(solution)/shard_map/etf,efd->td/dot_general | solution.py:113
  250.9 2.9 %collective-permute-done.61 = bf16[16,2048]{1,0:T(8,128)(2,1)S(1)} collective-permute-done((bf16[16,2048]{1,0:T(8,128)(2,1)S(1)}, bf16[16,2048]{1,0:T(8,128)(2,1)S(1)}, u32[]{:S(2)}, u32[]{:S(2)}) %collective-permute-start.61) | collective-permute-done | bytes 65568 | tf_op jit(solution)/shard_map/ppermute | solution.py:22
  (215 shorter events, 119.2 us)
Async XLA Ops:
  3.5 8.3 %collective-permute-start.2 = (bf16[17,2048]{1,0:T(8,128)(2,1)S(1)}, bf16[17,2048]{1,0:T(8,128)(2,1)S(1)}, u32[]{:S(2)}, u32[]{:S(2)}) collective-permute-start(bf16[17,2048]{1,0:T(8,128)(2,1)S(1)} %get-tuple-element.69), channel_id=1, source_target_pairs={{0,6},{1,7},{2,0},{3,1},{4,2},{5,3},{6,4},{7,5},{8,14},{9,15},{10,... | collective-permute-start | bytes 208904 | tf_op jit(solution)/shard_map/ppermute | solution.py:22
  8.6 8.7 %collective-permute-start.1 = (bf16[17,2048]{1,0:T(8,128)(2,1)S(1)}, bf16[17,2048]{1,0:T(8,128)(2,1)S(1)}, u32[]{:S(2)}, u32[]{:S(2)}) collective-permute-start(bf16[17,2048]{1,0:T(8,128)(2,1)S(1)} %get-tuple-element.69), channel_id=1, source_target_pairs={{0,4},{1,5},{2,6},{3,7},{4,0},{5,1},{6,2},{7,3},{8,12},{9,13},{10,... | collective-permute-start | bytes 208904 | tf_op jit(solution)/shard_map/ppermute | solution.py:22
  8.6 8.7 %collective-permute-start = (bf16[17,2048]{1,0:T(8,128)(2,1)S(1)}, bf16[17,2048]{1,0:T(8,128)(2,1)S(1)}, u32[]{:S(2)}, u32[]{:S(2)}) collective-permute-start(bf16[17,2048]{1,0:T(8,128)(2,1)S(1)} %get-tuple-element.69), channel_id=1, source_target_pairs={{0,2},{1,3},{2,4},{3,5},{4,6},{5,7},{6,0},{7,1},{8,10},{9,11},{10,... | collective-permute-start | bytes 208904 | tf_op jit(solution)/shard_map/ppermute | solution.py:22
  34.3 8.3 %collective-permute-start.6 = (bf16[16,2048]{1,0:T(8,128)(2,1)S(1)}, bf16[16,2048]{1,0:T(8,128)(2,1)S(1)}, u32[]{:S(2)}, u32[]{:S(2)}) collective-permute-start(bf16[16,2048]{1,0:T(8,128)(2,1)S(1)} %get-tuple-element.67), channel_id=1, source_target_pairs={{0,4},{1,5},{2,6},{3,7},{4,0},{5,1},{6,2},{7,3},{8,12},{9,13},{10,... | collective-permute-start | bytes 196616 | tf_op jit(solution)/shard_map/ppermute | solution.py:22
  43.2 7.0 %collective-permute-start.11 = (bf16[16,2048]{1,0:T(8,128)(2,1)S(1)}, bf16[16,2048]{1,0:T(8,128)(2,1)S(1)}, u32[]{:S(2)}, u32[]{:S(2)}) collective-permute-start(bf16[16,2048]{1,0:T(8,128)(2,1)S(1)} %get-tuple-element.27), channel_id=1, source_target_pairs={{0,14},{1,15},{2,8},{3,9},{4,10},{5,11},{6,12},{7,13},{8,22},{9,23... | collective-permute-start | bytes 196616 | tf_op jit(solution)/shard_map/ppermute | solution.py:55
  47.2 7.4 %collective-permute-start.10 = (bf16[16,2048]{1,0:T(8,128)(2,1)S(1)}, bf16[16,2048]{1,0:T(8,128)(2,1)S(1)}, u32[]{:S(2)}, u32[]{:S(2)}) collective-permute-start(bf16[16,2048]{1,0:T(8,128)(2,1)S(1)} %get-tuple-element.27), channel_id=1, source_target_pairs={{0,12},{1,13},{2,14},{3,15},{4,8},{5,9},{6,10},{7,11},{8,20},{9,21... | collective-permute-start | bytes 196616 | tf_op jit(solution)/shard_map/ppermute | solution.py:55
  47.9 8.0 %collective-permute-start.9 = (bf16[16,2048]{1,0:T(8,128)(2,1)S(1)}, bf16[16,2048]{1,0:T(8,128)(2,1)S(1)}, u32[]{:S(2)}, u32[]{:S(2)}) collective-permute-start(bf16[16,2048]{1,0:T(8,128)(2,1)S(1)} %get-tuple-element.27), channel_id=1, source_target_pairs={{0,10},{1,11},{2,12},{3,13},{4,14},{5,15},{6,8},{7,9},{8,18},{9,19... | collective-permute-start | bytes 196616 | tf_op jit(solution)/shard_map/ppermute | solution.py:55
  48.9 7.0 %collective-permute-start.8 = (bf16[16,2048]{1,0:T(8,128)(2,1)S(1)}, bf16[16,2048]{1,0:T(8,128)(2,1)S(1)}, u32[]{:S(2)}, u32[]{:S(2)}) collective-permute-start(bf16[16,2048]{1,0:T(8,128)(2,1)S(1)} %get-tuple-element.27), channel_id=1, source_target_pairs={{0,8},{1,9},{2,10},{3,11},{4,12},{5,13},{6,14},{7,15},{8,16},{9,17... | collective-permute-start | bytes 196616 | tf_op jit(solution)/shard_map/ppermute | solution.py:55
  71.9 7.0 %collective-permute-start.15 = (bf16[16,2048]{1,0:T(8,128)(2,1)S(1)}, bf16[16,2048]{1,0:T(8,128)(2,1)S(1)}, u32[]{:S(2)}, u32[]{:S(2)}) collective-permute-start(bf16[16,2048]{1,0:T(8,128)(2,1)S(1)} %get-tuple-element.62), channel_id=1, source_target_pairs={{0,4},{1,5},{2,6},{3,7},{4,0},{5,1},{6,2},{7,3},{8,12},{9,13},{10,... | collective-permute-start | bytes 196616 | tf_op jit(solution)/shard_map/ppermute | solution.py:22
  81.0 9.0 %collective-permute-start.19 = (bf16[16,2048]{1,0:T(8,128)(2,1)S(1)}, bf16[16,2048]{1,0:T(8,128)(2,1)S(1)}, u32[]{:S(2)}, u32[]{:S(2)}) collective-permute-start(bf16[16,2048]{1,0:T(8,128)(2,1)S(1)} %get-tuple-element.23), channel_id=1, source_target_pairs={{0,12},{1,13},{2,14},{3,15},{4,8},{5,9},{6,10},{7,11},{8,20},{9,21... | collective-permute-start | bytes 196616 | tf_op jit(solution)/shard_map/ppermute | solution.py:55
  83.4 7.9 %collective-permute-start.18 = (bf16[16,2048]{1,0:T(8,128)(2,1)S(1)}, bf16[16,2048]{1,0:T(8,128)(2,1)S(1)}, u32[]{:S(2)}, u32[]{:S(2)}) collective-permute-start(bf16[16,2048]{1,0:T(8,128)(2,1)S(1)} %get-tuple-element.23), channel_id=1, source_target_pairs={{0,10},{1,11},{2,12},{3,13},{4,14},{5,15},{6,8},{7,9},{8,18},{9,19... | collective-permute-start | bytes 196616 | tf_op jit(solution)/shard_map/ppermute | solution.py:55
  83.4 7.9 %collective-permute-start.17 = (bf16[16,2048]{1,0:T(8,128)(2,1)S(1)}, bf16[16,2048]{1,0:T(8,128)(2,1)S(1)}, u32[]{:S(2)}, u32[]{:S(2)}) collective-permute-start(bf16[16,2048]{1,0:T(8,128)(2,1)S(1)} %get-tuple-element.23), channel_id=1, source_target_pairs={{0,8},{1,9},{2,10},{3,11},{4,12},{5,13},{6,14},{7,15},{8,16},{9,17... | collective-permute-start | bytes 196616 | tf_op jit(solution)/shard_map/ppermute | solution.py:55
  105.5 8.6 %collective-permute-start.24 = (bf16[16,2048]{1,0:T(8,128)(2,1)S(1)}, bf16[16,2048]{1,0:T(8,128)(2,1)S(1)}, u32[]{:S(2)}, u32[]{:S(2)}) collective-permute-start(bf16[16,2048]{1,0:T(8,128)(2,1)S(1)} %get-tuple-element.57), channel_id=1, source_target_pairs={{0,4},{1,5},{2,6},{3,7},{4,0},{5,1},{6,2},{7,3},{8,12},{9,13},{10,... | collective-permute-start | bytes 196616 | tf_op jit(solution)/shard_map/ppermute | solution.py:22
  116.3 7.5 %collective-permute-start.28 = (bf16[16,2048]{1,0:T(8,128)(2,1)S(1)}, bf16[16,2048]{1,0:T(8,128)(2,1)S(1)}, u32[]{:S(2)}, u32[]{:S(2)}) collective-permute-start(bf16[16,2048]{1,0:T(8,128)(2,1)S(1)} %get-tuple-element.19), channel_id=1, source_target_pairs={{0,12},{1,13},{2,14},{3,15},{4,8},{5,9},{6,10},{7,11},{8,20},{9,21... | collective-permute-start | bytes 196616 | tf_op jit(solution)/shard_map/ppermute | solution.py:55
  118.8 7.9 %collective-permute-start.27 = (bf16[16,2048]{1,0:T(8,128)(2,1)S(1)}, bf16[16,2048]{1,0:T(8,128)(2,1)S(1)}, u32[]{:S(2)}, u32[]{:S(2)}) collective-permute-start(bf16[16,2048]{1,0:T(8,128)(2,1)S(1)} %get-tuple-element.19), channel_id=1, source_target_pairs={{0,10},{1,11},{2,12},{3,13},{4,14},{5,15},{6,8},{7,9},{8,18},{9,19... | collective-permute-start | bytes 196616 | tf_op jit(solution)/shard_map/ppermute | solution.py:55
  118.8 7.9 %collective-permute-start.26 = (bf16[16,2048]{1,0:T(8,128)(2,1)S(1)}, bf16[16,2048]{1,0:T(8,128)(2,1)S(1)}, u32[]{:S(2)}, u32[]{:S(2)}) collective-permute-start(bf16[16,2048]{1,0:T(8,128)(2,1)S(1)} %get-tuple-element.19), channel_id=1, source_target_pairs={{0,8},{1,9},{2,10},{3,11},{4,12},{5,13},{6,14},{7,15},{8,16},{9,17... | collective-permute-start | bytes 196616 | tf_op jit(solution)/shard_map/ppermute | solution.py:55
  140.9 8.6 %collective-permute-start.33 = (bf16[16,2048]{1,0:T(8,128)(2,1)S(1)}, bf16[16,2048]{1,0:T(8,128)(2,1)S(1)}, u32[]{:S(2)}, u32[]{:S(2)}) collective-permute-start(bf16[16,2048]{1,0:T(8,128)(2,1)S(1)} %get-tuple-element.52), channel_id=1, source_target_pairs={{0,4},{1,5},{2,6},{3,7},{4,0},{5,1},{6,2},{7,3},{8,12},{9,13},{10,... | collective-permute-start | bytes 196616 | tf_op jit(solution)/shard_map/ppermute | solution.py:22
  142.0 7.5 %collective-permute-start.32 = (bf16[16,2048]{1,0:T(8,128)(2,1)S(1)}, bf16[16,2048]{1,0:T(8,128)(2,1)S(1)}, u32[]{:S(2)}, u32[]{:S(2)}) collective-permute-start(bf16[16,2048]{1,0:T(8,128)(2,1)S(1)} %get-tuple-element.50), channel_id=1, source_target_pairs={{0,6},{1,7},{2,0},{3,1},{4,2},{5,3},{6,4},{7,5},{8,14},{9,15},{10,... | collective-permute-start | bytes 196616 | tf_op jit(solution)/shard_map/ppermute | solution.py:22
  151.8 8.6 %collective-permute-start.37 = (bf16[16,2048]{1,0:T(8,128)(2,1)S(1)}, bf16[16,2048]{1,0:T(8,128)(2,1)S(1)}, u32[]{:S(2)}, u32[]{:S(2)}) collective-permute-start(bf16[16,2048]{1,0:T(8,128)(2,1)S(1)} %get-tuple-element.15), channel_id=1, source_target_pairs={{0,12},{1,13},{2,14},{3,15},{4,8},{5,9},{6,10},{7,11},{8,20},{9,21... | collective-permute-start | bytes 196616 | tf_op jit(solution)/shard_map/ppermute | solution.py:55
  154.0 7.9 %collective-permute-start.36 = (bf16[16,2048]{1,0:T(8,128)(2,1)S(1)}, bf16[16,2048]{1,0:T(8,128)(2,1)S(1)}, u32[]{:S(2)}, u32[]{:S(2)}) collective-permute-start(bf16[16,2048]{1,0:T(8,128)(2,1)S(1)} %get-tuple-element.15), channel_id=1, source_target_pairs={{0,10},{1,11},{2,12},{3,13},{4,14},{5,15},{6,8},{7,9},{8,18},{9,19... | collective-permute-start | bytes 196616 | tf_op jit(solution)/shard_map/ppermute | solution.py:55
  154.0 7.9 %collective-permute-start.35 = (bf16[16,2048]{1,0:T(8,128)(2,1)S(1)}, bf16[16,2048]{1,0:T(8,128)(2,1)S(1)}, u32[]{:S(2)}, u32[]{:S(2)}) collective-permute-start(bf16[16,2048]{1,0:T(8,128)(2,1)S(1)} %get-tuple-element.15), channel_id=1, source_target_pairs={{0,8},{1,9},{2,10},{3,11},{4,12},{5,13},{6,14},{7,15},{8,16},{9,17... | collective-permute-start | bytes 196616 | tf_op jit(solution)/shard_map/ppermute | solution.py:55
  176.1 7.0 %collective-permute-start.43 = (bf16[16,2048]{1,0:T(8,128)(2,1)S(1)}, bf16[16,2048]{1,0:T(8,128)(2,1)S(1)}, u32[]{:S(2)}, u32[]{:S(2)}) collective-permute-start(bf16[16,2048]{1,0:T(8,128)(2,1)S(1)} %get-tuple-element.46), channel_id=1, source_target_pairs={{0,2},{1,3},{2,4},{3,5},{4,6},{5,7},{6,0},{7,1},{8,10},{9,11},{10,... | collective-permute-start | bytes 196616 | tf_op jit(solution)/shard_map/ppermute | solution.py:22
  176.6 8.4 %collective-permute-start.42 = (bf16[16,2048]{1,0:T(8,128)(2,1)S(1)}, bf16[16,2048]{1,0:T(8,128)(2,1)S(1)}, u32[]{:S(2)}, u32[]{:S(2)}) collective-permute-start(bf16[16,2048]{1,0:T(8,128)(2,1)S(1)} %get-tuple-element.47), channel_id=1, source_target_pairs={{0,4},{1,5},{2,6},{3,7},{4,0},{5,1},{6,2},{7,3},{8,12},{9,13},{10,... | collective-permute-start | bytes 196616 | tf_op jit(solution)/shard_map/ppermute | solution.py:22
  188.0 7.1 %collective-permute-start.46 = (bf16[16,2048]{1,0:T(8,128)(2,1)S(1)}, bf16[16,2048]{1,0:T(8,128)(2,1)S(1)}, u32[]{:S(2)}, u32[]{:S(2)}) collective-permute-start(bf16[16,2048]{1,0:T(8,128)(2,1)S(1)} %get-tuple-element.11), channel_id=1, source_target_pairs={{0,12},{1,13},{2,14},{3,15},{4,8},{5,9},{6,10},{7,11},{8,20},{9,21... | collective-permute-start | bytes 196616 | tf_op jit(solution)/shard_map/ppermute | solution.py:55
  190.2 7.9 %collective-permute-start.45 = (bf16[16,2048]{1,0:T(8,128)(2,1)S(1)}, bf16[16,2048]{1,0:T(8,128)(2,1)S(1)}, u32[]{:S(2)}, u32[]{:S(2)}) collective-permute-start(bf16[16,2048]{1,0:T(8,128)(2,1)S(1)} %get-tuple-element.11), channel_id=1, source_target_pairs={{0,10},{1,11},{2,12},{3,13},{4,14},{5,15},{6,8},{7,9},{8,18},{9,19... | collective-permute-start | bytes 196616 | tf_op jit(solution)/shard_map/ppermute | solution.py:55
  190.2 7.9 %collective-permute-start.44 = (bf16[16,2048]{1,0:T(8,128)(2,1)S(1)}, bf16[16,2048]{1,0:T(8,128)(2,1)S(1)}, u32[]{:S(2)}, u32[]{:S(2)}) collective-permute-start(bf16[16,2048]{1,0:T(8,128)(2,1)S(1)} %get-tuple-element.11), channel_id=1, source_target_pairs={{0,8},{1,9},{2,10},{3,11},{4,12},{5,13},{6,14},{7,15},{8,16},{9,17... | collective-permute-start | bytes 196616 | tf_op jit(solution)/shard_map/ppermute | solution.py:55
  212.3 8.6 %collective-permute-start.51 = (bf16[16,2048]{1,0:T(8,128)(2,1)S(1)}, bf16[16,2048]{1,0:T(8,128)(2,1)S(1)}, u32[]{:S(2)}, u32[]{:S(2)}) collective-permute-start(bf16[16,2048]{1,0:T(8,128)(2,1)S(1)} %get-tuple-element.42), channel_id=1, source_target_pairs={{0,4},{1,5},{2,6},{3,7},{4,0},{5,1},{6,2},{7,3},{8,12},{9,13},{10,... | collective-permute-start | bytes 196616 | tf_op jit(solution)/shard_map/ppermute | solution.py:22
  213.5 7.4 %collective-permute-start.50 = (bf16[16,2048]{1,0:T(8,128)(2,1)S(1)}, bf16[16,2048]{1,0:T(8,128)(2,1)S(1)}, u32[]{:S(2)}, u32[]{:S(2)}) collective-permute-start(bf16[16,2048]{1,0:T(8,128)(2,1)S(1)} %get-tuple-element.40), channel_id=1, source_target_pairs={{0,6},{1,7},{2,0},{3,1},{4,2},{5,3},{6,4},{7,5},{8,14},{9,15},{10,... | collective-permute-start | bytes 196616 | tf_op jit(solution)/shard_map/ppermute | solution.py:22
  222.8 8.5 %collective-permute-start.55 = (bf16[16,2048]{1,0:T(8,128)(2,1)S(1)}, bf16[16,2048]{1,0:T(8,128)(2,1)S(1)}, u32[]{:S(2)}, u32[]{:S(2)}) collective-permute-start(bf16[16,2048]{1,0:T(8,128)(2,1)S(1)} %get-tuple-element.7), channel_id=1, source_target_pairs={{0,12},{1,13},{2,14},{3,15},{4,8},{5,9},{6,10},{7,11},{8,20},{9,21... | collective-permute-start | bytes 196616 | tf_op jit(solution)/shard_map/ppermute | solution.py:55
  224.9 7.9 %collective-permute-start.54 = (bf16[16,2048]{1,0:T(8,128)(2,1)S(1)}, bf16[16,2048]{1,0:T(8,128)(2,1)S(1)}, u32[]{:S(2)}, u32[]{:S(2)}) collective-permute-start(bf16[16,2048]{1,0:T(8,128)(2,1)S(1)} %get-tuple-element.7), channel_id=1, source_target_pairs={{0,10},{1,11},{2,12},{3,13},{4,14},{5,15},{6,8},{7,9},{8,18},{9,19... | collective-permute-start | bytes 196616 | tf_op jit(solution)/shard_map/ppermute | solution.py:55
  224.9 7.9 %collective-permute-start.53 = (bf16[16,2048]{1,0:T(8,128)(2,1)S(1)}, bf16[16,2048]{1,0:T(8,128)(2,1)S(1)}, u32[]{:S(2)}, u32[]{:S(2)}) collective-permute-start(bf16[16,2048]{1,0:T(8,128)(2,1)S(1)} %get-tuple-element.7), channel_id=1, source_target_pairs={{0,8},{1,9},{2,10},{3,11},{4,12},{5,13},{6,14},{7,15},{8,16},{9,17... | collective-permute-start | bytes 196616 | tf_op jit(solution)/shard_map/ppermute | solution.py:55
  247.2 8.4 %collective-permute-start.60 = (bf16[16,2048]{1,0:T(8,128)(2,1)S(1)}, bf16[16,2048]{1,0:T(8,128)(2,1)S(1)}, u32[]{:S(2)}, u32[]{:S(2)}) collective-permute-start(bf16[16,2048]{1,0:T(8,128)(2,1)S(1)} %get-tuple-element.37), channel_id=1, source_target_pairs={{0,4},{1,5},{2,6},{3,7},{4,0},{5,1},{6,2},{7,3},{8,12},{9,13},{10,... | collective-permute-start | bytes 196616 | tf_op jit(solution)/shard_map/ppermute | solution.py:22
  (36 other events, 223.7 us)

commit v12 on v11

--- a/solution.py
+++ b/solution.py
@@ -15,10 +15,9 @@
     return lax.ppermute(array, axis, pairs)
 
 
-def chip_shift(array, axis, by):
+def chip_swap(array, axis, mask):
     count = lax.axis_size(axis)
-    chips = count // 2
-    pairs = [(i, ((i // 2 + by) % chips) * 2 + i % 2) for i in range(count)]
+    pairs = [(i, ((i // 2) ^ mask) * 2 + i % 2) for i in range(count)]
     return lax.ppermute(array, axis, pairs)
 
 
@@ -29,7 +28,7 @@
 
 def gather_blocks(array, axis):
     chips = lax.axis_size(axis) // 2
-    own = jnp.stack([array] + [chip_shift(array, axis, k) for k in range(1, chips)])
+    own = jnp.stack([array] + [chip_swap(array, axis, k) for k in range(1, chips)])
     return jnp.stack([own, core_swap(own, axis)])
 
 
@@ -39,7 +38,7 @@
     chip_sum = partial[0] + swapped.astype(jnp.float32)
     total = chip_sum[0]
     for k in range(1, chips):
-        total = total + chip_shift(chip_sum[k].astype(jnp.bfloat16), axis, -k).astype(jnp.float32)
+        total = total + chip_swap(chip_sum[k].astype(jnp.bfloat16), axis, k).astype(jnp.float32)
     return total
 
 
@@ -48,7 +47,7 @@
     count = lax.axis_size("expert")
     chips = count // 2
     pairs = [
-        (s * count + i, ((s + 1) % sections) * count + ((i // 2 + by) % chips) * 2 + i % 2)
+        (s * count + i, ((s + 1) % sections) * count + ((i // 2) ^ by) * 2 + i % 2)
         for s in range(sections)
         for i in range(count)
     ]

time: 257 us -> 256 us (level)
  waiting for transfers between devices: 93.9 us -> 82 us
  starting transfers between devices: 74.4 us -> 84.8 us
    ppermute x24, waiting for transfers between devices: 35.1 us -> 24.9 us  [to_next_section(): return lax.ppermute(array, ('section', 'expert'), pairs)]
    ppermute x24, starting transfers between devices: 37.2 us -> 46 us  [to_next_section(): return lax.ppermute(array, ('section', 'expert'), pairs)]
  transfers between devices with their start and end apart: 62 -> 62, of which waited for: 44 -> 53; matrix products, arithmetic and copies ran while one was open for 1% -> 1% of each run, Pallas kernels for 0% -> 0%
where the time goes in v12:
time: 256 us; the launch traced here: 255 us
  starting transfers between devices  84.8 us (33%)
  waiting for transfers between devices  82 us (32%)
  matrix products  72.6 us (28%)
  other arithmetic  10.3 us (4%)
  local copies, waits for them, and re-layouts  4.38 us (2%)
    dot_general x7, matrix products, on_device(): jnp.einsum('etf,efd->td', inner, w_down, preferred_element_type=jnp.float32)  46.3 us
    ppermute x24, starting transfers between devices, to_next_section(): return lax.ppermute(array, ('section', 'expert'), pairs)  46 us
    ppermute x24, waiting for transfers between devices, chip_swap(): return lax.ppermute(array, axis, pairs)  37.6 us
    ppermute x24, starting transfers between devices, chip_swap(): return lax.ppermute(array, axis, pairs)  36.9 us
    dot_general x7, matrix products, on_device(): jnp.einsum('td,edf->etf', rows, w_gate, preferred_element_type=jnp.float32)  26.4 us
    ppermute x24, waiting for transfers between devices, to_next_section(): return lax.ppermute(array, ('section', 'expert'), pairs)  24.9 us
    ppermute x14, waiting for transfers between devices, core_swap(): return lax.ppermute(array, axis, [(i, i ^ 1) for i in range(count)])  19.6 us
  transfers between devices with their start and end apart: 62, of which 53 were waited for; matrix products, arithmetic and copies ran while one was open for 1% of the time, Pallas kernels for 0%

profile of v12, /device:TPU:0, one launch (start us, length us, event | category | flops | bytes accessed | tf_op | source)
XLA Modules:
  0.0 254.9 jit_solution(8624863632186067430)
XLA Ops:
  3.5 5.1 %collective-permute-start.2 = (bf16[17,2048]{1,0:T(8,128)(2,1)S(1)}, bf16[17,2048]{1,0:T(8,128)(2,1)S(1)}, u32[]{:S(2)}, u32[]{:S(2)}) collective-permute-start(bf16[17,2048]{1,0:T(8,128)(2,1)S(1)} %get-tuple-element.69), channel_id=1, source_target_pairs={{0,6},{1,7},{2,4},{3,5},{4,2},{5,3},{6,0},{7,1},{8,14},{9,15},{10,... | collective-permute-start | bytes 208904 | tf_op jit(solution)/shard_map/ppermute | solution.py:21
  9.3 3.1 %collective-permute-done.2 = bf16[17,2048]{1,0:T(8,128)(2,1)S(1)} collective-permute-done((bf16[17,2048]{1,0:T(8,128)(2,1)S(1)}, bf16[17,2048]{1,0:T(8,128)(2,1)S(1)}, u32[]{:S(2)}, u32[]{:S(2)}) %collective-permute-start.2) | collective-permute-done | bytes 69664 | tf_op jit(solution)/shard_map/ppermute | solution.py:21
  12.3 4.6 %collective-permute-done.1 = bf16[17,2048]{1,0:T(8,128)(2,1)S(1)} collective-permute-done((bf16[17,2048]{1,0:T(8,128)(2,1)S(1)}, bf16[17,2048]{1,0:T(8,128)(2,1)S(1)}, u32[]{:S(2)}, u32[]{:S(2)}) %collective-permute-start.1) | collective-permute-done | bytes 69664 | tf_op jit(solution)/shard_map/ppermute | solution.py:21
  20.6 3.8 %fusion.63 = f32[2,128,768]{2,1,0:T(8,128)S(1)} fusion(bf16[128,2048,1]{1,0,2:T(8,128)(2,1)S(1)} %bitcast.594, bf16[1,2,2048,768]{3,2,1,0:T(8,128)(2,1)} %param.9), kind=kOutput, calls=%fused_computation.49 | convolution fusion | flops 805306368 | bytes 7602176 | tf_op jit(solution)/shard_map/td,edf->etf/dot_general | solution.py:109
  25.0 6.6 %fusion.42 = f32[128,2048]{1,0:T(8,128)S(1)} fusion(bf16[1,2,768,2048]{3,2,1,0:T(8,128)(2,1)} %param.11, bf16[128,2048,1]{1,0,2:T(8,128)(2,1)S(1)} %bitcast.595, bf16[1,2,2048,768]{3,2,1,0:T(8,128)(2,1)} %param.10, f32[2,128,768]{2,1,0:T(8,128)S(1)} %fusion.63, f32[2,128]{1,0:T(2,128)S(1)} %get-tuple-element.76), kind=kOutput, calls=%fused_computation.42 | convolution fusion | flops 1611988992 | bytes 14943232 | tf_op jit(solution)/shard_map/etf,efd->td/dot_general | solution.py:112
  33.4 2.6 %collective-permute-start.7 = (bf16[16,2048]{1,0:T(8,128)(2,1)S(1)}, bf16[16,2048]{1,0:T(8,128)(2,1)S(1)}, u32[]{:S(2)}, u32[]{:S(2)}) collective-permute-start(bf16[16,2048]{1,0:T(8,128)(2,1)S(1)} %get-tuple-element.66), channel_id=1, source_target_pairs={{0,6},{1,7},{2,4},{3,5},{4,2},{5,3},{6,0},{7,1},{8,14},{9,15},{10,... | collective-permute-start | bytes 196616 | tf_op jit(solution)/shard_map/ppermute | solution.py:21
  42.9 3.4 %collective-permute-start.11 = (bf16[16,2048]{1,0:T(8,128)(2,1)S(1)}, bf16[16,2048]{1,0:T(8,128)(2,1)S(1)}, u32[]{:S(2)}, u32[]{:S(2)}) collective-permute-start(bf16[16,2048]{1,0:T(8,128)(2,1)S(1)} %get-tuple-element.27), channel_id=1, source_target_pairs={{0,14},{1,15},{2,12},{3,13},{4,10},{5,11},{6,8},{7,9},{8,22},{9,23... | collective-permute-start | bytes 196616 | tf_op jit(solution)/shard_map/ppermute | solution.py:54
  47.0 3.1 %collective-permute-start.9 = (bf16[16,2048]{1,0:T(8,128)(2,1)S(1)}, bf16[16,2048]{1,0:T(8,128)(2,1)S(1)}, u32[]{:S(2)}, u32[]{:S(2)}) collective-permute-start(bf16[16,2048]{1,0:T(8,128)(2,1)S(1)} %get-tuple-element.27), channel_id=1, source_target_pairs={{0,10},{1,11},{2,8},{3,9},{4,14},{5,15},{6,12},{7,13},{8,18},{9,19... | collective-permute-start | bytes 196616 | tf_op jit(solution)/shard_map/ppermute | solution.py:54
  57.5 3.8 %fusion.66 = f32[2,128,768]{2,1,0:T(8,128)S(1)} fusion(bf16[128,2048,1]{1,0,2:T(8,128)(2,1)S(1)} %bitcast.598, bf16[1,2,2048,768]{3,2,1,0:T(8,128)(2,1)} %param.9), kind=kOutput, calls=%fused_computation.50 | convolution fusion | flops 805306368 | bytes 7602176 | tf_op jit(solution)/shard_map/td,edf->etf/dot_general | solution.py:109
  61.3 6.6 %fusion.45 = f32[128,2048]{1,0:T(8,128)S(1)} fusion(bf16[1,2,768,2048]{3,2,1,0:T(8,128)(2,1)} %param.11, bf16[128,2048,1]{1,0,2:T(8,128)(2,1)S(1)} %bitcast.599, bf16[1,2,2048,768]{3,2,1,0:T(8,128)(2,1)} %param.10, f32[2,128,768]{2,1,0:T(8,128)S(1)} %fusion.66, f32[2,128]{1,0:T(2,128)S(1)} %get-tuple-element.75), kind=kOutput, calls=%fused_computation.43 | convolution fusion | flops 1611988992 | bytes 14943232 | tf_op jit(solution)/shard_map/etf,efd->td/dot_general | solution.py:112
  69.6 2.3 collective-permute-start.16
  74.2 2.3 collective-permute-done.16
  92.4 3.8 %fusion.69 = f32[2,128,768]{2,1,0:T(8,128)S(1)} fusion(bf16[128,2048,1]{1,0,2:T(8,128)(2,1)S(1)} %bitcast.600, bf16[1,2,2048,768]{3,2,1,0:T(8,128)(2,1)} %param.9), kind=kOutput, calls=%fused_computation.51 | convolution fusion | flops 805306368 | bytes 7602176 | tf_op jit(solution)/shard_map/td,edf->etf/dot_general | solution.py:109
  96.2 6.6 %fusion.48 = f32[128,2048]{1,0:T(8,128)S(1)} fusion(bf16[1,2,768,2048]{3,2,1,0:T(8,128)(2,1)} %param.11, bf16[128,2048,1]{1,0,2:T(8,128)(2,1)S(1)} %bitcast.601, bf16[1,2,2048,768]{3,2,1,0:T(8,128)(2,1)} %param.10, f32[2,128,768]{2,1,0:T(8,128)S(1)} %fusion.69, f32[2,128]{1,0:T(2,128)S(1)} %get-tuple-element.74), kind=kOutput, calls=%fused_computation.44 | convolution fusion | flops 1611988992 | bytes 14943232 | tf_op jit(solution)/shard_map/etf,efd->td/dot_general | solution.py:112
  104.6 2.3 collective-permute-start.25
  109.1 2.3 collective-permute-done.25
  127.4 3.8 %fusion.72 = f32[2,128,768]{2,1,0:T(8,128)S(1)} fusion(bf16[128,2048,1]{1,0,2:T(8,128)(2,1)S(1)} %bitcast.602, bf16[1,2,2048,768]{3,2,1,0:T(8,128)(2,1)} %param.9), kind=kOutput, calls=%fused_computation.52 | convolution fusion | flops 805306368 | bytes 7602176 | tf_op jit(solution)/shard_map/td,edf->etf/dot_general | solution.py:109
  131.2 6.6 %fusion.51 = f32[128,2048]{1,0:T(8,128)S(1)} fusion(bf16[1,2,768,2048]{3,2,1,0:T(8,128)(2,1)} %param.11, bf16[128,2048,1]{1,0,2:T(8,128)(2,1)S(1)} %bitcast.603, bf16[1,2,2048,768]{3,2,1,0:T(8,128)(2,1)} %param.10, f32[2,128,768]{2,1,0:T(8,128)S(1)} %fusion.72, f32[2,128]{1,0:T(2,128)S(1)} %copy-done.5), kind=kOutput, calls=%fused_computation.45 | convolution fusion | flops 1611988992 | bytes 14943232 | tf_op jit(solution)/shard_map/etf,efd->td/dot_general | solution.py:112
  139.5 2.3 collective-permute-start.34
  144.0 2.3 collective-permute-done.34
  162.9 3.8 %fusion.75 = f32[2,128,768]{2,1,0:T(8,128)S(1)} fusion(bf16[128,2048,1]{1,0,2:T(8,128)(2,1)S(1)} %bitcast.604, bf16[1,2,2048,768]{3,2,1,0:T(8,128)(2,1)} %param.9), kind=kOutput, calls=%fused_computation.53 | convolution fusion | flops 805306368 | bytes 7602176 | tf_op jit(solution)/shard_map/td,edf->etf/dot_general | solution.py:109
  166.6 6.6 %fusion.54 = f32[128,2048]{1,0:T(8,128)S(1)} fusion(bf16[1,2,768,2048]{3,2,1,0:T(8,128)(2,1)} %param.11, bf16[128,2048,1]{1,0,2:T(8,128)(2,1)S(1)} %bitcast.605, bf16[1,2,2048,768]{3,2,1,0:T(8,128)(2,1)} %param.10, f32[2,128,768]{2,1,0:T(8,128)S(1)} %fusion.75, f32[2,128]{1,0:T(2,128)S(1)} %copy-done.4), kind=kOutput, calls=%fused_computation.46 | convolution fusion | flops 1611988992 | bytes 14943232 | tf_op jit(solution)/shard_map/etf,efd->td/dot_general | solution.py:112
  175.0 2.3 collective-permute-start.43
  198.3 3.8 %fusion.78 = f32[2,128,768]{2,1,0:T(8,128)S(1)} fusion(bf16[128,2048,1]{1,0,2:T(8,128)(2,1)S(1)} %bitcast.606, bf16[1,2,2048,768]{3,2,1,0:T(8,128)(2,1)} %param.9), kind=kOutput, calls=%fused_computation.54 | convolution fusion | flops 805306368 | bytes 7602176 | tf_op jit(solution)/shard_map/td,edf->etf/dot_general | solution.py:109
  202.1 6.6 %fusion.57 = f32[128,2048]{1,0:T(8,128)S(1)} fusion(bf16[1,2,768,2048]{3,2,1,0:T(8,128)(2,1)} %param.11, bf16[128,2048,1]{1,0,2:T(8,128)(2,1)S(1)} %bitcast.607, bf16[1,2,2048,768]{3,2,1,0:T(8,128)(2,1)} %param.10, f32[2,128,768]{2,1,0:T(8,128)S(1)} %fusion.78, f32[2,128]{1,0:T(2,128)S(1)} %get-tuple-element.71), kind=kOutput, calls=%fused_computation.47 | convolution fusion | flops 1611988992 | bytes 14943232 | tf_op jit(solution)/shard_map/etf,efd->td/dot_general | solution.py:112
  210.5 2.3 collective-permute-start.52
  215.0 2.3 collective-permute-done.52
  222.7 2.3 collective-permute-start.54
  233.3 3.8 %fusion.81 = f32[2,128,768]{2,1,0:T(8,128)S(1)} fusion(bf16[128,2048,1]{1,0,2:T(8,128)(2,1)S(1)} %bitcast.596, bf16[1,2,2048,768]{3,2,1,0:T(8,128)(2,1)} %param.9), kind=kOutput, calls=%fused_computation.55 | convolution fusion | flops 805306368 | bytes 7602176 | tf_op jit(solution)/shard_map/td,edf->etf/dot_general | solution.py:109
  237.1 6.6 %fusion.60 = f32[128,2048]{1,0:T(8,128)S(1)} fusion(bf16[1,2,768,2048]{3,2,1,0:T(8,128)(2,1)} %param.11, bf16[128,2048,1]{1,0,2:T(8,128)(2,1)S(1)} %bitcast.597, bf16[1,2,2048,768]{3,2,1,0:T(8,128)(2,1)} %param.10, f32[2,128,768]{2,1,0:T(8,128)S(1)} %fusion.81, f32[2,128]{1,0:T(2,128)S(1)} %get-tuple-element.70), kind=kOutput, calls=%fused_computation.48 | convolution fusion | flops 1611988992 | bytes 14943232 | tf_op jit(solution)/shard_map/etf,efd->td/dot_general | solution.py:112
  245.4 2.3 collective-permute-start.61
  250.0 2.3 collective-permute-done.61
  (215 shorter events, 132.0 us)
Async XLA Ops:
  3.5 8.8 %collective-permute-start.2 = (bf16[17,2048]{1,0:T(8,128)(2,1)S(1)}, bf16[17,2048]{1,0:T(8,128)(2,1)S(1)}, u32[]{:S(2)}, u32[]{:S(2)}) collective-permute-start(bf16[17,2048]{1,0:T(8,128)(2,1)S(1)} %get-tuple-element.69), channel_id=1, source_target_pairs={{0,6},{1,7},{2,4},{3,5},{4,2},{5,3},{6,0},{7,1},{8,14},{9,15},{10,... | collective-permute-start | bytes 208904 | tf_op jit(solution)/shard_map/ppermute | solution.py:21
  8.6 8.3 %collective-permute-start.1 = (bf16[17,2048]{1,0:T(8,128)(2,1)S(1)}, bf16[17,2048]{1,0:T(8,128)(2,1)S(1)}, u32[]{:S(2)}, u32[]{:S(2)}) collective-permute-start(bf16[17,2048]{1,0:T(8,128)(2,1)S(1)} %get-tuple-element.69), channel_id=1, source_target_pairs={{0,4},{1,5},{2,6},{3,7},{4,0},{5,1},{6,2},{7,3},{8,12},{9,13},{10,... | collective-permute-start | bytes 208904 | tf_op jit(solution)/shard_map/ppermute | solution.py:21
  8.6 8.3 %collective-permute-start = (bf16[17,2048]{1,0:T(8,128)(2,1)S(1)}, bf16[17,2048]{1,0:T(8,128)(2,1)S(1)}, u32[]{:S(2)}, u32[]{:S(2)}) collective-permute-start(bf16[17,2048]{1,0:T(8,128)(2,1)S(1)} %get-tuple-element.69), channel_id=1, source_target_pairs={{0,2},{1,3},{2,0},{3,1},{4,6},{5,7},{6,4},{7,5},{8,10},{9,11},{10,... | collective-permute-start | bytes 208904 | tf_op jit(solution)/shard_map/ppermute | solution.py:21
  33.4 6.8 %collective-permute-start.7 = (bf16[16,2048]{1,0:T(8,128)(2,1)S(1)}, bf16[16,2048]{1,0:T(8,128)(2,1)S(1)}, u32[]{:S(2)}, u32[]{:S(2)}) collective-permute-start(bf16[16,2048]{1,0:T(8,128)(2,1)S(1)} %get-tuple-element.66), channel_id=1, source_target_pairs={{0,6},{1,7},{2,4},{3,5},{4,2},{5,3},{6,0},{7,1},{8,14},{9,15},{10,... | collective-permute-start | bytes 196616 | tf_op jit(solution)/shard_map/ppermute | solution.py:21
  42.9 8.5 %collective-permute-start.11 = (bf16[16,2048]{1,0:T(8,128)(2,1)S(1)}, bf16[16,2048]{1,0:T(8,128)(2,1)S(1)}, u32[]{:S(2)}, u32[]{:S(2)}) collective-permute-start(bf16[16,2048]{1,0:T(8,128)(2,1)S(1)} %get-tuple-element.27), channel_id=1, source_target_pairs={{0,14},{1,15},{2,12},{3,13},{4,10},{5,11},{6,8},{7,9},{8,22},{9,23... | collective-permute-start | bytes 196616 | tf_op jit(solution)/shard_map/ppermute | solution.py:54
  46.3 7.1 %collective-permute-start.10 = (bf16[16,2048]{1,0:T(8,128)(2,1)S(1)}, bf16[16,2048]{1,0:T(8,128)(2,1)S(1)}, u32[]{:S(2)}, u32[]{:S(2)}) collective-permute-start(bf16[16,2048]{1,0:T(8,128)(2,1)S(1)} %get-tuple-element.27), channel_id=1, source_target_pairs={{0,12},{1,13},{2,14},{3,15},{4,8},{5,9},{6,10},{7,11},{8,20},{9,21... | collective-permute-start | bytes 196616 | tf_op jit(solution)/shard_map/ppermute | solution.py:54
  47.0 7.2 %collective-permute-start.9 = (bf16[16,2048]{1,0:T(8,128)(2,1)S(1)}, bf16[16,2048]{1,0:T(8,128)(2,1)S(1)}, u32[]{:S(2)}, u32[]{:S(2)}) collective-permute-start(bf16[16,2048]{1,0:T(8,128)(2,1)S(1)} %get-tuple-element.27), channel_id=1, source_target_pairs={{0,10},{1,11},{2,8},{3,9},{4,14},{5,15},{6,12},{7,13},{8,18},{9,19... | collective-permute-start | bytes 196616 | tf_op jit(solution)/shard_map/ppermute | solution.py:54
  69.6 6.8 %collective-permute-start.16 = (bf16[16,2048]{1,0:T(8,128)(2,1)S(1)}, bf16[16,2048]{1,0:T(8,128)(2,1)S(1)}, u32[]{:S(2)}, u32[]{:S(2)}) collective-permute-start(bf16[16,2048]{1,0:T(8,128)(2,1)S(1)} %get-tuple-element.61), channel_id=1, source_target_pairs={{0,6},{1,7},{2,4},{3,5},{4,2},{5,3},{6,0},{7,1},{8,14},{9,15},{10,... | collective-permute-start | bytes 196616 | tf_op jit(solution)/shard_map/ppermute | solution.py:21
  78.5 8.5 %collective-permute-start.20 = (bf16[16,2048]{1,0:T(8,128)(2,1)S(1)}, bf16[16,2048]{1,0:T(8,128)(2,1)S(1)}, u32[]{:S(2)}, u32[]{:S(2)}) collective-permute-start(bf16[16,2048]{1,0:T(8,128)(2,1)S(1)} %get-tuple-element.23), channel_id=1, source_target_pairs={{0,14},{1,15},{2,12},{3,13},{4,10},{5,11},{6,8},{7,9},{8,22},{9,23... | collective-permute-start | bytes 196616 | tf_op jit(solution)/shard_map/ppermute | solution.py:54
  80.7 8.5 %collective-permute-start.19 = (bf16[16,2048]{1,0:T(8,128)(2,1)S(1)}, bf16[16,2048]{1,0:T(8,128)(2,1)S(1)}, u32[]{:S(2)}, u32[]{:S(2)}) collective-permute-start(bf16[16,2048]{1,0:T(8,128)(2,1)S(1)} %get-tuple-element.23), channel_id=1, source_target_pairs={{0,12},{1,13},{2,14},{3,15},{4,8},{5,9},{6,10},{7,11},{8,20},{9,21... | collective-permute-start | bytes 196616 | tf_op jit(solution)/shard_map/ppermute | solution.py:54
  82.2 7.5 %collective-permute-start.18 = (bf16[16,2048]{1,0:T(8,128)(2,1)S(1)}, bf16[16,2048]{1,0:T(8,128)(2,1)S(1)}, u32[]{:S(2)}, u32[]{:S(2)}) collective-permute-start(bf16[16,2048]{1,0:T(8,128)(2,1)S(1)} %get-tuple-element.23), channel_id=1, source_target_pairs={{0,10},{1,11},{2,8},{3,9},{4,14},{5,15},{6,12},{7,13},{8,18},{9,19... | collective-permute-start | bytes 196616 | tf_op jit(solution)/shard_map/ppermute | solution.py:54
  104.6 6.8 %collective-permute-start.25 = (bf16[16,2048]{1,0:T(8,128)(2,1)S(1)}, bf16[16,2048]{1,0:T(8,128)(2,1)S(1)}, u32[]{:S(2)}, u32[]{:S(2)}) collective-permute-start(bf16[16,2048]{1,0:T(8,128)(2,1)S(1)} %get-tuple-element.56), channel_id=1, source_target_pairs={{0,6},{1,7},{2,4},{3,5},{4,2},{5,3},{6,0},{7,1},{8,14},{9,15},{10,... | collective-permute-start | bytes 196616 | tf_op jit(solution)/shard_map/ppermute | solution.py:21
  113.4 8.5 %collective-permute-start.29 = (bf16[16,2048]{1,0:T(8,128)(2,1)S(1)}, bf16[16,2048]{1,0:T(8,128)(2,1)S(1)}, u32[]{:S(2)}, u32[]{:S(2)}) collective-permute-start(bf16[16,2048]{1,0:T(8,128)(2,1)S(1)} %get-tuple-element.19), channel_id=1, source_target_pairs={{0,14},{1,15},{2,12},{3,13},{4,10},{5,11},{6,8},{7,9},{8,22},{9,23... | collective-permute-start | bytes 196616 | tf_op jit(solution)/shard_map/ppermute | solution.py:54
  115.4 8.6 %collective-permute-start.28 = (bf16[16,2048]{1,0:T(8,128)(2,1)S(1)}, bf16[16,2048]{1,0:T(8,128)(2,1)S(1)}, u32[]{:S(2)}, u32[]{:S(2)}) collective-permute-start(bf16[16,2048]{1,0:T(8,128)(2,1)S(1)} %get-tuple-element.19), channel_id=1, source_target_pairs={{0,12},{1,13},{2,14},{3,15},{4,8},{5,9},{6,10},{7,11},{8,20},{9,21... | collective-permute-start | bytes 196616 | tf_op jit(solution)/shard_map/ppermute | solution.py:54
  117.0 7.4 %collective-permute-start.27 = (bf16[16,2048]{1,0:T(8,128)(2,1)S(1)}, bf16[16,2048]{1,0:T(8,128)(2,1)S(1)}, u32[]{:S(2)}, u32[]{:S(2)}) collective-permute-start(bf16[16,2048]{1,0:T(8,128)(2,1)S(1)} %get-tuple-element.19), channel_id=1, source_target_pairs={{0,10},{1,11},{2,8},{3,9},{4,14},{5,15},{6,12},{7,13},{8,18},{9,19... | collective-permute-start | bytes 196616 | tf_op jit(solution)/shard_map/ppermute | solution.py:54
  139.5 6.8 %collective-permute-start.34 = (bf16[16,2048]{1,0:T(8,128)(2,1)S(1)}, bf16[16,2048]{1,0:T(8,128)(2,1)S(1)}, u32[]{:S(2)}, u32[]{:S(2)}) collective-permute-start(bf16[16,2048]{1,0:T(8,128)(2,1)S(1)} %get-tuple-element.51), channel_id=1, source_target_pairs={{0,6},{1,7},{2,4},{3,5},{4,2},{5,3},{6,0},{7,1},{8,14},{9,15},{10,... | collective-permute-start | bytes 196616 | tf_op jit(solution)/shard_map/ppermute | solution.py:21
  149.0 8.4 %collective-permute-start.38 = (bf16[16,2048]{1,0:T(8,128)(2,1)S(1)}, bf16[16,2048]{1,0:T(8,128)(2,1)S(1)}, u32[]{:S(2)}, u32[]{:S(2)}) collective-permute-start(bf16[16,2048]{1,0:T(8,128)(2,1)S(1)} %get-tuple-element.15), channel_id=1, source_target_pairs={{0,14},{1,15},{2,12},{3,13},{4,10},{5,11},{6,8},{7,9},{8,22},{9,23... | collective-permute-start | bytes 196616 | tf_op jit(solution)/shard_map/ppermute | solution.py:54
  150.8 8.7 %collective-permute-start.37 = (bf16[16,2048]{1,0:T(8,128)(2,1)S(1)}, bf16[16,2048]{1,0:T(8,128)(2,1)S(1)}, u32[]{:S(2)}, u32[]{:S(2)}) collective-permute-start(bf16[16,2048]{1,0:T(8,128)(2,1)S(1)} %get-tuple-element.15), channel_id=1, source_target_pairs={{0,12},{1,13},{2,14},{3,15},{4,8},{5,9},{6,10},{7,11},{8,20},{9,21... | collective-permute-start | bytes 196616 | tf_op jit(solution)/shard_map/ppermute | solution.py:54
  152.4 7.4 %collective-permute-start.36 = (bf16[16,2048]{1,0:T(8,128)(2,1)S(1)}, bf16[16,2048]{1,0:T(8,128)(2,1)S(1)}, u32[]{:S(2)}, u32[]{:S(2)}) collective-permute-start(bf16[16,2048]{1,0:T(8,128)(2,1)S(1)} %get-tuple-element.15), channel_id=1, source_target_pairs={{0,10},{1,11},{2,8},{3,9},{4,14},{5,15},{6,12},{7,13},{8,18},{9,19... | collective-permute-start | bytes 196616 | tf_op jit(solution)/shard_map/ppermute | solution.py:54
  175.0 6.8 %collective-permute-start.43 = (bf16[16,2048]{1,0:T(8,128)(2,1)S(1)}, bf16[16,2048]{1,0:T(8,128)(2,1)S(1)}, u32[]{:S(2)}, u32[]{:S(2)}) collective-permute-start(bf16[16,2048]{1,0:T(8,128)(2,1)S(1)} %get-tuple-element.46), channel_id=1, source_target_pairs={{0,6},{1,7},{2,4},{3,5},{4,2},{5,3},{6,0},{7,1},{8,14},{9,15},{10,... | collective-permute-start | bytes 196616 | tf_op jit(solution)/shard_map/ppermute | solution.py:21
  184.5 8.5 %collective-permute-start.47 = (bf16[16,2048]{1,0:T(8,128)(2,1)S(1)}, bf16[16,2048]{1,0:T(8,128)(2,1)S(1)}, u32[]{:S(2)}, u32[]{:S(2)}) collective-permute-start(bf16[16,2048]{1,0:T(8,128)(2,1)S(1)} %get-tuple-element.11), channel_id=1, source_target_pairs={{0,14},{1,15},{2,12},{3,13},{4,10},{5,11},{6,8},{7,9},{8,22},{9,23... | collective-permute-start | bytes 196616 | tf_op jit(solution)/shard_map/ppermute | solution.py:54
  186.4 8.6 %collective-permute-start.46 = (bf16[16,2048]{1,0:T(8,128)(2,1)S(1)}, bf16[16,2048]{1,0:T(8,128)(2,1)S(1)}, u32[]{:S(2)}, u32[]{:S(2)}) collective-permute-start(bf16[16,2048]{1,0:T(8,128)(2,1)S(1)} %get-tuple-element.11), channel_id=1, source_target_pairs={{0,12},{1,13},{2,14},{3,15},{4,8},{5,9},{6,10},{7,11},{8,20},{9,21... | collective-permute-start | bytes 196616 | tf_op jit(solution)/shard_map/ppermute | solution.py:54
  187.8 7.4 %collective-permute-start.45 = (bf16[16,2048]{1,0:T(8,128)(2,1)S(1)}, bf16[16,2048]{1,0:T(8,128)(2,1)S(1)}, u32[]{:S(2)}, u32[]{:S(2)}) collective-permute-start(bf16[16,2048]{1,0:T(8,128)(2,1)S(1)} %get-tuple-element.11), channel_id=1, source_target_pairs={{0,10},{1,11},{2,8},{3,9},{4,14},{5,15},{6,12},{7,13},{8,18},{9,19... | collective-permute-start | bytes 196616 | tf_op jit(solution)/shard_map/ppermute | solution.py:54
  210.5 6.8 %collective-permute-start.52 = (bf16[16,2048]{1,0:T(8,128)(2,1)S(1)}, bf16[16,2048]{1,0:T(8,128)(2,1)S(1)}, u32[]{:S(2)}, u32[]{:S(2)}) collective-permute-start(bf16[16,2048]{1,0:T(8,128)(2,1)S(1)} %get-tuple-element.41), channel_id=1, source_target_pairs={{0,6},{1,7},{2,4},{3,5},{4,2},{5,3},{6,0},{7,1},{8,14},{9,15},{10,... | collective-permute-start | bytes 196616 | tf_op jit(solution)/shard_map/ppermute | solution.py:21
  212.8 6.5 %collective-permute-start.51 = (bf16[16,2048]{1,0:T(8,128)(2,1)S(1)}, bf16[16,2048]{1,0:T(8,128)(2,1)S(1)}, u32[]{:S(2)}, u32[]{:S(2)}) collective-permute-start(bf16[16,2048]{1,0:T(8,128)(2,1)S(1)} %get-tuple-element.42), channel_id=1, source_target_pairs={{0,4},{1,5},{2,6},{3,7},{4,0},{5,1},{6,2},{7,3},{8,12},{9,13},{10,... | collective-permute-start | bytes 196616 | tf_op jit(solution)/shard_map/ppermute | solution.py:21
  212.8 6.5 %collective-permute-start.50 = (bf16[16,2048]{1,0:T(8,128)(2,1)S(1)}, bf16[16,2048]{1,0:T(8,128)(2,1)S(1)}, u32[]{:S(2)}, u32[]{:S(2)}) collective-permute-start(bf16[16,2048]{1,0:T(8,128)(2,1)S(1)} %get-tuple-element.40), channel_id=1, source_target_pairs={{0,2},{1,3},{2,0},{3,1},{4,6},{5,7},{6,4},{7,5},{8,10},{9,11},{10,... | collective-permute-start | bytes 196616 | tf_op jit(solution)/shard_map/ppermute | solution.py:21
  219.4 8.5 %collective-permute-start.56 = (bf16[16,2048]{1,0:T(8,128)(2,1)S(1)}, bf16[16,2048]{1,0:T(8,128)(2,1)S(1)}, u32[]{:S(2)}, u32[]{:S(2)}) collective-permute-start(bf16[16,2048]{1,0:T(8,128)(2,1)S(1)} %get-tuple-element.7), channel_id=1, source_target_pairs={{0,14},{1,15},{2,12},{3,13},{4,10},{5,11},{6,8},{7,9},{8,22},{9,23... | collective-permute-start | bytes 196616 | tf_op jit(solution)/shard_map/ppermute | solution.py:54
  221.3 8.6 %collective-permute-start.55 = (bf16[16,2048]{1,0:T(8,128)(2,1)S(1)}, bf16[16,2048]{1,0:T(8,128)(2,1)S(1)}, u32[]{:S(2)}, u32[]{:S(2)}) collective-permute-start(bf16[16,2048]{1,0:T(8,128)(2,1)S(1)} %get-tuple-element.7), channel_id=1, source_target_pairs={{0,12},{1,13},{2,14},{3,15},{4,8},{5,9},{6,10},{7,11},{8,20},{9,21... | collective-permute-start | bytes 196616 | tf_op jit(solution)/shard_map/ppermute | solution.py:54
  222.7 7.4 %collective-permute-start.54 = (bf16[16,2048]{1,0:T(8,128)(2,1)S(1)}, bf16[16,2048]{1,0:T(8,128)(2,1)S(1)}, u32[]{:S(2)}, u32[]{:S(2)}) collective-permute-start(bf16[16,2048]{1,0:T(8,128)(2,1)S(1)} %get-tuple-element.7), channel_id=1, source_target_pairs={{0,10},{1,11},{2,8},{3,9},{4,14},{5,15},{6,12},{7,13},{8,18},{9,19... | collective-permute-start | bytes 196616 | tf_op jit(solution)/shard_map/ppermute | solution.py:54
  245.4 6.8 %collective-permute-start.61 = (bf16[16,2048]{1,0:T(8,128)(2,1)S(1)}, bf16[16,2048]{1,0:T(8,128)(2,1)S(1)}, u32[]{:S(2)}, u32[]{:S(2)}) collective-permute-start(bf16[16,2048]{1,0:T(8,128)(2,1)S(1)} %get-tuple-element.36), channel_id=1, source_target_pairs={{0,6},{1,7},{2,4},{3,5},{4,2},{5,3},{6,0},{7,1},{8,14},{9,15},{10,... | collective-permute-start | bytes 196616 | tf_op jit(solution)/shard_map/ppermute | solution.py:21
  247.7 6.5 %collective-permute-start.60 = (bf16[16,2048]{1,0:T(8,128)(2,1)S(1)}, bf16[16,2048]{1,0:T(8,128)(2,1)S(1)}, u32[]{:S(2)}, u32[]{:S(2)}) collective-permute-start(bf16[16,2048]{1,0:T(8,128)(2,1)S(1)} %get-tuple-element.37), channel_id=1, source_target_pairs={{0,4},{1,5},{2,6},{3,7},{4,0},{5,1},{6,2},{7,3},{8,12},{9,13},{10,... | collective-permute-start | bytes 196616 | tf_op jit(solution)/shard_map/ppermute | solution.py:21
  247.7 6.5 %collective-permute-start.59 = (bf16[16,2048]{1,0:T(8,128)(2,1)S(1)}, bf16[16,2048]{1,0:T(8,128)(2,1)S(1)}, u32[]{:S(2)}, u32[]{:S(2)}) collective-permute-start(bf16[16,2048]{1,0:T(8,128)(2,1)S(1)} %get-tuple-element.35), channel_id=1, source_target_pairs={{0,2},{1,3},{2,0},{3,1},{4,6},{5,7},{6,4},{7,5},{8,10},{9,11},{10,... | collective-permute-start | bytes 196616 | tf_op jit(solution)/shard_map/ppermute | solution.py:21
  (36 other events, 221.6 us)

commit v13 on v12

--- a/solution.py
+++ b/solution.py
@@ -75,8 +75,7 @@
     experts = local_experts * devices
     chips = devices // 2
     gain = norm_gain[0]
-    w_gate = gate_weight[0]
-    w_up = up_weight[0]
+    w_gate_up = jnp.concatenate([gate_weight[0], up_weight[0]]).transpose(1, 0, 2)
     w_down = down_weight[0]
     tok_rows = tokens.shape[1]
     width = tokens.shape[2]
@@ -106,10 +105,11 @@
             rows = jnp.stack([blocks, core_swap(blocks, "expert")])
         values, normed = rms_normed(rows, gain)
         rows = normed.reshape(2 * chips * tok_rows, width)
-        gate_part = jnp.einsum("td,edf->etf", rows, w_gate, preferred_element_type=jnp.float32)
-        up_part = jnp.einsum("td,edf->etf", rows, w_up, preferred_element_type=jnp.float32)
-        inner = (jax.nn.silu(gate_part) * up_part * weight[:, :, None]).astype(jnp.bfloat16)
-        partial = jnp.einsum("etf,efd->td", inner, w_down, preferred_element_type=jnp.float32)
+        both = jnp.einsum("td,def->tef", rows, w_gate_up, preferred_element_type=jnp.float32)
+        gate_part = both[:, :local_experts]
+        up_part = both[:, local_experts:]
+        inner = (jax.nn.silu(gate_part) * up_part * weight.T[:, :, None]).astype(jnp.bfloat16)
+        partial = jnp.einsum("tef,efd->td", inner, w_down, preferred_element_type=jnp.float32)
         mixed = scatter_blocks(partial.reshape(2, chips, tok_rows, width), "expert")
         produced = (values[0, 0] + mixed).astype(jnp.bfloat16)
         updated = lax.dynamic_update_index_in_dim(collected, produced, clipped, 0)

time: 256 us -> 246 us (0.961)
  matrix products: 72.6 us -> 56.9 us
  waiting for transfers between devices: 82 us -> 89 us
  other arithmetic: 10.3 us -> 7.48 us
    dot_general x14, matrix products: 72.6 us -> 56.9 us  [the longest x7 40.5 us: on_device(): jnp.einsum('td,def->tef', rows, w_gate_up, preferred_element_type=jnp.flo...]
    ppermute x24, waiting for transfers between devices: 24.9 us -> 29.8 us  [to_next_section(): return lax.ppermute(array, ('section', 'expert'), pairs)]
  transfers between devices with their start and end apart: 62 -> 62, of which waited for: 53 -> 39; matrix products, arithmetic and copies ran while one was open for 1% -> 0% of each run, Pallas kernels for 0% -> 0%
where the time goes in v13:
time: 246 us; the launch traced here: 245 us
  waiting for transfers between devices  89 us (36%)
  starting transfers between devices  85 us (35%)
  matrix products  56.9 us (23%)
  other arithmetic  7.48 us (3%)
  local copies, waits for them, and re-layouts  5.91 us (2%)
    ppermute x24, starting transfers between devices, to_next_section(): return lax.ppermute(array, ('section', 'expert'), pairs)  46.2 us
    dot_general x7, matrix products, on_device(): jnp.einsum('td,def->tef', rows, w_gate_up, preferred_element_type=jnp.flo...  40.5 us
    ppermute x24, waiting for transfers between devices, chip_swap(): return lax.ppermute(array, axis, pairs)  39 us
    ppermute x24, starting transfers between devices, chip_swap(): return lax.ppermute(array, axis, pairs)  36.8 us
    ppermute x24, waiting for transfers between devices, to_next_section(): return lax.ppermute(array, ('section', 'expert'), pairs)  29.8 us
    ppermute x14, waiting for transfers between devices, core_swap(): return lax.ppermute(array, axis, [(i, i ^ 1) for i in range(count)])  20.1 us
    dot_general x7, matrix products, on_device(): jnp.einsum('tef,efd->td', inner, w_down, preferred_element_type=jnp.float32)  16.5 us
  transfers between devices with their start and end apart: 62, of which 39 were waited for; matrix products, arithmetic and copies ran while one was open for 0% of the time, Pallas kernels for 0%

profile of v13, /device:TPU:0, one launch (start us, length us, event | category | flops | bytes accessed | tf_op | source)
XLA Modules:
  0.0 245.3 jit_solution(8757374370731188931)
XLA Ops:
  3.5 3.1 %collective-permute-start = (bf16[17,2048]{1,0:T(8,128)(2,1)S(1)}, bf16[17,2048]{1,0:T(8,128)(2,1)S(1)}, u32[]{:S(2)}, u32[]{:S(2)}) collective-permute-start(bf16[17,2048]{1,0:T(8,128)(2,1)S(1)} %get-tuple-element.69), channel_id=1, source_target_pairs={{0,2},{1,3},{2,0},{3,1},{4,6},{5,7},{6,4},{7,5},{8,10},{9,11},{10,... | collective-permute-start | bytes 208904 | tf_op jit(solution)/shard_map/ppermute | solution.py:21
  9.4 7.6 %collective-permute-done.1 = bf16[17,2048]{1,0:T(8,128)(2,1)S(1)} collective-permute-done((bf16[17,2048]{1,0:T(8,128)(2,1)S(1)}, bf16[17,2048]{1,0:T(8,128)(2,1)S(1)}, u32[]{:S(2)}, u32[]{:S(2)}) %collective-permute-start.1) | collective-permute-done | bytes 69664 | tf_op jit(solution)/shard_map/ppermute | solution.py:21
  20.9 5.9 %fusion.162 = f32[128,4,768]{2,0,1:T(8,128)S(1)} fusion(bf16[128,2048,1]{1,0,2:T(8,128)(2,1)S(1)} %bitcast.464, bf16[2,2048,768]{2,1,0:T(8,128)(2,1)} %bitcast.509, bf16[2,2048,768]{2,1,0:T(8,128)(2,1)} %bitcast.516), kind=kOutput, calls=%fused_computation.264 | convolution fusion | flops 1635778560 | bytes 14680064 | tf_op jit(solution)/shard_map/td,def->tef/dot_general | solution.py:108
  34.4 5.4 %collective-permute-done.6 = bf16[16,2048]{1,0:T(8,128)(2,1)S(1)} collective-permute-done((bf16[16,2048]{1,0:T(8,128)(2,1)S(1)}, bf16[16,2048]{1,0:T(8,128)(2,1)S(1)}, u32[]{:S(2)}, u32[]{:S(2)}) %collective-permute-start.6) | collective-permute-done | bytes 65568 | tf_op jit(solution)/shard_map/ppermute | solution.py:21
  47.5 5.0 %collective-permute-done.10 = bf16[16,2048]{1,0:T(8,128)(2,1)S(1)} collective-permute-done((bf16[16,2048]{1,0:T(8,128)(2,1)S(1)}, bf16[16,2048]{1,0:T(8,128)(2,1)S(1)}, u32[]{:S(2)}, u32[]{:S(2)}) %collective-permute-start.10) | collective-permute-done | bytes 65568 | tf_op jit(solution)/shard_map/ppermute | solution.py:54
  56.1 5.8 %fusion.73 = f32[128,4,768]{2,0,1:T(8,128)S(1)} fusion(bf16[128,2048]{1,0:T(8,128)(2,1)S(1)} %fusion.46, bf16[2,2048,768]{2,1,0:T(8,128)(2,1)} %bitcast.510, bf16[2,2048,768]{2,1,0:T(8,128)(2,1)} %bitcast.517), kind=kOutput, calls=%fused_computation.96 | convolution fusion | flops 1635778560 | bytes 14680064 | tf_op jit(solution)/shard_map/td,def->tef/dot_general | solution.py:108
  70.4 4.1 %collective-permute-done.15 = bf16[16,2048]{1,0:T(8,128)(2,1)S(1)} collective-permute-done((bf16[16,2048]{1,0:T(8,128)(2,1)S(1)}, bf16[16,2048]{1,0:T(8,128)(2,1)S(1)}, u32[]{:S(2)}, u32[]{:S(2)}) %collective-permute-start.15) | collective-permute-done | bytes 65568 | tf_op jit(solution)/shard_map/ppermute | solution.py:21
  74.6 2.7 %collective-permute-start.18 = (bf16[16,2048]{1,0:T(8,128)(2,1)S(1)}, bf16[16,2048]{1,0:T(8,128)(2,1)S(1)}, u32[]{:S(2)}, u32[]{:S(2)}) collective-permute-start(bf16[16,2048]{1,0:T(8,128)(2,1)S(1)} %get-tuple-element.23), channel_id=1, source_target_pairs={{0,10},{1,11},{2,8},{3,9},{4,14},{5,15},{6,12},{7,13},{8,18},{9,19... | collective-permute-start | bytes 196616 | tf_op jit(solution)/shard_map/ppermute | solution.py:54
  78.4 3.9 %collective-permute-start.20 = (bf16[16,2048]{1,0:T(8,128)(2,1)S(1)}, bf16[16,2048]{1,0:T(8,128)(2,1)S(1)}, u32[]{:S(2)}, u32[]{:S(2)}) collective-permute-start(bf16[16,2048]{1,0:T(8,128)(2,1)S(1)} %get-tuple-element.23), channel_id=1, source_target_pairs={{0,14},{1,15},{2,12},{3,13},{4,10},{5,11},{6,8},{7,9},{8,22},{9,23... | collective-permute-start | bytes 196616 | tf_op jit(solution)/shard_map/ppermute | solution.py:54
  82.2 2.7 %collective-permute-done.19 = bf16[16,2048]{1,0:T(8,128)(2,1)S(1)} collective-permute-done((bf16[16,2048]{1,0:T(8,128)(2,1)S(1)}, bf16[16,2048]{1,0:T(8,128)(2,1)S(1)}, u32[]{:S(2)}, u32[]{:S(2)}) %collective-permute-start.19) | collective-permute-done | bytes 65568 | tf_op jit(solution)/shard_map/ppermute | solution.py:54
  88.5 5.8 %fusion.71 = f32[128,4,768]{2,0,1:T(8,128)S(1)} fusion(bf16[128,2048]{1,0:T(8,128)(2,1)S(1)} %fusion.44, bf16[2,2048,768]{2,1,0:T(8,128)(2,1)} %bitcast.511, bf16[2,2048,768]{2,1,0:T(8,128)(2,1)} %bitcast.518), kind=kOutput, calls=%fused_computation.94 | convolution fusion | flops 1635778560 | bytes 14680064 | tf_op jit(solution)/shard_map/td,def->tef/dot_general | solution.py:108
  103.0 3.5 %collective-permute-done.24 = bf16[16,2048]{1,0:T(8,128)(2,1)S(1)} collective-permute-done((bf16[16,2048]{1,0:T(8,128)(2,1)S(1)}, bf16[16,2048]{1,0:T(8,128)(2,1)S(1)}, u32[]{:S(2)}, u32[]{:S(2)}) %collective-permute-start.24) | collective-permute-done | bytes 65568 | tf_op jit(solution)/shard_map/ppermute | solution.py:21
  111.5 2.9 %collective-permute-start.29 = (bf16[16,2048]{1,0:T(8,128)(2,1)S(1)}, bf16[16,2048]{1,0:T(8,128)(2,1)S(1)}, u32[]{:S(2)}, u32[]{:S(2)}) collective-permute-start(bf16[16,2048]{1,0:T(8,128)(2,1)S(1)} %get-tuple-element.19), channel_id=1, source_target_pairs={{0,14},{1,15},{2,12},{3,13},{4,10},{5,11},{6,8},{7,9},{8,22},{9,23... | collective-permute-start | bytes 196616 | tf_op jit(solution)/shard_map/ppermute | solution.py:54
  114.3 3.9 %collective-permute-done.28 = bf16[16,2048]{1,0:T(8,128)(2,1)S(1)} collective-permute-done((bf16[16,2048]{1,0:T(8,128)(2,1)S(1)}, bf16[16,2048]{1,0:T(8,128)(2,1)S(1)}, u32[]{:S(2)}, u32[]{:S(2)}) %collective-permute-start.28) | collective-permute-done | bytes 65568 | tf_op jit(solution)/shard_map/ppermute | solution.py:54
  121.6 5.8 %fusion.69 = f32[128,4,768]{2,0,1:T(8,128)S(1)} fusion(bf16[128,2048]{1,0:T(8,128)(2,1)S(1)} %fusion.42, bf16[2,2048,768]{2,1,0:T(8,128)(2,1)} %bitcast.512, bf16[2,2048,768]{2,1,0:T(8,128)(2,1)} %bitcast.519), kind=kOutput, calls=%fused_computation.92 | convolution fusion | flops 1635778560 | bytes 14680064 | tf_op jit(solution)/shard_map/td,def->tef/dot_general | solution.py:108
  135.3 4.7 %collective-permute-done.33 = bf16[16,2048]{1,0:T(8,128)(2,1)S(1)} collective-permute-done((bf16[16,2048]{1,0:T(8,128)(2,1)S(1)}, bf16[16,2048]{1,0:T(8,128)(2,1)S(1)}, u32[]{:S(2)}, u32[]{:S(2)}) %collective-permute-start.33) | collective-permute-done | bytes 65568 | tf_op jit(solution)/shard_map/ppermute | solution.py:21
  140.2 3.1 %collective-permute-start.36 = (bf16[16,2048]{1,0:T(8,128)(2,1)S(1)}, bf16[16,2048]{1,0:T(8,128)(2,1)S(1)}, u32[]{:S(2)}, u32[]{:S(2)}) collective-permute-start(bf16[16,2048]{1,0:T(8,128)(2,1)S(1)} %get-tuple-element.15), channel_id=1, source_target_pairs={{0,10},{1,11},{2,8},{3,9},{4,14},{5,15},{6,12},{7,13},{8,18},{9,19... | collective-permute-start | bytes 196616 | tf_op jit(solution)/shard_map/ppermute | solution.py:54
  144.7 3.1 %collective-permute-start.38 = (bf16[16,2048]{1,0:T(8,128)(2,1)S(1)}, bf16[16,2048]{1,0:T(8,128)(2,1)S(1)}, u32[]{:S(2)}, u32[]{:S(2)}) collective-permute-start(bf16[16,2048]{1,0:T(8,128)(2,1)S(1)} %get-tuple-element.15), channel_id=1, source_target_pairs={{0,14},{1,15},{2,12},{3,13},{4,10},{5,11},{6,8},{7,9},{8,22},{9,23... | collective-permute-start | bytes 196616 | tf_op jit(solution)/shard_map/ppermute | solution.py:54
  147.8 3.2 %collective-permute-done.37 = bf16[16,2048]{1,0:T(8,128)(2,1)S(1)} collective-permute-done((bf16[16,2048]{1,0:T(8,128)(2,1)S(1)}, bf16[16,2048]{1,0:T(8,128)(2,1)S(1)}, u32[]{:S(2)}, u32[]{:S(2)}) %collective-permute-start.37) | collective-permute-done | bytes 65568 | tf_op jit(solution)/shard_map/ppermute | solution.py:54
  154.7 5.7 %fusion.67 = f32[128,4,768]{2,0,1:T(8,128)S(1)} fusion(bf16[128,2048]{1,0:T(8,128)(2,1)S(1)} %fusion.40, bf16[2,2048,768]{2,1,0:T(8,128)(2,1)} %bitcast.513, bf16[2,2048,768]{2,1,0:T(8,128)(2,1)} %bitcast.520), kind=kOutput, calls=%fused_computation.90 | convolution fusion | flops 1635778560 | bytes 14680064 | tf_op jit(solution)/shard_map/td,def->tef/dot_general | solution.py:108
  160.4 3.9 %fusion.26 = f32[128,2048]{1,0:T(8,128)S(1)} fusion(bf16[1,2,768,2048]{3,2,1,0:T(8,128)(2,1)} %param.11, f32[128,4,768]{2,0,1:T(8,128)S(1)} %fusion.67, f32[128,2]{0,1:T(2,128)S(1)} %get-tuple-element.72), kind=kOutput, calls=%fused_computation.19 | convolution fusion | flops 806682624 | bytes 8913920 | tf_op jit(solution)/shard_map/tef,efd->td/dot_general | solution.py:112
  171.3 3.5 %collective-permute-done.42 = bf16[16,2048]{1,0:T(8,128)(2,1)S(1)} collective-permute-done((bf16[16,2048]{1,0:T(8,128)(2,1)S(1)}, bf16[16,2048]{1,0:T(8,128)(2,1)S(1)}, u32[]{:S(2)}, u32[]{:S(2)}) %collective-permute-start.42) | collective-permute-done | bytes 65568 | tf_op jit(solution)/shard_map/ppermute | solution.py:21
  179.6 3.0 %collective-permute-start.47 = (bf16[16,2048]{1,0:T(8,128)(2,1)S(1)}, bf16[16,2048]{1,0:T(8,128)(2,1)S(1)}, u32[]{:S(2)}, u32[]{:S(2)}) collective-permute-start(bf16[16,2048]{1,0:T(8,128)(2,1)S(1)} %get-tuple-element.11), channel_id=1, source_target_pairs={{0,14},{1,15},{2,12},{3,13},{4,10},{5,11},{6,8},{7,9},{8,22},{9,23... | collective-permute-start | bytes 196616 | tf_op jit(solution)/shard_map/ppermute | solution.py:54
  182.6 3.2 %collective-permute-done.46 = bf16[16,2048]{1,0:T(8,128)(2,1)S(1)} collective-permute-done((bf16[16,2048]{1,0:T(8,128)(2,1)S(1)}, bf16[16,2048]{1,0:T(8,128)(2,1)S(1)}, u32[]{:S(2)}, u32[]{:S(2)}) %collective-permute-start.46) | collective-permute-done | bytes 65568 | tf_op jit(solution)/shard_map/ppermute | solution.py:54
  189.7 5.7 %fusion.65 = f32[128,4,768]{2,0,1:T(8,128)S(1)} fusion(bf16[128,2048]{1,0:T(8,128)(2,1)S(1)} %fusion.38, bf16[2,2048,768]{2,1,0:T(8,128)(2,1)} %bitcast.514, bf16[2,2048,768]{2,1,0:T(8,128)(2,1)} %bitcast.521), kind=kOutput, calls=%fused_computation.88 | convolution fusion | flops 1635778560 | bytes 14680064 | tf_op jit(solution)/shard_map/td,def->tef/dot_general | solution.py:108
  195.4 3.9 %fusion.29 = f32[128,2048]{1,0:T(8,128)S(1)} fusion(bf16[1,2,768,2048]{3,2,1,0:T(8,128)(2,1)} %param.11, f32[128,4,768]{2,0,1:T(8,128)S(1)} %fusion.65, f32[128,2]{0,1:T(2,128)S(1)} %get-tuple-element.71), kind=kOutput, calls=%fused_computation.20 | convolution fusion | flops 806682624 | bytes 8913920 | tf_op jit(solution)/shard_map/tef,efd->td/dot_general | solution.py:112
  206.3 3.5 %collective-permute-done.51 = bf16[16,2048]{1,0:T(8,128)(2,1)S(1)} collective-permute-done((bf16[16,2048]{1,0:T(8,128)(2,1)S(1)}, bf16[16,2048]{1,0:T(8,128)(2,1)S(1)}, u32[]{:S(2)}, u32[]{:S(2)}) %collective-permute-start.51) | collective-permute-done | bytes 65568 | tf_op jit(solution)/shard_map/ppermute | solution.py:21
  214.4 3.2 %collective-permute-start.56 = (bf16[16,2048]{1,0:T(8,128)(2,1)S(1)}, bf16[16,2048]{1,0:T(8,128)(2,1)S(1)}, u32[]{:S(2)}, u32[]{:S(2)}) collective-permute-start(bf16[16,2048]{1,0:T(8,128)(2,1)S(1)} %get-tuple-element.7), channel_id=1, source_target_pairs={{0,14},{1,15},{2,12},{3,13},{4,10},{5,11},{6,8},{7,9},{8,22},{9,23... | collective-permute-start | bytes 196616 | tf_op jit(solution)/shard_map/ppermute | solution.py:54
  217.6 3.1 %collective-permute-done.55 = bf16[16,2048]{1,0:T(8,128)(2,1)S(1)} collective-permute-done((bf16[16,2048]{1,0:T(8,128)(2,1)S(1)}, bf16[16,2048]{1,0:T(8,128)(2,1)S(1)}, u32[]{:S(2)}, u32[]{:S(2)}) %collective-permute-start.55) | collective-permute-done | bytes 65568 | tf_op jit(solution)/shard_map/ppermute | solution.py:54
  224.5 5.7 %fusion.63 = f32[128,4,768]{2,0,1:T(8,128)S(1)} fusion(bf16[128,2048]{1,0:T(8,128)(2,1)S(1)} %fusion.36, bf16[2,2048,768]{2,1,0:T(8,128)(2,1)} %bitcast.515, bf16[2,2048,768]{2,1,0:T(8,128)(2,1)} %bitcast.522), kind=kOutput, calls=%fused_computation.86 | convolution fusion | flops 1635778560 | bytes 14680064 | tf_op jit(solution)/shard_map/td,def->tef/dot_general | solution.py:108
  230.2 3.9 %fusion.32 = f32[128,2048]{1,0:T(8,128)S(1)} fusion(bf16[1,2,768,2048]{3,2,1,0:T(8,128)(2,1)} %param.11, f32[128,4,768]{2,0,1:T(8,128)S(1)} %fusion.63, f32[128,2]{0,1:T(2,128)S(1)} %get-tuple-element.70), kind=kOutput, calls=%fused_computation.21 | convolution fusion | flops 806682624 | bytes 8913920 | tf_op jit(solution)/shard_map/tef,efd->td/dot_general | solution.py:112
  241.1 3.5 %collective-permute-done.60 = bf16[16,2048]{1,0:T(8,128)(2,1)S(1)} collective-permute-done((bf16[16,2048]{1,0:T(8,128)(2,1)S(1)}, bf16[16,2048]{1,0:T(8,128)(2,1)S(1)}, u32[]{:S(2)}, u32[]{:S(2)}) %collective-permute-start.60) | collective-permute-done | bytes 65568 | tf_op jit(solution)/shard_map/ppermute | solution.py:21
  (233 shorter events, 110.1 us)
Async XLA Ops:
  6.6 10.4 %collective-permute-start.1 = (bf16[17,2048]{1,0:T(8,128)(2,1)S(1)}, bf16[17,2048]{1,0:T(8,128)(2,1)S(1)}, u32[]{:S(2)}, u32[]{:S(2)}) collective-permute-start(bf16[17,2048]{1,0:T(8,128)(2,1)S(1)} %get-tuple-element.69), channel_id=1, source_target_pairs={{0,4},{1,5},{2,6},{3,7},{4,0},{5,1},{6,2},{7,3},{8,12},{9,13},{10,... | collective-permute-start | bytes 208904 | tf_op jit(solution)/shard_map/ppermute | solution.py:21
  9.2 7.8 %collective-permute-start.2 = (bf16[17,2048]{1,0:T(8,128)(2,1)S(1)}, bf16[17,2048]{1,0:T(8,128)(2,1)S(1)}, u32[]{:S(2)}, u32[]{:S(2)}) collective-permute-start(bf16[17,2048]{1,0:T(8,128)(2,1)S(1)} %get-tuple-element.69), channel_id=1, source_target_pairs={{0,6},{1,7},{2,4},{3,5},{4,2},{5,3},{6,0},{7,1},{8,14},{9,15},{10,... | collective-permute-start | bytes 208904 | tf_op jit(solution)/shard_map/ppermute | solution.py:21
  31.5 8.2 %collective-permute-start.6 = (bf16[16,2048]{1,0:T(8,128)(2,1)S(1)}, bf16[16,2048]{1,0:T(8,128)(2,1)S(1)}, u32[]{:S(2)}, u32[]{:S(2)}) collective-permute-start(bf16[16,2048]{1,0:T(8,128)(2,1)S(1)} %get-tuple-element.67), channel_id=1, source_target_pairs={{0,4},{1,5},{2,6},{3,7},{4,0},{5,1},{6,2},{7,3},{8,12},{9,13},{10,... | collective-permute-start | bytes 196616 | tf_op jit(solution)/shard_map/ppermute | solution.py:21
  32.9 6.8 %collective-permute-start.7 = (bf16[16,2048]{1,0:T(8,128)(2,1)S(1)}, bf16[16,2048]{1,0:T(8,128)(2,1)S(1)}, u32[]{:S(2)}, u32[]{:S(2)}) collective-permute-start(bf16[16,2048]{1,0:T(8,128)(2,1)S(1)} %get-tuple-element.66), channel_id=1, source_target_pairs={{0,6},{1,7},{2,4},{3,5},{4,2},{5,3},{6,0},{7,1},{8,14},{9,15},{10,... | collective-permute-start | bytes 196616 | tf_op jit(solution)/shard_map/ppermute | solution.py:21
  39.8 7.7 %collective-permute-start.8 = (bf16[16,2048]{1,0:T(8,128)(2,1)S(1)}, bf16[16,2048]{1,0:T(8,128)(2,1)S(1)}, u32[]{:S(2)}, u32[]{:S(2)}) collective-permute-start(bf16[16,2048]{1,0:T(8,128)(2,1)S(1)} %get-tuple-element.27), channel_id=1, source_target_pairs={{0,8},{1,9},{2,10},{3,11},{4,12},{5,13},{6,14},{7,15},{8,16},{9,17... | collective-permute-start | bytes 196616 | tf_op jit(solution)/shard_map/ppermute | solution.py:54
  43.6 8.9 %collective-permute-start.10 = (bf16[16,2048]{1,0:T(8,128)(2,1)S(1)}, bf16[16,2048]{1,0:T(8,128)(2,1)S(1)}, u32[]{:S(2)}, u32[]{:S(2)}) collective-permute-start(bf16[16,2048]{1,0:T(8,128)(2,1)S(1)} %get-tuple-element.27), channel_id=1, source_target_pairs={{0,12},{1,13},{2,14},{3,15},{4,8},{5,9},{6,10},{7,11},{8,20},{9,21... | collective-permute-start | bytes 196616 | tf_op jit(solution)/shard_map/ppermute | solution.py:54
  45.9 8.0 %collective-permute-start.11 = (bf16[16,2048]{1,0:T(8,128)(2,1)S(1)}, bf16[16,2048]{1,0:T(8,128)(2,1)S(1)}, u32[]{:S(2)}, u32[]{:S(2)}) collective-permute-start(bf16[16,2048]{1,0:T(8,128)(2,1)S(1)} %get-tuple-element.27), channel_id=1, source_target_pairs={{0,14},{1,15},{2,12},{3,13},{4,10},{5,11},{6,8},{7,9},{8,22},{9,23... | collective-permute-start | bytes 196616 | tf_op jit(solution)/shard_map/ppermute | solution.py:54
  66.2 8.3 %collective-permute-start.15 = (bf16[16,2048]{1,0:T(8,128)(2,1)S(1)}, bf16[16,2048]{1,0:T(8,128)(2,1)S(1)}, u32[]{:S(2)}, u32[]{:S(2)}) collective-permute-start(bf16[16,2048]{1,0:T(8,128)(2,1)S(1)} %get-tuple-element.62), channel_id=1, source_target_pairs={{0,4},{1,5},{2,6},{3,7},{4,0},{5,1},{6,2},{7,3},{8,12},{9,13},{10,... | collective-permute-start | bytes 196616 | tf_op jit(solution)/shard_map/ppermute | solution.py:21
  67.7 6.8 %collective-permute-start.16 = (bf16[16,2048]{1,0:T(8,128)(2,1)S(1)}, bf16[16,2048]{1,0:T(8,128)(2,1)S(1)}, u32[]{:S(2)}, u32[]{:S(2)}) collective-permute-start(bf16[16,2048]{1,0:T(8,128)(2,1)S(1)} %get-tuple-element.61), channel_id=1, source_target_pairs={{0,6},{1,7},{2,4},{3,5},{4,2},{5,3},{6,0},{7,1},{8,14},{9,15},{10,... | collective-permute-start | bytes 196616 | tf_op jit(solution)/shard_map/ppermute | solution.py:21
  74.5 7.7 %collective-permute-start.17 = (bf16[16,2048]{1,0:T(8,128)(2,1)S(1)}, bf16[16,2048]{1,0:T(8,128)(2,1)S(1)}, u32[]{:S(2)}, u32[]{:S(2)}) collective-permute-start(bf16[16,2048]{1,0:T(8,128)(2,1)S(1)} %get-tuple-element.23), channel_id=1, source_target_pairs={{0,8},{1,9},{2,10},{3,11},{4,12},{5,13},{6,14},{7,15},{8,16},{9,17... | collective-permute-start | bytes 196616 | tf_op jit(solution)/shard_map/ppermute | solution.py:54
  74.6 7.6 %collective-permute-start.18 = (bf16[16,2048]{1,0:T(8,128)(2,1)S(1)}, bf16[16,2048]{1,0:T(8,128)(2,1)S(1)}, u32[]{:S(2)}, u32[]{:S(2)}) collective-permute-start(bf16[16,2048]{1,0:T(8,128)(2,1)S(1)} %get-tuple-element.23), channel_id=1, source_target_pairs={{0,10},{1,11},{2,8},{3,9},{4,14},{5,15},{6,12},{7,13},{8,18},{9,19... | collective-permute-start | bytes 196616 | tf_op jit(solution)/shard_map/ppermute | solution.py:54
  77.3 7.7 %collective-permute-start.19 = (bf16[16,2048]{1,0:T(8,128)(2,1)S(1)}, bf16[16,2048]{1,0:T(8,128)(2,1)S(1)}, u32[]{:S(2)}, u32[]{:S(2)}) collective-permute-start(bf16[16,2048]{1,0:T(8,128)(2,1)S(1)} %get-tuple-element.23), channel_id=1, source_target_pairs={{0,12},{1,13},{2,14},{3,15},{4,8},{5,9},{6,10},{7,11},{8,20},{9,21... | collective-permute-start | bytes 196616 | tf_op jit(solution)/shard_map/ppermute | solution.py:54
  78.4 7.9 %collective-permute-start.20 = (bf16[16,2048]{1,0:T(8,128)(2,1)S(1)}, bf16[16,2048]{1,0:T(8,128)(2,1)S(1)}, u32[]{:S(2)}, u32[]{:S(2)}) collective-permute-start(bf16[16,2048]{1,0:T(8,128)(2,1)S(1)} %get-tuple-element.23), channel_id=1, source_target_pairs={{0,14},{1,15},{2,12},{3,13},{4,10},{5,11},{6,8},{7,9},{8,22},{9,23... | collective-permute-start | bytes 196616 | tf_op jit(solution)/shard_map/ppermute | solution.py:54
  97.9 8.7 %collective-permute-start.24 = (bf16[16,2048]{1,0:T(8,128)(2,1)S(1)}, bf16[16,2048]{1,0:T(8,128)(2,1)S(1)}, u32[]{:S(2)}, u32[]{:S(2)}) collective-permute-start(bf16[16,2048]{1,0:T(8,128)(2,1)S(1)} %get-tuple-element.57), channel_id=1, source_target_pairs={{0,4},{1,5},{2,6},{3,7},{4,0},{5,1},{6,2},{7,3},{8,12},{9,13},{10,... | collective-permute-start | bytes 196616 | tf_op jit(solution)/shard_map/ppermute | solution.py:21
  106.6 7.7 %collective-permute-start.26 = (bf16[16,2048]{1,0:T(8,128)(2,1)S(1)}, bf16[16,2048]{1,0:T(8,128)(2,1)S(1)}, u32[]{:S(2)}, u32[]{:S(2)}) collective-permute-start(bf16[16,2048]{1,0:T(8,128)(2,1)S(1)} %get-tuple-element.19), channel_id=1, source_target_pairs={{0,8},{1,9},{2,10},{3,11},{4,12},{5,13},{6,14},{7,15},{8,16},{9,17... | collective-permute-start | bytes 196616 | tf_op jit(solution)/shard_map/ppermute | solution.py:54
  110.5 7.7 %collective-permute-start.28 = (bf16[16,2048]{1,0:T(8,128)(2,1)S(1)}, bf16[16,2048]{1,0:T(8,128)(2,1)S(1)}, u32[]{:S(2)}, u32[]{:S(2)}) collective-permute-start(bf16[16,2048]{1,0:T(8,128)(2,1)S(1)} %get-tuple-element.19), channel_id=1, source_target_pairs={{0,12},{1,13},{2,14},{3,15},{4,8},{5,9},{6,10},{7,11},{8,20},{9,21... | collective-permute-start | bytes 196616 | tf_op jit(solution)/shard_map/ppermute | solution.py:54
  111.5 8.0 %collective-permute-start.29 = (bf16[16,2048]{1,0:T(8,128)(2,1)S(1)}, bf16[16,2048]{1,0:T(8,128)(2,1)S(1)}, u32[]{:S(2)}, u32[]{:S(2)}) collective-permute-start(bf16[16,2048]{1,0:T(8,128)(2,1)S(1)} %get-tuple-element.19), channel_id=1, source_target_pairs={{0,14},{1,15},{2,12},{3,13},{4,10},{5,11},{6,8},{7,9},{8,22},{9,23... | collective-permute-start | bytes 196616 | tf_op jit(solution)/shard_map/ppermute | solution.py:54
  131.8 8.3 %collective-permute-start.33 = (bf16[16,2048]{1,0:T(8,128)(2,1)S(1)}, bf16[16,2048]{1,0:T(8,128)(2,1)S(1)}, u32[]{:S(2)}, u32[]{:S(2)}) collective-permute-start(bf16[16,2048]{1,0:T(8,128)(2,1)S(1)} %get-tuple-element.52), channel_id=1, source_target_pairs={{0,4},{1,5},{2,6},{3,7},{4,0},{5,1},{6,2},{7,3},{8,12},{9,13},{10,... | collective-permute-start | bytes 196616 | tf_op jit(solution)/shard_map/ppermute | solution.py:21
  140.1 7.7 %collective-permute-start.35 = (bf16[16,2048]{1,0:T(8,128)(2,1)S(1)}, bf16[16,2048]{1,0:T(8,128)(2,1)S(1)}, u32[]{:S(2)}, u32[]{:S(2)}) collective-permute-start(bf16[16,2048]{1,0:T(8,128)(2,1)S(1)} %get-tuple-element.15), channel_id=1, source_target_pairs={{0,8},{1,9},{2,10},{3,11},{4,12},{5,13},{6,14},{7,15},{8,16},{9,17... | collective-permute-start | bytes 196616 | tf_op jit(solution)/shard_map/ppermute | solution.py:54
  140.2 7.6 %collective-permute-start.36 = (bf16[16,2048]{1,0:T(8,128)(2,1)S(1)}, bf16[16,2048]{1,0:T(8,128)(2,1)S(1)}, u32[]{:S(2)}, u32[]{:S(2)}) collective-permute-start(bf16[16,2048]{1,0:T(8,128)(2,1)S(1)} %get-tuple-element.15), channel_id=1, source_target_pairs={{0,10},{1,11},{2,8},{3,9},{4,14},{5,15},{6,12},{7,13},{8,18},{9,19... | collective-permute-start | bytes 196616 | tf_op jit(solution)/shard_map/ppermute | solution.py:54
  143.3 7.7 %collective-permute-start.37 = (bf16[16,2048]{1,0:T(8,128)(2,1)S(1)}, bf16[16,2048]{1,0:T(8,128)(2,1)S(1)}, u32[]{:S(2)}, u32[]{:S(2)}) collective-permute-start(bf16[16,2048]{1,0:T(8,128)(2,1)S(1)} %get-tuple-element.15), channel_id=1, source_target_pairs={{0,12},{1,13},{2,14},{3,15},{4,8},{5,9},{6,10},{7,11},{8,20},{9,21... | collective-permute-start | bytes 196616 | tf_op jit(solution)/shard_map/ppermute | solution.py:54
  144.7 7.9 %collective-permute-start.38 = (bf16[16,2048]{1,0:T(8,128)(2,1)S(1)}, bf16[16,2048]{1,0:T(8,128)(2,1)S(1)}, u32[]{:S(2)}, u32[]{:S(2)}) collective-permute-start(bf16[16,2048]{1,0:T(8,128)(2,1)S(1)} %get-tuple-element.15), channel_id=1, source_target_pairs={{0,14},{1,15},{2,12},{3,13},{4,10},{5,11},{6,8},{7,9},{8,22},{9,23... | collective-permute-start | bytes 196616 | tf_op jit(solution)/shard_map/ppermute | solution.py:54
  166.2 8.7 %collective-permute-start.42 = (bf16[16,2048]{1,0:T(8,128)(2,1)S(1)}, bf16[16,2048]{1,0:T(8,128)(2,1)S(1)}, u32[]{:S(2)}, u32[]{:S(2)}) collective-permute-start(bf16[16,2048]{1,0:T(8,128)(2,1)S(1)} %get-tuple-element.47), channel_id=1, source_target_pairs={{0,4},{1,5},{2,6},{3,7},{4,0},{5,1},{6,2},{7,3},{8,12},{9,13},{10,... | collective-permute-start | bytes 196616 | tf_op jit(solution)/shard_map/ppermute | solution.py:21
  174.9 7.7 %collective-permute-start.44 = (bf16[16,2048]{1,0:T(8,128)(2,1)S(1)}, bf16[16,2048]{1,0:T(8,128)(2,1)S(1)}, u32[]{:S(2)}, u32[]{:S(2)}) collective-permute-start(bf16[16,2048]{1,0:T(8,128)(2,1)S(1)} %get-tuple-element.11), channel_id=1, source_target_pairs={{0,8},{1,9},{2,10},{3,11},{4,12},{5,13},{6,14},{7,15},{8,16},{9,17... | collective-permute-start | bytes 196616 | tf_op jit(solution)/shard_map/ppermute | solution.py:54
  178.1 7.7 %collective-permute-start.46 = (bf16[16,2048]{1,0:T(8,128)(2,1)S(1)}, bf16[16,2048]{1,0:T(8,128)(2,1)S(1)}, u32[]{:S(2)}, u32[]{:S(2)}) collective-permute-start(bf16[16,2048]{1,0:T(8,128)(2,1)S(1)} %get-tuple-element.11), channel_id=1, source_target_pairs={{0,12},{1,13},{2,14},{3,15},{4,8},{5,9},{6,10},{7,11},{8,20},{9,21... | collective-permute-start | bytes 196616 | tf_op jit(solution)/shard_map/ppermute | solution.py:54
  179.6 7.9 %collective-permute-start.47 = (bf16[16,2048]{1,0:T(8,128)(2,1)S(1)}, bf16[16,2048]{1,0:T(8,128)(2,1)S(1)}, u32[]{:S(2)}, u32[]{:S(2)}) collective-permute-start(bf16[16,2048]{1,0:T(8,128)(2,1)S(1)} %get-tuple-element.11), channel_id=1, source_target_pairs={{0,14},{1,15},{2,12},{3,13},{4,10},{5,11},{6,8},{7,9},{8,22},{9,23... | collective-permute-start | bytes 196616 | tf_op jit(solution)/shard_map/ppermute | solution.py:54
  201.1 8.7 %collective-permute-start.51 = (bf16[16,2048]{1,0:T(8,128)(2,1)S(1)}, bf16[16,2048]{1,0:T(8,128)(2,1)S(1)}, u32[]{:S(2)}, u32[]{:S(2)}) collective-permute-start(bf16[16,2048]{1,0:T(8,128)(2,1)S(1)} %get-tuple-element.42), channel_id=1, source_target_pairs={{0,4},{1,5},{2,6},{3,7},{4,0},{5,1},{6,2},{7,3},{8,12},{9,13},{10,... | collective-permute-start | bytes 196616 | tf_op jit(solution)/shard_map/ppermute | solution.py:21
  209.9 7.7 %collective-permute-start.53 = (bf16[16,2048]{1,0:T(8,128)(2,1)S(1)}, bf16[16,2048]{1,0:T(8,128)(2,1)S(1)}, u32[]{:S(2)}, u32[]{:S(2)}) collective-permute-start(bf16[16,2048]{1,0:T(8,128)(2,1)S(1)} %get-tuple-element.7), channel_id=1, source_target_pairs={{0,8},{1,9},{2,10},{3,11},{4,12},{5,13},{6,14},{7,15},{8,16},{9,17... | collective-permute-start | bytes 196616 | tf_op jit(solution)/shard_map/ppermute | solution.py:54
  210.6 7.0 %collective-permute-start.54 = (bf16[16,2048]{1,0:T(8,128)(2,1)S(1)}, bf16[16,2048]{1,0:T(8,128)(2,1)S(1)}, u32[]{:S(2)}, u32[]{:S(2)}) collective-permute-start(bf16[16,2048]{1,0:T(8,128)(2,1)S(1)} %get-tuple-element.7), channel_id=1, source_target_pairs={{0,10},{1,11},{2,8},{3,9},{4,14},{5,15},{6,12},{7,13},{8,18},{9,19... | collective-permute-start | bytes 196616 | tf_op jit(solution)/shard_map/ppermute | solution.py:54
  213.1 7.7 %collective-permute-start.55 = (bf16[16,2048]{1,0:T(8,128)(2,1)S(1)}, bf16[16,2048]{1,0:T(8,128)(2,1)S(1)}, u32[]{:S(2)}, u32[]{:S(2)}) collective-permute-start(bf16[16,2048]{1,0:T(8,128)(2,1)S(1)} %get-tuple-element.7), channel_id=1, source_target_pairs={{0,12},{1,13},{2,14},{3,15},{4,8},{5,9},{6,10},{7,11},{8,20},{9,21... | collective-permute-start | bytes 196616 | tf_op jit(solution)/shard_map/ppermute | solution.py:54
  214.4 7.9 %collective-permute-start.56 = (bf16[16,2048]{1,0:T(8,128)(2,1)S(1)}, bf16[16,2048]{1,0:T(8,128)(2,1)S(1)}, u32[]{:S(2)}, u32[]{:S(2)}) collective-permute-start(bf16[16,2048]{1,0:T(8,128)(2,1)S(1)} %get-tuple-element.7), channel_id=1, source_target_pairs={{0,14},{1,15},{2,12},{3,13},{4,10},{5,11},{6,8},{7,9},{8,22},{9,23... | collective-permute-start | bytes 196616 | tf_op jit(solution)/shard_map/ppermute | solution.py:54
  235.9 8.7 %collective-permute-start.60 = (bf16[16,2048]{1,0:T(8,128)(2,1)S(1)}, bf16[16,2048]{1,0:T(8,128)(2,1)S(1)}, u32[]{:S(2)}, u32[]{:S(2)}) collective-permute-start(bf16[16,2048]{1,0:T(8,128)(2,1)S(1)} %get-tuple-element.37), channel_id=1, source_target_pairs={{0,4},{1,5},{2,6},{3,7},{4,0},{5,1},{6,2},{7,3},{8,12},{9,13},{10,... | collective-permute-start | bytes 196616 | tf_op jit(solution)/shard_map/ppermute | solution.py:21
  (40 other events, 204.7 us)

commit v14 on v13

--- a/solution.py
+++ b/solution.py
@@ -109,7 +109,9 @@
         gate_part = both[:, :local_experts]
         up_part = both[:, local_experts:]
         inner = (jax.nn.silu(gate_part) * up_part * weight.T[:, :, None]).astype(jnp.bfloat16)
-        partial = jnp.einsum("tef,efd->td", inner, w_down, preferred_element_type=jnp.float32)
+        partial = jnp.dot(
+            inner.reshape(inner.shape[0], -1), w_down.reshape(-1, width), preferred_element_type=jnp.float32
+        )
         mixed = scatter_blocks(partial.reshape(2, chips, tok_rows, width), "expert")
         produced = (values[0, 0] + mixed).astype(jnp.bfloat16)
         updated = lax.dynamic_update_index_in_dim(collected, produced, clipped, 0)

time: 246 us -> 257 us (1.045)
  matrix products: 56.9 us -> 66.6 us
    dot_general x7, matrix products: 16.5 us -> 26.7 us  [on_device(): jnp.dot(inner.reshape(inner.shape[0], -1), w_down.reshape(-1, width), pre...]
where the time goes in v14:
time: 257 us
  waiting for transfers between devices  89.4 us (35%)
  starting transfers between devices  85 us (33%)
  matrix products  66.6 us (26%)
  other arithmetic  9.03 us (4%)
  local copies, waits for them, and re-layouts  5.87 us (2%)
    ppermute x24, starting transfers between devices, to_next_section(): return lax.ppermute(array, ('section', 'expert'), pairs)  46.2 us
    dot_general x7, matrix products, on_device(): jnp.einsum('td,def->tef', rows, w_gate_up, preferred_element_type=jnp.flo...  39.9 us
    ppermute x24, waiting for transfers between devices, chip_swap(): return lax.ppermute(array, axis, pairs)  39.5 us
    ppermute x24, starting transfers between devices, chip_swap(): return lax.ppermute(array, axis, pairs)  36.8 us
    ppermute x24, waiting for transfers between devices, to_next_section(): return lax.ppermute(array, ('section', 'expert'), pairs)  29.8 us
    dot_general x7, matrix products, on_device(): jnp.dot(inner.reshape(inner.shape[0], -1), w_down.reshape(-1, width), pre...  26.7 us
    ppermute x14, waiting for transfers between devices, core_swap(): return lax.ppermute(array, axis, [(i, i ^ 1) for i in range(count)])  20.1 us
  transfers between devices with their start and end apart: 62, of which 39 were waited for; matrix products, arithmetic and copies ran while one was open for 0% of the time, Pallas kernels for 0%

profile of v14, /device:TPU:0, one launch (start us, length us, event | category | flops | bytes accessed | tf_op | source)
XLA Modules:
  0.0 256.8 jit_solution(1560559337087851101)
XLA Ops:
  3.5 3.1 %collective-permute-start = (bf16[17,2048]{1,0:T(8,128)(2,1)S(1)}, bf16[17,2048]{1,0:T(8,128)(2,1)S(1)}, u32[]{:S(2)}, u32[]{:S(2)}) collective-permute-start(bf16[17,2048]{1,0:T(8,128)(2,1)S(1)} %get-tuple-element.69), channel_id=1, source_target_pairs={{0,2},{1,3},{2,0},{3,1},{4,6},{5,7},{6,4},{7,5},{8,10},{9,11},{10,... | collective-permute-start | bytes 208904 | tf_op jit(solution)/shard_map/ppermute | solution.py:21
  9.4 7.6 %collective-permute-done.1 = bf16[17,2048]{1,0:T(8,128)(2,1)S(1)} collective-permute-done((bf16[17,2048]{1,0:T(8,128)(2,1)S(1)}, bf16[17,2048]{1,0:T(8,128)(2,1)S(1)}, u32[]{:S(2)}, u32[]{:S(2)}) %collective-permute-start.1) | collective-permute-done | bytes 69664 | tf_op jit(solution)/shard_map/ppermute | solution.py:21
  20.7 5.7 %fusion.99 = f32[128,4,768]{2,0,1:T(8,128)S(1)} fusion(bf16[128,2048,1]{1,0,2:T(8,128)(2,1)S(1)} %bitcast.457, bf16[2,2048,768]{2,1,0:T(8,128)(2,1)} %bitcast.502, bf16[2,2048,768]{2,1,0:T(8,128)(2,1)} %bitcast.509), kind=kOutput, calls=%fused_computation.222 | convolution fusion | flops 1635778560 | bytes 14680064 | tf_op jit(solution)/shard_map/td,def->tef/dot_general | solution.py:108
  27.0 3.9 %fusion.113 = f32[128,2048]{1,0:T(8,128)S(1)} fusion(bf16[128,1536]{0,1:T(8,128)(2,1)S(1)} %bitcast.431, bf16[1536,2048]{1,0:T(8,128)(2,1)} %bitcast.419), kind=kOutput, calls=%fused_computation.230 | convolution fusion | flops 805306368 | bytes 7733248 | tf_op jit(solution)/shard_map/dot_general | solution.py:112
  37.1 5.4 %collective-permute-done.6 = bf16[16,2048]{1,0:T(8,128)(2,1)S(1)} collective-permute-done((bf16[16,2048]{1,0:T(8,128)(2,1)S(1)}, bf16[16,2048]{1,0:T(8,128)(2,1)S(1)}, u32[]{:S(2)}, u32[]{:S(2)}) %collective-permute-start.6) | collective-permute-done | bytes 65568 | tf_op jit(solution)/shard_map/ppermute | solution.py:21
  50.3 5.0 %collective-permute-done.10 = bf16[16,2048]{1,0:T(8,128)(2,1)S(1)} collective-permute-done((bf16[16,2048]{1,0:T(8,128)(2,1)S(1)}, bf16[16,2048]{1,0:T(8,128)(2,1)S(1)}, u32[]{:S(2)}, u32[]{:S(2)}) %collective-permute-start.10) | collective-permute-done | bytes 65568 | tf_op jit(solution)/shard_map/ppermute | solution.py:54
  58.8 5.7 %fusion.38 = f32[128,4,768]{2,0,1:T(8,128)S(1)} fusion(bf16[128,2048]{1,0:T(8,128)(2,1)S(1)} %fusion.11, bf16[2,2048,768]{2,1,0:T(8,128)(2,1)} %bitcast.503, bf16[2,2048,768]{2,1,0:T(8,128)(2,1)} %bitcast.510), kind=kOutput, calls=%fused_computation.75 | convolution fusion | flops 1635778560 | bytes 14680064 | tf_op jit(solution)/shard_map/td,def->tef/dot_general | solution.py:108
  65.0 3.8 %fusion.114 = f32[128,2048]{1,0:T(8,128)S(1)} fusion(bf16[128,1536]{0,1:T(8,128)(2,1)S(1)} %bitcast.432, bf16[1536,2048]{1,0:T(8,128)(2,1)} %bitcast.420), kind=kOutput, calls=%fused_computation.231 | convolution fusion | flops 805306368 | bytes 7733248 | tf_op jit(solution)/shard_map/dot_general | solution.py:112
  75.6 4.1 %collective-permute-done.15 = bf16[16,2048]{1,0:T(8,128)(2,1)S(1)} collective-permute-done((bf16[16,2048]{1,0:T(8,128)(2,1)S(1)}, bf16[16,2048]{1,0:T(8,128)(2,1)S(1)}, u32[]{:S(2)}, u32[]{:S(2)}) %collective-permute-start.15) | collective-permute-done | bytes 65568 | tf_op jit(solution)/shard_map/ppermute | solution.py:21
  83.5 3.9 %collective-permute-start.20 = (bf16[16,2048]{1,0:T(8,128)(2,1)S(1)}, bf16[16,2048]{1,0:T(8,128)(2,1)S(1)}, u32[]{:S(2)}, u32[]{:S(2)}) collective-permute-start(bf16[16,2048]{1,0:T(8,128)(2,1)S(1)} %get-tuple-element.23), channel_id=1, source_target_pairs={{0,14},{1,15},{2,12},{3,13},{4,10},{5,11},{6,8},{7,9},{8,22},{9,23... | collective-permute-start | bytes 196616 | tf_op jit(solution)/shard_map/ppermute | solution.py:54
  93.7 5.7 %fusion.36 = f32[128,4,768]{2,0,1:T(8,128)S(1)} fusion(bf16[128,2048]{1,0:T(8,128)(2,1)S(1)} %fusion.9, bf16[2,2048,768]{2,1,0:T(8,128)(2,1)} %bitcast.504, bf16[2,2048,768]{2,1,0:T(8,128)(2,1)} %bitcast.511), kind=kOutput, calls=%fused_computation.73 | convolution fusion | flops 1635778560 | bytes 14680064 | tf_op jit(solution)/shard_map/td,def->tef/dot_general | solution.py:108
  99.9 3.8 %fusion.115 = f32[128,2048]{1,0:T(8,128)S(1)} fusion(bf16[128,1536]{0,1:T(8,128)(2,1)S(1)} %bitcast.433, bf16[1536,2048]{1,0:T(8,128)(2,1)} %bitcast.421), kind=kOutput, calls=%fused_computation.232 | convolution fusion | flops 805306368 | bytes 7733248 | tf_op jit(solution)/shard_map/dot_general | solution.py:112
  110.4 3.9 %collective-permute-done.24 = bf16[16,2048]{1,0:T(8,128)(2,1)S(1)} collective-permute-done((bf16[16,2048]{1,0:T(8,128)(2,1)S(1)}, bf16[16,2048]{1,0:T(8,128)(2,1)S(1)}, u32[]{:S(2)}, u32[]{:S(2)}) %collective-permute-start.24) | collective-permute-done | bytes 65568 | tf_op jit(solution)/shard_map/ppermute | solution.py:21
  119.1 3.0 %collective-permute-start.29 = (bf16[16,2048]{1,0:T(8,128)(2,1)S(1)}, bf16[16,2048]{1,0:T(8,128)(2,1)S(1)}, u32[]{:S(2)}, u32[]{:S(2)}) collective-permute-start(bf16[16,2048]{1,0:T(8,128)(2,1)S(1)} %get-tuple-element.19), channel_id=1, source_target_pairs={{0,14},{1,15},{2,12},{3,13},{4,10},{5,11},{6,8},{7,9},{8,22},{9,23... | collective-permute-start | bytes 196616 | tf_op jit(solution)/shard_map/ppermute | solution.py:54
  122.1 3.8 %collective-permute-done.28 = bf16[16,2048]{1,0:T(8,128)(2,1)S(1)} collective-permute-done((bf16[16,2048]{1,0:T(8,128)(2,1)S(1)}, bf16[16,2048]{1,0:T(8,128)(2,1)S(1)}, u32[]{:S(2)}, u32[]{:S(2)}) %collective-permute-start.28) | collective-permute-done | bytes 65568 | tf_op jit(solution)/shard_map/ppermute | solution.py:54
  129.2 5.7 %fusion.34 = f32[128,4,768]{2,0,1:T(8,128)S(1)} fusion(bf16[128,2048]{1,0:T(8,128)(2,1)S(1)} %fusion.7, bf16[2,2048,768]{2,1,0:T(8,128)(2,1)} %bitcast.505, bf16[2,2048,768]{2,1,0:T(8,128)(2,1)} %bitcast.512), kind=kOutput, calls=%fused_computation.71 | convolution fusion | flops 1635778560 | bytes 14680064 | tf_op jit(solution)/shard_map/td,def->tef/dot_general | solution.py:108
  135.4 3.8 %fusion.116 = f32[128,2048]{1,0:T(8,128)S(1)} fusion(bf16[128,1536]{0,1:T(8,128)(2,1)S(1)} %bitcast.434, bf16[1536,2048]{1,0:T(8,128)(2,1)} %bitcast.422), kind=kOutput, calls=%fused_computation.233 | convolution fusion | flops 805306368 | bytes 7733248 | tf_op jit(solution)/shard_map/dot_general | solution.py:112
  145.4 4.7 %collective-permute-done.33 = bf16[16,2048]{1,0:T(8,128)(2,1)S(1)} collective-permute-done((bf16[16,2048]{1,0:T(8,128)(2,1)S(1)}, bf16[16,2048]{1,0:T(8,128)(2,1)S(1)}, u32[]{:S(2)}, u32[]{:S(2)}) %collective-permute-start.33) | collective-permute-done | bytes 65568 | tf_op jit(solution)/shard_map/ppermute | solution.py:21
  154.7 3.1 %collective-permute-start.38 = (bf16[16,2048]{1,0:T(8,128)(2,1)S(1)}, bf16[16,2048]{1,0:T(8,128)(2,1)S(1)}, u32[]{:S(2)}, u32[]{:S(2)}) collective-permute-start(bf16[16,2048]{1,0:T(8,128)(2,1)S(1)} %get-tuple-element.15), channel_id=1, source_target_pairs={{0,14},{1,15},{2,12},{3,13},{4,10},{5,11},{6,8},{7,9},{8,22},{9,23... | collective-permute-start | bytes 196616 | tf_op jit(solution)/shard_map/ppermute | solution.py:54
  157.9 3.2 %collective-permute-done.37 = bf16[16,2048]{1,0:T(8,128)(2,1)S(1)} collective-permute-done((bf16[16,2048]{1,0:T(8,128)(2,1)S(1)}, bf16[16,2048]{1,0:T(8,128)(2,1)S(1)}, u32[]{:S(2)}, u32[]{:S(2)}) %collective-permute-start.37) | collective-permute-done | bytes 65568 | tf_op jit(solution)/shard_map/ppermute | solution.py:54
  164.8 5.7 %fusion.32 = f32[128,4,768]{2,0,1:T(8,128)S(1)} fusion(bf16[128,2048]{1,0:T(8,128)(2,1)S(1)} %fusion.5, bf16[2,2048,768]{2,1,0:T(8,128)(2,1)} %bitcast.506, bf16[2,2048,768]{2,1,0:T(8,128)(2,1)} %bitcast.513), kind=kOutput, calls=%fused_computation.69 | convolution fusion | flops 1635778560 | bytes 14680064 | tf_op jit(solution)/shard_map/td,def->tef/dot_general | solution.py:108
  171.0 3.8 %fusion.117 = f32[128,2048]{1,0:T(8,128)S(1)} fusion(bf16[128,1536]{0,1:T(8,128)(2,1)S(1)} %bitcast.435, bf16[1536,2048]{1,0:T(8,128)(2,1)} %bitcast.423), kind=kOutput, calls=%fused_computation.234 | convolution fusion | flops 805306368 | bytes 7733248 | tf_op jit(solution)/shard_map/dot_general | solution.py:112
  181.7 3.5 %collective-permute-done.42 = bf16[16,2048]{1,0:T(8,128)(2,1)S(1)} collective-permute-done((bf16[16,2048]{1,0:T(8,128)(2,1)S(1)}, bf16[16,2048]{1,0:T(8,128)(2,1)S(1)}, u32[]{:S(2)}, u32[]{:S(2)}) %collective-permute-start.42) | collective-permute-done | bytes 65568 | tf_op jit(solution)/shard_map/ppermute | solution.py:21
  193.0 3.2 %collective-permute-done.46 = bf16[16,2048]{1,0:T(8,128)(2,1)S(1)} collective-permute-done((bf16[16,2048]{1,0:T(8,128)(2,1)S(1)}, bf16[16,2048]{1,0:T(8,128)(2,1)S(1)}, u32[]{:S(2)}, u32[]{:S(2)}) %collective-permute-start.46) | collective-permute-done | bytes 65568 | tf_op jit(solution)/shard_map/ppermute | solution.py:54
  200.1 5.7 %fusion.30 = f32[128,4,768]{2,0,1:T(8,128)S(1)} fusion(bf16[128,2048]{1,0:T(8,128)(2,1)S(1)} %fusion.3, bf16[2,2048,768]{2,1,0:T(8,128)(2,1)} %bitcast.507, bf16[2,2048,768]{2,1,0:T(8,128)(2,1)} %bitcast.514), kind=kOutput, calls=%fused_computation.67 | convolution fusion | flops 1635778560 | bytes 14680064 | tf_op jit(solution)/shard_map/td,def->tef/dot_general | solution.py:108
  206.3 3.8 %fusion.118 = f32[128,2048]{1,0:T(8,128)S(1)} fusion(bf16[128,1536]{0,1:T(8,128)(2,1)S(1)} %bitcast.436, bf16[1536,2048]{1,0:T(8,128)(2,1)} %bitcast.424), kind=kOutput, calls=%fused_computation.235 | convolution fusion | flops 805306368 | bytes 7733248 | tf_op jit(solution)/shard_map/dot_general | solution.py:112
  217.0 3.5 %collective-permute-done.51 = bf16[16,2048]{1,0:T(8,128)(2,1)S(1)} collective-permute-done((bf16[16,2048]{1,0:T(8,128)(2,1)S(1)}, bf16[16,2048]{1,0:T(8,128)(2,1)S(1)}, u32[]{:S(2)}, u32[]{:S(2)}) %collective-permute-start.51) | collective-permute-done | bytes 65568 | tf_op jit(solution)/shard_map/ppermute | solution.py:21
  225.2 3.1 %collective-permute-start.56 = (bf16[16,2048]{1,0:T(8,128)(2,1)S(1)}, bf16[16,2048]{1,0:T(8,128)(2,1)S(1)}, u32[]{:S(2)}, u32[]{:S(2)}) collective-permute-start(bf16[16,2048]{1,0:T(8,128)(2,1)S(1)} %get-tuple-element.7), channel_id=1, source_target_pairs={{0,14},{1,15},{2,12},{3,13},{4,10},{5,11},{6,8},{7,9},{8,22},{9,23... | collective-permute-start | bytes 196616 | tf_op jit(solution)/shard_map/ppermute | solution.py:54
  228.4 3.5 %collective-permute-done.55 = bf16[16,2048]{1,0:T(8,128)(2,1)S(1)} collective-permute-done((bf16[16,2048]{1,0:T(8,128)(2,1)S(1)}, bf16[16,2048]{1,0:T(8,128)(2,1)S(1)}, u32[]{:S(2)}, u32[]{:S(2)}) %collective-permute-start.55) | collective-permute-done | bytes 65568 | tf_op jit(solution)/shard_map/ppermute | solution.py:54
  235.3 5.7 %fusion.28 = f32[128,4,768]{2,0,1:T(8,128)S(1)} fusion(bf16[128,2048]{1,0:T(8,128)(2,1)S(1)} %fusion.1, bf16[2,2048,768]{2,1,0:T(8,128)(2,1)} %bitcast.508, bf16[2,2048,768]{2,1,0:T(8,128)(2,1)} %bitcast.515), kind=kOutput, calls=%fused_computation.65 | convolution fusion | flops 1635778560 | bytes 14680064 | tf_op jit(solution)/shard_map/td,def->tef/dot_general | solution.py:108
  241.5 3.8 %fusion.119 = f32[128,2048]{1,0:T(8,128)S(1)} fusion(bf16[128,1536]{0,1:T(8,128)(2,1)S(1)} %bitcast.437, bf16[1536,2048]{1,0:T(8,128)(2,1)} %bitcast.425), kind=kOutput, calls=%fused_computation.236 | convolution fusion | flops 805306368 | bytes 7733248 | tf_op jit(solution)/shard_map/dot_general | solution.py:112
  252.3 3.8 %collective-permute-done.60 = bf16[16,2048]{1,0:T(8,128)(2,1)S(1)} collective-permute-done((bf16[16,2048]{1,0:T(8,128)(2,1)S(1)}, bf16[16,2048]{1,0:T(8,128)(2,1)S(1)}, u32[]{:S(2)}, u32[]{:S(2)}) %collective-permute-start.60) | collective-permute-done | bytes 65568 | tf_op jit(solution)/shard_map/ppermute | solution.py:21
  (227 shorter events, 117.8 us)
Async XLA Ops:
  6.6 10.4 %collective-permute-start.1 = (bf16[17,2048]{1,0:T(8,128)(2,1)S(1)}, bf16[17,2048]{1,0:T(8,128)(2,1)S(1)}, u32[]{:S(2)}, u32[]{:S(2)}) collective-permute-start(bf16[17,2048]{1,0:T(8,128)(2,1)S(1)} %get-tuple-element.69), channel_id=1, source_target_pairs={{0,4},{1,5},{2,6},{3,7},{4,0},{5,1},{6,2},{7,3},{8,12},{9,13},{10,... | collective-permute-start | bytes 208904 | tf_op jit(solution)/shard_map/ppermute | solution.py:21
  9.2 7.8 %collective-permute-start.2 = (bf16[17,2048]{1,0:T(8,128)(2,1)S(1)}, bf16[17,2048]{1,0:T(8,128)(2,1)S(1)}, u32[]{:S(2)}, u32[]{:S(2)}) collective-permute-start(bf16[17,2048]{1,0:T(8,128)(2,1)S(1)} %get-tuple-element.69), channel_id=1, source_target_pairs={{0,6},{1,7},{2,4},{3,5},{4,2},{5,3},{6,0},{7,1},{8,14},{9,15},{10,... | collective-permute-start | bytes 208904 | tf_op jit(solution)/shard_map/ppermute | solution.py:21
  34.3 8.2 %collective-permute-start.6 = (bf16[16,2048]{1,0:T(8,128)(2,1)S(1)}, bf16[16,2048]{1,0:T(8,128)(2,1)S(1)}, u32[]{:S(2)}, u32[]{:S(2)}) collective-permute-start(bf16[16,2048]{1,0:T(8,128)(2,1)S(1)} %get-tuple-element.67), channel_id=1, source_target_pairs={{0,4},{1,5},{2,6},{3,7},{4,0},{5,1},{6,2},{7,3},{8,12},{9,13},{10,... | collective-permute-start | bytes 196616 | tf_op jit(solution)/shard_map/ppermute | solution.py:21
  35.7 6.8 %collective-permute-start.7 = (bf16[16,2048]{1,0:T(8,128)(2,1)S(1)}, bf16[16,2048]{1,0:T(8,128)(2,1)S(1)}, u32[]{:S(2)}, u32[]{:S(2)}) collective-permute-start(bf16[16,2048]{1,0:T(8,128)(2,1)S(1)} %get-tuple-element.66), channel_id=1, source_target_pairs={{0,6},{1,7},{2,4},{3,5},{4,2},{5,3},{6,0},{7,1},{8,14},{9,15},{10,... | collective-permute-start | bytes 196616 | tf_op jit(solution)/shard_map/ppermute | solution.py:21
  42.6 7.7 %collective-permute-start.8 = (bf16[16,2048]{1,0:T(8,128)(2,1)S(1)}, bf16[16,2048]{1,0:T(8,128)(2,1)S(1)}, u32[]{:S(2)}, u32[]{:S(2)}) collective-permute-start(bf16[16,2048]{1,0:T(8,128)(2,1)S(1)} %get-tuple-element.27), channel_id=1, source_target_pairs={{0,8},{1,9},{2,10},{3,11},{4,12},{5,13},{6,14},{7,15},{8,16},{9,17... | collective-permute-start | bytes 196616 | tf_op jit(solution)/shard_map/ppermute | solution.py:54
  46.4 8.9 %collective-permute-start.10 = (bf16[16,2048]{1,0:T(8,128)(2,1)S(1)}, bf16[16,2048]{1,0:T(8,128)(2,1)S(1)}, u32[]{:S(2)}, u32[]{:S(2)}) collective-permute-start(bf16[16,2048]{1,0:T(8,128)(2,1)S(1)} %get-tuple-element.27), channel_id=1, source_target_pairs={{0,12},{1,13},{2,14},{3,15},{4,8},{5,9},{6,10},{7,11},{8,20},{9,21... | collective-permute-start | bytes 196616 | tf_op jit(solution)/shard_map/ppermute | solution.py:54
  48.7 8.0 %collective-permute-start.11 = (bf16[16,2048]{1,0:T(8,128)(2,1)S(1)}, bf16[16,2048]{1,0:T(8,128)(2,1)S(1)}, u32[]{:S(2)}, u32[]{:S(2)}) collective-permute-start(bf16[16,2048]{1,0:T(8,128)(2,1)S(1)} %get-tuple-element.27), channel_id=1, source_target_pairs={{0,14},{1,15},{2,12},{3,13},{4,10},{5,11},{6,8},{7,9},{8,22},{9,23... | collective-permute-start | bytes 196616 | tf_op jit(solution)/shard_map/ppermute | solution.py:54
  71.4 8.3 %collective-permute-start.15 = (bf16[16,2048]{1,0:T(8,128)(2,1)S(1)}, bf16[16,2048]{1,0:T(8,128)(2,1)S(1)}, u32[]{:S(2)}, u32[]{:S(2)}) collective-permute-start(bf16[16,2048]{1,0:T(8,128)(2,1)S(1)} %get-tuple-element.62), channel_id=1, source_target_pairs={{0,4},{1,5},{2,6},{3,7},{4,0},{5,1},{6,2},{7,3},{8,12},{9,13},{10,... | collective-permute-start | bytes 196616 | tf_op jit(solution)/shard_map/ppermute | solution.py:21
  72.8 6.8 %collective-permute-start.16 = (bf16[16,2048]{1,0:T(8,128)(2,1)S(1)}, bf16[16,2048]{1,0:T(8,128)(2,1)S(1)}, u32[]{:S(2)}, u32[]{:S(2)}) collective-permute-start(bf16[16,2048]{1,0:T(8,128)(2,1)S(1)} %get-tuple-element.61), channel_id=1, source_target_pairs={{0,6},{1,7},{2,4},{3,5},{4,2},{5,3},{6,0},{7,1},{8,14},{9,15},{10,... | collective-permute-start | bytes 196616 | tf_op jit(solution)/shard_map/ppermute | solution.py:21
  79.7 7.7 %collective-permute-start.17 = (bf16[16,2048]{1,0:T(8,128)(2,1)S(1)}, bf16[16,2048]{1,0:T(8,128)(2,1)S(1)}, u32[]{:S(2)}, u32[]{:S(2)}) collective-permute-start(bf16[16,2048]{1,0:T(8,128)(2,1)S(1)} %get-tuple-element.23), channel_id=1, source_target_pairs={{0,8},{1,9},{2,10},{3,11},{4,12},{5,13},{6,14},{7,15},{8,16},{9,17... | collective-permute-start | bytes 196616 | tf_op jit(solution)/shard_map/ppermute | solution.py:54
  79.8 7.6 %collective-permute-start.18 = (bf16[16,2048]{1,0:T(8,128)(2,1)S(1)}, bf16[16,2048]{1,0:T(8,128)(2,1)S(1)}, u32[]{:S(2)}, u32[]{:S(2)}) collective-permute-start(bf16[16,2048]{1,0:T(8,128)(2,1)S(1)} %get-tuple-element.23), channel_id=1, source_target_pairs={{0,10},{1,11},{2,8},{3,9},{4,14},{5,15},{6,12},{7,13},{8,18},{9,19... | collective-permute-start | bytes 196616 | tf_op jit(solution)/shard_map/ppermute | solution.py:54
  82.4 7.7 %collective-permute-start.19 = (bf16[16,2048]{1,0:T(8,128)(2,1)S(1)}, bf16[16,2048]{1,0:T(8,128)(2,1)S(1)}, u32[]{:S(2)}, u32[]{:S(2)}) collective-permute-start(bf16[16,2048]{1,0:T(8,128)(2,1)S(1)} %get-tuple-element.23), channel_id=1, source_target_pairs={{0,12},{1,13},{2,14},{3,15},{4,8},{5,9},{6,10},{7,11},{8,20},{9,21... | collective-permute-start | bytes 196616 | tf_op jit(solution)/shard_map/ppermute | solution.py:54
  83.5 8.0 %collective-permute-start.20 = (bf16[16,2048]{1,0:T(8,128)(2,1)S(1)}, bf16[16,2048]{1,0:T(8,128)(2,1)S(1)}, u32[]{:S(2)}, u32[]{:S(2)}) collective-permute-start(bf16[16,2048]{1,0:T(8,128)(2,1)S(1)} %get-tuple-element.23), channel_id=1, source_target_pairs={{0,14},{1,15},{2,12},{3,13},{4,10},{5,11},{6,8},{7,9},{8,22},{9,23... | collective-permute-start | bytes 196616 | tf_op jit(solution)/shard_map/ppermute | solution.py:54
  106.1 8.3 %collective-permute-start.24 = (bf16[16,2048]{1,0:T(8,128)(2,1)S(1)}, bf16[16,2048]{1,0:T(8,128)(2,1)S(1)}, u32[]{:S(2)}, u32[]{:S(2)}) collective-permute-start(bf16[16,2048]{1,0:T(8,128)(2,1)S(1)} %get-tuple-element.57), channel_id=1, source_target_pairs={{0,4},{1,5},{2,6},{3,7},{4,0},{5,1},{6,2},{7,3},{8,12},{9,13},{10,... | collective-permute-start | bytes 196616 | tf_op jit(solution)/shard_map/ppermute | solution.py:21
  114.4 7.7 %collective-permute-start.26 = (bf16[16,2048]{1,0:T(8,128)(2,1)S(1)}, bf16[16,2048]{1,0:T(8,128)(2,1)S(1)}, u32[]{:S(2)}, u32[]{:S(2)}) collective-permute-start(bf16[16,2048]{1,0:T(8,128)(2,1)S(1)} %get-tuple-element.19), channel_id=1, source_target_pairs={{0,8},{1,9},{2,10},{3,11},{4,12},{5,13},{6,14},{7,15},{8,16},{9,17... | collective-permute-start | bytes 196616 | tf_op jit(solution)/shard_map/ppermute | solution.py:54
  118.2 7.7 %collective-permute-start.28 = (bf16[16,2048]{1,0:T(8,128)(2,1)S(1)}, bf16[16,2048]{1,0:T(8,128)(2,1)S(1)}, u32[]{:S(2)}, u32[]{:S(2)}) collective-permute-start(bf16[16,2048]{1,0:T(8,128)(2,1)S(1)} %get-tuple-element.19), channel_id=1, source_target_pairs={{0,12},{1,13},{2,14},{3,15},{4,8},{5,9},{6,10},{7,11},{8,20},{9,21... | collective-permute-start | bytes 196616 | tf_op jit(solution)/shard_map/ppermute | solution.py:54
  119.1 8.0 %collective-permute-start.29 = (bf16[16,2048]{1,0:T(8,128)(2,1)S(1)}, bf16[16,2048]{1,0:T(8,128)(2,1)S(1)}, u32[]{:S(2)}, u32[]{:S(2)}) collective-permute-start(bf16[16,2048]{1,0:T(8,128)(2,1)S(1)} %get-tuple-element.19), channel_id=1, source_target_pairs={{0,14},{1,15},{2,12},{3,13},{4,10},{5,11},{6,8},{7,9},{8,22},{9,23... | collective-permute-start | bytes 196616 | tf_op jit(solution)/shard_map/ppermute | solution.py:54
  141.8 8.3 %collective-permute-start.33 = (bf16[16,2048]{1,0:T(8,128)(2,1)S(1)}, bf16[16,2048]{1,0:T(8,128)(2,1)S(1)}, u32[]{:S(2)}, u32[]{:S(2)}) collective-permute-start(bf16[16,2048]{1,0:T(8,128)(2,1)S(1)} %get-tuple-element.52), channel_id=1, source_target_pairs={{0,4},{1,5},{2,6},{3,7},{4,0},{5,1},{6,2},{7,3},{8,12},{9,13},{10,... | collective-permute-start | bytes 196616 | tf_op jit(solution)/shard_map/ppermute | solution.py:21
  150.2 7.7 %collective-permute-start.35 = (bf16[16,2048]{1,0:T(8,128)(2,1)S(1)}, bf16[16,2048]{1,0:T(8,128)(2,1)S(1)}, u32[]{:S(2)}, u32[]{:S(2)}) collective-permute-start(bf16[16,2048]{1,0:T(8,128)(2,1)S(1)} %get-tuple-element.15), channel_id=1, source_target_pairs={{0,8},{1,9},{2,10},{3,11},{4,12},{5,13},{6,14},{7,15},{8,16},{9,17... | collective-permute-start | bytes 196616 | tf_op jit(solution)/shard_map/ppermute | solution.py:54
  150.7 7.2 %collective-permute-start.36 = (bf16[16,2048]{1,0:T(8,128)(2,1)S(1)}, bf16[16,2048]{1,0:T(8,128)(2,1)S(1)}, u32[]{:S(2)}, u32[]{:S(2)}) collective-permute-start(bf16[16,2048]{1,0:T(8,128)(2,1)S(1)} %get-tuple-element.15), channel_id=1, source_target_pairs={{0,10},{1,11},{2,8},{3,9},{4,14},{5,15},{6,12},{7,13},{8,18},{9,19... | collective-permute-start | bytes 196616 | tf_op jit(solution)/shard_map/ppermute | solution.py:54
  153.4 7.7 %collective-permute-start.37 = (bf16[16,2048]{1,0:T(8,128)(2,1)S(1)}, bf16[16,2048]{1,0:T(8,128)(2,1)S(1)}, u32[]{:S(2)}, u32[]{:S(2)}) collective-permute-start(bf16[16,2048]{1,0:T(8,128)(2,1)S(1)} %get-tuple-element.15), channel_id=1, source_target_pairs={{0,12},{1,13},{2,14},{3,15},{4,8},{5,9},{6,10},{7,11},{8,20},{9,21... | collective-permute-start | bytes 196616 | tf_op jit(solution)/shard_map/ppermute | solution.py:54
  154.7 7.9 %collective-permute-start.38 = (bf16[16,2048]{1,0:T(8,128)(2,1)S(1)}, bf16[16,2048]{1,0:T(8,128)(2,1)S(1)}, u32[]{:S(2)}, u32[]{:S(2)}) collective-permute-start(bf16[16,2048]{1,0:T(8,128)(2,1)S(1)} %get-tuple-element.15), channel_id=1, source_target_pairs={{0,14},{1,15},{2,12},{3,13},{4,10},{5,11},{6,8},{7,9},{8,22},{9,23... | collective-permute-start | bytes 196616 | tf_op jit(solution)/shard_map/ppermute | solution.py:54
  176.6 8.7 %collective-permute-start.42 = (bf16[16,2048]{1,0:T(8,128)(2,1)S(1)}, bf16[16,2048]{1,0:T(8,128)(2,1)S(1)}, u32[]{:S(2)}, u32[]{:S(2)}) collective-permute-start(bf16[16,2048]{1,0:T(8,128)(2,1)S(1)} %get-tuple-element.47), channel_id=1, source_target_pairs={{0,4},{1,5},{2,6},{3,7},{4,0},{5,1},{6,2},{7,3},{8,12},{9,13},{10,... | collective-permute-start | bytes 196616 | tf_op jit(solution)/shard_map/ppermute | solution.py:21
  185.3 7.7 %collective-permute-start.44 = (bf16[16,2048]{1,0:T(8,128)(2,1)S(1)}, bf16[16,2048]{1,0:T(8,128)(2,1)S(1)}, u32[]{:S(2)}, u32[]{:S(2)}) collective-permute-start(bf16[16,2048]{1,0:T(8,128)(2,1)S(1)} %get-tuple-element.11), channel_id=1, source_target_pairs={{0,8},{1,9},{2,10},{3,11},{4,12},{5,13},{6,14},{7,15},{8,16},{9,17... | collective-permute-start | bytes 196616 | tf_op jit(solution)/shard_map/ppermute | solution.py:54
  188.6 7.7 %collective-permute-start.46 = (bf16[16,2048]{1,0:T(8,128)(2,1)S(1)}, bf16[16,2048]{1,0:T(8,128)(2,1)S(1)}, u32[]{:S(2)}, u32[]{:S(2)}) collective-permute-start(bf16[16,2048]{1,0:T(8,128)(2,1)S(1)} %get-tuple-element.11), channel_id=1, source_target_pairs={{0,12},{1,13},{2,14},{3,15},{4,8},{5,9},{6,10},{7,11},{8,20},{9,21... | collective-permute-start | bytes 196616 | tf_op jit(solution)/shard_map/ppermute | solution.py:54
  190.0 7.9 %collective-permute-start.47 = (bf16[16,2048]{1,0:T(8,128)(2,1)S(1)}, bf16[16,2048]{1,0:T(8,128)(2,1)S(1)}, u32[]{:S(2)}, u32[]{:S(2)}) collective-permute-start(bf16[16,2048]{1,0:T(8,128)(2,1)S(1)} %get-tuple-element.11), channel_id=1, source_target_pairs={{0,14},{1,15},{2,12},{3,13},{4,10},{5,11},{6,8},{7,9},{8,22},{9,23... | collective-permute-start | bytes 196616 | tf_op jit(solution)/shard_map/ppermute | solution.py:54
  211.9 8.7 %collective-permute-start.51 = (bf16[16,2048]{1,0:T(8,128)(2,1)S(1)}, bf16[16,2048]{1,0:T(8,128)(2,1)S(1)}, u32[]{:S(2)}, u32[]{:S(2)}) collective-permute-start(bf16[16,2048]{1,0:T(8,128)(2,1)S(1)} %get-tuple-element.42), channel_id=1, source_target_pairs={{0,4},{1,5},{2,6},{3,7},{4,0},{5,1},{6,2},{7,3},{8,12},{9,13},{10,... | collective-permute-start | bytes 196616 | tf_op jit(solution)/shard_map/ppermute | solution.py:21
  220.6 7.7 %collective-permute-start.53 = (bf16[16,2048]{1,0:T(8,128)(2,1)S(1)}, bf16[16,2048]{1,0:T(8,128)(2,1)S(1)}, u32[]{:S(2)}, u32[]{:S(2)}) collective-permute-start(bf16[16,2048]{1,0:T(8,128)(2,1)S(1)} %get-tuple-element.7), channel_id=1, source_target_pairs={{0,8},{1,9},{2,10},{3,11},{4,12},{5,13},{6,14},{7,15},{8,16},{9,17... | collective-permute-start | bytes 196616 | tf_op jit(solution)/shard_map/ppermute | solution.py:54
  221.4 7.0 %collective-permute-start.54 = (bf16[16,2048]{1,0:T(8,128)(2,1)S(1)}, bf16[16,2048]{1,0:T(8,128)(2,1)S(1)}, u32[]{:S(2)}, u32[]{:S(2)}) collective-permute-start(bf16[16,2048]{1,0:T(8,128)(2,1)S(1)} %get-tuple-element.7), channel_id=1, source_target_pairs={{0,10},{1,11},{2,8},{3,9},{4,14},{5,15},{6,12},{7,13},{8,18},{9,19... | collective-permute-start | bytes 196616 | tf_op jit(solution)/shard_map/ppermute | solution.py:54
  223.8 8.0 %collective-permute-start.55 = (bf16[16,2048]{1,0:T(8,128)(2,1)S(1)}, bf16[16,2048]{1,0:T(8,128)(2,1)S(1)}, u32[]{:S(2)}, u32[]{:S(2)}) collective-permute-start(bf16[16,2048]{1,0:T(8,128)(2,1)S(1)} %get-tuple-element.7), channel_id=1, source_target_pairs={{0,12},{1,13},{2,14},{3,15},{4,8},{5,9},{6,10},{7,11},{8,20},{9,21... | collective-permute-start | bytes 196616 | tf_op jit(solution)/shard_map/ppermute | solution.py:54
  225.2 8.0 %collective-permute-start.56 = (bf16[16,2048]{1,0:T(8,128)(2,1)S(1)}, bf16[16,2048]{1,0:T(8,128)(2,1)S(1)}, u32[]{:S(2)}, u32[]{:S(2)}) collective-permute-start(bf16[16,2048]{1,0:T(8,128)(2,1)S(1)} %get-tuple-element.7), channel_id=1, source_target_pairs={{0,14},{1,15},{2,12},{3,13},{4,10},{5,11},{6,8},{7,9},{8,22},{9,23... | collective-permute-start | bytes 196616 | tf_op jit(solution)/shard_map/ppermute | solution.py:54
  247.8 8.3 %collective-permute-start.60 = (bf16[16,2048]{1,0:T(8,128)(2,1)S(1)}, bf16[16,2048]{1,0:T(8,128)(2,1)S(1)}, u32[]{:S(2)}, u32[]{:S(2)}) collective-permute-start(bf16[16,2048]{1,0:T(8,128)(2,1)S(1)} %get-tuple-element.37), channel_id=1, source_target_pairs={{0,4},{1,5},{2,6},{3,7},{4,0},{5,1},{6,2},{7,3},{8,12},{9,13},{10,... | collective-permute-start | bytes 196616 | tf_op jit(solution)/shard_map/ppermute | solution.py:21
  (32 other events, 157.5 us)
